TPU v7x, 256 devices: a whole 4x4x8 slice. The times are simulated.
256 devices in a mesh: gx: 32 (over z, y), gy: 4 (over x_lo, core), ga: 2 (over x_hi).
Axes of the slice: x: 4 (x_hi: 2, x_lo: 2; x = x_hi * 2 + x_lo), y: 4, z: 8, core: 2. Of those that a mesh axis runs over, the one named last changes fastest.
Arguments:
- velocity: float32 [2, 80, 64, 4096], P(None, None, ('gy', 'ga'), 'gx'), may hold values from -4 to 4
- tracers: float32 [2, 80, 64, 4096], P(None, None, ('gy', 'ga'), 'gx'), may hold values from -6 to 6
- mixing: float32 [80, 64, 4096], P(None, ('gy', 'ga'), 'gx'), may hold values from 0.05 to 400
- thickness: float32 [80], replicated, may hold values from 0.5 to 4
- coriolis: float32 [64], P(('gy', 'ga')), may hold values from -1.5 to 1.5
- land: int32 [64, 4096], P(('gy', 'ga'), 'gx'), may hold values 0 or 1
- bottom: int32 [64, 4096], P(('gy', 'ga'), 'gx'), may hold values from 70 to 80
- surface: float32 [64, 4096], P(('gy', 'ga'), 'gx'), may hold values from -4 to 4
- barotropic: float32 [2, 64, 4096], P(None, ('gy', 'ga'), 'gx'), may hold values from -3 to 3
Outputs:
- new_velocity: float32 [2, 80, 64, 4096], P(None, None, ('gy', 'ga'), 'gx')
- new_tracers: float32 [2, 80, 64, 4096], P(None, None, ('gy', 'ga'), 'gx')
- new_surface: float32 [64, 4096], P(('gy', 'ga'), 'gx')
- new_barotropic: float32 [2, 64, 4096], P(None, ('gy', 'ga'), 'gx')
All inputs are finite; a program needn't handle non-finite values. No bound on the sum of `land` on one device may be relied on, other than what follows from the above.
Results may differ from a plain program's by a relative error of at most 0.0003.
Values sent between devices are 32-bit elements; how exact they have to be, the bound alone decides.
No kernel may reach another device: no remote copies, remote signals or barrier semaphores. Data moves between devices by JAX's collectives and lax.ppermute only.
A program may use at most 64 MiB of HBM per device.

v0:
```python
import jax
import jax.numpy as jnp
from jax import lax
from jax.sharding import PartitionSpec as P

NSUB = 30


step_main = 0.1
visc_four = 0.02
diff_four = 0.02
press_scale = 0.02
step_baro = 0.1
grav_baro = 25.0
expand_temp = 0.2
contract_salt = 0.1


def padded_2(block, sides, width, periodic):
    for axis, dim in sides:
        count = lax.axis_size(axis)
        forward = [(i, i + 1) for i in range(count - 1)]
        if periodic:
            forward.append((count - 1, 0))
        backward = [(target, source) for source, target in forward]
        low = lax.ppermute(
            lax.slice_in_dim(block, block.shape[dim] - width, None, axis=dim), axis, forward
        )
        high = lax.ppermute(lax.slice_in_dim(block, 0, width, axis=dim), axis, backward)
        block = jnp.concatenate([low, block, high], axis=dim)
    return block


def laplace(quantity, wet_mask):
    centre = quantity[..., 1:-1, 1:-1]
    beside_all = (
        quantity[..., 1:-1, 2:]
        + quantity[..., 1:-1, :-2]
        + quantity[..., 2:, 1:-1]
        + quantity[..., :-2, 1:-1]
    )
    return (beside_all - 4.0 * centre) * wet_mask[..., 1:-1, 1:-1]


def diff_x(quantity):
    return 0.5 * (quantity[..., 2:-2, 3:-1] - quantity[..., 2:-2, 1:-3])


def diff_y(quantity):
    return 0.5 * (quantity[..., 3:-1, 2:-2] - quantity[..., 1:-3, 2:-2])


def tendency(padded, pressure, coriolis):
    east_vel = padded[0]
    north_vel = padded[1]
    wet_mask = padded[4]
    inner_wet = wet_mask[..., 2:-2, 2:-2]
    rotate = coriolis[:, None]
    changes = []
    for component in range(4):
        quantity = padded[component]
        advect = diff_x(east_vel * quantity) + diff_y(north_vel * quantity)
        smooth = laplace(laplace(quantity, wet_mask), wet_mask[..., 1:-1, 1:-1])
        if component == 0:
            change = rotate * north_vel[..., 2:-2, 2:-2] - diff_x(pressure) - visc_four * smooth
        elif component == 1:
            change = -rotate * east_vel[..., 2:-2, 2:-2] - diff_y(pressure) - visc_four * smooth
        else:
            change = -diff_four * smooth
        changes.append((change - advect) * inner_wet)
    return jnp.stack(changes)


def vertical_solve(provisional, mixing, wet_mask, thickness):
    levels = thickness.shape[0]
    tail_ones = (1,) * (mixing.ndim - 1)
    depth_col = thickness.reshape((levels,) + tail_ones)
    middle = (0.5 * (thickness[:-1] + thickness[1:])).reshape((levels - 1,) + tail_ones)
    coupling = mixing[:-1] * wet_mask[:-1] * wet_mask[1:] / middle
    zeros_row = jnp.zeros((1,) + mixing.shape[1:], jnp.float32)
    below_link = jnp.concatenate([coupling, zeros_row], axis=0)
    upper_link = jnp.concatenate([zeros_row, coupling], axis=0)
    diagonal = depth_col + upper_link + below_link
    source = depth_col[:, None] * provisional

    def forward(sweep, inputs):
        ratio_prev, value_prev = sweep
        upper_now, diag_now, below_now, source_now = inputs
        divisor = diag_now - upper_now * ratio_prev
        sweep_ratio = below_now / divisor
        sweep_value = (source_now + upper_now[None] * value_prev) / divisor[None]
        return ((sweep_ratio, sweep_value), (sweep_ratio, sweep_value))

    start_sweep = (
        jnp.zeros(mixing.shape[1:], jnp.float32),
        jnp.zeros(provisional.shape[1:], jnp.float32),
    )
    unused, (ratios, values) = lax.scan(
        forward, start_sweep, (upper_link, diagonal, below_link, source)
    )

    def backward(following, inputs):
        sweep_ratio, sweep_value = inputs
        result = sweep_value + sweep_ratio[None] * following
        return (result, result)

    unused_last, solved = lax.scan(
        backward, jnp.zeros(provisional.shape[1:], jnp.float32), (ratios, values), reverse=True
    )
    return solved


def zero_diff(quantity, along):
    extent = quantity.shape[along]
    ahead_part = lax.slice_in_dim(quantity, 1, extent, axis=along)
    behind = lax.slice_in_dim(quantity, 0, extent - 1, axis=along)
    zeros_row = jnp.zeros_like(lax.slice_in_dim(quantity, 0, 1, axis=along))
    return 0.5 * (
        jnp.concatenate([ahead_part, zeros_row], axis=along)
        - jnp.concatenate([zeros_row, behind], axis=along)
    )


def east_zero(quantity):
    return zero_diff(quantity, quantity.ndim - 1)


def north_zero(quantity):
    return zero_diff(quantity, quantity.ndim - 2)


def baro_step(baro_state, statics, east_diff, north_diff):
    height = baro_state[0]
    east_vel = baro_state[1]
    north_vel = baro_state[2]
    depth_ratio = statics[0]
    sea_mask = statics[1]
    rotate = statics[2]
    push_east = statics[3]
    push_north = statics[4]
    new_height = (
        height
        - step_baro * (east_diff(depth_ratio * east_vel) + north_diff(depth_ratio * north_vel))
    ) * sea_mask
    new_east = (
        east_vel + step_baro * (push_east + rotate * north_vel - grav_baro * east_diff(new_height))
    ) * sea_mask
    new_north = (
        north_vel
        + step_baro * (push_north - rotate * east_vel - grav_baro * north_diff(new_height))
    ) * sea_mask
    return jnp.stack([new_height, new_east, new_north])


def zonal_rims(stacked):
    return padded_2(stacked, (("gx", 3),), 2, True)


def merid_rims(stacked):
    return padded_2(stacked, ((("gy", "ga"), 2),), 2, False)


def baro_zonal(operand, halo_width):
    return padded_2(operand, (("gx", 2),), halo_width, True)


def baro_merid_all(operand, halo_width):
    return padded_2(operand, ((("gy", "ga"), 1),), halo_width, False)


def shards(velocity, tracers, mixing, thickness, coriolis, land, bottom, surface, barotropic):
    levels = thickness.shape[0]
    land_f = land.astype(jnp.float32)
    level_ids = lax.broadcasted_iota(jnp.int32, (levels,) + land.shape, 0)
    wet_mask = land_f[None] * (level_ids < bottom[None]).astype(jnp.float32)
    stacked = jnp.concatenate(
        [velocity * wet_mask[None], tracers * wet_mask[None], wet_mask[None]], axis=0
    )
    padded = merid_rims(zonal_rims(stacked))
    depth_col = thickness.reshape((levels, 1, 1))
    weight = (contract_salt * padded[3] - expand_temp * padded[2]) * padded[4] * depth_col
    pressure = press_scale * (jnp.cumsum(weight, axis=0) - weight + 0.5 * weight)
    growth = tendency(padded, pressure, coriolis)
    provisional = stacked[:4] + step_main * growth
    forcing = jnp.sum(depth_col * growth[:2], axis=1)
    depth_sum = jnp.sum(depth_col * wet_mask, axis=0)
    safe_depth = jnp.maximum(depth_sum, 1.0)
    statics = jnp.stack(
        [
            depth_sum / jnp.sum(thickness),
            land_f,
            coriolis[:, None] * jnp.ones_like(land_f),
            forcing[0] / safe_depth * land_f,
            forcing[1] / safe_depth * land_f,
        ]
    )
    combined = jnp.concatenate([statics, surface[None], barotropic], axis=0)
    per_halo = 1
    halo_width = 2 * per_halo

    def extend(operand):
        return baro_merid_all(baro_zonal(operand, halo_width), halo_width)

    extended = extend(combined)
    ext_statics = extended[:5]

    def run_group(ext_state, total_sum):
        ext_state = baro_step(ext_state, ext_statics, east_zero, north_zero)
        total_sum = total_sum + ext_state[1:, halo_width:-halo_width, halo_width:-halo_width]
        return (ext_state[:, halo_width:-halo_width, halo_width:-halo_width], total_sum)

    def loop_body(turn_index, loop_carry):
        state_now, total_sum = loop_carry
        return run_group(extend(state_now), total_sum)

    start_sum = jnp.zeros((2,) + combined.shape[1:], jnp.float32)
    state_now, total_sum = run_group(extended[5:], start_sum)
    state_now, total_sum = lax.fori_loop(1, NSUB // per_halo, loop_body, (state_now, total_sum))
    average = total_sum / NSUB
    solved = vertical_solve(jnp.moveaxis(provisional, 1, 0), mixing, wet_mask, thickness)
    thick_col = thickness.reshape((levels, 1, 1, 1))
    depth_mean = jnp.sum(thick_col * wet_mask[:, None] * solved[:, :2], axis=0) / safe_depth
    new_velocity = (
        jnp.moveaxis(solved[:, :2], 0, 1) - depth_mean[:, None] + average[:, None]
    ) * wet_mask[None]
    new_tracers = jnp.moveaxis(solved[:, 2:], 0, 1)
    return (new_velocity, new_tracers, state_now[0], state_now[1:])


def solution(mesh):
    return jax.shard_map(
        shards,
        mesh=mesh,
        in_specs=(
            P(None, None, ("gy", "ga"), "gx"),
            P(None, None, ("gy", "ga"), "gx"),
            P(None, ("gy", "ga"), "gx"),
            P(),
            P(("gy", "ga")),
            P(("gy", "ga"), "gx"),
            P(("gy", "ga"), "gx"),
            P(("gy", "ga"), "gx"),
            P(None, ("gy", "ga"), "gx"),
        ),
        out_specs=(
            P(None, None, ("gy", "ga"), "gx"),
            P(None, None, ("gy", "ga"), "gx"),
            P(("gy", "ga"), "gx"),
            P(None, ("gy", "ga"), "gx"),
        ),
        check_vma=False,
    )
```

profile of v0, /device:TPU:3, one launch (start us, length us, event | category | flops | bytes accessed | tf_op | source)
XLA Modules:
  0.0 843.8 jit_solution(10344189145541242960)
XLA Ops:
  10.7 6.8 collective-permute-start.5
  23.1 7.1 pad_maximum_fusion.13
  33.3 3.7 collective-permute-start.6
  40.2 3.5 collective-permute-start.7
  45.9 5.1 collective-permute-done.6
  54.0 7.1 collective-permute-done.7
  64.1 5.7 pad_maximum_fusion.7
  74.0 20.1 %add_multiply_fusion = f32[80,12,132]{2,1,0:T(8,128)S(1)} fusion(f32[80,12,132]{2,1,0:T(8,128)S(1)} %get-tuple-element.364), kind=kOutput, calls=%fused_computation.77 | output fusion | flops 10517760 | bytes 1013760 | tf_op jit(solution)/shard_map/jit(cumsum)/reduce_window_sum | solution.py:182
  94.1 4.6 fusion.22
  101.5 4.8 collective-permute-start.9
  110.1 106.0 %while.50 = (s32[]{:T(128)}, f32[8,128]{1,0:T(8,128)S(1)}, f32[4,8,128]{2,1,0:T(8,128)S(1)}, f32[80,8,128]{2,1,0:T(8,128)S(1)}, f32[80,4,8,128]{3,2,1,0:T(8,128)...) while((s32[]{:T(128)}, f32[8,128]{1,0:T(8,128)S(1)}, ...), condition=%wide.region_2.3_spmd.clone, body=%wide.region_1.2_spmd.clone.sunk | while | flops 20483 | bytes 107132 | solution.py:98
  216.8 112.9 %while.51 = (s32[]{:T(128)}, f32[4,8,128]{2,1,0:T(8,128)S(1)}, f32[80,4,8,128]{3,2,0,1:T(8,128)S(1)}, f32[80,4,8,128]{3,2,1,0:T(8,128)}, f32[80,8,128]{2,1,0:T(8,128)}, /*index=5*/s32[]{:T(128)}, s32[]{:T(128)}, s32[]{:T(128)}) while((s32[]{:T(128)}, f32[4,8,128]{2,1,0:T(8,128)S(1)}, f32[80,4,8,128]{3,2,0,1:T(8,128)S(1)}, ...), condition=%wide.region_4.5_spmd.clone, body=%wide.region_3.4_spmd.clone.sunk | while | flops 12292 | bytes 77939 | solution.py:107
  331.8 5.1 collective-permute-start.11
  338.5 502.9 %while.49 = (s32[]{:T(128)}, f32[3,8,128]{2,1,0:T(8,128)S(1)}, f32[2,8,128]{2,1,0:T(8,128)S(1)}, f32[5,12,132]{2,1,0:T(8,128)S(1)}, s32[]{:T(128)}) while((s32[]{:T(128)}, f32[3,8,128]{2,1,0:T(8,128)S(1)}, f32[2,8,128]{2,1,0:T(8,128)S(1)}, f32[5,12,132]{2,1,0:T(8,128)S(1)}, s32[]{:T(128)}) %tuple.156), condition=%wide.region_10.11_spmd, body=%wide.region_9.10_spmd.sunk | while | flops 70434 | bytes 391773 | solution.py:218
  341.1 3.4 collective-permute-done.1
  344.6 14.5 %collective-permute-start.2 = (f32[3,2,132]{2,1,0:T(2,128)S(1)}, f32[3,2,132]{2,1,0:T(2,128)S(1)}, u32[]{:S(2)}, u32[]{:S(2)}) collective-permute-start(f32[3,2,132]{2,1,0:T(2,128)S(1)} %get-tuple-element.528), channel_id=1, source_target_pairs={{1,0},{2,1},{3,2},{4,3},{5,4},{6,5},{7,6},{9,8},{10,9},{11,10},{12... | collective-permute-start | bytes 9512 | tf_op jit(solution)/shard_map/while/body/eval_jaxpr/ppermute | solution.py:29
  361.1 5.1 collective-permute-done.3
  369.4 3.4 collective-permute-done.1
  372.9 6.9 collective-permute-start.2
  381.7 4.5 collective-permute-done.3
  392.9 3.6 collective-permute-start.2
  399.8 3.3 collective-permute-done.3
  409.8 3.6 collective-permute-start.2
  416.6 3.3 collective-permute-done.3
  426.6 3.6 collective-permute-start.2
  433.4 3.3 collective-permute-done.3
  443.5 3.6 collective-permute-start.2
  460.3 3.6 collective-permute-start.2
  467.1 3.3 collective-permute-done.3
  477.1 3.6 collective-permute-start.2
  483.9 3.3 collective-permute-done.3
  494.0 3.6 collective-permute-start.2
  500.8 3.3 collective-permute-done.3
  510.8 3.6 collective-permute-start.2
  517.6 3.3 collective-permute-done.3
  527.6 3.6 collective-permute-start.2
  544.5 3.6 collective-permute-start.2
  551.3 3.3 collective-permute-done.3
  561.3 3.6 collective-permute-start.2
  568.1 3.3 collective-permute-done.3
  578.1 3.6 collective-permute-start.2
  585.0 3.3 collective-permute-done.3
  595.0 3.6 collective-permute-start.2
  601.8 3.3 collective-permute-done.3
  611.8 3.6 collective-permute-start.2
  628.7 3.6 collective-permute-start.2
  635.5 3.3 collective-permute-done.3
  645.5 3.6 collective-permute-start.2
  652.3 3.3 collective-permute-done.3
  662.3 3.6 collective-permute-start.2
  669.1 3.3 collective-permute-done.3
  679.2 3.6 collective-permute-start.2
  686.0 3.3 collective-permute-done.3
  696.0 3.6 collective-permute-start.2
  712.8 3.6 collective-permute-start.2
  719.6 3.3 collective-permute-done.3
  729.7 3.6 collective-permute-start.2
  736.5 3.3 collective-permute-done.3
  746.5 3.6 collective-permute-start.2
  763.3 3.6 collective-permute-start.2
  780.2 3.6 collective-permute-start.2
  797.0 3.6 collective-permute-start.2
  813.9 3.6 collective-permute-start.2
  830.7 3.6 collective-permute-start.2
  (945 shorter events, 574.7 us)
Async XLA Ops:
  8.8 12.0 %collective-permute-start.4 = (f32[5,80,8,2]{1,2,3,0:T(8,128)S(1)}, f32[5,80,8,2]{1,2,3,0:T(8,128)S(1)}, u32[]{:S(2)}, u32[]{:S(2)}) collective-permute-start(f32[5,80,8,2]{1,2,3,0:T(8,128)S(1)} %copy.16), channel_id=1, source_target_pairs={{0,8},{8,16},{16,24},{24,32},{32,40},{40,48},{48,56},{56,64},{64,7... | collective-permute-start | bytes 76808 | tf_op jit(solution)/shard_map/ppermute | solution.py:26
  10.7 10.7 %collective-permute-start.5 = (f32[5,80,8,2]{1,2,3,0:T(8,128)S(1)}, f32[5,80,8,2]{1,2,3,0:T(8,128)S(1)}, u32[]{:S(2)}, u32[]{:S(2)}) collective-permute-start(f32[5,80,8,2]{1,2,3,0:T(8,128)S(1)} %copy.17), channel_id=1, source_target_pairs={{8,0},{16,8},{24,16},{32,24},{40,32},{48,40},{56,48},{64,56},{72,6... | collective-permute-start | bytes 76808 | tf_op jit(solution)/shard_map/ppermute | solution.py:29
  33.3 17.6 %collective-permute-start.6 = (f32[5,80,2,132]{1,2,3,0:T(2,128)}, f32[5,80,2,132]{1,2,3,0:T(2,128)}, u32[]{:S(2)}, u32[]{:S(2)}) collective-permute-start(f32[5,80,2,132]{1,2,3,0:T(2,128)} %copy.20), channel_id=1, source_target_pairs={{0,1},{1,2},{2,3},{3,4},{4,5},{5,6},{6,7},{8,9},{9,10},{10,11},{11... | collective-permute-start | bytes 1267208 | tf_op jit(solution)/shard_map/ppermute | solution.py:26
  40.2 20.9 %collective-permute-start.7 = (f32[5,80,2,132]{1,2,3,0:T(2,128)}, f32[5,80,2,132]{1,2,3,0:T(2,128)}, u32[]{:S(2)}, u32[]{:S(2)}) collective-permute-start(f32[5,80,2,132]{1,2,3,0:T(2,128)} %copy.21), channel_id=1, source_target_pairs={{1,0},{2,1},{3,2},{4,3},{5,4},{6,5},{7,6},{9,8},{10,9},{11,10},{12... | collective-permute-start | bytes 1267208 | tf_op jit(solution)/shard_map/ppermute | solution.py:29
  101.4 228.3 %collective-permute-start.8 = (f32[8,8,2]{2,1,0:T(8,128)S(1)}, f32[8,8,2]{2,1,0:T(8,128)S(1)}, u32[]{:S(2)}, u32[]{:S(2)}) collective-permute-start(f32[8,8,2]{2,1,0:T(8,128)S(1)} %get-tuple-element.390), channel_id=1, source_target_pairs={{0,8},{8,16},{16,24},{24,32},{32,40},{40,48},{48,56},{56,64},{64,7... | collective-permute-start | bytes 1544 | tf_op jit(solution)/shard_map/ppermute | solution.py:26
  101.5 228.3 %collective-permute-start.9 = (f32[8,8,2]{2,1,0:T(8,128)S(1)}, f32[8,8,2]{2,1,0:T(8,128)S(1)}, u32[]{:S(2)}, u32[]{:S(2)}) collective-permute-start(f32[8,8,2]{2,1,0:T(8,128)S(1)} %get-tuple-element.391), channel_id=1, source_target_pairs={{8,0},{16,8},{24,16},{32,24},{40,32},{48,40},{56,48},{64,56},{72,6... | collective-permute-start | bytes 1544 | tf_op jit(solution)/shard_map/ppermute | solution.py:29
  329.9 7.2 collective-permute-start.10
  344.6 16.5 %collective-permute-start.2 = (f32[3,2,132]{2,1,0:T(2,128)S(1)}, f32[3,2,132]{2,1,0:T(2,128)S(1)}, u32[]{:S(2)}, u32[]{:S(2)}) collective-permute-start(f32[3,2,132]{2,1,0:T(2,128)S(1)} %get-tuple-element.528), channel_id=1, source_target_pairs={{1,0},{2,1},{3,2},{4,3},{5,4},{6,5},{7,6},{9,8},{10,9},{11,10},{12... | collective-permute-start | bytes 9512 | tf_op jit(solution)/shard_map/while/body/eval_jaxpr/ppermute | solution.py:29
  359.1 7.0 collective-permute-start.3
  372.9 8.8 %collective-permute-start.2 = (f32[3,2,132]{2,1,0:T(2,128)S(1)}, f32[3,2,132]{2,1,0:T(2,128)S(1)}, u32[]{:S(2)}, u32[]{:S(2)}) collective-permute-start(f32[3,2,132]{2,1,0:T(2,128)S(1)} %get-tuple-element.528), channel_id=1, source_target_pairs={{1,0},{2,1},{3,2},{4,3},{5,4},{6,5},{7,6},{9,8},{10,9},{11,10},{12... | collective-permute-start | bytes 9512 | tf_op jit(solution)/shard_map/while/body/eval_jaxpr/ppermute | solution.py:29
  379.8 6.5 collective-permute-start.3
  392.9 6.8 collective-permute-start.2
  396.6 6.5 collective-permute-start.3
  409.8 6.8 collective-permute-start.2
  413.4 6.5 collective-permute-start.3
  426.6 6.8 collective-permute-start.2
  430.3 6.5 collective-permute-start.3
  443.5 6.8 collective-permute-start.2
  447.1 6.5 collective-permute-start.3
  460.3 6.8 collective-permute-start.2
  463.9 6.5 collective-permute-start.3
  477.1 6.8 collective-permute-start.2
  480.8 6.5 collective-permute-start.3
  494.0 6.8 collective-permute-start.2
  497.6 6.5 collective-permute-start.3
  510.8 6.8 collective-permute-start.2
  514.5 6.5 collective-permute-start.3
  527.6 6.8 collective-permute-start.2
  531.3 6.5 collective-permute-start.3
  544.5 6.8 collective-permute-start.2
  548.1 6.5 collective-permute-start.3
  561.3 6.8 collective-permute-start.2
  565.0 6.5 collective-permute-start.3
  578.1 6.8 collective-permute-start.2
  581.8 6.5 collective-permute-start.3
  595.0 6.8 collective-permute-start.2
  598.6 6.5 collective-permute-start.3
  611.8 6.8 collective-permute-start.2
  615.5 6.5 collective-permute-start.3
  628.7 6.8 collective-permute-start.2
  632.3 6.5 collective-permute-start.3
  645.5 6.8 collective-permute-start.2
  649.1 6.5 collective-permute-start.3
  662.3 6.8 collective-permute-start.2
  666.0 6.5 collective-permute-start.3
  679.2 6.8 collective-permute-start.2
  682.8 6.5 collective-permute-start.3
  696.0 6.8 collective-permute-start.2
  699.7 6.5 collective-permute-start.3
  712.8 6.8 collective-permute-start.2
  716.5 6.5 collective-permute-start.3
  729.7 6.8 collective-permute-start.2
  733.3 6.5 collective-permute-start.3
  746.5 6.8 collective-permute-start.2
  750.2 6.5 collective-permute-start.3
  763.3 6.8 collective-permute-start.2
  767.0 6.5 collective-permute-start.3
  780.2 6.8 collective-permute-start.2
  797.0 6.8 collective-permute-start.2
  800.7 6.5 collective-permute-start.3
  813.9 6.8 collective-permute-start.2
  817.5 6.5 collective-permute-start.3
  830.7 6.8 collective-permute-start.2
  834.3 6.5 collective-permute-start.3
  (73 other events, 544.3 us)
where the time goes:
time: 861 us; the launch traced here: 844 us
  starting transfers between devices  278 us (32%)
  waiting for transfers between devices  242 us (28%)
  other arithmetic  236 us (27%)
  local copies, waits for them, and re-layouts  84.4 us (10%)
    ppermute x62, waiting for transfers between devices, padded_2(): lax.ppermute(lax.slice_in_dim(block, block.shape[dim] - width, None, axis...  195 us
    dynamic_update_slice x240, other arithmetic, vertical_solve(): lax.scan(forward, start_sweep, (upper_link, diagonal, below_link, source))  164 us
    ppermute x62, starting transfers between devices, padded_2(): lax.ppermute(lax.slice_in_dim(block, 0, width, axis=dim), axis, backward)  140 us
    ppermute x62, starting transfers between devices, padded_2(): lax.ppermute(lax.slice_in_dim(block, block.shape[dim] - width, None, axis...  138 us
    mul x80, local copies, waits for them, and re-layouts, backward(): result = sweep_value + sweep_ratio[None] * following  55 us
    ppermute x62, waiting for transfers between devices, padded_2(): lax.ppermute(lax.slice_in_dim(block, 0, width, axis=dim), axis, backward)  47.1 us
    another operation x1, other arithmetic, shards(): jnp.cumsum(weight, axis=0) - weight + 0.5 * weight  20.1 us
  transfers between devices with their start and end apart: 124, of which 90 were waited for; matrix products, arithmetic and copies ran while one was open for 28% of the time, Pallas kernels for 0%

commit v1 on v0

--- a/solution.py
+++ b/solution.py
@@ -2,6 +2,8 @@
 import jax.numpy as jnp
 from jax import lax
 from jax.sharding import PartitionSpec as P
+from jax.experimental import pallas as pl
+from jax.experimental.pallas import tpu as pltpu
 
 NSUB = 30
 
@@ -185,46 +187,141 @@
     forcing = jnp.sum(depth_col * growth[:2], axis=1)
     depth_sum = jnp.sum(depth_col * wet_mask, axis=0)
     safe_depth = jnp.maximum(depth_sum, 1.0)
-    statics = jnp.stack(
-        [
-            depth_sum / jnp.sum(thickness),
-            land_f,
-            coriolis[:, None] * jnp.ones_like(land_f),
-            forcing[0] / safe_depth * land_f,
-            forcing[1] / safe_depth * land_f,
-        ]
-    )
-    combined = jnp.concatenate([statics, surface[None], barotropic], axis=0)
-    per_halo = 1
-    halo_width = 2 * per_halo
-
-    def extend(operand):
-        return baro_merid_all(baro_zonal(operand, halo_width), halo_width)
-
-    extended = extend(combined)
-    ext_statics = extended[:5]
-
-    def run_group(ext_state, total_sum):
-        ext_state = baro_step(ext_state, ext_statics, east_zero, north_zero)
-        total_sum = total_sum + ext_state[1:, halo_width:-halo_width, halo_width:-halo_width]
-        return (ext_state[:, halo_width:-halo_width, halo_width:-halo_width], total_sum)
-
-    def loop_body(turn_index, loop_carry):
-        state_now, total_sum = loop_carry
-        return run_group(extend(state_now), total_sum)
-
-    start_sum = jnp.zeros((2,) + combined.shape[1:], jnp.float32)
-    state_now, total_sum = run_group(extended[5:], start_sum)
-    state_now, total_sum = lax.fori_loop(1, NSUB // per_halo, loop_body, (state_now, total_sum))
-    average = total_sum / NSUB
-    solved = vertical_solve(jnp.moveaxis(provisional, 1, 0), mixing, wet_mask, thickness)
-    thick_col = thickness.reshape((levels, 1, 1, 1))
-    depth_mean = jnp.sum(thick_col * wet_mask[:, None] * solved[:, :2], axis=0) / safe_depth
-    new_velocity = (
-        jnp.moveaxis(solved[:, :2], 0, 1) - depth_mean[:, None] + average[:, None]
-    ) * wet_mask[None]
-    new_tracers = jnp.moveaxis(solved[:, 2:], 0, 1)
-    return (new_velocity, new_tracers, state_now[0], state_now[1:])
+    dr = depth_sum / jnp.sum(thickness)
+    push_u = forcing[0] / safe_depth * land_f
+    push_v = forcing[1] / safe_depth * land_f
+    rotate = coriolis[:, None] * jnp.ones_like(land_f)
+    fields = jnp.stack([dr, land_f, rotate, push_u, push_v, surface, barotropic[0], barotropic[1]])
+    whole = gather_baro(fields)
+    baro_out = baro_run(whole)
+    rows = land.shape[0]
+    cols = land.shape[1]
+    merid = lax.axis_index(("gy", "ga"))
+    mine = lax.dynamic_slice_in_dim(baro_out, merid * rows, rows, axis=1)[:, :, BARO_HALO:BARO_HALO + cols]
+    average = mine[3:] / NSUB
+    solved = solve_columns(provisional, mixing, wet_mask, thickness)
+    thick_col = thickness.reshape((levels, 1, 1))
+    depth_mean = jnp.sum(thick_col[None] * wet_mask[None] * solved[:2], axis=1) / safe_depth
+    new_velocity = (solved[:2] - depth_mean[:, None] + average[:, None]) * wet_mask[None]
+    new_tracers = solved[2:]
+    return (new_velocity, new_tracers, mine[0], mine[1:3])
+
+
+BARO_HALO = 64
+
+
+def gather_baro(fields):
+    count = lax.axis_size("gx")
+    forward = [(i, (i + 1) % count) for i in range(count)]
+    backward = [(target, source) for source, target in forward]
+    low = lax.ppermute(fields[..., -BARO_HALO:], "gx", forward)
+    high = lax.ppermute(fields[..., :BARO_HALO], "gx", backward)
+    wide = jnp.concatenate([low, fields, high], axis=-1)
+    return lax.all_gather(wide, ("gy", "ga"), axis=1, tiled=True)
+
+
+def baro_kernel(f_ref, o_ref):
+    rows = f_ref.shape[1]
+    cols = f_ref.shape[2]
+    depth_ratio = f_ref[0]
+    sea_mask = f_ref[1]
+    rotate = f_ref[2]
+    push_east = f_ref[3]
+    push_north = f_ref[4]
+    row = lax.broadcasted_iota(jnp.int32, (rows, cols), 0)
+    not_last = row < rows - 1
+    not_first = row > 0
+
+    def east_diff(q):
+        return 0.5 * (pltpu.roll(q, cols - 1, 1) - pltpu.roll(q, 1, 1))
+
+    def north_diff(q):
+        ahead = jnp.where(not_last, pltpu.roll(q, rows - 1, 0), 0.0)
+        behind = jnp.where(not_first, pltpu.roll(q, 1, 0), 0.0)
+        return 0.5 * (ahead - behind)
+
+    def body(turn, carry):
+        height, east_vel, north_vel, sum_east, sum_north = carry
+        height = (
+            height
+            - step_baro * (east_diff(depth_ratio * east_vel) + north_diff(depth_ratio * north_vel))
+        ) * sea_mask
+        new_east = (
+            east_vel + step_baro * (push_east + rotate * north_vel - grav_baro * east_diff(height))
+        ) * sea_mask
+        new_north = (
+            north_vel
+            + step_baro * (push_north - rotate * east_vel - grav_baro * north_diff(height))
+        ) * sea_mask
+        return (height, new_east, new_north, sum_east + new_east, sum_north + new_north)
+
+    zeros = jnp.zeros((rows, cols), jnp.float32)
+    carry = (f_ref[5], f_ref[6], f_ref[7], zeros, zeros)
+    carry = lax.fori_loop(0, NSUB, body, carry)
+    for index in range(5):
+        o_ref[index] = carry[index]
+
+
+def baro_run(whole):
+    return pl.pallas_call(
+        baro_kernel,
+        out_shape=jax.ShapeDtypeStruct((5,) + whole.shape[1:], jnp.float32),
+        in_specs=[pl.BlockSpec(memory_space=pltpu.VMEM)],
+        out_specs=pl.BlockSpec(memory_space=pltpu.VMEM),
+    )(whole)
+
+
+def solve_kernel(th_ref, prov_ref, mix_ref, wet_ref, o_ref, ratio_ref):
+    levels = mix_ref.shape[0]
+    shape = mix_ref.shape[1:]
+    comps = prov_ref.shape[0]
+
+    def below_of(k):
+        nxt = jnp.minimum(k + 1, levels - 1)
+        middle = 0.5 * (th_ref[k] + th_ref[nxt])
+        coupling = mix_ref[k] * wet_ref[k] * wet_ref[nxt] / middle
+        return jnp.where(k < levels - 1, coupling, 0.0)
+
+    def forward(k, carry):
+        upper, ratio_prev, value_prev = carry
+        below = below_of(k)
+        depth = th_ref[k]
+        diagonal = depth + upper + below
+        divisor = diagonal - upper * ratio_prev
+        ratio = below / divisor
+        ratio_ref[k] = ratio
+        values = []
+        for c in range(comps):
+            value = (depth * prov_ref[c, k] + upper * value_prev[c]) / divisor
+            o_ref[c, k] = value
+            values.append(value)
+        return (below, ratio, tuple(values))
+
+    zeros = jnp.zeros(shape, jnp.float32)
+    lax.fori_loop(0, levels, forward, (zeros, zeros, (zeros,) * comps))
+
+    def backward(step, following):
+        k = levels - 1 - step
+        ratio = ratio_ref[k]
+        results = []
+        for c in range(comps):
+            result = o_ref[c, k] + ratio * following[c]
+            o_ref[c, k] = result
+            results.append(result)
+        return tuple(results)
+
+    lax.fori_loop(0, levels, backward, (zeros,) * comps)
+
+
+def solve_columns(provisional, mixing, wet_mask, thickness):
+    return pl.pallas_call(
+        solve_kernel,
+        out_shape=jax.ShapeDtypeStruct(provisional.shape, jnp.float32),
+        in_specs=[pl.BlockSpec(memory_space=pltpu.SMEM)]
+        + [pl.BlockSpec(memory_space=pltpu.VMEM)] * 3,
+        out_specs=pl.BlockSpec(memory_space=pltpu.VMEM),
+        scratch_shapes=[pltpu.VMEM(mixing.shape, jnp.float32)],
+    )(thickness, provisional, mixing, wet_mask)
 
 
 def solution(mesh):

time: 861 us -> 167 us (0.19)
  the two profiles are of different devices: /device:TPU:3 before, /device:TPU:1 now
where the time goes in v1:
time: 167 us; the launch traced here: 166 us
  other arithmetic  54.4 us (33%)
  blocking collectives  37.2 us (22%)
  local copies, waits for them, and re-layouts  21.2 us (13%)
  starting transfers between devices  19.1 us (11%)
  waiting for transfers between devices  18.5 us (11%)
  Pallas kernels  14.5 us (9%)
    all_gather x1, blocking collectives, gather_baro(): return lax.all_gather(wide, ('gy', 'ga'), axis=1, tiled=True)  37.2 us
    another operation x1, other arithmetic, shards(): jnp.cumsum(weight, axis=0) - weight + 0.5 * weight  20.2 us
    ppermute x2, starting transfers between devices, padded_2(): lax.ppermute(lax.slice_in_dim(block, 0, width, axis=dim), axis, backward)  15.5 us
    ppermute x2, waiting for transfers between devices, padded_2(): lax.ppermute(lax.slice_in_dim(block, block.shape[dim] - width, None, axis...  12 us
    pallas_call x1, Pallas kernels, baro_run(): pl.pallas_call(baro_kernel, out_shape=jax.ShapeDtypeStruct((5,) + whole.s...  9.35 us
    slice x1, other arithmetic, padded_2(): lax.slice_in_dim(block, block.shape[dim] - width, None, axis=dim)  6.5 us
    ppermute x2, waiting for transfers between devices, padded_2(): lax.ppermute(lax.slice_in_dim(block, 0, width, axis=dim), axis, backward)  6.44 us
    mul x2, other arithmetic, laplace(): return (beside_all - 4.0 * centre) * wet_mask[..., 1:-1, 1:-1]  6.38 us
  transfers between devices with their start and end apart: 6, of which 3 were waited for; matrix products, arithmetic and copies ran while one was open for 8% of the time, Pallas kernels for 3%

profile of v1, /device:TPU:1, one launch (start us, length us, event | category | flops | bytes accessed | tf_op | source)
XLA Modules:
  0.0 165.9 jit_solution(7384958031594380562)
XLA Ops:
  0.6 0.0 copy-start.4
  0.6 0.8 convert_element_type.4
  1.4 0.7 fusion.48
  2.1 1.6 broadcast_multiply_fusion.2
  3.7 0.0 copy-done.4
  3.7 1.3 broadcast_multiply_fusion.1
  5.0 0.0 copy-done.1
  5.0 0.1 pad_maximum_fusion.1
  5.1 1.7 %fusion.63 = (f32[5,80,8,2]{3,2,1,0:T(8,128)S(1)}, f32[5,80,8,2]{3,2,1,0:T(8,128)}) fusion(f32[5,80,8,128]{3,2,1,0:T(8,128)S(1)} %pad_maximum_fusion.1), kind=kLoop, calls=%fused_computation.145 | loop fusion | bytes 102400 | tf_op jit(solution)/shard_map/slice | solution.py:29
  6.9 2.0 %copy.14 = f32[5,80,8,2]{1,2,3,0:T(8,128)S(1)} copy(f32[5,80,8,2]{3,2,1,0:T(8,128)} %get-tuple-element.20) | data formatting | bytes 51200 | tf_op jit(solution)/shard_map/slice | solution.py:31
  8.8 8.9 %collective-permute-start.1 = (f32[5,80,8,2]{1,2,3,0:T(8,128)S(1)}, f32[5,80,8,2]{1,2,3,0:T(8,128)S(1)}, u32[]{:S(2)}, u32[]{:S(2)}) collective-permute-start(f32[5,80,8,2]{1,2,3,0:T(8,128)S(1)} %copy.14), channel_id=1, source_target_pairs={{8,0},{16,8},{24,16},{32,24},{40,32},{48,40},{56,48},{64,56},{72,6... | collective-permute-start | bytes 76808 | tf_op jit(solution)/shard_map/ppermute | solution.py:31
  17.7 0.5 copy.13
  18.3 0.1 collective-permute-start
  18.4 0.0 copy-done.6
  18.4 0.6 reduce_sum.38
  19.0 0.6 constant_dynamic-update-slice_fusion.6
  19.6 0.0 copy-done.5
  19.6 0.0 copy-done.9
  19.7 0.0 collective-permute-done.1
  19.7 0.6 copy.16
  20.3 4.2 %collective-permute-done = f32[5,80,8,2]{1,2,3,0:T(8,128)S(1)} collective-permute-done((f32[5,80,8,2]{1,2,3,0:T(8,128)S(1)}, f32[5,80,8,2]{1,2,3,0:T(8,128)S(1)}, u32[]{:S(2)}, u32[]{:S(2)}) %collective-permute-start) | collective-permute-done | bytes 25632 | tf_op jit(solution)/shard_map/ppermute | solution.py:28
  24.5 1.7 %copy.15 = f32[5,80,8,2]{3,2,1,0:T(8,128)} copy(f32[5,80,8,2]{1,2,3,0:T(8,128)S(1)} %collective-permute-done) | data formatting | bytes 51200 | tf_op jit(solution)/shard_map/ppermute | solution.py:28
  26.3 6.5 %pad_maximum_fusion.6 = (f32[5,80,2,132]{3,2,1,0:T(2,128)}, f32[5,80,2,132]{3,2,1,0:T(2,128)}) fusion(f32[5,80,8,2]{3,2,1,0:T(8,128)S(1)} %copy.16, f32[5,80,8,2]{3,2,1,0:T(8,128)} %copy.15, f32[1,80,8,128]{3,2,1,0:T(8,128)S(1)} %fusion.48, f32[2,80,8,128]{3,2,1,0:T(8,128)S(1)} %get-tuple-element.29, f32[2,80,8,128]{3,2,1,0:T(8,128)S(1)} %get-tuple-element.28), kind=kLoop, calls=%fused_computation.39 | loop fusion | flops 844800 | bytes 2534400 | tf_op jit(solution)/shard_map/slice | solution.py:29
  32.8 3.1 %copy.18 = f32[5,80,2,132]{1,2,3,0:T(2,128)} copy(f32[5,80,2,132]{3,2,1,0:T(2,128)} %get-tuple-element.18) | data formatting | bytes 844800 | tf_op jit(solution)/shard_map/slice | solution.py:31
  35.8 6.6 %collective-permute-start.3 = (f32[5,80,2,132]{1,2,3,0:T(2,128)}, f32[5,80,2,132]{1,2,3,0:T(2,128)}, u32[]{:S(2)}, u32[]{:S(2)}) collective-permute-start(f32[5,80,2,132]{1,2,3,0:T(2,128)} %copy.18), channel_id=1, source_target_pairs={{1,0},{2,1},{3,2},{4,3},{5,4},{6,5},{7,6},{9,8},{10,9},{11,10},{12... | collective-permute-start | bytes 1267208 | tf_op jit(solution)/shard_map/ppermute | solution.py:31
  42.5 3.1 %copy.17 = f32[5,80,2,132]{1,2,3,0:T(2,128)} copy(f32[5,80,2,132]{3,2,1,0:T(2,128)} %get-tuple-element.17) | data formatting | bytes 844800 | tf_op jit(solution)/shard_map/slice | solution.py:29
  45.5 2.1 %collective-permute-start.2 = (f32[5,80,2,132]{1,2,3,0:T(2,128)}, f32[5,80,2,132]{1,2,3,0:T(2,128)}, u32[]{:S(2)}, u32[]{:S(2)}) collective-permute-start(f32[5,80,2,132]{1,2,3,0:T(2,128)} %copy.17), channel_id=1, source_target_pairs={{0,1},{1,2},{2,3},{3,4},{4,5},{5,6},{6,7},{8,9},{9,10},{10,11},{11... | collective-permute-start | bytes 1267208 | tf_op jit(solution)/shard_map/ppermute | solution.py:28
  47.6 0.1 constant_dynamic-update-slice_fusion.4
  47.7 6.4 %collective-permute-done.3 = f32[5,80,2,132]{1,2,3,0:T(2,128)} collective-permute-done((f32[5,80,2,132]{1,2,3,0:T(2,128)}, f32[5,80,2,132]{1,2,3,0:T(2,128)}, u32[]{:S(2)}, u32[]{:S(2)}) %collective-permute-start.3) | collective-permute-done | bytes 422432 | tf_op jit(solution)/shard_map/ppermute | solution.py:31
  54.2 3.1 %copy.20 = f32[5,80,2,132]{3,2,1,0:T(2,128)} copy(f32[5,80,2,132]{1,2,3,0:T(2,128)} %collective-permute-done.3) | data formatting | bytes 844800 | tf_op jit(solution)/shard_map/ppermute | solution.py:31
  57.2 7.8 %collective-permute-done.2 = f32[5,80,2,132]{1,2,3,0:T(2,128)} collective-permute-done((f32[5,80,2,132]{1,2,3,0:T(2,128)}, f32[5,80,2,132]{1,2,3,0:T(2,128)}, u32[]{:S(2)}, u32[]{:S(2)}) %collective-permute-start.2) | collective-permute-done | bytes 422432 | tf_op jit(solution)/shard_map/ppermute | solution.py:28
  65.0 3.0 %copy.19 = f32[5,80,2,132]{3,2,1,0:T(2,128)} copy(f32[5,80,2,132]{1,2,3,0:T(2,128)} %collective-permute-done.2) | data formatting | bytes 844800 | tf_op jit(solution)/shard_map/ppermute | solution.py:28
  68.1 5.6 %pad_maximum_fusion = f32[5,80,12,132]{3,2,1,0:T(8,128)S(1)} fusion(f32[5,80,2,132]{3,2,1,0:T(2,128)} %copy.20, f32[5,80,8,2]{3,2,1,0:T(8,128)S(1)} %copy.16, f32[1,80,8,128]{3,2,1,0:T(8,128)S(1)} %fusion.48, f32[2,80,8,128]{3,2,1,0:T(8,128)S(1)} %get-tuple-element.29, f32[2,80,8,128]{3,2,1,0:T(8,128)S(1)} %get-tuple-element.28, f32[5,80,8,2]{3,2,1,0:T(8,128)} %copy.15, ...), kind=kLoop, calls=%fused_computation | loop fusion | flops 3801600 | bytes 5068800 | tf_op jit(solution)/shard_map/concatenate | solution.py:32
  73.7 0.7 fusion.62
  74.4 0.8 slice_bitcast_fusion
  75.2 20.2 %add_multiply_fusion = f32[80,12,132]{2,1,0:T(8,128)S(1)} fusion(f32[80,12,132]{2,1,0:T(8,128)S(1)} %get-tuple-element.11), kind=kOutput, calls=%fused_computation.33 | output fusion | flops 10517760 | bytes 1013760 | tf_op jit(solution)/shard_map/jit(cumsum)/reduce_window_sum | solution.py:184
  95.4 1.8 %fusion.1 = f32[80,10,130]{2,1,0:T(8,128)S(1)} fusion(f32[80,12,132]{2,1,0:T(8,128)S(1)} %get-tuple-element.15, f32[80,12,132]{2,1,0:T(8,128)S(1)} %get-tuple-element.13), kind=kLoop, calls=%fused_computation.4 | loop fusion | flops 624000 | bytes 2912000 | tf_op jit(solution)/shard_map/mul | solution.py:44
  97.2 4.6 %fusion.7 = (f32[80,10,130]{2,1,0:T(8,128)S(1)}, f32[80,10,130]{2,1,0:T(8,128)S(1)}, f32[80,10,130]{2,1,0:T(8,128)S(1)}) fusion(f32[80,12,132]{2,1,0:T(8,128)S(1)} %get-tuple-element.12, f32[80,12,132]{2,1,0:T(8,128)S(1)} %get-tuple-element.13, f32[80,12,132]{2,1,0:T(8,128)S(1)} %get-tuple-element.16, f32[80,12,132]{2,1,0:T(8,128)S(1)} %get-tuple-element.14), kind=kLoop, calls=%fused_computation.22 | loop fusion | flops 1872000 | bytes 7904000 | tf_op jit(solution)/shard_map/mul | solution.py:44
  101.8 1.2 fusion.40
  103.0 0.0 copy-start.8
  103.0 0.0 copy-start.7
  103.0 1.1 fusion.29
  104.1 0.2 fusion.8
  104.3 0.0 copy-done.8
  104.3 0.0 copy-done.7
  104.3 0.1 fusion.66
  104.4 0.0 collective-permute-start.5
  104.4 1.5 collective-permute-start.4
  105.9 0.8 fusion.13
  106.7 0.8 fusion.21
  107.5 1.3 maximum_add_fusion.prov_ref
  108.9 5.1 %shard_map.120 = f32[4,80,8,128]{3,2,1,0:T(8,128)} custom-call(f32[80]{0:T(128)} %th_ref.1, f32[4,80,8,128]{3,2,1,0:T(8,128)} %maximum_add_fusion.prov_ref, f32[80,8,128]{2,1,0:T(8,128)} %mix_ref.1, f32[80,8,128]{2,1,0:T(8,128)} %copy-done.1), custom_call_target="tpu_custom_call" | custom-call | tf_op jit(solution)/shard_map/pallas_call | solution.py:317
  114.0 0.0 copy-done.3
  114.0 1.3 multiply_reduce_fusion
  115.3 0.0 collective-permute-done.5
  115.3 0.0 collective-permute-done.4
  115.3 0.1 pad_maximum_fusion.7
  115.4 37.2 %all_gather.3.f_ref = f32[8,64,256]{2,1,0:T(8,128)} all-gather(f32[8,8,256]{2,1,0:T(8,128)S(1)} %pad_maximum_fusion.7), channel_id=1, replica_groups=mesh['gx'=32,'gy'=4,'ga'=2] {'gy','ga'}, dimensions={1}, use_global_device_ids=true | all-gather | bytes 589824 | tf_op jit(solution)/shard_map/all_gather | solution.py:220
  152.6 9.4 %shard_map.121 = f32[5,64,256]{2,1,0:T(8,128)} custom-call(f32[8,64,256]{2,1,0:T(8,128)} %all_gather.3.f_ref), custom_call_target="tpu_custom_call" | custom-call | tf_op jit(solution)/shard_map/pallas_call | solution.py:266
  161.9 1.4 dynamic-slice_bitcast_fusion
  163.3 1.4 fusion.65
  164.7 0.0 copy-done
  164.7 0.0 copy-done.2
  164.7 1.2 fusion.64
  (14 shorter events, 0.0 us)
Async XLA Ops:
  0.6 3.1 %copy-start.4 = (f32[2,80,8,128]{3,2,1,0:T(8,128)S(1)}, f32[2,80,8,128]{3,2,1,0:T(8,128)}, u32[]{:S(2)}) copy-start(f32[2,80,8,128]{3,2,1,0:T(8,128)} %param.9) | copy-start | bytes 1966084
  3.7 1.3 copy-start.1
  6.8 11.5 %copy-start.6 = (f32[80]{0:T(128)S(1)}, f32[80]{0:T(128)}, u32[]{:S(2)}) copy-start(f32[80]{0:T(128)} %th_ref.1) | copy-start | bytes 964
  6.8 12.8 %copy-start.5 = (s32[8,128]{1,0:T(8,128)S(1)}, s32[8,128]{1,0:T(8,128)}, u32[]{:S(2)}) copy-start(s32[8,128]{1,0:T(8,128)} %param.14) | copy-start | bytes 12292
  6.8 12.8 %copy-start.9 = (f32[8]{0:T(128)S(1)}, f32[8]{0:T(128)}, u32[]{:S(2)}) copy-start(f32[8]{0:T(128)} %param.13) | copy-start | bytes 100
  8.8 10.8 %collective-permute-start.1 = (f32[5,80,8,2]{1,2,3,0:T(8,128)S(1)}, f32[5,80,8,2]{1,2,3,0:T(8,128)S(1)}, u32[]{:S(2)}, u32[]{:S(2)}) collective-permute-start(f32[5,80,8,2]{1,2,3,0:T(8,128)S(1)} %copy.14), channel_id=1, source_target_pairs={{8,0},{16,8},{24,16},{32,24},{40,32},{48,40},{56,48},{64,56},{72,6... | collective-permute-start | bytes 76808 | tf_op jit(solution)/shard_map/ppermute | solution.py:31
  18.3 6.2 %collective-permute-start = (f32[5,80,8,2]{1,2,3,0:T(8,128)S(1)}, f32[5,80,8,2]{1,2,3,0:T(8,128)S(1)}, u32[]{:S(2)}, u32[]{:S(2)}) collective-permute-start(f32[5,80,8,2]{1,2,3,0:T(8,128)S(1)} %copy.13), channel_id=1, source_target_pairs={{0,8},{8,16},{16,24},{24,32},{32,40},{40,48},{48,56},{56,64},{64,7... | collective-permute-start | bytes 76808 | tf_op jit(solution)/shard_map/ppermute | solution.py:28
  35.8 18.3 %collective-permute-start.3 = (f32[5,80,2,132]{1,2,3,0:T(2,128)}, f32[5,80,2,132]{1,2,3,0:T(2,128)}, u32[]{:S(2)}, u32[]{:S(2)}) collective-permute-start(f32[5,80,2,132]{1,2,3,0:T(2,128)} %copy.18), channel_id=1, source_target_pairs={{1,0},{2,1},{3,2},{4,3},{5,4},{6,5},{7,6},{9,8},{10,9},{11,10},{12... | collective-permute-start | bytes 1267208 | tf_op jit(solution)/shard_map/ppermute | solution.py:31
  45.5 19.5 %collective-permute-start.2 = (f32[5,80,2,132]{1,2,3,0:T(2,128)}, f32[5,80,2,132]{1,2,3,0:T(2,128)}, u32[]{:S(2)}, u32[]{:S(2)}) collective-permute-start(f32[5,80,2,132]{1,2,3,0:T(2,128)} %copy.17), channel_id=1, source_target_pairs={{0,1},{1,2},{2,3},{3,4},{4,5},{5,6},{6,7},{8,9},{9,10},{10,11},{11... | collective-permute-start | bytes 1267208 | tf_op jit(solution)/shard_map/ppermute | solution.py:28
  103.0 1.3 copy-start.8
  103.0 1.3 copy-start.7
  104.4 10.9 %collective-permute-start.5 = (f32[8,8,64]{2,1,0:T(8,128)S(1)}, f32[8,8,64]{2,1,0:T(8,128)S(1)}, u32[]{:S(2)}, u32[]{:S(2)}) collective-permute-start(f32[8,8,64]{2,1,0:T(8,128)S(1)} %get-tuple-element.31), channel_id=1, source_target_pairs={{8,0},{16,8},{24,16},{32,24},{40,32},{48,40},{56,48},{64,56},{72,6... | collective-permute-start | bytes 49160 | tf_op jit(solution)/shard_map/ppermute | solution.py:218
  104.4 10.9 %collective-permute-start.4 = (f32[8,8,64]{2,1,0:T(8,128)S(1)}, f32[8,8,64]{2,1,0:T(8,128)S(1)}, u32[]{:S(2)}, u32[]{:S(2)}) collective-permute-start(f32[8,8,64]{2,1,0:T(8,128)S(1)} %get-tuple-element.30), channel_id=1, source_target_pairs={{0,8},{8,16},{16,24},{24,32},{32,40},{40,48},{48,56},{56,64},{64,7... | collective-permute-start | bytes 49160 | tf_op jit(solution)/shard_map/ppermute | solution.py:217
  108.8 5.1 %copy-start.3 = (f32[80,8,128]{2,1,0:T(8,128)S(1)}, f32[80,8,128]{2,1,0:T(8,128)}, u32[]{:S(2)}) copy-start(f32[80,8,128]{2,1,0:T(8,128)} %get-tuple-element.32) | copy-start | bytes 983044
  114.0 50.7 %copy-start = (f32[4,80,8,128]{3,2,1,0:T(8,128)S(1)}, f32[4,80,8,128]{3,2,1,0:T(8,128)}, u32[]{:S(2)}) copy-start(f32[4,80,8,128]{3,2,1,0:T(8,128)} %shard_map.120) | copy-start | bytes 3932164
  114.0 50.7 %copy-start.2 = (f32[80,8,128]{2,1,0:T(8,128)S(1)}, f32[80,8,128]{2,1,0:T(8,128)}, u32[]{:S(2)}) copy-start(f32[80,8,128]{2,1,0:T(8,128)} %copy-done.1) | copy-start | bytes 983044

commit v2 on v1

--- a/solution.py
+++ b/solution.py
@@ -193,12 +193,10 @@
     rotate = coriolis[:, None] * jnp.ones_like(land_f)
     fields = jnp.stack([dr, land_f, rotate, push_u, push_v, surface, barotropic[0], barotropic[1]])
     whole = gather_baro(fields)
-    baro_out = baro_run(whole)
     rows = land.shape[0]
-    cols = land.shape[1]
-    merid = lax.axis_index(("gy", "ga"))
-    mine = lax.dynamic_slice_in_dim(baro_out, merid * rows, rows, axis=1)[:, :, BARO_HALO:BARO_HALO + cols]
-    average = mine[3:] / NSUB
+    row_offset = jnp.full((1,), lax.axis_index(("gy", "ga")) * rows, jnp.int32)
+    mine = baro_run(whole, row_offset, land.shape[1])
+    average = mine[3:]
     solved = solve_columns(provisional, mixing, wet_mask, thickness)
     thick_col = thickness.reshape((levels, 1, 1))
     depth_mean = jnp.sum(thick_col[None] * wet_mask[None] * solved[:2], axis=1) / safe_depth
@@ -217,20 +215,35 @@
     low = lax.ppermute(fields[..., -BARO_HALO:], "gx", forward)
     high = lax.ppermute(fields[..., :BARO_HALO], "gx", backward)
     wide = jnp.concatenate([low, fields, high], axis=-1)
-    return lax.all_gather(wide, ("gy", "ga"), axis=1, tiled=True)
-
-
-def baro_kernel(f_ref, o_ref):
-    rows = f_ref.shape[1]
-    cols = f_ref.shape[2]
-    depth_ratio = f_ref[0]
-    sea_mask = f_ref[1]
-    rotate = f_ref[2]
-    push_east = f_ref[3]
-    push_north = f_ref[4]
+    merid = ("gy", "ga")
+    parts = lax.axis_size(merid)
+    blocks = [wide]
+    for shift in range(1, parts):
+        pairs = [(d, (d - shift) % parts) for d in range(parts)]
+        blocks.append(lax.ppermute(wide, merid, pairs))
+    return jnp.stack(blocks)
+
+
+def baro_kernel(off_ref, f_ref, o_ref):
+    parts = f_ref.shape[0]
+    block_rows = f_ref.shape[2]
+    rows = parts * block_rows
+    cols = f_ref.shape[3]
+
+    def field(index):
+        return jnp.concatenate([f_ref[part, index] for part in range(parts)], axis=0)
+
+    depth_ratio = field(0)
+    sea_mask = field(1)
+    rotate = field(2)
+    push_east = field(3)
+    push_north = field(4)
+    offset = off_ref[0]
+    last_local = rows - 1 - offset
+    first_local = jnp.where(offset == 0, 0, rows - offset)
     row = lax.broadcasted_iota(jnp.int32, (rows, cols), 0)
-    not_last = row < rows - 1
-    not_first = row > 0
+    not_last = row != last_local
+    not_first = row != first_local
 
     def east_diff(q):
         return 0.5 * (pltpu.roll(q, cols - 1, 1) - pltpu.roll(q, 1, 1))
@@ -256,19 +269,21 @@
         return (height, new_east, new_north, sum_east + new_east, sum_north + new_north)
 
     zeros = jnp.zeros((rows, cols), jnp.float32)
-    carry = (f_ref[5], f_ref[6], f_ref[7], zeros, zeros)
-    carry = lax.fori_loop(0, NSUB, body, carry)
+    carry = (field(5), field(6), field(7), zeros, zeros)
+    height, east_vel, north_vel, sum_east, sum_north = lax.fori_loop(0, NSUB, body, carry)
+    finals = (height, east_vel, north_vel, sum_east / NSUB, sum_north / NSUB)
+    out_cols = o_ref.shape[2]
     for index in range(5):
-        o_ref[index] = carry[index]
-
-
-def baro_run(whole):
+        o_ref[index] = pltpu.roll(finals[index][:block_rows], cols - BARO_HALO, 1)[:, :out_cols]
+
+
+def baro_run(whole, row_offset, out_cols):
     return pl.pallas_call(
         baro_kernel,
-        out_shape=jax.ShapeDtypeStruct((5,) + whole.shape[1:], jnp.float32),
-        in_specs=[pl.BlockSpec(memory_space=pltpu.VMEM)],
+        out_shape=jax.ShapeDtypeStruct((5, whole.shape[2], out_cols), jnp.float32),
+        in_specs=[pl.BlockSpec(memory_space=pltpu.SMEM), pl.BlockSpec(memory_space=pltpu.VMEM)],
         out_specs=pl.BlockSpec(memory_space=pltpu.VMEM),
-    )(whole)
+    )(row_offset, whole)
 
 
 def solve_kernel(th_ref, prov_ref, mix_ref, wet_ref, o_ref, ratio_ref):

time: 167 us -> 151 us (0.904)
  blocking collectives: 37.2 us -> 0 us
  starting transfers between devices: 19.1 us -> 36.5 us
  waiting for transfers between devices: 18.5 us -> 21.3 us
    all_gather x1 -> x0, blocking collectives: 37.2 us -> none  [gather_baro(): return lax.all_gather(wide, ('gy', 'ga'), axis=1, tiled=True)]
    ppermute x0 -> x7, starting transfers between devices: none -> 17.3 us  [gather_baro(): blocks.append(lax.ppermute(wide, merid, pairs))]
    ppermute x0 -> x7, waiting for transfers between devices: none -> 2.82 us  [gather_baro(): blocks.append(lax.ppermute(wide, merid, pairs))]
  transfers between devices with their start and end apart: 6 -> 13, of which waited for: 3 -> 4; matrix products, arithmetic and copies ran while one was open for 8% -> 9% of each run, Pallas kernels for 3% -> 3%
where the time goes in v2:
time: 151 us
  other arithmetic  55.6 us (37%)
  starting transfers between devices  36.5 us (24%)
  local copies, waits for them, and re-layouts  22.2 us (15%)
  waiting for transfers between devices  21.3 us (14%)
  Pallas kernels  14 us (9%)
    another operation x1, other arithmetic, shards(): jnp.cumsum(weight, axis=0) - weight + 0.5 * weight  20.2 us
    ppermute x7, starting transfers between devices, gather_baro(): blocks.append(lax.ppermute(wide, merid, pairs))  17.3 us
    ppermute x2, starting transfers between devices, padded_2(): lax.ppermute(lax.slice_in_dim(block, 0, width, axis=dim), axis, backward)  15.5 us
    ppermute x2, waiting for transfers between devices, padded_2(): lax.ppermute(lax.slice_in_dim(block, block.shape[dim] - width, None, axis...  12 us
    pallas_call x1, Pallas kernels, baro_run(): pl.pallas_call(baro_kernel, out_shape=jax.ShapeDtypeStruct((5, whole.shap...  8.88 us
    slice x1, other arithmetic, padded_2(): lax.slice_in_dim(block, block.shape[dim] - width, None, axis=dim)  6.48 us
    ppermute x2, waiting for transfers between devices, padded_2(): lax.ppermute(lax.slice_in_dim(block, 0, width, axis=dim), axis, backward)  6.44 us
    mul x2, other arithmetic, laplace(): return (beside_all - 4.0 * centre) * wet_mask[..., 1:-1, 1:-1]  6.38 us
  transfers between devices with their start and end apart: 13, of which 4 were waited for; matrix products, arithmetic and copies ran while one was open for 9% of the time, Pallas kernels for 3%

profile of v2, /device:TPU:1, one launch (start us, length us, event | category | flops | bytes accessed | tf_op | source)
XLA Modules:
  0.0 150.6 jit_solution(10749083003333556573)
XLA Ops:
  0.6 0.8 convert_element_type.4
  1.4 0.7 fusion.48
  2.1 1.6 %broadcast_multiply_fusion.2 = (f32[80,8,128]{2,1,0:T(8,128)}, f32[8,128]{1,0:T(8,128)S(1)}, f32[80,8,128]{2,1,0:T(8,128)S(1)}) fusion(f32[80]{0:T(128)} %th_ref.1, f32[8,128]{1,0:T(8,128)S(1)} %convert_element_type.4, s32[8,128]{1,0:T(8,128)} %param.15), kind=kLoop, calls=%fused_computation.116 | loop fusion | flops 326656 | bytes 667968 | tf_op jit(solution)/shard_map/mul | solution.py:202
  3.7 1.3 broadcast_multiply_fusion.1
  5.0 0.1 pad_maximum_fusion.1
  5.1 1.7 %fusion.63 = (f32[5,80,8,2]{3,2,1,0:T(8,128)S(1)}, f32[5,80,8,2]{3,2,1,0:T(8,128)}) fusion(f32[5,80,8,128]{3,2,1,0:T(8,128)S(1)} %pad_maximum_fusion.1), kind=kLoop, calls=%fused_computation.152 | loop fusion | bytes 102400 | tf_op jit(solution)/shard_map/slice | solution.py:29
  6.9 2.0 %copy.14 = f32[5,80,8,2]{1,2,3,0:T(8,128)S(1)} copy(f32[5,80,8,2]{3,2,1,0:T(8,128)} %get-tuple-element.22) | data formatting | bytes 51200 | tf_op jit(solution)/shard_map/slice | solution.py:31
  8.9 8.9 %collective-permute-start.1 = (f32[5,80,8,2]{1,2,3,0:T(8,128)S(1)}, f32[5,80,8,2]{1,2,3,0:T(8,128)S(1)}, u32[]{:S(2)}, u32[]{:S(2)}) collective-permute-start(f32[5,80,8,2]{1,2,3,0:T(8,128)S(1)} %copy.14), channel_id=1, source_target_pairs={{8,0},{16,8},{24,16},{32,24},{40,32},{48,40},{56,48},{64,56},{72,6... | collective-permute-start | bytes 76808 | tf_op jit(solution)/shard_map/ppermute | solution.py:31
  17.8 0.5 copy.13
  18.3 0.1 collective-permute-start
  18.4 0.6 reduce_sum.38
  19.0 0.6 constant_dynamic-update-slice_fusion.6
  19.7 0.0 collective-permute-done.1
  19.7 0.6 copy.16
  20.3 4.2 %collective-permute-done = f32[5,80,8,2]{1,2,3,0:T(8,128)S(1)} collective-permute-done((f32[5,80,8,2]{1,2,3,0:T(8,128)S(1)}, f32[5,80,8,2]{1,2,3,0:T(8,128)S(1)}, u32[]{:S(2)}, u32[]{:S(2)}) %collective-permute-start) | collective-permute-done | bytes 25632 | tf_op jit(solution)/shard_map/ppermute | solution.py:28
  24.5 1.8 %copy.15 = f32[5,80,8,2]{3,2,1,0:T(8,128)} copy(f32[5,80,8,2]{1,2,3,0:T(8,128)S(1)} %collective-permute-done) | data formatting | bytes 51200 | tf_op jit(solution)/shard_map/ppermute | solution.py:28
  26.3 6.5 %pad_maximum_fusion.6 = (f32[5,80,2,132]{3,2,1,0:T(2,128)}, f32[5,80,2,132]{3,2,1,0:T(2,128)}) fusion(f32[5,80,8,2]{3,2,1,0:T(8,128)S(1)} %copy.16, f32[5,80,8,2]{3,2,1,0:T(8,128)} %copy.15, f32[1,80,8,128]{3,2,1,0:T(8,128)S(1)} %fusion.48, f32[2,80,8,128]{3,2,1,0:T(8,128)S(1)} %get-tuple-element.29, f32[2,80,8,128]{3,2,1,0:T(8,128)S(1)} %get-tuple-element.28), kind=kLoop, calls=%fused_computation.39 | loop fusion | flops 844800 | bytes 2534400 | tf_op jit(solution)/shard_map/slice | solution.py:29
  32.8 3.1 %copy.18 = f32[5,80,2,132]{1,2,3,0:T(2,128)} copy(f32[5,80,2,132]{3,2,1,0:T(2,128)} %get-tuple-element.20) | data formatting | bytes 844800 | tf_op jit(solution)/shard_map/slice | solution.py:31
  35.8 6.6 %collective-permute-start.3 = (f32[5,80,2,132]{1,2,3,0:T(2,128)}, f32[5,80,2,132]{1,2,3,0:T(2,128)}, u32[]{:S(2)}, u32[]{:S(2)}) collective-permute-start(f32[5,80,2,132]{1,2,3,0:T(2,128)} %copy.18), channel_id=1, source_target_pairs={{1,0},{2,1},{3,2},{4,3},{5,4},{6,5},{7,6},{9,8},{10,9},{11,10},{12... | collective-permute-start | bytes 1267208 | tf_op jit(solution)/shard_map/ppermute | solution.py:31
  42.5 3.1 %copy.17 = f32[5,80,2,132]{1,2,3,0:T(2,128)} copy(f32[5,80,2,132]{3,2,1,0:T(2,128)} %get-tuple-element.19) | data formatting | bytes 844800 | tf_op jit(solution)/shard_map/slice | solution.py:29
  45.5 2.1 %collective-permute-start.2 = (f32[5,80,2,132]{1,2,3,0:T(2,128)}, f32[5,80,2,132]{1,2,3,0:T(2,128)}, u32[]{:S(2)}, u32[]{:S(2)}) collective-permute-start(f32[5,80,2,132]{1,2,3,0:T(2,128)} %copy.17), channel_id=1, source_target_pairs={{0,1},{1,2},{2,3},{3,4},{4,5},{5,6},{6,7},{8,9},{9,10},{10,11},{11... | collective-permute-start | bytes 1267208 | tf_op jit(solution)/shard_map/ppermute | solution.py:28
  47.6 0.1 constant_dynamic-update-slice_fusion.4
  47.7 6.4 %collective-permute-done.3 = f32[5,80,2,132]{1,2,3,0:T(2,128)} collective-permute-done((f32[5,80,2,132]{1,2,3,0:T(2,128)}, f32[5,80,2,132]{1,2,3,0:T(2,128)}, u32[]{:S(2)}, u32[]{:S(2)}) %collective-permute-start.3) | collective-permute-done | bytes 422432 | tf_op jit(solution)/shard_map/ppermute | solution.py:31
  54.1 3.1 %copy.20 = f32[5,80,2,132]{3,2,1,0:T(2,128)} copy(f32[5,80,2,132]{1,2,3,0:T(2,128)} %collective-permute-done.3) | data formatting | bytes 844800 | tf_op jit(solution)/shard_map/ppermute | solution.py:31
  57.2 7.8 %collective-permute-done.2 = f32[5,80,2,132]{1,2,3,0:T(2,128)} collective-permute-done((f32[5,80,2,132]{1,2,3,0:T(2,128)}, f32[5,80,2,132]{1,2,3,0:T(2,128)}, u32[]{:S(2)}, u32[]{:S(2)}) %collective-permute-start.2) | collective-permute-done | bytes 422432 | tf_op jit(solution)/shard_map/ppermute | solution.py:28
  65.0 3.0 %copy.19 = f32[5,80,2,132]{3,2,1,0:T(2,128)} copy(f32[5,80,2,132]{1,2,3,0:T(2,128)} %collective-permute-done.2) | data formatting | bytes 844800 | tf_op jit(solution)/shard_map/ppermute | solution.py:28
  68.1 5.6 %pad_maximum_fusion = f32[5,80,12,132]{3,2,1,0:T(8,128)S(1)} fusion(f32[5,80,2,132]{3,2,1,0:T(2,128)} %copy.20, f32[5,80,8,2]{3,2,1,0:T(8,128)S(1)} %copy.16, f32[1,80,8,128]{3,2,1,0:T(8,128)S(1)} %fusion.48, f32[2,80,8,128]{3,2,1,0:T(8,128)S(1)} %get-tuple-element.29, f32[2,80,8,128]{3,2,1,0:T(8,128)S(1)} %get-tuple-element.28, f32[5,80,8,2]{3,2,1,0:T(8,128)} %copy.15, ...), kind=kLoop, calls=%fused_computation | loop fusion | flops 3801600 | bytes 5068800 | tf_op jit(solution)/shard_map/concatenate | solution.py:32
  73.7 2.2 %fusion.62 = (f32[80,12,132]{2,1,0:T(8,128)}, f32[80,12,132]{2,1,0:T(8,128)S(1)}, f32[80,12,132]{2,1,0:T(8,128)}, f32[80,12,132]{2,1,0:T(8,128)S(1)}, f32[80,12,...) fusion(f32[5,80,12,132]{3,2,1,0:T(8,128)S(1)} %pad_maximum_fusion, ...), kind=kLoop, calls=%fused_computation.151 | loop fusion | flops 1520640 | bytes 6589760 | tf_op jit(solution)/shard_map/mul | solution.py:64
  75.9 0.8 slice_bitcast_fusion
  76.7 20.2 %add_multiply_fusion = f32[80,12,132]{2,1,0:T(8,128)S(1)} fusion(f32[80,12,132]{2,1,0:T(8,128)S(1)} %get-tuple-element.13), kind=kOutput, calls=%fused_computation.33 | output fusion | flops 10517760 | bytes 1013760 | tf_op jit(solution)/shard_map/jit(cumsum)/reduce_window_sum | solution.py:184
  96.9 1.8 %fusion.1 = f32[80,10,130]{2,1,0:T(8,128)S(1)} fusion(f32[80,12,132]{2,1,0:T(8,128)S(1)} %get-tuple-element.17, f32[80,12,132]{2,1,0:T(8,128)S(1)} %get-tuple-element.15), kind=kLoop, calls=%fused_computation.4 | loop fusion | flops 624000 | bytes 2912000 | tf_op jit(solution)/shard_map/mul | solution.py:44
  98.7 4.6 %fusion.7 = (f32[80,10,130]{2,1,0:T(8,128)S(1)}, f32[80,10,130]{2,1,0:T(8,128)S(1)}, f32[80,10,130]{2,1,0:T(8,128)S(1)}) fusion(f32[80,12,132]{2,1,0:T(8,128)S(1)} %get-tuple-element.14, f32[80,12,132]{2,1,0:T(8,128)S(1)} %get-tuple-element.15, f32[80,12,132]{2,1,0:T(8,128)S(1)} %get-tuple-element.18, f32[80,12,132]{2,1,0:T(8,128)S(1)} %get-tuple-element.16), kind=kLoop, calls=%fused_computation.22 | loop fusion | flops 1872000 | bytes 7904000 | tf_op jit(solution)/shard_map/mul | solution.py:44
  103.3 1.1 fusion.40
  104.4 0.2 copy-done.3
  104.6 1.1 fusion.29
  105.7 0.2 fusion.8
  105.9 0.1 fusion.65
  106.0 0.0 collective-permute-start.5
  106.1 1.5 collective-permute-start.4
  107.5 0.9 fusion.13
  108.4 0.8 fusion.21
  109.2 1.3 maximum_add_fusion.prov_ref
  110.5 5.1 %shard_map.120 = f32[4,80,8,128]{3,2,1,0:T(8,128)} custom-call(f32[80]{0:T(128)} %th_ref.1, f32[4,80,8,128]{3,2,1,0:T(8,128)} %maximum_add_fusion.prov_ref, f32[80,8,128]{2,1,0:T(8,128)} %mix_ref.1, f32[80,8,128]{2,1,0:T(8,128)} %copy-done.1), custom_call_target="tpu_custom_call" | custom-call | tf_op jit(solution)/shard_map/pallas_call | solution.py:332
  115.6 0.0 collective-permute-done.5
  115.6 0.0 collective-permute-done.4
  115.6 0.1 bitcast_dynamic-update-slice_fusion.7
  115.7 0.0 copy-start.2
  115.8 3.5 %collective-permute-start.6 = (f32[8,8,256]{2,1,0:T(8,128)S(1)}, f32[8,8,256]{2,1,0:T(8,128)S(1)}, u32[]{:S(2)}, u32[]{:S(2)}) collective-permute-start(f32[8,8,256]{2,1,0:T(8,128)S(1)} %get-tuple-element.5), channel_id=1, source_target_pairs={{0,7},{1,0},{2,1},{3,2},{4,3},{5,4},{6,5},{7,6},{8,15},{9,8},{10,9... | collective-permute-start | bytes 196616 | tf_op jit(solution)/shard_map/ppermute | solution.py:223
  119.2 1.2 multiply_reduce_fusion
  120.4 0.2 collective-permute-start.7
  120.6 9.1 %collective-permute-start.8 = (f32[8,8,256]{2,1,0:T(8,128)S(1)}, f32[8,8,256]{2,1,0:T(8,128)S(1)}, u32[]{:S(2)}, u32[]{:S(2)}) collective-permute-start(f32[8,8,256]{2,1,0:T(8,128)S(1)} %get-tuple-element.5), channel_id=1, source_target_pairs={{0,5},{1,6},{2,7},{3,0},{4,1},{5,2},{6,3},{7,4},{8,13},{9,14},{10,... | collective-permute-start | bytes 196616 | tf_op jit(solution)/shard_map/ppermute | solution.py:223
  129.8 0.0 collective-permute-start.9
  129.8 1.3 collective-permute-start.10
  131.1 0.0 collective-permute-done.6
  131.1 0.7 collective-permute-start.11
  131.8 2.5 %collective-permute-start.12 = (f32[8,8,256]{2,1,0:T(8,128)S(1)}, f32[8,8,256]{2,1,0:T(8,128)S(1)}, u32[]{:S(2)}, u32[]{:S(2)}) collective-permute-start(f32[8,8,256]{2,1,0:T(8,128)S(1)} %get-tuple-element.5), channel_id=1, source_target_pairs={{0,1},{1,2},{2,3},{3,4},{4,5},{5,6},{6,7},{7,0},{8,9},{9,10},{10,1... | collective-permute-start | bytes 196616 | tf_op jit(solution)/shard_map/ppermute | solution.py:223
  134.3 0.0 collective-permute-done.10
  134.3 0.0 collective-permute-done.11
  134.4 2.8 %collective-permute-done.12 = f32[8,8,256]{2,1,0:T(8,128)S(1)} collective-permute-done((f32[8,8,256]{2,1,0:T(8,128)S(1)}, f32[8,8,256]{2,1,0:T(8,128)S(1)}, u32[]{:S(2)}, u32[]{:S(2)}) %collective-permute-start.12) | collective-permute-done | bytes 65568 | tf_op jit(solution)/shard_map/ppermute | solution.py:223
  137.2 0.8 copy-done.6
  138.0 8.9 %shard_map.121 = f32[5,8,128]{2,1,0:T(8,128)} custom-call(s32[1]{0:T(128)} %bitcast.9.off_ref, f32[8,8,8,256]{3,2,1,0:T(8,128)} %copy-done.6), custom_call_target="tpu_custom_call" | custom-call | tf_op jit(solution)/shard_map/pallas_call | solution.py:281
  146.8 1.3 slice_bitcast_fusion.5
  148.1 1.3 fusion.66
  149.4 1.2 fusion.64
  (40 shorter events, 0.1 us)
Async XLA Ops:
  0.6 3.1 %copy-start.7 = (f32[2,80,8,128]{3,2,1,0:T(8,128)S(1)}, f32[2,80,8,128]{3,2,1,0:T(8,128)}, u32[]{:S(2)}) copy-start(f32[2,80,8,128]{3,2,1,0:T(8,128)} %param.9) | copy-start | bytes 1966084
  3.7 1.3 copy-start.1
  6.9 11.5 %copy-start.9 = (f32[80]{0:T(128)S(1)}, f32[80]{0:T(128)}, u32[]{:S(2)}) copy-start(f32[80]{0:T(128)} %th_ref.1) | copy-start | bytes 964
  6.9 12.8 %copy-start.8 = (s32[8,128]{1,0:T(8,128)S(1)}, s32[8,128]{1,0:T(8,128)}, u32[]{:S(2)}) copy-start(s32[8,128]{1,0:T(8,128)} %param.14) | copy-start | bytes 12292
  6.9 12.8 %copy-start.12 = (f32[8]{0:T(128)S(1)}, f32[8]{0:T(128)}, u32[]{:S(2)}) copy-start(f32[8]{0:T(128)} %param.13) | copy-start | bytes 100
  8.9 10.8 %collective-permute-start.1 = (f32[5,80,8,2]{1,2,3,0:T(8,128)S(1)}, f32[5,80,8,2]{1,2,3,0:T(8,128)S(1)}, u32[]{:S(2)}, u32[]{:S(2)}) collective-permute-start(f32[5,80,8,2]{1,2,3,0:T(8,128)S(1)} %copy.14), channel_id=1, source_target_pairs={{8,0},{16,8},{24,16},{32,24},{40,32},{48,40},{56,48},{64,56},{72,6... | collective-permute-start | bytes 76808 | tf_op jit(solution)/shard_map/ppermute | solution.py:31
  18.3 6.2 %collective-permute-start = (f32[5,80,8,2]{1,2,3,0:T(8,128)S(1)}, f32[5,80,8,2]{1,2,3,0:T(8,128)S(1)}, u32[]{:S(2)}, u32[]{:S(2)}) collective-permute-start(f32[5,80,8,2]{1,2,3,0:T(8,128)S(1)} %copy.13), channel_id=1, source_target_pairs={{0,8},{8,16},{16,24},{24,32},{32,40},{40,48},{48,56},{56,64},{64,7... | collective-permute-start | bytes 76808 | tf_op jit(solution)/shard_map/ppermute | solution.py:28
  35.8 18.3 %collective-permute-start.3 = (f32[5,80,2,132]{1,2,3,0:T(2,128)}, f32[5,80,2,132]{1,2,3,0:T(2,128)}, u32[]{:S(2)}, u32[]{:S(2)}) collective-permute-start(f32[5,80,2,132]{1,2,3,0:T(2,128)} %copy.18), channel_id=1, source_target_pairs={{1,0},{2,1},{3,2},{4,3},{5,4},{6,5},{7,6},{9,8},{10,9},{11,10},{12... | collective-permute-start | bytes 1267208 | tf_op jit(solution)/shard_map/ppermute | solution.py:31
  45.5 19.5 %collective-permute-start.2 = (f32[5,80,2,132]{1,2,3,0:T(2,128)}, f32[5,80,2,132]{1,2,3,0:T(2,128)}, u32[]{:S(2)}, u32[]{:S(2)}) collective-permute-start(f32[5,80,2,132]{1,2,3,0:T(2,128)} %copy.17), channel_id=1, source_target_pairs={{0,1},{1,2},{2,3},{3,4},{4,5},{5,6},{6,7},{8,9},{9,10},{10,11},{11... | collective-permute-start | bytes 1267208 | tf_op jit(solution)/shard_map/ppermute | solution.py:28
  98.7 4.6 %copy-start.4 = (f32[80,12,132]{2,1,0:T(8,128)S(1)}, f32[80,12,132]{2,1,0:T(8,128)}, u32[]{:S(2)}) copy-start(f32[80,12,132]{2,1,0:T(8,128)} %get-tuple-element.6) | copy-start | bytes 1520644
  103.3 1.3 copy-start.3
  104.6 1.3 copy-start.11
  104.6 1.3 copy-start.10
  106.0 9.6 %collective-permute-start.5 = (f32[8,8,64]{2,1,0:T(8,128)S(1)}, f32[8,8,64]{2,1,0:T(8,128)S(1)}, u32[]{:S(2)}, u32[]{:S(2)}) collective-permute-start(f32[8,8,64]{2,1,0:T(8,128)S(1)} %get-tuple-element.31), channel_id=1, source_target_pairs={{8,0},{16,8},{24,16},{32,24},{40,32},{48,40},{56,48},{64,56},{72,6... | collective-permute-start | bytes 49160 | tf_op jit(solution)/shard_map/ppermute | solution.py:216
  106.1 9.6 %collective-permute-start.4 = (f32[8,8,64]{2,1,0:T(8,128)S(1)}, f32[8,8,64]{2,1,0:T(8,128)S(1)}, u32[]{:S(2)}, u32[]{:S(2)}) collective-permute-start(f32[8,8,64]{2,1,0:T(8,128)S(1)} %get-tuple-element.30), channel_id=1, source_target_pairs={{0,8},{8,16},{16,24},{24,32},{32,40},{40,48},{48,56},{56,64},{64,7... | collective-permute-start | bytes 49160 | tf_op jit(solution)/shard_map/ppermute | solution.py:215
  110.5 8.7 %copy-start.5 = (f32[80,8,128]{2,1,0:T(8,128)S(1)}, f32[80,8,128]{2,1,0:T(8,128)}, u32[]{:S(2)}) copy-start(f32[80,8,128]{2,1,0:T(8,128)} %get-tuple-element.34) | copy-start | bytes 983044
  115.7 33.7 %copy-start = (f32[4,80,8,128]{3,2,1,0:T(8,128)S(1)}, f32[4,80,8,128]{3,2,1,0:T(8,128)}, u32[]{:S(2)}) copy-start(f32[4,80,8,128]{3,2,1,0:T(8,128)} %shard_map.120) | copy-start | bytes 3932164
  115.7 33.7 %copy-start.2 = (f32[80,8,128]{2,1,0:T(8,128)S(1)}, f32[80,8,128]{2,1,0:T(8,128)}, u32[]{:S(2)}) copy-start(f32[80,8,128]{2,1,0:T(8,128)} %copy-done.1) | copy-start | bytes 983044
  115.8 15.3 %collective-permute-start.6 = (f32[8,8,256]{2,1,0:T(8,128)S(1)}, f32[8,8,256]{2,1,0:T(8,128)S(1)}, u32[]{:S(2)}, u32[]{:S(2)}) collective-permute-start(f32[8,8,256]{2,1,0:T(8,128)S(1)} %get-tuple-element.5), channel_id=1, source_target_pairs={{0,7},{1,0},{2,1},{3,2},{4,3},{5,4},{6,5},{7,6},{8,15},{9,8},{10,9... | collective-permute-start | bytes 196616 | tf_op jit(solution)/shard_map/ppermute | solution.py:223
  120.4 11.4 %collective-permute-start.7 = (f32[8,8,256]{2,1,0:T(8,128)S(1)}, f32[8,8,256]{2,1,0:T(8,128)S(1)}, u32[]{:S(2)}, u32[]{:S(2)}) collective-permute-start(f32[8,8,256]{2,1,0:T(8,128)S(1)} %get-tuple-element.5), channel_id=1, source_target_pairs={{0,6},{1,7},{2,0},{3,1},{4,2},{5,3},{6,4},{7,5},{8,14},{9,15},{10,... | collective-permute-start | bytes 196616 | tf_op jit(solution)/shard_map/ppermute | solution.py:223
  120.6 13.7 %collective-permute-start.8 = (f32[8,8,256]{2,1,0:T(8,128)S(1)}, f32[8,8,256]{2,1,0:T(8,128)S(1)}, u32[]{:S(2)}, u32[]{:S(2)}) collective-permute-start(f32[8,8,256]{2,1,0:T(8,128)S(1)} %get-tuple-element.5), channel_id=1, source_target_pairs={{0,5},{1,6},{2,7},{3,0},{4,1},{5,2},{6,3},{7,4},{8,13},{9,14},{10,... | collective-permute-start | bytes 196616 | tf_op jit(solution)/shard_map/ppermute | solution.py:223
  129.8 4.5 %collective-permute-start.9 = (f32[8,8,256]{2,1,0:T(8,128)S(1)}, f32[8,8,256]{2,1,0:T(8,128)S(1)}, u32[]{:S(2)}, u32[]{:S(2)}) collective-permute-start(f32[8,8,256]{2,1,0:T(8,128)S(1)} %get-tuple-element.5), channel_id=1, source_target_pairs={{0,4},{1,5},{2,6},{3,7},{4,0},{5,1},{6,2},{7,3},{8,12},{9,13},{10,... | collective-permute-start | bytes 196616 | tf_op jit(solution)/shard_map/ppermute | solution.py:223
  129.8 4.6 %collective-permute-start.10 = (f32[8,8,256]{2,1,0:T(8,128)S(1)}, f32[8,8,256]{2,1,0:T(8,128)S(1)}, u32[]{:S(2)}, u32[]{:S(2)}) collective-permute-start(f32[8,8,256]{2,1,0:T(8,128)S(1)} %get-tuple-element.5), channel_id=1, source_target_pairs={{0,3},{1,4},{2,5},{3,6},{4,7},{5,0},{6,1},{7,2},{8,11},{9,12},{10,... | collective-permute-start | bytes 196616 | tf_op jit(solution)/shard_map/ppermute | solution.py:223
  131.1 3.3 %collective-permute-start.11 = (f32[8,8,256]{2,1,0:T(8,128)S(1)}, f32[8,8,256]{2,1,0:T(8,128)S(1)}, u32[]{:S(2)}, u32[]{:S(2)}) collective-permute-start(f32[8,8,256]{2,1,0:T(8,128)S(1)} %get-tuple-element.5), channel_id=1, source_target_pairs={{0,2},{1,3},{2,4},{3,5},{4,6},{5,7},{6,0},{7,1},{8,10},{9,11},{10,... | collective-permute-start | bytes 196616 | tf_op jit(solution)/shard_map/ppermute | solution.py:223
  131.8 5.4 %collective-permute-start.12 = (f32[8,8,256]{2,1,0:T(8,128)S(1)}, f32[8,8,256]{2,1,0:T(8,128)S(1)}, u32[]{:S(2)}, u32[]{:S(2)}) collective-permute-start(f32[8,8,256]{2,1,0:T(8,128)S(1)} %get-tuple-element.5), channel_id=1, source_target_pairs={{0,1},{1,2},{2,3},{3,4},{4,5},{5,6},{6,7},{7,0},{8,9},{9,10},{10,1... | collective-permute-start | bytes 196616 | tf_op jit(solution)/shard_map/ppermute | solution.py:223
  137.2 0.8 copy-start.6

commit v3 on v2

--- a/solution.py
+++ b/solution.py
@@ -16,21 +16,6 @@
 grav_baro = 25.0
 expand_temp = 0.2
 contract_salt = 0.1
-
-
-def padded_2(block, sides, width, periodic):
-    for axis, dim in sides:
-        count = lax.axis_size(axis)
-        forward = [(i, i + 1) for i in range(count - 1)]
-        if periodic:
-            forward.append((count - 1, 0))
-        backward = [(target, source) for source, target in forward]
-        low = lax.ppermute(
-            lax.slice_in_dim(block, block.shape[dim] - width, None, axis=dim), axis, forward
-        )
-        high = lax.ppermute(lax.slice_in_dim(block, 0, width, axis=dim), axis, backward)
-        block = jnp.concatenate([low, block, high], axis=dim)
-    return block
 
 
 def laplace(quantity, wet_mask):
@@ -154,20 +139,42 @@
     return jnp.stack([new_height, new_east, new_north])
 
 
-def zonal_rims(stacked):
-    return padded_2(stacked, (("gx", 3),), 2, True)
-
-
-def merid_rims(stacked):
-    return padded_2(stacked, ((("gy", "ga"), 2),), 2, False)
-
-
-def baro_zonal(operand, halo_width):
-    return padded_2(operand, (("gx", 2),), halo_width, True)
-
-
-def baro_merid_all(operand, halo_width):
-    return padded_2(operand, ((("gy", "ga"), 1),), halo_width, False)
+def halo_3d(block):
+    zonal = "gx"
+    merid = ("gy", "ga")
+    both = ("gx", "gy", "ga")
+    zonal_n = lax.axis_size(zonal)
+    merid_n = lax.axis_size(merid)
+
+    def send(piece, d_zonal, d_merid):
+        if d_merid == 0:
+            pairs = [(g, (g + d_zonal) % zonal_n) for g in range(zonal_n)]
+            return lax.ppermute(piece, zonal, pairs)
+        pairs = []
+        for g in range(zonal_n):
+            for m in range(merid_n):
+                target = m + d_merid
+                if 0 <= target < merid_n:
+                    pairs.append((g * merid_n + m, ((g + d_zonal) % zonal_n) * merid_n + target))
+        if d_zonal == 0:
+            return lax.ppermute(piece, merid, [(s % merid_n, t % merid_n) for s, t in pairs[:merid_n - 1]])
+        return lax.ppermute(piece, both, pairs)
+
+    w = 2
+    last_rows = block[..., -w:, :]
+    first_rows = block[..., :w, :]
+    west = send(block[..., -w:], 1, 0)
+    east = send(block[..., :w], -1, 0)
+    low = send(last_rows, 0, 1)
+    high = send(first_rows, 0, -1)
+    low_west = send(last_rows[..., -w:], 1, 1)
+    low_east = send(last_rows[..., :w], -1, 1)
+    high_west = send(first_rows[..., -w:], 1, -1)
+    high_east = send(first_rows[..., :w], -1, -1)
+    low_band = jnp.concatenate([low_west, low, low_east], axis=-1)
+    middle = jnp.concatenate([west, block, east], axis=-1)
+    high_band = jnp.concatenate([high_west, high, high_east], axis=-1)
+    return jnp.concatenate([low_band, middle, high_band], axis=-2)
 
 
 def shards(velocity, tracers, mixing, thickness, coriolis, land, bottom, surface, barotropic):
@@ -178,7 +185,7 @@
     stacked = jnp.concatenate(
         [velocity * wet_mask[None], tracers * wet_mask[None], wet_mask[None]], axis=0
     )
-    padded = merid_rims(zonal_rims(stacked))
+    padded = halo_3d(stacked)
     depth_col = thickness.reshape((levels, 1, 1))
     weight = (contract_salt * padded[3] - expand_temp * padded[2]) * padded[4] * depth_col
     pressure = press_scale * (jnp.cumsum(weight, axis=0) - weight + 0.5 * weight)

time: 151 us -> 151 us (level)
  starting transfers between devices: 36.5 us -> 52.5 us
  local copies, waits for them, and re-layouts: 22.2 us -> 13.6 us
  waiting for transfers between devices: 21.3 us -> 17.2 us
  other arithmetic: 55.6 us -> 51.7 us
    ppermute x4 -> x8, starting transfers between devices: 17.7 us -> 35.2 us  [the longest x4 26.9 us: send(): return lax.ppermute(piece, both, pairs)]
    ppermute x1, starting transfers between devices: 0.03 us -> 6.99 us  [gather_baro(): high = lax.ppermute(fields[..., :BARO_HALO], 'gx', backward)]
    ppermute x7, starting transfers between devices: 17.3 us -> 10.4 us  [gather_baro(): blocks.append(lax.ppermute(wide, merid, pairs))]
    slice x1 -> x0, other arithmetic: 6.48 us -> none  [padded_2(): lax.slice_in_dim(block, block.shape[dim] - width, None, axis=dim)]
    ppermute x4 -> x2, local copies, waits for them, and re-layouts: 8.48 us -> 2.39 us  [send(): return lax.ppermute(piece, zonal, pairs)]
    ppermute x4 -> x8, waiting for transfers between devices: 18.5 us -> 14.4 us  [the longest x4 14.4 us: send(): return lax.ppermute(piece, both, pairs)]
    concatenate x1, other arithmetic: 5.62 us -> 9.53 us  [halo_3d(): return jnp.concatenate([low_band, middle, high_band], axis=-2)]
    slice x5, local copies, waits for them, and re-layouts: 10.4 us -> 8.06 us  [the longest x1 2.62 us: halo_3d(): east = send(block[..., :w], -1, 0)]
  transfers between devices with their start and end apart: 13 -> 17, of which waited for: 4 -> 3; matrix products, arithmetic and copies ran while one was open for 9% -> 9% of each run, Pallas kernels for 3% -> 3%
where the time goes in v3:
time: 151 us; the launch traced here: 150 us
  starting transfers between devices  52.5 us (35%)
  other arithmetic  51.7 us (34%)
  waiting for transfers between devices  17.2 us (11%)
  Pallas kernels  14 us (9%)
  local copies, waits for them, and re-layouts  13.6 us (9%)
    ppermute x4, starting transfers between devices, send(): return lax.ppermute(piece, both, pairs)  26.9 us
    another operation x1, other arithmetic, shards(): jnp.cumsum(weight, axis=0) - weight + 0.5 * weight  20.2 us
    ppermute x4, waiting for transfers between devices, send(): return lax.ppermute(piece, both, pairs)  14.4 us
    ppermute x7, starting transfers between devices, gather_baro(): blocks.append(lax.ppermute(wide, merid, pairs))  10.4 us
    concatenate x1, other arithmetic, halo_3d(): return jnp.concatenate([low_band, middle, high_band], axis=-2)  9.53 us
    pallas_call x1, Pallas kernels, baro_run(): pl.pallas_call(baro_kernel, out_shape=jax.ShapeDtypeStruct((5, whole.shap...  8.88 us
    ppermute x1, starting transfers between devices, gather_baro(): high = lax.ppermute(fields[..., :BARO_HALO], 'gx', backward)  6.99 us
    ppermute x2, starting transfers between devices, send(): lax.ppermute(piece, merid, [(s % merid_n, t % merid_n) for s, t in pairs[...  6.76 us
  transfers between devices with their start and end apart: 17, of which 3 were waited for; matrix products, arithmetic and copies ran while one was open for 9% of the time, Pallas kernels for 3%

profile of v3, /device:TPU:1, one launch (start us, length us, event | category | flops | bytes accessed | tf_op | source)
XLA Modules:
  0.0 150.0 jit_solution(8956653676953531087)
XLA Ops:
  0.6 0.8 convert_element_type.4
  1.4 0.7 fusion.48
  2.1 1.6 %broadcast_multiply_fusion.2 = (f32[80,8,128]{2,1,0:T(8,128)}, f32[8,128]{1,0:T(8,128)S(1)}, f32[80,8,128]{2,1,0:T(8,128)S(1)}) fusion(f32[80]{0:T(128)} %th_ref.1, f32[8,128]{1,0:T(8,128)S(1)} %convert_element_type.4, s32[8,128]{1,0:T(8,128)} %param.15), kind=kLoop, calls=%fused_computation.111 | loop fusion | flops 326656 | bytes 667968 | tf_op jit(solution)/shard_map/mul | solution.py:209
  3.8 1.3 broadcast_multiply_fusion.1
  5.1 0.1 pad_maximum_fusion
  5.2 2.0 %fusion.63 = (f32[5,80,2,2]{3,2,1,0:T(2,128)}, f32[5,80,2,2]{3,2,1,0:T(2,128)}, f32[5,80,2,2]{3,2,1,0:T(2,128)S(1)}, f32[5,80,2,2]{3,2,1,0:T(2,128)}) fusion(f32[5,80,8,128]{3,2,1,0:T(8,128)S(1)} %pad_maximum_fusion), kind=kLoop, calls=%fused_computation.147 | loop fusion | bytes 51200 | tf_op jit(solution)/shard_map/slice | solution.py:170
  7.2 13.8 %collective-permute-start.7 = (f32[5,80,2,2]{3,2,1,0:T(2,128)S(1)}, f32[5,80,2,2]{3,2,1,0:T(2,128)}, u32[]{:S(2)}, u32[]{:S(2)}) collective-permute-start(f32[5,80,2,2]{3,2,1,0:T(2,128)S(1)} %get-tuple-element.21), channel_id=1, source_target_pairs={{1,248},{2,249},{3,250},{4,251},{5,252},{6,253},{7,254},{9,0},{10,... | collective-permute-start | bytes 19208 | tf_op jit(solution)/shard_map/ppermute | solution.py:161
  21.0 1.2 fusion.64
  22.1 2.4 %collective-permute-start.6 = (f32[5,80,2,128]{3,2,1,0:T(2,128)}, f32[5,80,2,128]{3,2,1,0:T(2,128)}, u32[]{:S(2)}, u32[]{:S(2)}) collective-permute-start(f32[5,80,2,128]{3,2,1,0:T(2,128)} %get-tuple-element.24), channel_id=1, source_target_pairs={{1,0},{2,1},{3,2},{4,3},{5,4},{6,5},{7,6},{9,8},{10,9},{11,10},{12... | collective-permute-start | bytes 1228808 | tf_op jit(solution)/shard_map/ppermute | solution.py:160
  24.6 1.7 %fusion.65 = (f32[5,80,8,2]{3,2,1,0:T(8,128)S(1)}, f32[5,80,8,2]{3,2,1,0:T(8,128)}) fusion(f32[5,80,8,128]{3,2,1,0:T(8,128)S(1)} %pad_maximum_fusion), kind=kLoop, calls=%fused_computation.149 | loop fusion | bytes 102400 | tf_op jit(solution)/shard_map/slice | solution.py:166
  26.3 2.6 %copy.14 = f32[5,80,8,2]{1,2,3,0:T(8,128)} copy(f32[5,80,8,2]{3,2,1,0:T(8,128)} %get-tuple-element.26) | data formatting | bytes 51200 | tf_op jit(solution)/shard_map/slice | solution.py:167
  28.9 0.5 collective-permute-start.4
  29.4 0.5 copy.13
  29.9 1.1 collective-permute-start.3
  31.0 4.4 %collective-permute-start.1 = (f32[5,80,2,128]{3,2,1,0:T(2,128)}, f32[5,80,2,128]{3,2,1,0:T(2,128)}, u32[]{:S(2)}, u32[]{:S(2)}) collective-permute-start(f32[5,80,2,128]{3,2,1,0:T(2,128)} %get-tuple-element.23), channel_id=1, source_target_pairs={{0,1},{1,2},{2,3},{3,4},{4,5},{5,6},{6,7},{8,9},{9,10},{10,11},{11... | collective-permute-start | bytes 1228808 | tf_op jit(solution)/shard_map/ppermute | solution.py:160
  35.4 0.6 reduce_sum.38
  36.0 0.6 constant_dynamic-update-slice_fusion.6
  36.6 0.0 collective-permute-done.7
  36.7 2.4 %collective-permute-start.5 = (f32[5,80,2,2]{3,2,1,0:T(2,128)}, f32[5,80,2,2]{3,2,1,0:T(2,128)}, u32[]{:S(2)}, u32[]{:S(2)}) collective-permute-start(f32[5,80,2,2]{3,2,1,0:T(2,128)} %get-tuple-element.20), channel_id=1, source_target_pairs={{1,8},{2,9},{3,10},{4,11},{5,12},{6,13},{7,14},{9,16},{10,17},{11,... | collective-permute-start | bytes 19208 | tf_op jit(solution)/shard_map/ppermute | solution.py:161
  39.1 0.0 collective-permute-done.4
  39.1 8.6 %collective-permute-start.2 = (f32[5,80,2,2]{3,2,1,0:T(2,128)}, f32[5,80,2,2]{3,2,1,0:T(2,128)}, u32[]{:S(2)}, u32[]{:S(2)}) collective-permute-start(f32[5,80,2,2]{3,2,1,0:T(2,128)} %get-tuple-element.22), channel_id=1, source_target_pairs={{0,249},{1,250},{2,251},{3,252},{4,253},{5,254},{6,255},{8,1},{9,2... | collective-permute-start | bytes 19208 | tf_op jit(solution)/shard_map/ppermute | solution.py:161
  47.7 0.0 collective-permute-done.3
  47.7 2.1 %collective-permute-start = (f32[5,80,2,2]{3,2,1,0:T(2,128)}, f32[5,80,2,2]{3,2,1,0:T(2,128)}, u32[]{:S(2)}, u32[]{:S(2)}) collective-permute-start(f32[5,80,2,2]{3,2,1,0:T(2,128)} %get-tuple-element.19), channel_id=1, source_target_pairs={{0,9},{1,10},{2,11},{3,12},{4,13},{5,14},{6,15},{8,17},{9,18},{10,... | collective-permute-start | bytes 19208 | tf_op jit(solution)/shard_map/ppermute | solution.py:161
  49.8 0.1 constant_dynamic-update-slice_fusion.4
  49.9 0.6 copy.16
  50.5 1.8 %copy.15 = f32[5,80,8,2]{3,2,1,0:T(8,128)} copy(f32[5,80,8,2]{1,2,3,0:T(8,128)S(1)} %collective-permute-done.3) | data formatting | bytes 51200 | tf_op jit(solution)/shard_map/ppermute | solution.py:152
  52.3 8.9 %collective-permute-done.5 = f32[5,80,2,2]{3,2,1,0:T(2,128)} collective-permute-done((f32[5,80,2,2]{3,2,1,0:T(2,128)}, f32[5,80,2,2]{3,2,1,0:T(2,128)}, u32[]{:S(2)}, u32[]{:S(2)}) %collective-permute-start.5) | collective-permute-done | bytes 6432 | tf_op jit(solution)/shard_map/ppermute | solution.py:161
  61.2 0.0 collective-permute-done.2
  61.2 5.5 %collective-permute-done = f32[5,80,2,2]{3,2,1,0:T(2,128)} collective-permute-done((f32[5,80,2,2]{3,2,1,0:T(2,128)}, f32[5,80,2,2]{3,2,1,0:T(2,128)}, u32[]{:S(2)}, u32[]{:S(2)}) %collective-permute-start) | collective-permute-done | bytes 6432 | tf_op jit(solution)/shard_map/ppermute | solution.py:161
  66.7 0.0 collective-permute-done.6
  66.7 0.0 collective-permute-done.1
  66.7 9.5 %maximum_maximum_fusion = f32[5,80,12,132]{3,2,1,0:T(8,128)S(1)} fusion(f32[5,80,2,2]{3,2,1,0:T(2,128)} %collective-permute-done.7, f32[5,80,2,128]{3,2,1,0:T(2,128)} %collective-permute-done.6, f32[5,80,2,2]{3,2,1,0:T(2,128)} %collective-permute-done.5, f32[5,80,8,2]{3,2,1,0:T(8,128)S(1)} %copy.16, f32[1,80,8,128]{3,2,1,0:T(8,128)S(1)} %copy-done.4, ...), kind=kLoop, calls=%fused_computation | loop fusion | flops 6336000 | bytes 5068800 | tf_op jit(solution)/shard_map/concatenate | solution.py:177
  76.3 0.7 fusion.62
  77.0 0.8 slice_bitcast_fusion
  77.8 20.2 %add_multiply_fusion = f32[80,12,132]{2,1,0:T(8,128)S(1)} fusion(f32[80,12,132]{2,1,0:T(8,128)S(1)} %get-tuple-element.13), kind=kOutput, calls=%fused_computation.33 | output fusion | flops 10517760 | bytes 1013760 | tf_op jit(solution)/shard_map/jit(cumsum)/reduce_window_sum | solution.py:191
  98.0 1.8 %fusion.1 = f32[80,10,130]{2,1,0:T(8,128)S(1)} fusion(f32[80,12,132]{2,1,0:T(8,128)S(1)} %get-tuple-element.17, f32[80,12,132]{2,1,0:T(8,128)S(1)} %get-tuple-element.15), kind=kLoop, calls=%fused_computation.4 | loop fusion | flops 624000 | bytes 2912000 | tf_op jit(solution)/shard_map/mul | solution.py:29
  99.7 4.6 %fusion.7 = (f32[80,10,130]{2,1,0:T(8,128)S(1)}, f32[80,10,130]{2,1,0:T(8,128)S(1)}, f32[80,10,130]{2,1,0:T(8,128)S(1)}) fusion(f32[80,12,132]{2,1,0:T(8,128)S(1)} %get-tuple-element.14, f32[80,12,132]{2,1,0:T(8,128)S(1)} %get-tuple-element.15, f32[80,12,132]{2,1,0:T(8,128)S(1)} %get-tuple-element.18, f32[80,12,132]{2,1,0:T(8,128)S(1)} %get-tuple-element.16), kind=kLoop, calls=%fused_computation.22 | loop fusion | flops 1872000 | bytes 7904000 | tf_op jit(solution)/shard_map/mul | solution.py:29
  104.4 1.1 fusion.40
  105.5 0.0 copy-start.11
  105.5 0.0 copy-start.10
  105.5 1.1 fusion.29
  106.6 0.2 fusion.8
  106.8 0.1 fusion.67
  106.9 7.0 %collective-permute-start.9 = (f32[8,8,64]{2,1,0:T(8,128)S(1)}, f32[8,8,64]{2,1,0:T(8,128)S(1)}, u32[]{:S(2)}, u32[]{:S(2)}) collective-permute-start(f32[8,8,64]{2,1,0:T(8,128)S(1)} %get-tuple-element.35), channel_id=1, source_target_pairs={{8,0},{16,8},{24,16},{32,24},{40,32},{48,40},{56,48},{64,56},{72,6... | collective-permute-start | bytes 49160 | tf_op jit(solution)/shard_map/ppermute | solution.py:223
  113.9 0.0 collective-permute-start.8
  113.9 0.8 fusion.13
  114.7 0.8 fusion.21
  115.5 1.3 maximum_add_fusion.prov_ref
  116.9 5.1 %shard_map.120 = f32[4,80,8,128]{3,2,1,0:T(8,128)} custom-call(f32[80]{0:T(128)} %th_ref.1, f32[4,80,8,128]{3,2,1,0:T(8,128)} %maximum_add_fusion.prov_ref, f32[80,8,128]{2,1,0:T(8,128)} %mix_ref.1, f32[80,8,128]{2,1,0:T(8,128)} %copy-done.1), custom_call_target="tpu_custom_call" | custom-call | tf_op jit(solution)/shard_map/pallas_call | solution.py:339
  122.0 0.0 collective-permute-done.9
  122.0 0.1 bitcast_dynamic-update-slice_fusion.7
  122.1 0.1 collective-permute-start.10
  122.2 1.3 multiply_reduce_fusion
  123.5 0.1 collective-permute-start.11
  123.6 5.7 %collective-permute-start.12 = (f32[8,8,256]{2,1,0:T(8,128)S(1)}, f32[8,8,256]{2,1,0:T(8,128)S(1)}, u32[]{:S(2)}, u32[]{:S(2)}) collective-permute-start(f32[8,8,256]{2,1,0:T(8,128)S(1)} %get-tuple-element.5), channel_id=1, source_target_pairs={{0,5},{1,6},{2,7},{3,0},{4,1},{5,2},{6,3},{7,4},{8,13},{9,14},{10,... | collective-permute-start | bytes 196616 | tf_op jit(solution)/shard_map/ppermute | solution.py:230
  129.3 0.2 collective-permute-start.14
  129.5 1.8 %collective-permute-start.15 = (f32[8,8,256]{2,1,0:T(8,128)S(1)}, f32[8,8,256]{2,1,0:T(8,128)S(1)}, u32[]{:S(2)}, u32[]{:S(2)}) collective-permute-start(f32[8,8,256]{2,1,0:T(8,128)S(1)} %get-tuple-element.5), channel_id=1, source_target_pairs={{0,2},{1,3},{2,4},{3,5},{4,6},{5,7},{6,0},{7,1},{8,10},{9,11},{10,... | collective-permute-start | bytes 196616 | tf_op jit(solution)/shard_map/ppermute | solution.py:230
  131.3 2.5 %collective-permute-start.16 = (f32[8,8,256]{2,1,0:T(8,128)S(1)}, f32[8,8,256]{2,1,0:T(8,128)S(1)}, u32[]{:S(2)}, u32[]{:S(2)}) collective-permute-start(f32[8,8,256]{2,1,0:T(8,128)S(1)} %get-tuple-element.5), channel_id=1, source_target_pairs={{0,1},{1,2},{2,3},{3,4},{4,5},{5,6},{6,7},{7,0},{8,9},{9,10},{10,1... | collective-permute-start | bytes 196616 | tf_op jit(solution)/shard_map/ppermute | solution.py:230
  133.9 2.7 %collective-permute-done.16 = f32[8,8,256]{2,1,0:T(8,128)S(1)} collective-permute-done((f32[8,8,256]{2,1,0:T(8,128)S(1)}, f32[8,8,256]{2,1,0:T(8,128)S(1)}, u32[]{:S(2)}, u32[]{:S(2)}) %collective-permute-start.16) | collective-permute-done | bytes 65568 | tf_op jit(solution)/shard_map/ppermute | solution.py:230
  136.6 0.8 copy-done.6
  137.4 8.9 %shard_map.121 = f32[5,8,128]{2,1,0:T(8,128)} custom-call(s32[1]{0:T(128)} %bitcast.9.off_ref, f32[8,8,8,256]{3,2,1,0:T(8,128)} %copy-done.6), custom_call_target="tpu_custom_call" | custom-call | tf_op jit(solution)/shard_map/pallas_call | solution.py:288
  146.3 1.3 slice_bitcast_fusion.5
  147.6 1.3 fusion.68
  148.9 1.2 fusion.66
  (45 shorter events, 0.1 us)
Async XLA Ops:
  0.6 3.1 %copy-start.7 = (f32[2,80,8,128]{3,2,1,0:T(8,128)S(1)}, f32[2,80,8,128]{3,2,1,0:T(8,128)}, u32[]{:S(2)}) copy-start(f32[2,80,8,128]{3,2,1,0:T(8,128)} %param.9) | copy-start | bytes 1966084
  2.1 3.0 %copy-start.3 = (f32[1,80,8,128]{3,2,1,0:T(8,128)}, f32[1,80,8,128]{3,2,1,0:T(8,128)S(1)}, u32[]{:S(2)}) copy-start(f32[1,80,8,128]{3,2,1,0:T(8,128)S(1)} %fusion.48) | copy-start | bytes 983044
  3.8 1.3 copy-start.1
  7.2 29.4 %collective-permute-start.7 = (f32[5,80,2,2]{3,2,1,0:T(2,128)S(1)}, f32[5,80,2,2]{3,2,1,0:T(2,128)}, u32[]{:S(2)}, u32[]{:S(2)}) collective-permute-start(f32[5,80,2,2]{3,2,1,0:T(2,128)S(1)} %get-tuple-element.21), channel_id=1, source_target_pairs={{1,248},{2,249},{3,250},{4,251},{5,252},{6,253},{7,254},{9,0},{10,... | collective-permute-start | bytes 19208 | tf_op jit(solution)/shard_map/ppermute | solution.py:161
  22.1 44.6 %collective-permute-start.6 = (f32[5,80,2,128]{3,2,1,0:T(2,128)}, f32[5,80,2,128]{3,2,1,0:T(2,128)}, u32[]{:S(2)}, u32[]{:S(2)}) collective-permute-start(f32[5,80,2,128]{3,2,1,0:T(2,128)} %get-tuple-element.24), channel_id=1, source_target_pairs={{1,0},{2,1},{3,2},{4,3},{5,4},{6,5},{7,6},{9,8},{10,9},{11,10},{12... | collective-permute-start | bytes 1228808 | tf_op jit(solution)/shard_map/ppermute | solution.py:160
  26.3 9.1 %copy-start.9 = (f32[80]{0:T(128)S(1)}, f32[80]{0:T(128)}, u32[]{:S(2)}) copy-start(f32[80]{0:T(128)} %th_ref.1) | copy-start | bytes 964
  26.3 10.3 %copy-start.8 = (s32[8,128]{1,0:T(8,128)S(1)}, s32[8,128]{1,0:T(8,128)}, u32[]{:S(2)}) copy-start(s32[8,128]{1,0:T(8,128)} %param.14) | copy-start | bytes 12292
  26.3 23.5 %copy-start.12 = (f32[8]{0:T(128)S(1)}, f32[8]{0:T(128)}, u32[]{:S(2)}) copy-start(f32[8]{0:T(128)} %param.13) | copy-start | bytes 100
  28.9 10.2 %collective-permute-start.4 = (f32[5,80,8,2]{1,2,3,0:T(8,128)}, f32[5,80,8,2]{1,2,3,0:T(8,128)S(1)}, u32[]{:S(2)}, u32[]{:S(2)}) collective-permute-start(f32[5,80,8,2]{1,2,3,0:T(8,128)} %copy.14), channel_id=1, source_target_pairs={{0,248},{8,0},{16,8},{24,16},{32,24},{40,32},{48,40},{56,48},{64,5... | collective-permute-start | bytes 76808 | tf_op jit(solution)/shard_map/ppermute | solution.py:152
  29.9 17.8 %collective-permute-start.3 = (f32[5,80,8,2]{1,2,3,0:T(8,128)S(1)}, f32[5,80,8,2]{1,2,3,0:T(8,128)S(1)}, u32[]{:S(2)}, u32[]{:S(2)}) collective-permute-start(f32[5,80,8,2]{1,2,3,0:T(8,128)S(1)} %copy.13), channel_id=1, source_target_pairs={{0,8},{8,16},{16,24},{24,32},{32,40},{40,48},{48,56},{56,64},{64,7... | collective-permute-start | bytes 76808 | tf_op jit(solution)/shard_map/ppermute | solution.py:152
  31.0 35.7 %collective-permute-start.1 = (f32[5,80,2,128]{3,2,1,0:T(2,128)}, f32[5,80,2,128]{3,2,1,0:T(2,128)}, u32[]{:S(2)}, u32[]{:S(2)}) collective-permute-start(f32[5,80,2,128]{3,2,1,0:T(2,128)} %get-tuple-element.23), channel_id=1, source_target_pairs={{0,1},{1,2},{2,3},{3,4},{4,5},{5,6},{6,7},{8,9},{9,10},{10,11},{11... | collective-permute-start | bytes 1228808 | tf_op jit(solution)/shard_map/ppermute | solution.py:160
  36.7 24.6 %collective-permute-start.5 = (f32[5,80,2,2]{3,2,1,0:T(2,128)}, f32[5,80,2,2]{3,2,1,0:T(2,128)}, u32[]{:S(2)}, u32[]{:S(2)}) collective-permute-start(f32[5,80,2,2]{3,2,1,0:T(2,128)} %get-tuple-element.20), channel_id=1, source_target_pairs={{1,8},{2,9},{3,10},{4,11},{5,12},{6,13},{7,14},{9,16},{10,17},{11,... | collective-permute-start | bytes 19208 | tf_op jit(solution)/shard_map/ppermute | solution.py:161
  39.1 22.1 %collective-permute-start.2 = (f32[5,80,2,2]{3,2,1,0:T(2,128)}, f32[5,80,2,2]{3,2,1,0:T(2,128)}, u32[]{:S(2)}, u32[]{:S(2)}) collective-permute-start(f32[5,80,2,2]{3,2,1,0:T(2,128)} %get-tuple-element.22), channel_id=1, source_target_pairs={{0,249},{1,250},{2,251},{3,252},{4,253},{5,254},{6,255},{8,1},{9,2... | collective-permute-start | bytes 19208 | tf_op jit(solution)/shard_map/ppermute | solution.py:161
  47.7 19.0 %collective-permute-start = (f32[5,80,2,2]{3,2,1,0:T(2,128)}, f32[5,80,2,2]{3,2,1,0:T(2,128)}, u32[]{:S(2)}, u32[]{:S(2)}) collective-permute-start(f32[5,80,2,2]{3,2,1,0:T(2,128)} %get-tuple-element.19), channel_id=1, source_target_pairs={{0,9},{1,10},{2,11},{3,12},{4,13},{5,14},{6,15},{8,17},{9,18},{10,... | collective-permute-start | bytes 19208 | tf_op jit(solution)/shard_map/ppermute | solution.py:161
  49.9 16.8 %copy-start.4 = (f32[1,80,8,128]{3,2,1,0:T(8,128)S(1)}, f32[1,80,8,128]{3,2,1,0:T(8,128)}, u32[]{:S(2)}) copy-start(f32[1,80,8,128]{3,2,1,0:T(8,128)} %copy-done.3) | copy-start | bytes 983044
  105.5 1.3 copy-start.11
  105.5 1.3 copy-start.10
  106.9 15.1 %collective-permute-start.9 = (f32[8,8,64]{2,1,0:T(8,128)S(1)}, f32[8,8,64]{2,1,0:T(8,128)S(1)}, u32[]{:S(2)}, u32[]{:S(2)}) collective-permute-start(f32[8,8,64]{2,1,0:T(8,128)S(1)} %get-tuple-element.35), channel_id=1, source_target_pairs={{8,0},{16,8},{24,16},{32,24},{40,32},{48,40},{56,48},{64,56},{72,6... | collective-permute-start | bytes 49160 | tf_op jit(solution)/shard_map/ppermute | solution.py:223
  113.9 8.1 %collective-permute-start.8 = (f32[8,8,64]{2,1,0:T(8,128)S(1)}, f32[8,8,64]{2,1,0:T(8,128)S(1)}, u32[]{:S(2)}, u32[]{:S(2)}) collective-permute-start(f32[8,8,64]{2,1,0:T(8,128)S(1)} %get-tuple-element.34), channel_id=1, source_target_pairs={{0,8},{8,16},{16,24},{24,32},{32,40},{40,48},{48,56},{56,64},{64,7... | collective-permute-start | bytes 49160 | tf_op jit(solution)/shard_map/ppermute | solution.py:222
  116.9 5.3 %copy-start.5 = (f32[80,8,128]{2,1,0:T(8,128)S(1)}, f32[80,8,128]{2,1,0:T(8,128)}, u32[]{:S(2)}) copy-start(f32[80,8,128]{2,1,0:T(8,128)} %get-tuple-element.38) | copy-start | bytes 983044
  122.1 26.8 %copy-start = (f32[4,80,8,128]{3,2,1,0:T(8,128)S(1)}, f32[4,80,8,128]{3,2,1,0:T(8,128)}, u32[]{:S(2)}) copy-start(f32[4,80,8,128]{3,2,1,0:T(8,128)} %shard_map.120) | copy-start | bytes 3932164
  122.1 26.8 %copy-start.2 = (f32[80,8,128]{2,1,0:T(8,128)S(1)}, f32[80,8,128]{2,1,0:T(8,128)}, u32[]{:S(2)}) copy-start(f32[80,8,128]{2,1,0:T(8,128)} %copy-done.1) | copy-start | bytes 983044
  122.1 7.4 %collective-permute-start.10 = (f32[8,8,256]{2,1,0:T(8,128)S(1)}, f32[8,8,256]{2,1,0:T(8,128)S(1)}, u32[]{:S(2)}, u32[]{:S(2)}) collective-permute-start(f32[8,8,256]{2,1,0:T(8,128)S(1)} %get-tuple-element.5), channel_id=1, source_target_pairs={{0,7},{1,0},{2,1},{3,2},{4,3},{5,4},{6,5},{7,6},{8,15},{9,8},{10,9... | collective-permute-start | bytes 196616 | tf_op jit(solution)/shard_map/ppermute | solution.py:230
  123.5 7.8 %collective-permute-start.11 = (f32[8,8,256]{2,1,0:T(8,128)S(1)}, f32[8,8,256]{2,1,0:T(8,128)S(1)}, u32[]{:S(2)}, u32[]{:S(2)}) collective-permute-start(f32[8,8,256]{2,1,0:T(8,128)S(1)} %get-tuple-element.5), channel_id=1, source_target_pairs={{0,6},{1,7},{2,0},{3,1},{4,2},{5,3},{6,4},{7,5},{8,14},{9,15},{10,... | collective-permute-start | bytes 196616 | tf_op jit(solution)/shard_map/ppermute | solution.py:230
  123.6 10.2 %collective-permute-start.12 = (f32[8,8,256]{2,1,0:T(8,128)S(1)}, f32[8,8,256]{2,1,0:T(8,128)S(1)}, u32[]{:S(2)}, u32[]{:S(2)}) collective-permute-start(f32[8,8,256]{2,1,0:T(8,128)S(1)} %get-tuple-element.5), channel_id=1, source_target_pairs={{0,5},{1,6},{2,7},{3,0},{4,1},{5,2},{6,3},{7,4},{8,13},{9,14},{10,... | collective-permute-start | bytes 196616 | tf_op jit(solution)/shard_map/ppermute | solution.py:230
  129.3 4.5 %collective-permute-start.13 = (f32[8,8,256]{2,1,0:T(8,128)S(1)}, f32[8,8,256]{2,1,0:T(8,128)S(1)}, u32[]{:S(2)}, u32[]{:S(2)}) collective-permute-start(f32[8,8,256]{2,1,0:T(8,128)S(1)} %get-tuple-element.5), channel_id=1, source_target_pairs={{0,4},{1,5},{2,6},{3,7},{4,0},{5,1},{6,2},{7,3},{8,12},{9,13},{10,... | collective-permute-start | bytes 196616 | tf_op jit(solution)/shard_map/ppermute | solution.py:230
  129.3 4.6 %collective-permute-start.14 = (f32[8,8,256]{2,1,0:T(8,128)S(1)}, f32[8,8,256]{2,1,0:T(8,128)S(1)}, u32[]{:S(2)}, u32[]{:S(2)}) collective-permute-start(f32[8,8,256]{2,1,0:T(8,128)S(1)} %get-tuple-element.5), channel_id=1, source_target_pairs={{0,3},{1,4},{2,5},{3,6},{4,7},{5,0},{6,1},{7,2},{8,11},{9,12},{10,... | collective-permute-start | bytes 196616 | tf_op jit(solution)/shard_map/ppermute | solution.py:230
  129.5 4.4 %collective-permute-start.15 = (f32[8,8,256]{2,1,0:T(8,128)S(1)}, f32[8,8,256]{2,1,0:T(8,128)S(1)}, u32[]{:S(2)}, u32[]{:S(2)}) collective-permute-start(f32[8,8,256]{2,1,0:T(8,128)S(1)} %get-tuple-element.5), channel_id=1, source_target_pairs={{0,2},{1,3},{2,4},{3,5},{4,6},{5,7},{6,0},{7,1},{8,10},{9,11},{10,... | collective-permute-start | bytes 196616 | tf_op jit(solution)/shard_map/ppermute | solution.py:230
  131.3 5.3 %collective-permute-start.16 = (f32[8,8,256]{2,1,0:T(8,128)S(1)}, f32[8,8,256]{2,1,0:T(8,128)S(1)}, u32[]{:S(2)}, u32[]{:S(2)}) collective-permute-start(f32[8,8,256]{2,1,0:T(8,128)S(1)} %get-tuple-element.5), channel_id=1, source_target_pairs={{0,1},{1,2},{2,3},{3,4},{4,5},{5,6},{6,7},{7,0},{8,9},{9,10},{10,1... | collective-permute-start | bytes 196616 | tf_op jit(solution)/shard_map/ppermute | solution.py:230
  136.6 0.8 copy-start.6

commit v4 on v3

--- a/solution.py
+++ b/solution.py
@@ -224,14 +224,11 @@
     wide = jnp.concatenate([low, fields, high], axis=-1)
     merid = ("gy", "ga")
     parts = lax.axis_size(merid)
-    blocks = [wide]
-    for shift in range(1, parts):
-        pairs = [(d, (d - shift) % parts) for d in range(parts)]
-        blocks.append(lax.ppermute(wide, merid, pairs))
-    return jnp.stack(blocks)
-
-
-def baro_kernel(off_ref, f_ref, o_ref):
+    copies = jnp.broadcast_to(wide[None], (parts,) + wide.shape)
+    return lax.all_to_all(copies, merid, 0, 0)
+
+
+def baro_kernel(off_ref, f_ref, o_ref, keep_ref):
     parts = f_ref.shape[0]
     block_rows = f_ref.shape[2]
     rows = parts * block_rows
@@ -245,12 +242,9 @@
     rotate = field(2)
     push_east = field(3)
     push_north = field(4)
-    offset = off_ref[0]
-    last_local = rows - 1 - offset
-    first_local = jnp.where(offset == 0, 0, rows - offset)
     row = lax.broadcasted_iota(jnp.int32, (rows, cols), 0)
-    not_last = row != last_local
-    not_first = row != first_local
+    not_last = row != rows - 1
+    not_first = row != 0
 
     def east_diff(q):
         return 0.5 * (pltpu.roll(q, cols - 1, 1) - pltpu.roll(q, 1, 1))
@@ -280,8 +274,10 @@
     height, east_vel, north_vel, sum_east, sum_north = lax.fori_loop(0, NSUB, body, carry)
     finals = (height, east_vel, north_vel, sum_east / NSUB, sum_north / NSUB)
     out_cols = o_ref.shape[2]
+    start = pl.multiple_of(off_ref[0], block_rows)
     for index in range(5):
-        o_ref[index] = pltpu.roll(finals[index][:block_rows], cols - BARO_HALO, 1)[:, :out_cols]
+        keep_ref[...] = pltpu.roll(finals[index], cols - BARO_HALO, 1)
+        o_ref[index] = keep_ref[pl.ds(start, block_rows), :out_cols]
 
 
 def baro_run(whole, row_offset, out_cols):
@@ -290,6 +286,7 @@
         out_shape=jax.ShapeDtypeStruct((5, whole.shape[2], out_cols), jnp.float32),
         in_specs=[pl.BlockSpec(memory_space=pltpu.SMEM), pl.BlockSpec(memory_space=pltpu.VMEM)],
         out_specs=pl.BlockSpec(memory_space=pltpu.VMEM),
+        scratch_shapes=[pltpu.VMEM((whole.shape[0] * whole.shape[2], whole.shape[3]), jnp.float32)],
     )(row_offset, whole)
 
 

time: 151 us -> 156 us (1.033)
  other arithmetic: 51.7 us -> 59.1 us
  starting transfers between devices: 52.5 us -> 48.6 us
  waiting for transfers between devices: 17.2 us -> 19.4 us
    ppermute x7 -> x0, starting transfers between devices: 10.4 us -> none  [gather_baro(): blocks.append(lax.ppermute(wide, merid, pairs))]
    all_to_all x0 -> x1, starting transfers between devices: none -> 6.27 us  [gather_baro(): return lax.all_to_all(copies, merid, 0, 0)]
    another operation x4, other arithmetic: 3.83 us -> 9.03 us  [tendency(): return jnp.stack(changes)]
    ppermute x1, waiting for transfers between devices: 0.01 us -> 4.88 us  [gather_baro(): low = lax.ppermute(fields[..., -BARO_HALO:], 'gx', forward)]
    ppermute x7 -> x0, waiting for transfers between devices: 2.72 us -> none  [gather_baro(): blocks.append(lax.ppermute(wide, merid, pairs))]
  transfers between devices with their start and end apart: 17 -> 11, of which waited for: 3 -> 3; matrix products, arithmetic and copies ran while one was open for 9% -> 12% of each run, Pallas kernels for 3% -> 3%
where the time goes in v4:
time: 156 us; the launch traced here: 155 us
  other arithmetic  59.1 us (38%)
  starting transfers between devices  48.6 us (31%)
  waiting for transfers between devices  19.4 us (12%)
  Pallas kernels  14.5 us (9%)
  local copies, waits for them, and re-layouts  12.9 us (8%)
    ppermute x4, starting transfers between devices, send(): return lax.ppermute(piece, both, pairs)  26.9 us
    another operation x1, other arithmetic, shards(): jnp.cumsum(weight, axis=0) - weight + 0.5 * weight  20.2 us
    ppermute x4, waiting for transfers between devices, send(): return lax.ppermute(piece, both, pairs)  14.5 us
    concatenate x1, other arithmetic, halo_3d(): return jnp.concatenate([low_band, middle, high_band], axis=-2)  9.52 us
    pallas_call x1, Pallas kernels, baro_run(): pl.pallas_call(baro_kernel, out_shape=jax.ShapeDtypeStruct((5, whole.shap...  9.34 us
    another operation x4, other arithmetic, tendency(): return jnp.stack(changes)  9.03 us
    mul x2, other arithmetic, laplace(): return (beside_all - 4.0 * centre) * wet_mask[..., 1:-1, 1:-1]  7.25 us
    ppermute x1, starting transfers between devices, gather_baro(): high = lax.ppermute(fields[..., :BARO_HALO], 'gx', backward)  7.09 us
  transfers between devices with their start and end apart: 11, of which 3 were waited for; matrix products, arithmetic and copies ran while one was open for 12% of the time, Pallas kernels for 3%

profile of v4, /device:TPU:1, one launch (start us, length us, event | category | flops | bytes accessed | tf_op | source)
XLA Modules:
  0.0 155.4 jit_solution(3601171484178637464)
XLA Ops:
  0.6 0.8 convert_element_type.4
  1.4 0.7 fusion.48
  2.1 1.6 %broadcast_multiply_fusion.2 = (f32[80,8,128]{2,1,0:T(8,128)}, f32[8,128]{1,0:T(8,128)S(1)}, f32[80,8,128]{2,1,0:T(8,128)S(1)}) fusion(f32[80]{0:T(128)} %th_ref.1, f32[8,128]{1,0:T(8,128)S(1)} %convert_element_type.4, s32[8,128]{1,0:T(8,128)} %param.15), kind=kLoop, calls=%fused_computation.111 | loop fusion | flops 326656 | bytes 667968 | tf_op jit(solution)/shard_map/mul | solution.py:209
  3.7 0.0 copy-done.5
  3.7 1.3 broadcast_multiply_fusion.1
  5.0 0.1 pad_maximum_fusion
  5.1 2.1 %fusion.63 = (f32[5,80,2,2]{3,2,1,0:T(2,128)}, f32[5,80,2,2]{3,2,1,0:T(2,128)}, f32[5,80,2,2]{3,2,1,0:T(2,128)}, f32[5,80,2,2]{3,2,1,0:T(2,128)}) fusion(f32[5,80,8,128]{3,2,1,0:T(8,128)S(1)} %pad_maximum_fusion), kind=kLoop, calls=%fused_computation.139 | loop fusion | bytes 51200 | tf_op jit(solution)/shard_map/slice | solution.py:170
  7.3 13.8 %collective-permute-start.7 = (f32[5,80,2,2]{3,2,1,0:T(2,128)}, f32[5,80,2,2]{3,2,1,0:T(2,128)}, u32[]{:S(2)}, u32[]{:S(2)}) collective-permute-start(f32[5,80,2,2]{3,2,1,0:T(2,128)} %get-tuple-element.19), channel_id=1, source_target_pairs={{1,248},{2,249},{3,250},{4,251},{5,252},{6,253},{7,254},{9,0},{10,... | collective-permute-start | bytes 19208 | tf_op jit(solution)/shard_map/ppermute | solution.py:161
  21.0 1.1 fusion.64
  22.2 2.4 %collective-permute-start.6 = (f32[5,80,2,128]{3,2,1,0:T(2,128)}, f32[5,80,2,128]{3,2,1,0:T(2,128)}, u32[]{:S(2)}, u32[]{:S(2)}) collective-permute-start(f32[5,80,2,128]{3,2,1,0:T(2,128)} %get-tuple-element.22), channel_id=1, source_target_pairs={{1,0},{2,1},{3,2},{4,3},{5,4},{6,5},{7,6},{9,8},{10,9},{11,10},{12... | collective-permute-start | bytes 1228808 | tf_op jit(solution)/shard_map/ppermute | solution.py:160
  24.6 1.7 %fusion.65 = (f32[5,80,8,2]{3,2,1,0:T(8,128)S(1)}, f32[5,80,8,2]{3,2,1,0:T(8,128)}) fusion(f32[5,80,8,128]{3,2,1,0:T(8,128)S(1)} %pad_maximum_fusion), kind=kLoop, calls=%fused_computation.141 | loop fusion | bytes 102400 | tf_op jit(solution)/shard_map/slice | solution.py:166
  26.3 2.0 %copy.14 = f32[5,80,8,2]{1,2,3,0:T(8,128)S(1)} copy(f32[5,80,8,2]{3,2,1,0:T(8,128)} %get-tuple-element.24) | data formatting | bytes 51200 | tf_op jit(solution)/shard_map/slice | solution.py:167
  28.3 0.5 collective-permute-start.4
  28.8 0.5 copy.13
  29.3 1.1 collective-permute-start.3
  30.4 4.4 %collective-permute-start.1 = (f32[5,80,2,128]{3,2,1,0:T(2,128)}, f32[5,80,2,128]{3,2,1,0:T(2,128)}, u32[]{:S(2)}, u32[]{:S(2)}) collective-permute-start(f32[5,80,2,128]{3,2,1,0:T(2,128)} %get-tuple-element.21), channel_id=1, source_target_pairs={{0,1},{1,2},{2,3},{3,4},{4,5},{5,6},{6,7},{8,9},{9,10},{10,11},{11... | collective-permute-start | bytes 1228808 | tf_op jit(solution)/shard_map/ppermute | solution.py:160
  34.8 0.0 copy-done.7
  34.8 0.6 reduce_sum.38
  35.4 0.6 constant_dynamic-update-slice_fusion.6
  36.0 0.0 copy-done.6
  36.1 0.0 collective-permute-done.7
  36.1 2.4 %collective-permute-start.5 = (f32[5,80,2,2]{3,2,1,0:T(2,128)}, f32[5,80,2,2]{3,2,1,0:T(2,128)}, u32[]{:S(2)}, u32[]{:S(2)}) collective-permute-start(f32[5,80,2,2]{3,2,1,0:T(2,128)} %get-tuple-element.18), channel_id=1, source_target_pairs={{1,8},{2,9},{3,10},{4,11},{5,12},{6,13},{7,14},{9,16},{10,17},{11,... | collective-permute-start | bytes 19208 | tf_op jit(solution)/shard_map/ppermute | solution.py:161
  38.5 0.0 collective-permute-done.4
  38.5 8.6 %collective-permute-start.2 = (f32[5,80,2,2]{3,2,1,0:T(2,128)}, f32[5,80,2,2]{3,2,1,0:T(2,128)}, u32[]{:S(2)}, u32[]{:S(2)}) collective-permute-start(f32[5,80,2,2]{3,2,1,0:T(2,128)} %get-tuple-element.20), channel_id=1, source_target_pairs={{0,249},{1,250},{2,251},{3,252},{4,253},{5,254},{6,255},{8,1},{9,2... | collective-permute-start | bytes 19208 | tf_op jit(solution)/shard_map/ppermute | solution.py:161
  47.1 0.0 collective-permute-done.3
  47.1 2.1 %collective-permute-start = (f32[5,80,2,2]{3,2,1,0:T(2,128)}, f32[5,80,2,2]{3,2,1,0:T(2,128)}, u32[]{:S(2)}, u32[]{:S(2)}) collective-permute-start(f32[5,80,2,2]{3,2,1,0:T(2,128)} %get-tuple-element.17), channel_id=1, source_target_pairs={{0,9},{1,10},{2,11},{3,12},{4,13},{5,14},{6,15},{8,17},{9,18},{10,... | collective-permute-start | bytes 19208 | tf_op jit(solution)/shard_map/ppermute | solution.py:161
  49.2 0.1 constant_dynamic-update-slice_fusion.4
  49.3 0.6 copy.16
  49.9 1.7 %copy.15 = f32[5,80,8,2]{3,2,1,0:T(8,128)} copy(f32[5,80,8,2]{1,2,3,0:T(8,128)S(1)} %collective-permute-done.3) | data formatting | bytes 51200 | tf_op jit(solution)/shard_map/ppermute | solution.py:152
  51.7 9.0 %collective-permute-done.5 = f32[5,80,2,2]{3,2,1,0:T(2,128)} collective-permute-done((f32[5,80,2,2]{3,2,1,0:T(2,128)}, f32[5,80,2,2]{3,2,1,0:T(2,128)}, u32[]{:S(2)}, u32[]{:S(2)}) %collective-permute-start.5) | collective-permute-done | bytes 6432 | tf_op jit(solution)/shard_map/ppermute | solution.py:161
  60.6 0.0 collective-permute-done.2
  60.6 5.5 %collective-permute-done = f32[5,80,2,2]{3,2,1,0:T(2,128)} collective-permute-done((f32[5,80,2,2]{3,2,1,0:T(2,128)}, f32[5,80,2,2]{3,2,1,0:T(2,128)}, u32[]{:S(2)}, u32[]{:S(2)}) %collective-permute-start) | collective-permute-done | bytes 6432 | tf_op jit(solution)/shard_map/ppermute | solution.py:161
  66.1 0.0 collective-permute-done.6
  66.1 0.0 collective-permute-done.1
  66.1 9.5 %maximum_maximum_fusion = f32[5,80,12,132]{3,2,1,0:T(8,128)S(1)} fusion(f32[5,80,2,2]{3,2,1,0:T(2,128)} %collective-permute-done.7, f32[5,80,2,128]{3,2,1,0:T(2,128)} %collective-permute-done.6, f32[5,80,2,2]{3,2,1,0:T(2,128)} %collective-permute-done.5, f32[5,80,8,2]{3,2,1,0:T(8,128)S(1)} %copy.16, f32[1,80,8,128]{3,2,1,0:T(8,128)S(1)} %fusion.48, ...), kind=kLoop, calls=%fused_computation | loop fusion | flops 6336000 | bytes 5068800 | tf_op jit(solution)/shard_map/concatenate | solution.py:177
  75.7 2.2 %fusion.62 = (f32[80,12,132]{2,1,0:T(8,128)S(1)}, f32[80,12,132]{2,1,0:T(8,128)S(1)}, f32[80,12,132]{2,1,0:T(8,128)S(1)}, f32[80,12,132]{2,1,0:T(8,128)}, f32[80...) fusion(f32[5,80,12,132]{3,2,1,0:T(8,128)S(1)} %maximum_maximum_fusio, ...), kind=kLoop, calls=%fused_computation.138 | loop fusion | flops 1520640 | bytes 6589760 | tf_op jit(solution)/shard_map/mul | solution.py:49
  77.8 0.8 slice_bitcast_fusion
  78.6 20.2 %add_multiply_fusion = f32[80,12,132]{2,1,0:T(8,128)S(1)} fusion(f32[80,12,132]{2,1,0:T(8,128)S(1)} %get-tuple-element.11), kind=kOutput, calls=%fused_computation.33 | output fusion | flops 10517760 | bytes 1013760 | tf_op jit(solution)/shard_map/jit(cumsum)/reduce_window_sum | solution.py:191
  98.8 1.8 %fusion.1 = f32[80,10,130]{2,1,0:T(8,128)S(1)} fusion(f32[80,12,132]{2,1,0:T(8,128)S(1)} %get-tuple-element.15, f32[80,12,132]{2,1,0:T(8,128)S(1)} %get-tuple-element.13), kind=kLoop, calls=%fused_computation.4 | loop fusion | flops 624000 | bytes 2912000 | tf_op jit(solution)/shard_map/mul | solution.py:29
  100.6 5.5 %fusion.7 = (f32[80,10,130]{2,1,0:T(8,128)S(1)}, f32[80,10,130]{2,1,0:T(8,128)S(1)}, f32[80,10,130]{2,1,0:T(8,128)}) fusion(f32[80,12,132]{2,1,0:T(8,128)S(1)} %get-tuple-element.12, f32[80,12,132]{2,1,0:T(8,128)S(1)} %get-tuple-element.13, f32[80,12,132]{2,1,0:T(8,128)S(1)} %get-tuple-element.16, f32[80,12,132]{2,1,0:T(8,128)S(1)} %get-tuple-element.14), kind=kLoop, calls=%fused_computation.22 | loop fusion | flops 1872000 | bytes 7904000 | tf_op jit(solution)/shard_map/mul | solution.py:29
  106.1 1.1 fusion.40
  107.2 0.0 copy-start.9
  107.2 0.0 copy-start.8
  107.3 1.2 fusion.29
  108.4 0.2 fusion.8
  108.7 0.1 fusion.67
  108.7 7.1 %collective-permute-start.9 = (f32[8,8,64]{2,1,0:T(8,128)S(1)}, f32[8,8,64]{2,1,0:T(8,128)S(1)}, u32[]{:S(2)}, u32[]{:S(2)}) collective-permute-start(f32[8,8,64]{2,1,0:T(8,128)S(1)} %get-tuple-element.33), channel_id=1, source_target_pairs={{8,0},{16,8},{24,16},{32,24},{40,32},{48,40},{56,48},{64,56},{72,6... | collective-permute-start | bytes 49160 | tf_op jit(solution)/shard_map/ppermute | solution.py:223
  115.8 0.0 collective-permute-start.8
  115.8 1.6 %fusion.13 = f32[1,80,8,128]{3,2,1,0:T(8,128)} fusion(f32[80,12,132]{2,1,0:T(8,128)S(1)} %get-tuple-element.9, f32[80,12,132]{2,1,0:T(8,128)S(1)} %get-tuple-element.10, f32[80,10,130]{2,1,0:T(8,128)S(1)} %fusion.1, f32[80,12,132]{2,1,0:T(8,128)S(1)} %get-tuple-element.13), kind=kLoop, calls=%fused_computation.44 | loop fusion | flops 1064960 | bytes 3604480 | tf_op jit(solution)/shard_map/stack | solution.py:58
  117.4 0.0 collective-permute-done.9
  117.4 4.9 %collective-permute-done.8 = f32[8,8,64]{2,1,0:T(8,128)S(1)} collective-permute-done((f32[8,8,64]{2,1,0:T(8,128)S(1)}, f32[8,8,64]{2,1,0:T(8,128)S(1)}, u32[]{:S(2)}, u32[]{:S(2)}) %collective-permute-start.8) | collective-permute-done | bytes 16416 | tf_op jit(solution)/shard_map/ppermute | solution.py:222
  122.3 0.1 pad_maximum_fusion.1
  122.4 0.8 broadcast_in_dim.8
  123.2 6.3 %all-to-all-start = ((f32[8,8,8,256]{3,2,1,0:T(8,128)}), f32[8,8,8,256]{3,2,1,0:T(8,128)}, u32[]{:S(2)}, u32[]{:S(2)}) async-start(f32[8,8,8,256]{3,2,1,0:T(8,128)} %broadcast_in_dim.8), calls=%async_computation | async-start | bytes 1048576 | tf_op jit(solution)/shard_map/all_to_all | solution.py:228
  129.5 5.2 %fusion.21 = f32[1,80,8,128]{3,2,1,0:T(8,128)S(1)} fusion(f32[80,12,132]{2,1,0:T(8,128)} %get-tuple-element.7, f32[80,12,132]{2,1,0:T(8,128)} %get-tuple-element.8, f32[80,10,130]{2,1,0:T(8,128)} %get-tuple-element.29, f32[80,12,132]{2,1,0:T(8,128)S(1)} %get-tuple-element.13), kind=kLoop, calls=%fused_computation.58 | loop fusion | flops 1064960 | bytes 3604480 | tf_op jit(solution)/shard_map/stack | solution.py:58
  134.7 1.2 maximum_add_fusion.prov_ref
  135.9 5.1 %shard_map.120 = f32[4,80,8,128]{3,2,1,0:T(8,128)} custom-call(f32[80]{0:T(128)} %th_ref.1, f32[4,80,8,128]{3,2,1,0:T(8,128)} %maximum_add_fusion.prov_ref, f32[80,8,128]{2,1,0:T(8,128)} %mix_ref.1, f32[80,8,128]{2,1,0:T(8,128)} %copy-done.1), custom_call_target="tpu_custom_call" | custom-call | tf_op jit(solution)/shard_map/pallas_call | solution.py:336
  141.1 1.3 multiply_reduce_fusion
  142.3 0.0 all-to-all-done.f_ref
  142.3 9.3 %shard_map.121 = f32[5,8,128]{2,1,0:T(8,128)} custom-call(s32[1]{0:T(128)} %bitcast.9.off_ref, f32[8,8,8,256]{3,2,1,0:T(8,128)} %all-to-all-done.f_ref), custom_call_target="tpu_custom_call" | custom-call | tf_op jit(solution)/shard_map/pallas_call | solution.py:284
  151.7 1.3 slice_bitcast_fusion.5
  153.0 1.3 fusion.68
  154.3 0.0 copy-done
  154.3 1.2 fusion.66
  (23 shorter events, 0.1 us)
Async XLA Ops:
  0.6 3.1 %copy-start.5 = (f32[2,80,8,128]{3,2,1,0:T(8,128)S(1)}, f32[2,80,8,128]{3,2,1,0:T(8,128)}, u32[]{:S(2)}) copy-start(f32[2,80,8,128]{3,2,1,0:T(8,128)} %param.9) | copy-start | bytes 1966084
  3.7 1.3 copy-start.1
  7.3 28.8 %collective-permute-start.7 = (f32[5,80,2,2]{3,2,1,0:T(2,128)}, f32[5,80,2,2]{3,2,1,0:T(2,128)}, u32[]{:S(2)}, u32[]{:S(2)}) collective-permute-start(f32[5,80,2,2]{3,2,1,0:T(2,128)} %get-tuple-element.19), channel_id=1, source_target_pairs={{1,248},{2,249},{3,250},{4,251},{5,252},{6,253},{7,254},{9,0},{10,... | collective-permute-start | bytes 19208 | tf_op jit(solution)/shard_map/ppermute | solution.py:161
  22.2 44.0 %collective-permute-start.6 = (f32[5,80,2,128]{3,2,1,0:T(2,128)}, f32[5,80,2,128]{3,2,1,0:T(2,128)}, u32[]{:S(2)}, u32[]{:S(2)}) collective-permute-start(f32[5,80,2,128]{3,2,1,0:T(2,128)} %get-tuple-element.22), channel_id=1, source_target_pairs={{1,0},{2,1},{3,2},{4,3},{5,4},{6,5},{7,6},{9,8},{10,9},{11,10},{12... | collective-permute-start | bytes 1228808 | tf_op jit(solution)/shard_map/ppermute | solution.py:160
  26.3 8.5 %copy-start.7 = (f32[80]{0:T(128)S(1)}, f32[80]{0:T(128)}, u32[]{:S(2)}) copy-start(f32[80]{0:T(128)} %th_ref.1) | copy-start | bytes 964
  26.3 9.8 %copy-start.6 = (s32[8,128]{1,0:T(8,128)S(1)}, s32[8,128]{1,0:T(8,128)}, u32[]{:S(2)}) copy-start(s32[8,128]{1,0:T(8,128)} %param.14) | copy-start | bytes 12292
  26.3 22.9 %copy-start.10 = (f32[8]{0:T(128)S(1)}, f32[8]{0:T(128)}, u32[]{:S(2)}) copy-start(f32[8]{0:T(128)} %param.13) | copy-start | bytes 100
  28.3 10.2 %collective-permute-start.4 = (f32[5,80,8,2]{1,2,3,0:T(8,128)S(1)}, f32[5,80,8,2]{1,2,3,0:T(8,128)S(1)}, u32[]{:S(2)}, u32[]{:S(2)}) collective-permute-start(f32[5,80,8,2]{1,2,3,0:T(8,128)S(1)} %copy.14), channel_id=1, source_target_pairs={{0,248},{8,0},{16,8},{24,16},{32,24},{40,32},{48,40},{56,48},{64,5... | collective-permute-start | bytes 76808 | tf_op jit(solution)/shard_map/ppermute | solution.py:152
  29.3 17.8 %collective-permute-start.3 = (f32[5,80,8,2]{1,2,3,0:T(8,128)S(1)}, f32[5,80,8,2]{1,2,3,0:T(8,128)S(1)}, u32[]{:S(2)}, u32[]{:S(2)}) collective-permute-start(f32[5,80,8,2]{1,2,3,0:T(8,128)S(1)} %copy.13), channel_id=1, source_target_pairs={{0,8},{8,16},{16,24},{24,32},{32,40},{40,48},{48,56},{56,64},{64,7... | collective-permute-start | bytes 76808 | tf_op jit(solution)/shard_map/ppermute | solution.py:152
  30.4 35.7 %collective-permute-start.1 = (f32[5,80,2,128]{3,2,1,0:T(2,128)}, f32[5,80,2,128]{3,2,1,0:T(2,128)}, u32[]{:S(2)}, u32[]{:S(2)}) collective-permute-start(f32[5,80,2,128]{3,2,1,0:T(2,128)} %get-tuple-element.21), channel_id=1, source_target_pairs={{0,1},{1,2},{2,3},{3,4},{4,5},{5,6},{6,7},{8,9},{9,10},{10,11},{11... | collective-permute-start | bytes 1228808 | tf_op jit(solution)/shard_map/ppermute | solution.py:160
  36.1 24.6 %collective-permute-start.5 = (f32[5,80,2,2]{3,2,1,0:T(2,128)}, f32[5,80,2,2]{3,2,1,0:T(2,128)}, u32[]{:S(2)}, u32[]{:S(2)}) collective-permute-start(f32[5,80,2,2]{3,2,1,0:T(2,128)} %get-tuple-element.18), channel_id=1, source_target_pairs={{1,8},{2,9},{3,10},{4,11},{5,12},{6,13},{7,14},{9,16},{10,17},{11,... | collective-permute-start | bytes 19208 | tf_op jit(solution)/shard_map/ppermute | solution.py:161
  38.5 22.1 %collective-permute-start.2 = (f32[5,80,2,2]{3,2,1,0:T(2,128)}, f32[5,80,2,2]{3,2,1,0:T(2,128)}, u32[]{:S(2)}, u32[]{:S(2)}) collective-permute-start(f32[5,80,2,2]{3,2,1,0:T(2,128)} %get-tuple-element.20), channel_id=1, source_target_pairs={{0,249},{1,250},{2,251},{3,252},{4,253},{5,254},{6,255},{8,1},{9,2... | collective-permute-start | bytes 19208 | tf_op jit(solution)/shard_map/ppermute | solution.py:161
  47.1 19.0 %collective-permute-start = (f32[5,80,2,2]{3,2,1,0:T(2,128)}, f32[5,80,2,2]{3,2,1,0:T(2,128)}, u32[]{:S(2)}, u32[]{:S(2)}) collective-permute-start(f32[5,80,2,2]{3,2,1,0:T(2,128)} %get-tuple-element.17), channel_id=1, source_target_pairs={{0,9},{1,10},{2,11},{3,12},{4,13},{5,14},{6,15},{8,17},{9,18},{10,... | collective-permute-start | bytes 19208 | tf_op jit(solution)/shard_map/ppermute | solution.py:161
  107.2 1.4 copy-start.9
  107.2 1.4 copy-start.8
  108.7 8.7 %collective-permute-start.9 = (f32[8,8,64]{2,1,0:T(8,128)S(1)}, f32[8,8,64]{2,1,0:T(8,128)S(1)}, u32[]{:S(2)}, u32[]{:S(2)}) collective-permute-start(f32[8,8,64]{2,1,0:T(8,128)S(1)} %get-tuple-element.33), channel_id=1, source_target_pairs={{8,0},{16,8},{24,16},{32,24},{40,32},{48,40},{56,48},{64,56},{72,6... | collective-permute-start | bytes 49160 | tf_op jit(solution)/shard_map/ppermute | solution.py:223
  115.8 6.4 %collective-permute-start.8 = (f32[8,8,64]{2,1,0:T(8,128)S(1)}, f32[8,8,64]{2,1,0:T(8,128)S(1)}, u32[]{:S(2)}, u32[]{:S(2)}) collective-permute-start(f32[8,8,64]{2,1,0:T(8,128)S(1)} %get-tuple-element.32), channel_id=1, source_target_pairs={{0,8},{8,16},{16,24},{24,32},{32,40},{40,48},{48,56},{56,64},{64,7... | collective-permute-start | bytes 49160 | tf_op jit(solution)/shard_map/ppermute | solution.py:222
  123.2 19.1 %all-to-all-start = ((f32[8,8,8,256]{3,2,1,0:T(8,128)}), f32[8,8,8,256]{3,2,1,0:T(8,128)}, u32[]{:S(2)}, u32[]{:S(2)}) async-start(f32[8,8,8,256]{3,2,1,0:T(8,128)} %broadcast_in_dim.8), calls=%async_computation | async-start | bytes 1048576 | tf_op jit(solution)/shard_map/all_to_all | solution.py:228
  129.5 5.2 %copy-start.4 = (f32[1,80,8,128]{3,2,1,0:T(8,128)S(1)}, f32[1,80,8,128]{3,2,1,0:T(8,128)}, u32[]{:S(2)}) copy-start(f32[1,80,8,128]{3,2,1,0:T(8,128)} %fusion.13) | copy-start | bytes 983044
  135.9 5.2 %copy-start.3 = (f32[80,8,128]{2,1,0:T(8,128)S(1)}, f32[80,8,128]{2,1,0:T(8,128)}, u32[]{:S(2)}) copy-start(f32[80,8,128]{2,1,0:T(8,128)} %get-tuple-element.36) | copy-start | bytes 983044
  135.9 18.4 %copy-start.2 = (f32[80,8,128]{2,1,0:T(8,128)S(1)}, f32[80,8,128]{2,1,0:T(8,128)}, u32[]{:S(2)}) copy-start(f32[80,8,128]{2,1,0:T(8,128)} %copy-done.1) | copy-start | bytes 983044
  141.0 13.2 %copy-start = (f32[4,80,8,128]{3,2,1,0:T(8,128)S(1)}, f32[4,80,8,128]{3,2,1,0:T(8,128)}, u32[]{:S(2)}) copy-start(f32[4,80,8,128]{3,2,1,0:T(8,128)} %shard_map.120) | copy-start | bytes 3932164

commit v5 on v3

--- a/solution.py
+++ b/solution.py
@@ -187,8 +187,7 @@
     )
     padded = halo_3d(stacked)
     depth_col = thickness.reshape((levels, 1, 1))
-    weight = (contract_salt * padded[3] - expand_temp * padded[2]) * padded[4] * depth_col
-    pressure = press_scale * (jnp.cumsum(weight, axis=0) - weight + 0.5 * weight)
+    pressure = pressure_run(thickness, padded)
     growth = tendency(padded, pressure, coriolis)
     provisional = stacked[:4] + step_main * growth
     forcing = jnp.sum(depth_col * growth[:2], axis=1)
@@ -291,6 +290,26 @@
         in_specs=[pl.BlockSpec(memory_space=pltpu.SMEM), pl.BlockSpec(memory_space=pltpu.VMEM)],
         out_specs=pl.BlockSpec(memory_space=pltpu.VMEM),
     )(row_offset, whole)
+
+
+def pressure_kernel(th_ref, pad_ref, o_ref):
+    levels = pad_ref.shape[1]
+
+    def body(k, overlying):
+        weight = (contract_salt * pad_ref[3, k] - expand_temp * pad_ref[2, k]) * pad_ref[4, k] * th_ref[k]
+        o_ref[k] = press_scale * (overlying + 0.5 * weight)
+        return overlying + weight
+
+    lax.fori_loop(0, levels, body, jnp.zeros(pad_ref.shape[2:], jnp.float32))
+
+
+def pressure_run(thickness, padded):
+    return pl.pallas_call(
+        pressure_kernel,
+        out_shape=jax.ShapeDtypeStruct(padded.shape[1:], jnp.float32),
+        in_specs=[pl.BlockSpec(memory_space=pltpu.SMEM), pl.BlockSpec(memory_space=pltpu.VMEM)],
+        out_specs=pl.BlockSpec(memory_space=pltpu.VMEM),
+    )(thickness, padded)
 
 
 def solve_kernel(th_ref, prov_ref, mix_ref, wet_ref, o_ref, ratio_ref):

time: 151 us -> 148 us (0.980)
  other arithmetic: 51.7 us -> 39 us
  Pallas kernels: 14 us -> 18.9 us
  local copies, waits for them, and re-layouts: 13.6 us -> 17.1 us
    another operation x1 -> x0, other arithmetic: 20.2 us -> none  [shards(): jnp.cumsum(weight, axis=0) - weight + 0.5 * weight]
    pallas_call x0 -> x1, Pallas kernels: none -> 4.9 us  [pressure_run(): pl.pallas_call(pressure_kernel, out_shape=jax.ShapeDtypeStruct(padded.sha...]
    mul x2, other arithmetic: 6.38 us -> 10.4 us  [laplace(): return (beside_all - 4.0 * centre) * wet_mask[..., 1:-1, 1:-1]]
    mul x1, other arithmetic: 0.7 us -> 4.24 us  [tendency(): advect = diff_x(east_vel * quantity) + diff_y(north_vel * quantity)]
    unnamed x34 -> x58, local copies, waits for them, and re-layouts: 0.95 us -> 3.51 us
    squeeze x1, local copies, waits for them, and re-layouts: 0.79 us -> 2.35 us  [tendency(): quantity = padded[component]]
  transfers between devices with their start and end apart: 17 -> 17, of which waited for: 3 -> 3; matrix products, arithmetic and copies ran while one was open for 9% -> 9% of each run, Pallas kernels for 3% -> 4%
where the time goes in v5:
time: 148 us; the launch traced here: 147 us
  starting transfers between devices  53.6 us (36%)
  other arithmetic  39 us (26%)
  Pallas kernels  18.9 us (13%)
  waiting for transfers between devices  17.2 us (12%)
  local copies, waits for them, and re-layouts  17.1 us (12%)
    ppermute x4, starting transfers between devices, send(): return lax.ppermute(piece, both, pairs)  26.9 us
    ppermute x4, waiting for transfers between devices, send(): return lax.ppermute(piece, both, pairs)  14.4 us
    ppermute x7, starting transfers between devices, gather_baro(): blocks.append(lax.ppermute(wide, merid, pairs))  11.1 us
    mul x2, other arithmetic, laplace(): return (beside_all - 4.0 * centre) * wet_mask[..., 1:-1, 1:-1]  10.4 us
    concatenate x1, other arithmetic, halo_3d(): return jnp.concatenate([low_band, middle, high_band], axis=-2)  9.53 us
    pallas_call x1, Pallas kernels, baro_run(): pl.pallas_call(baro_kernel, out_shape=jax.ShapeDtypeStruct((5, whole.shap...  8.88 us
    ppermute x1, starting transfers between devices, gather_baro(): high = lax.ppermute(fields[..., :BARO_HALO], 'gx', backward)  7.31 us
    ppermute x2, starting transfers between devices, send(): lax.ppermute(piece, merid, [(s % merid_n, t % merid_n) for s, t in pairs[...  6.76 us
  transfers between devices with their start and end apart: 17, of which 3 were waited for; matrix products, arithmetic and copies ran while one was open for 9% of the time, Pallas kernels for 4%

profile of v5, /device:TPU:1, one launch (start us, length us, event | category | flops | bytes accessed | tf_op | source)
XLA Modules:
  0.0 147.0 jit_solution(7959501780470481819)
XLA Ops:
  0.6 0.8 convert_element_type.4
  1.4 0.7 fusion.48
  2.1 1.6 %broadcast_multiply_fusion.2 = (f32[80,8,128]{2,1,0:T(8,128)}, f32[8,128]{1,0:T(8,128)S(1)}, f32[80,8,128]{2,1,0:T(8,128)S(1)}) fusion(f32[80]{0:T(128)} %th_ref.3, f32[8,128]{1,0:T(8,128)S(1)} %convert_element_type.4, s32[8,128]{1,0:T(8,128)} %param.15), kind=kLoop, calls=%fused_computation.109 | loop fusion | flops 326656 | bytes 667968 | tf_op jit(solution)/shard_map/mul | solution.py:208
  3.7 1.3 broadcast_multiply_fusion.1
  5.0 0.0 copy-start.3
  5.0 0.1 pad_maximum_fusion
  5.1 2.1 %fusion.63 = (f32[5,80,2,2]{3,2,1,0:T(2,128)}, f32[5,80,2,2]{3,2,1,0:T(2,128)}, f32[5,80,2,2]{3,2,1,0:T(2,128)}, f32[5,80,2,2]{3,2,1,0:T(2,128)}) fusion(f32[5,80,8,128]{3,2,1,0:T(8,128)S(1)} %pad_maximum_fusion), kind=kLoop, calls=%fused_computation.145 | loop fusion | bytes 51200 | tf_op jit(solution)/shard_map/slice | solution.py:170
  7.3 13.8 %collective-permute-start.7 = (f32[5,80,2,2]{3,2,1,0:T(2,128)}, f32[5,80,2,2]{3,2,1,0:T(2,128)}, u32[]{:S(2)}, u32[]{:S(2)}) collective-permute-start(f32[5,80,2,2]{3,2,1,0:T(2,128)} %get-tuple-element.20), channel_id=1, source_target_pairs={{1,248},{2,249},{3,250},{4,251},{5,252},{6,253},{7,254},{9,0},{10,... | collective-permute-start | bytes 19208 | tf_op jit(solution)/shard_map/ppermute | solution.py:161
  21.0 1.2 fusion.64
  22.2 2.4 %collective-permute-start.6 = (f32[5,80,2,128]{3,2,1,0:T(2,128)}, f32[5,80,2,128]{3,2,1,0:T(2,128)}, u32[]{:S(2)}, u32[]{:S(2)}) collective-permute-start(f32[5,80,2,128]{3,2,1,0:T(2,128)} %get-tuple-element.23), channel_id=1, source_target_pairs={{1,0},{2,1},{3,2},{4,3},{5,4},{6,5},{7,6},{9,8},{10,9},{11,10},{12... | collective-permute-start | bytes 1228808 | tf_op jit(solution)/shard_map/ppermute | solution.py:160
  24.6 1.7 %fusion.65 = (f32[5,80,8,2]{3,2,1,0:T(8,128)S(1)}, f32[5,80,8,2]{3,2,1,0:T(8,128)}) fusion(f32[5,80,8,128]{3,2,1,0:T(8,128)S(1)} %pad_maximum_fusion), kind=kLoop, calls=%fused_computation.147 | loop fusion | bytes 102400 | tf_op jit(solution)/shard_map/slice | solution.py:166
  26.3 2.0 %copy.14 = f32[5,80,8,2]{1,2,3,0:T(8,128)S(1)} copy(f32[5,80,8,2]{3,2,1,0:T(8,128)} %get-tuple-element.25) | data formatting | bytes 51200 | tf_op jit(solution)/shard_map/slice | solution.py:167
  28.3 0.5 collective-permute-start.4
  28.9 0.5 copy.13
  29.4 1.1 collective-permute-start.3
  30.5 4.4 %collective-permute-start.1 = (f32[5,80,2,128]{3,2,1,0:T(2,128)}, f32[5,80,2,128]{3,2,1,0:T(2,128)}, u32[]{:S(2)}, u32[]{:S(2)}) collective-permute-start(f32[5,80,2,128]{3,2,1,0:T(2,128)} %get-tuple-element.22), channel_id=1, source_target_pairs={{0,1},{1,2},{2,3},{3,4},{4,5},{5,6},{6,7},{8,9},{9,10},{10,11},{11... | collective-permute-start | bytes 1228808 | tf_op jit(solution)/shard_map/ppermute | solution.py:160
  34.8 0.6 reduce_sum.38
  35.4 0.6 constant_dynamic-update-slice_fusion.6
  36.1 0.0 collective-permute-done.7
  36.1 2.4 %collective-permute-start.5 = (f32[5,80,2,2]{3,2,1,0:T(2,128)}, f32[5,80,2,2]{3,2,1,0:T(2,128)}, u32[]{:S(2)}, u32[]{:S(2)}) collective-permute-start(f32[5,80,2,2]{3,2,1,0:T(2,128)} %get-tuple-element.19), channel_id=1, source_target_pairs={{1,8},{2,9},{3,10},{4,11},{5,12},{6,13},{7,14},{9,16},{10,17},{11,... | collective-permute-start | bytes 19208 | tf_op jit(solution)/shard_map/ppermute | solution.py:161
  38.6 0.0 collective-permute-done.4
  38.6 8.6 %collective-permute-start.2 = (f32[5,80,2,2]{3,2,1,0:T(2,128)}, f32[5,80,2,2]{3,2,1,0:T(2,128)}, u32[]{:S(2)}, u32[]{:S(2)}) collective-permute-start(f32[5,80,2,2]{3,2,1,0:T(2,128)} %get-tuple-element.21), channel_id=1, source_target_pairs={{0,249},{1,250},{2,251},{3,252},{4,253},{5,254},{6,255},{8,1},{9,2... | collective-permute-start | bytes 19208 | tf_op jit(solution)/shard_map/ppermute | solution.py:161
  47.2 0.0 collective-permute-done.3
  47.2 2.1 %collective-permute-start = (f32[5,80,2,2]{3,2,1,0:T(2,128)}, f32[5,80,2,2]{3,2,1,0:T(2,128)}, u32[]{:S(2)}, u32[]{:S(2)}) collective-permute-start(f32[5,80,2,2]{3,2,1,0:T(2,128)} %get-tuple-element.18), channel_id=1, source_target_pairs={{0,9},{1,10},{2,11},{3,12},{4,13},{5,14},{6,15},{8,17},{9,18},{10,... | collective-permute-start | bytes 19208 | tf_op jit(solution)/shard_map/ppermute | solution.py:161
  49.3 0.1 constant_dynamic-update-slice_fusion.4
  49.4 0.6 copy.16
  50.0 1.8 %copy.15 = f32[5,80,8,2]{3,2,1,0:T(8,128)} copy(f32[5,80,8,2]{1,2,3,0:T(8,128)S(1)} %collective-permute-done.3) | data formatting | bytes 51200 | tf_op jit(solution)/shard_map/ppermute | solution.py:152
  51.7 8.9 %collective-permute-done.5 = f32[5,80,2,2]{3,2,1,0:T(2,128)} collective-permute-done((f32[5,80,2,2]{3,2,1,0:T(2,128)}, f32[5,80,2,2]{3,2,1,0:T(2,128)}, u32[]{:S(2)}, u32[]{:S(2)}) %collective-permute-start.5) | collective-permute-done | bytes 6432 | tf_op jit(solution)/shard_map/ppermute | solution.py:161
  60.7 5.5 %collective-permute-done = f32[5,80,2,2]{3,2,1,0:T(2,128)} collective-permute-done((f32[5,80,2,2]{3,2,1,0:T(2,128)}, f32[5,80,2,2]{3,2,1,0:T(2,128)}, u32[]{:S(2)}, u32[]{:S(2)}) %collective-permute-start) | collective-permute-done | bytes 6432 | tf_op jit(solution)/shard_map/ppermute | solution.py:161
  66.2 0.0 collective-permute-done.1
  66.2 9.5 %maximum_maximum_fusion.pad_ref = f32[5,80,12,132]{3,2,1,0:T(8,128)S(1)} fusion(f32[5,80,2,2]{3,2,1,0:T(2,128)} %collective-permute-done.7, f32[5,80,2,128]{3,2,1,0:T(2,128)} %collective-permute-done.6, f32[5,80,2,2]{3,2,1,0:T(2,128)} %collective-permute-done.5, f32[5,80,8,2]{3,2,1,0:T(8,128)S(1)} %copy.16, f32[1,80,8,128]{3,2,1,0:T(8,128)S(1)} %fusion.48, ...), kind=kLoop, calls=%fused_computation | loop fusion | flops 6336000 | bytes 5068800 | tf_op jit(solution)/shard_map/concatenate | solution.py:177
  75.7 4.2 %fusion.62 = (f32[80,12,132]{2,1,0:T(8,128)}, f32[80,12,132]{2,1,0:T(8,128)}, f32[80,12,132]{2,1,0:T(8,128)}, f32[80,12,132]{2,1,0:T(8,128)}, f32[80,12,132]{2,1...) fusion(f32[5,80,12,132]{3,2,1,0:T(8,128)S(1)} %maximum_maximum_fusion.pad_ref), kind=kLoop, calls=%fused_computation.144 | loop fusion | flops 887040 | bytes 5575680 | tf_op jit(solution)/shard_map/mul | solution.py:49
  80.0 1.2 copy-done
  81.2 2.3 %slice_bitcast_fusion.3 = (f32[80,12,132]{2,1,0:T(8,128)S(1)}, f32[80,12,132]{2,1,0:T(8,128)}, f32[80,12,132]{2,1,0:T(8,128)}, f32[80,12,132]{2,1,0:T(8,128)}, f32[80,12,132]{2,1,0:T(8,128)S(1)}) fusion(f32[5,80,12,132]{3,2,1,0:T(8,128)S(1)} %maximum_maximum_fusion.pad_ref), kind=kLoop, calls=%fused_computation.29 | loop fusion | bytes 5068800 | tf_op jit(solution)/shard_map/squeeze | solution.py:48
  83.5 4.9 %shard_map.120 = f32[80,12,132]{2,1,0:T(8,128)} custom-call(f32[80]{0:T(128)} %th_ref.3, f32[5,80,12,132]{3,2,1,0:T(8,128)} %copy-done), custom_call_target="tpu_custom_call" | custom-call | tf_op jit(solution)/shard_map/pallas_call | solution.py:307
  88.4 5.8 %fusion.1 = f32[80,10,130]{2,1,0:T(8,128)S(1)} fusion(f32[80,12,132]{2,1,0:T(8,128)} %get-tuple-element.14, f32[80,12,132]{2,1,0:T(8,128)} %get-tuple-element.16), kind=kLoop, calls=%fused_computation.4 | loop fusion | flops 624000 | bytes 2912000 | tf_op jit(solution)/shard_map/mul | solution.py:29
  94.3 4.6 %fusion.7 = (f32[80,10,130]{2,1,0:T(8,128)S(1)}, f32[80,10,130]{2,1,0:T(8,128)S(1)}, f32[80,10,130]{2,1,0:T(8,128)S(1)}) fusion(f32[80,12,132]{2,1,0:T(8,128)S(1)} %get-tuple-element.13, f32[80,12,132]{2,1,0:T(8,128)S(1)} %copy-done.2, f32[80,12,132]{2,1,0:T(8,128)S(1)} %get-tuple-element.17, f32[80,12,132]{2,1,0:T(8,128)S(1)} %copy-done.1), kind=kLoop, calls=%fused_computation.25 | loop fusion | flops 1872000 | bytes 7904000 | tf_op jit(solution)/shard_map/mul | solution.py:29
  99.0 1.1 fusion.40
  100.1 0.2 copy-done.14
  100.3 1.1 fusion.29
  101.4 0.2 fusion.8
  101.6 0.1 fusion.67
  101.7 7.3 %collective-permute-start.9 = (f32[8,8,64]{2,1,0:T(8,128)S(1)}, f32[8,8,64]{2,1,0:T(8,128)S(1)}, u32[]{:S(2)}, u32[]{:S(2)}) collective-permute-start(f32[8,8,64]{2,1,0:T(8,128)S(1)} %get-tuple-element.34), channel_id=1, source_target_pairs={{8,0},{16,8},{24,16},{32,24},{40,32},{48,40},{56,48},{64,56},{72,6... | collective-permute-start | bytes 49160 | tf_op jit(solution)/shard_map/ppermute | solution.py:222
  109.0 0.8 fusion.13
  109.9 0.5 copy-done.10
  110.3 0.4 copy-done.11
  110.7 0.8 fusion.21
  111.6 0.2 copy-done.4
  111.8 1.3 maximum_add_fusion.prov_ref
  113.1 5.1 %shard_map.121 = f32[4,80,8,128]{3,2,1,0:T(8,128)} custom-call(f32[80]{0:T(128)} %th_ref.3, f32[4,80,8,128]{3,2,1,0:T(8,128)} %maximum_add_fusion.prov_ref, f32[80,8,128]{2,1,0:T(8,128)} %mix_ref.1, f32[80,8,128]{2,1,0:T(8,128)} %copy-done.8), custom_call_target="tpu_custom_call" | custom-call | tf_op jit(solution)/shard_map/pallas_call | solution.py:358
  118.2 0.1 bitcast_dynamic-update-slice_fusion.7
  118.4 0.1 collective-permute-start.10
  118.5 1.3 multiply_reduce_fusion
  119.7 0.1 collective-permute-start.11
  119.8 6.4 %collective-permute-start.12 = (f32[8,8,256]{2,1,0:T(8,128)S(1)}, f32[8,8,256]{2,1,0:T(8,128)S(1)}, u32[]{:S(2)}, u32[]{:S(2)}) collective-permute-start(f32[8,8,256]{2,1,0:T(8,128)S(1)} %get-tuple-element.5), channel_id=1, source_target_pairs={{0,5},{1,6},{2,7},{3,0},{4,1},{5,2},{6,3},{7,4},{8,13},{9,14},{10,... | collective-permute-start | bytes 196616 | tf_op jit(solution)/shard_map/ppermute | solution.py:229
  126.3 0.2 collective-permute-start.14
  126.4 1.8 %collective-permute-start.15 = (f32[8,8,256]{2,1,0:T(8,128)S(1)}, f32[8,8,256]{2,1,0:T(8,128)S(1)}, u32[]{:S(2)}, u32[]{:S(2)}) collective-permute-start(f32[8,8,256]{2,1,0:T(8,128)S(1)} %get-tuple-element.5), channel_id=1, source_target_pairs={{0,2},{1,3},{2,4},{3,5},{4,6},{5,7},{6,0},{7,1},{8,10},{9,11},{10,... | collective-permute-start | bytes 196616 | tf_op jit(solution)/shard_map/ppermute | solution.py:229
  128.3 2.5 %collective-permute-start.16 = (f32[8,8,256]{2,1,0:T(8,128)S(1)}, f32[8,8,256]{2,1,0:T(8,128)S(1)}, u32[]{:S(2)}, u32[]{:S(2)}) collective-permute-start(f32[8,8,256]{2,1,0:T(8,128)S(1)} %get-tuple-element.5), channel_id=1, source_target_pairs={{0,1},{1,2},{2,3},{3,4},{4,5},{5,6},{6,7},{7,0},{8,9},{9,10},{10,1... | collective-permute-start | bytes 196616 | tf_op jit(solution)/shard_map/ppermute | solution.py:229
  130.9 2.7 %collective-permute-done.16 = f32[8,8,256]{2,1,0:T(8,128)S(1)} collective-permute-done((f32[8,8,256]{2,1,0:T(8,128)S(1)}, f32[8,8,256]{2,1,0:T(8,128)S(1)}, u32[]{:S(2)}, u32[]{:S(2)}) %collective-permute-start.16) | collective-permute-done | bytes 65568 | tf_op jit(solution)/shard_map/ppermute | solution.py:229
  133.6 0.8 copy-done.17
  134.4 8.9 %shard_map.122 = f32[5,8,128]{2,1,0:T(8,128)} custom-call(s32[1]{0:T(128)} %bitcast.9.off_ref, f32[8,8,8,256]{3,2,1,0:T(8,128)} %copy-done.17), custom_call_target="tpu_custom_call" | custom-call | tf_op jit(solution)/shard_map/pallas_call | solution.py:287
  143.2 1.3 slice_bitcast_fusion.5
  144.5 1.3 fusion.68
  145.8 1.2 fusion.66
  (69 shorter events, 0.2 us)
Async XLA Ops:
  0.6 3.1 %copy-start.18 = (f32[2,80,8,128]{3,2,1,0:T(8,128)S(1)}, f32[2,80,8,128]{3,2,1,0:T(8,128)}, u32[]{:S(2)}) copy-start(f32[2,80,8,128]{3,2,1,0:T(8,128)} %param.9) | copy-start | bytes 1966084
  3.7 1.3 copy-start.8
  5.0 61.2 %copy-start.3 = (f32[2,80,8,128]{3,2,1,0:T(8,128)}, f32[2,80,8,128]{3,2,1,0:T(8,128)S(1)}, u32[]{:S(2)}) copy-start(f32[2,80,8,128]{3,2,1,0:T(8,128)S(1)} %get-tuple-element.32) | copy-start | bytes 1966084
  7.3 28.8 %collective-permute-start.7 = (f32[5,80,2,2]{3,2,1,0:T(2,128)}, f32[5,80,2,2]{3,2,1,0:T(2,128)}, u32[]{:S(2)}, u32[]{:S(2)}) collective-permute-start(f32[5,80,2,2]{3,2,1,0:T(2,128)} %get-tuple-element.20), channel_id=1, source_target_pairs={{1,248},{2,249},{3,250},{4,251},{5,252},{6,253},{7,254},{9,0},{10,... | collective-permute-start | bytes 19208 | tf_op jit(solution)/shard_map/ppermute | solution.py:161
  22.2 44.0 %collective-permute-start.6 = (f32[5,80,2,128]{3,2,1,0:T(2,128)}, f32[5,80,2,128]{3,2,1,0:T(2,128)}, u32[]{:S(2)}, u32[]{:S(2)}) collective-permute-start(f32[5,80,2,128]{3,2,1,0:T(2,128)} %get-tuple-element.23), channel_id=1, source_target_pairs={{1,0},{2,1},{3,2},{4,3},{5,4},{6,5},{7,6},{9,8},{10,9},{11,10},{12... | collective-permute-start | bytes 1228808 | tf_op jit(solution)/shard_map/ppermute | solution.py:160
  26.3 8.5 %copy-start.21 = (f32[80]{0:T(128)S(1)}, f32[80]{0:T(128)}, u32[]{:S(2)}) copy-start(f32[80]{0:T(128)} %th_ref.3) | copy-start | bytes 964
  26.3 9.8 %copy-start.19 = (s32[8,128]{1,0:T(8,128)S(1)}, s32[8,128]{1,0:T(8,128)}, u32[]{:S(2)}) copy-start(s32[8,128]{1,0:T(8,128)} %param.14) | copy-start | bytes 12292
  26.3 22.9 %copy-start.24 = (f32[8]{0:T(128)S(1)}, f32[8]{0:T(128)}, u32[]{:S(2)}) copy-start(f32[8]{0:T(128)} %param.13) | copy-start | bytes 100
  28.3 10.2 %collective-permute-start.4 = (f32[5,80,8,2]{1,2,3,0:T(8,128)S(1)}, f32[5,80,8,2]{1,2,3,0:T(8,128)S(1)}, u32[]{:S(2)}, u32[]{:S(2)}) collective-permute-start(f32[5,80,8,2]{1,2,3,0:T(8,128)S(1)} %copy.14), channel_id=1, source_target_pairs={{0,248},{8,0},{16,8},{24,16},{32,24},{40,32},{48,40},{56,48},{64,5... | collective-permute-start | bytes 76808 | tf_op jit(solution)/shard_map/ppermute | solution.py:152
  29.4 17.8 %collective-permute-start.3 = (f32[5,80,8,2]{1,2,3,0:T(8,128)S(1)}, f32[5,80,8,2]{1,2,3,0:T(8,128)S(1)}, u32[]{:S(2)}, u32[]{:S(2)}) collective-permute-start(f32[5,80,8,2]{1,2,3,0:T(8,128)S(1)} %copy.13), channel_id=1, source_target_pairs={{0,8},{8,16},{16,24},{24,32},{32,40},{40,48},{48,56},{56,64},{64,7... | collective-permute-start | bytes 76808 | tf_op jit(solution)/shard_map/ppermute | solution.py:152
  30.5 35.7 %collective-permute-start.1 = (f32[5,80,2,128]{3,2,1,0:T(2,128)}, f32[5,80,2,128]{3,2,1,0:T(2,128)}, u32[]{:S(2)}, u32[]{:S(2)}) collective-permute-start(f32[5,80,2,128]{3,2,1,0:T(2,128)} %get-tuple-element.22), channel_id=1, source_target_pairs={{0,1},{1,2},{2,3},{3,4},{4,5},{5,6},{6,7},{8,9},{9,10},{10,11},{11... | collective-permute-start | bytes 1228808 | tf_op jit(solution)/shard_map/ppermute | solution.py:160
  36.1 24.6 %collective-permute-start.5 = (f32[5,80,2,2]{3,2,1,0:T(2,128)}, f32[5,80,2,2]{3,2,1,0:T(2,128)}, u32[]{:S(2)}, u32[]{:S(2)}) collective-permute-start(f32[5,80,2,2]{3,2,1,0:T(2,128)} %get-tuple-element.19), channel_id=1, source_target_pairs={{1,8},{2,9},{3,10},{4,11},{5,12},{6,13},{7,14},{9,16},{10,17},{11,... | collective-permute-start | bytes 19208 | tf_op jit(solution)/shard_map/ppermute | solution.py:161
  38.6 22.1 %collective-permute-start.2 = (f32[5,80,2,2]{3,2,1,0:T(2,128)}, f32[5,80,2,2]{3,2,1,0:T(2,128)}, u32[]{:S(2)}, u32[]{:S(2)}) collective-permute-start(f32[5,80,2,2]{3,2,1,0:T(2,128)} %get-tuple-element.21), channel_id=1, source_target_pairs={{0,249},{1,250},{2,251},{3,252},{4,253},{5,254},{6,255},{8,1},{9,2... | collective-permute-start | bytes 19208 | tf_op jit(solution)/shard_map/ppermute | solution.py:161
  47.2 19.0 %collective-permute-start = (f32[5,80,2,2]{3,2,1,0:T(2,128)}, f32[5,80,2,2]{3,2,1,0:T(2,128)}, u32[]{:S(2)}, u32[]{:S(2)}) collective-permute-start(f32[5,80,2,2]{3,2,1,0:T(2,128)} %get-tuple-element.18), channel_id=1, source_target_pairs={{0,9},{1,10},{2,11},{3,12},{4,13},{5,14},{6,15},{8,17},{9,18},{10,... | collective-permute-start | bytes 19208 | tf_op jit(solution)/shard_map/ppermute | solution.py:161
  75.7 5.5 %copy-start = (f32[5,80,12,132]{3,2,1,0:T(8,128)}, f32[5,80,12,132]{3,2,1,0:T(8,128)S(1)}, u32[]{:S(2)}) copy-start(f32[5,80,12,132]{3,2,1,0:T(8,128)S(1)} %maximum_maximum_fusion.pad_ref) | copy-start | bytes 7603204
  88.4 5.8 %copy-start.1 = (f32[80,12,132]{2,1,0:T(8,128)S(1)}, f32[80,12,132]{2,1,0:T(8,128)}, u32[]{:S(2)}) copy-start(f32[80,12,132]{2,1,0:T(8,128)} %get-tuple-element.15) | copy-start | bytes 1520644
  88.4 5.8 %copy-start.2 = (f32[80,12,132]{2,1,0:T(8,128)S(1)}, f32[80,12,132]{2,1,0:T(8,128)}, u32[]{:S(2)}) copy-start(f32[80,12,132]{2,1,0:T(8,128)} %get-tuple-element.16) | copy-start | bytes 1520644
  94.2 4.7 %copy-start.6 = (f32[80,12,132]{2,1,0:T(8,128)S(1)}, f32[80,12,132]{2,1,0:T(8,128)}, u32[]{:S(2)}) copy-start(f32[80,12,132]{2,1,0:T(8,128)} %get-tuple-element.7) | copy-start | bytes 1520644
  94.3 4.7 %copy-start.7 = (f32[80,12,132]{2,1,0:T(8,128)S(1)}, f32[80,12,132]{2,1,0:T(8,128)}, u32[]{:S(2)}) copy-start(f32[80,12,132]{2,1,0:T(8,128)} %shard_map.120) | copy-start | bytes 1520644
  94.3 4.7 %copy-start.15 = (f32[80,12,132]{2,1,0:T(8,128)S(1)}, f32[80,12,132]{2,1,0:T(8,128)}, u32[]{:S(2)}) copy-start(f32[80,12,132]{2,1,0:T(8,128)} %get-tuple-element.6) | copy-start | bytes 1520644
  98.9 1.3 copy-start.14
  100.3 1.1 copy-start.22
  100.3 1.3 copy-start.23
  100.3 1.3 copy-start.20
  100.3 8.7 %copy-start.12 = (f32[80,12,132]{2,1,0:T(8,128)S(1)}, f32[80,12,132]{2,1,0:T(8,128)}, u32[]{:S(2)}) copy-start(f32[80,12,132]{2,1,0:T(8,128)} %get-tuple-element.9) | copy-start | bytes 1520644
  100.3 8.7 %copy-start.13 = (f32[80,12,132]{2,1,0:T(8,128)S(1)}, f32[80,12,132]{2,1,0:T(8,128)}, u32[]{:S(2)}) copy-start(f32[80,12,132]{2,1,0:T(8,128)} %get-tuple-element.10) | copy-start | bytes 1520644
  101.7 16.5 %collective-permute-start.9 = (f32[8,8,64]{2,1,0:T(8,128)S(1)}, f32[8,8,64]{2,1,0:T(8,128)S(1)}, u32[]{:S(2)}, u32[]{:S(2)}) collective-permute-start(f32[8,8,64]{2,1,0:T(8,128)S(1)} %get-tuple-element.34), channel_id=1, source_target_pairs={{8,0},{16,8},{24,16},{32,24},{40,32},{48,40},{56,48},{64,56},{72,6... | collective-permute-start | bytes 49160 | tf_op jit(solution)/shard_map/ppermute | solution.py:222
  109.0 9.2 %collective-permute-start.8 = (f32[8,8,64]{2,1,0:T(8,128)S(1)}, f32[8,8,64]{2,1,0:T(8,128)S(1)}, u32[]{:S(2)}, u32[]{:S(2)}) collective-permute-start(f32[8,8,64]{2,1,0:T(8,128)S(1)} %get-tuple-element.33), channel_id=1, source_target_pairs={{0,8},{8,16},{16,24},{24,32},{32,40},{40,48},{48,56},{56,64},{64,7... | collective-permute-start | bytes 49160 | tf_op jit(solution)/shard_map/ppermute | solution.py:221
  109.0 1.3 copy-start.10
  109.0 1.7 %copy-start.11 = (f32[80,12,132]{2,1,0:T(8,128)S(1)}, f32[80,12,132]{2,1,0:T(8,128)}, u32[]{:S(2)}) copy-start(f32[80,12,132]{2,1,0:T(8,128)} %get-tuple-element.12) | copy-start | bytes 1520644
  110.7 1.1 copy-start.4
  113.1 5.4 %copy-start.16 = (f32[80,8,128]{2,1,0:T(8,128)S(1)}, f32[80,8,128]{2,1,0:T(8,128)}, u32[]{:S(2)}) copy-start(f32[80,8,128]{2,1,0:T(8,128)} %get-tuple-element.37) | copy-start | bytes 983044
  118.3 27.5 %copy-start.5 = (f32[4,80,8,128]{3,2,1,0:T(8,128)S(1)}, f32[4,80,8,128]{3,2,1,0:T(8,128)}, u32[]{:S(2)}) copy-start(f32[4,80,8,128]{3,2,1,0:T(8,128)} %shard_map.121) | copy-start | bytes 3932164
  118.3 27.5 %copy-start.9 = (f32[80,8,128]{2,1,0:T(8,128)S(1)}, f32[80,8,128]{2,1,0:T(8,128)}, u32[]{:S(2)}) copy-start(f32[80,8,128]{2,1,0:T(8,128)} %copy-done.8) | copy-start | bytes 983044
  118.4 8.1 %collective-permute-start.10 = (f32[8,8,256]{2,1,0:T(8,128)S(1)}, f32[8,8,256]{2,1,0:T(8,128)S(1)}, u32[]{:S(2)}, u32[]{:S(2)}) collective-permute-start(f32[8,8,256]{2,1,0:T(8,128)S(1)} %get-tuple-element.5), channel_id=1, source_target_pairs={{0,7},{1,0},{2,1},{3,2},{4,3},{5,4},{6,5},{7,6},{8,15},{9,8},{10,9... | collective-permute-start | bytes 196616 | tf_op jit(solution)/shard_map/ppermute | solution.py:229
  119.7 8.5 %collective-permute-start.11 = (f32[8,8,256]{2,1,0:T(8,128)S(1)}, f32[8,8,256]{2,1,0:T(8,128)S(1)}, u32[]{:S(2)}, u32[]{:S(2)}) collective-permute-start(f32[8,8,256]{2,1,0:T(8,128)S(1)} %get-tuple-element.5), channel_id=1, source_target_pairs={{0,6},{1,7},{2,0},{3,1},{4,2},{5,3},{6,4},{7,5},{8,14},{9,15},{10,... | collective-permute-start | bytes 196616 | tf_op jit(solution)/shard_map/ppermute | solution.py:229
  119.8 10.9 %collective-permute-start.12 = (f32[8,8,256]{2,1,0:T(8,128)S(1)}, f32[8,8,256]{2,1,0:T(8,128)S(1)}, u32[]{:S(2)}, u32[]{:S(2)}) collective-permute-start(f32[8,8,256]{2,1,0:T(8,128)S(1)} %get-tuple-element.5), channel_id=1, source_target_pairs={{0,5},{1,6},{2,7},{3,0},{4,1},{5,2},{6,3},{7,4},{8,13},{9,14},{10,... | collective-permute-start | bytes 196616 | tf_op jit(solution)/shard_map/ppermute | solution.py:229
  126.3 4.5 %collective-permute-start.13 = (f32[8,8,256]{2,1,0:T(8,128)S(1)}, f32[8,8,256]{2,1,0:T(8,128)S(1)}, u32[]{:S(2)}, u32[]{:S(2)}) collective-permute-start(f32[8,8,256]{2,1,0:T(8,128)S(1)} %get-tuple-element.5), channel_id=1, source_target_pairs={{0,4},{1,5},{2,6},{3,7},{4,0},{5,1},{6,2},{7,3},{8,12},{9,13},{10,... | collective-permute-start | bytes 196616 | tf_op jit(solution)/shard_map/ppermute | solution.py:229
  126.3 4.6 %collective-permute-start.14 = (f32[8,8,256]{2,1,0:T(8,128)S(1)}, f32[8,8,256]{2,1,0:T(8,128)S(1)}, u32[]{:S(2)}, u32[]{:S(2)}) collective-permute-start(f32[8,8,256]{2,1,0:T(8,128)S(1)} %get-tuple-element.5), channel_id=1, source_target_pairs={{0,3},{1,4},{2,5},{3,6},{4,7},{5,0},{6,1},{7,2},{8,11},{9,12},{10,... | collective-permute-start | bytes 196616 | tf_op jit(solution)/shard_map/ppermute | solution.py:229
  126.4 4.4 %collective-permute-start.15 = (f32[8,8,256]{2,1,0:T(8,128)S(1)}, f32[8,8,256]{2,1,0:T(8,128)S(1)}, u32[]{:S(2)}, u32[]{:S(2)}) collective-permute-start(f32[8,8,256]{2,1,0:T(8,128)S(1)} %get-tuple-element.5), channel_id=1, source_target_pairs={{0,2},{1,3},{2,4},{3,5},{4,6},{5,7},{6,0},{7,1},{8,10},{9,11},{10,... | collective-permute-start | bytes 196616 | tf_op jit(solution)/shard_map/ppermute | solution.py:229
  128.3 5.3 %collective-permute-start.16 = (f32[8,8,256]{2,1,0:T(8,128)S(1)}, f32[8,8,256]{2,1,0:T(8,128)S(1)}, u32[]{:S(2)}, u32[]{:S(2)}) collective-permute-start(f32[8,8,256]{2,1,0:T(8,128)S(1)} %get-tuple-element.5), channel_id=1, source_target_pairs={{0,1},{1,2},{2,3},{3,4},{4,5},{5,6},{6,7},{7,0},{8,9},{9,10},{10,1... | collective-permute-start | bytes 196616 | tf_op jit(solution)/shard_map/ppermute | solution.py:229
  133.6 0.8 copy-start.17

commit v6 on v5

--- a/solution.py
+++ b/solution.py
@@ -139,7 +139,7 @@
     return jnp.stack([new_height, new_east, new_north])
 
 
-def halo_3d(block):
+def halo_3d(block, centre):
     zonal = "gx"
     merid = ("gy", "ga")
     both = ("gx", "gy", "ga")
@@ -160,19 +160,26 @@
             return lax.ppermute(piece, merid, [(s % merid_n, t % merid_n) for s, t in pairs[:merid_n - 1]])
         return lax.ppermute(piece, both, pairs)
 
+    def masked(piece):
+        wet = piece[-1:]
+        return jnp.concatenate([piece[:-1] * wet, wet], axis=0)
+
+    def take(piece, d_zonal, d_merid):
+        return masked(send(piece, d_zonal, d_merid))
+
     w = 2
     last_rows = block[..., -w:, :]
     first_rows = block[..., :w, :]
-    west = send(block[..., -w:], 1, 0)
-    east = send(block[..., :w], -1, 0)
-    low = send(last_rows, 0, 1)
-    high = send(first_rows, 0, -1)
-    low_west = send(last_rows[..., -w:], 1, 1)
-    low_east = send(last_rows[..., :w], -1, 1)
-    high_west = send(first_rows[..., -w:], 1, -1)
-    high_east = send(first_rows[..., :w], -1, -1)
+    west = take(block[..., -w:], 1, 0)
+    east = take(block[..., :w], -1, 0)
+    low = take(last_rows, 0, 1)
+    high = take(first_rows, 0, -1)
+    low_west = take(last_rows[..., -w:], 1, 1)
+    low_east = take(last_rows[..., :w], -1, 1)
+    high_west = take(first_rows[..., -w:], 1, -1)
+    high_east = take(first_rows[..., :w], -1, -1)
     low_band = jnp.concatenate([low_west, low, low_east], axis=-1)
-    middle = jnp.concatenate([west, block, east], axis=-1)
+    middle = jnp.concatenate([west, centre, east], axis=-1)
     high_band = jnp.concatenate([high_west, high, high_east], axis=-1)
     return jnp.concatenate([low_band, middle, high_band], axis=-2)
 
@@ -185,7 +192,8 @@
     stacked = jnp.concatenate(
         [velocity * wet_mask[None], tracers * wet_mask[None], wet_mask[None]], axis=0
     )
-    padded = halo_3d(stacked)
+    raw = jnp.concatenate([velocity, tracers, wet_mask[None]], axis=0)
+    padded = halo_3d(raw, stacked)
     depth_col = thickness.reshape((levels, 1, 1))
     pressure = pressure_run(thickness, padded)
     growth = tendency(padded, pressure, coriolis)

time: 148 us -> 169 us (1.14)
  the two profiles are of different devices: /device:TPU:1 before, /device:TPU:227 now
where the time goes in v6:
time: 169 us; the launch traced here: 168 us
  starting transfers between devices  60.2 us (36%)
  other arithmetic  51.1 us (30%)
  local copies, waits for them, and re-layouts  21 us (12%)
  Pallas kernels  18.9 us (11%)
  waiting for transfers between devices  15.2 us (9%)
    ppermute x7, starting transfers between devices, gather_baro(): blocks.append(lax.ppermute(wide, merid, pairs))  28.3 us
    ppermute x4, starting transfers between devices, send(): return lax.ppermute(piece, both, pairs)  19 us
    concatenate x1, other arithmetic, halo_3d(): return jnp.concatenate([low_band, middle, high_band], axis=-2)  11.7 us
    ppermute x4, waiting for transfers between devices, send(): return lax.ppermute(piece, both, pairs)  11.1 us
    mul x2, other arithmetic, laplace(): return (beside_all - 4.0 * centre) * wet_mask[..., 1:-1, 1:-1]  10.7 us
    pallas_call x1, Pallas kernels, baro_run(): pl.pallas_call(baro_kernel, out_shape=jax.ShapeDtypeStruct((5, whole.shap...  8.88 us
    mul x8, other arithmetic, masked(): return jnp.concatenate([piece[:-1] * wet, wet], axis=0)  7.63 us
    ppermute x2, starting transfers between devices, send(): lax.ppermute(piece, merid, [(s % merid_n, t % merid_n) for s, t in pairs[...  5.55 us
  transfers between devices with their start and end apart: 17, of which 4 were waited for; matrix products, arithmetic and copies ran while one was open for 15% of the time, Pallas kernels for 3%

profile of v6, /device:TPU:227, one launch (start us, length us, event | category | flops | bytes accessed | tf_op | source)
XLA Modules:
  0.0 167.8 jit_solution(2003878820448958008)
XLA Ops:
  0.6 0.7 convert_element_type.4
  1.3 0.7 fusion.48
  2.0 0.7 copy-done.18
  2.8 1.4 pad_maximum_fusion
  4.2 2.1 %fusion.63 = (f32[5,80,2,2]{3,2,1,0:T(2,128)}, f32[5,80,2,2]{3,2,1,0:T(2,128)}, f32[5,80,2,2]{3,2,1,0:T(2,128)}, f32[5,80,2,2]{3,2,1,0:T(2,128)}) fusion(f32[5,80,8,128]{3,2,1,0:T(8,128)S(1)} %pad_maximum_fusion), kind=kLoop, calls=%fused_computation.163 | loop fusion | bytes 51200 | tf_op jit(solution)/shard_map/slice | solution.py:177
  6.3 7.2 %collective-permute-start.7 = (f32[5,80,2,2]{3,2,1,0:T(2,128)}, f32[5,80,2,2]{3,2,1,0:T(2,128)}, u32[]{:S(2)}, u32[]{:S(2)}) collective-permute-start(f32[5,80,2,2]{3,2,1,0:T(2,128)} %get-tuple-element.19), channel_id=1, source_target_pairs={{1,248},{2,249},{3,250},{4,251},{5,252},{6,253},{7,254},{9,0},{10,... | collective-permute-start | bytes 19208 | tf_op jit(solution)/shard_map/ppermute | solution.py:161
  13.5 1.2 fusion.64
  14.7 3.3 %collective-permute-start.6 = (f32[5,80,2,128]{3,2,1,0:T(2,128)}, f32[5,80,2,128]{3,2,1,0:T(2,128)}, u32[]{:S(2)}, u32[]{:S(2)}) collective-permute-start(f32[5,80,2,128]{3,2,1,0:T(2,128)} %get-tuple-element.23), channel_id=1, source_target_pairs={{1,0},{2,1},{3,2},{4,3},{5,4},{6,5},{7,6},{9,8},{10,9},{11,10},{12... | collective-permute-start | bytes 1228808 | tf_op jit(solution)/shard_map/ppermute | solution.py:160
  18.0 1.9 %collective-permute-start.5 = (f32[5,80,2,2]{3,2,1,0:T(2,128)}, f32[5,80,2,2]{3,2,1,0:T(2,128)}, u32[]{:S(2)}, u32[]{:S(2)}) collective-permute-start(f32[5,80,2,2]{3,2,1,0:T(2,128)} %get-tuple-element.20), channel_id=1, source_target_pairs={{1,8},{2,9},{3,10},{4,11},{5,12},{6,13},{7,14},{9,16},{10,17},{11,... | collective-permute-start | bytes 19208 | tf_op jit(solution)/shard_map/ppermute | solution.py:161
  20.5 1.2 copy.34
  21.7 4.2 %collective-permute-start.4 = (f32[5,80,8,2]{1,2,3,0:T(8,128)}, f32[5,80,8,2]{1,2,3,0:T(8,128)S(1)}, u32[]{:S(2)}, u32[]{:S(2)}) collective-permute-start(f32[5,80,8,2]{1,2,3,0:T(8,128)} %copy.34), channel_id=1, source_target_pairs={{0,248},{8,0},{16,8},{24,16},{32,24},{40,32},{48,40},{56,48},{64,5... | collective-permute-start | bytes 76808 | tf_op jit(solution)/shard_map/ppermute | solution.py:152
  26.5 0.9 broadcast_multiply_fusion.2
  27.4 0.7 copy-done.10
  28.1 1.1 broadcast_multiply_fusion.1
  29.3 0.7 reduce_sum.38
  29.9 0.6 broadcast_maximum_fusion
  30.5 0.7 constant_dynamic-update-slice_fusion.6
  31.8 8.0 %collective-permute-start.2 = (f32[5,80,2,2]{3,2,1,0:T(2,128)S(1)}, f32[5,80,2,2]{3,2,1,0:T(2,128)S(1)}, u32[]{:S(2)}, u32[]{:S(2)}) collective-permute-start(f32[5,80,2,2]{3,2,1,0:T(2,128)S(1)} %copy-done.26), channel_id=1, source_target_pairs={{0,249},{1,250},{2,251},{3,252},{4,253},{5,254},{6,255},{8,1},{9,2... | collective-permute-start | bytes 19208 | tf_op jit(solution)/shard_map/ppermute | solution.py:161
  39.8 0.9 slice_bitcast_fusion.10
  40.7 1.8 %slice_multiply_fusion.10 = f32[4,80,2,2]{3,2,1,0:T(2,128)} fusion(f32[5,80,2,2]{3,2,1,0:T(2,128)} %collective-permute-done.7, f32[80,2,2]{2,1,0:T(2,128)S(1)} %get-tuple-element.41), kind=kLoop, calls=%fused_computation.103 | loop fusion | flops 1280 | bytes 11520 | tf_op jit(solution)/shard_map/mul | solution.py:165
  42.6 2.2 %collective-permute-start.1 = (f32[5,80,2,128]{3,2,1,0:T(2,128)}, f32[5,80,2,128]{3,2,1,0:T(2,128)}, u32[]{:S(2)}, u32[]{:S(2)}) collective-permute-start(f32[5,80,2,128]{3,2,1,0:T(2,128)} %get-tuple-element.22), channel_id=1, source_target_pairs={{0,1},{1,2},{2,3},{3,4},{4,5},{5,6},{6,7},{8,9},{9,10},{10,11},{11... | collective-permute-start | bytes 1228808 | tf_op jit(solution)/shard_map/ppermute | solution.py:160
  44.8 0.9 slice_bitcast_fusion.12
  45.8 1.8 %slice_multiply_fusion.12 = f32[4,80,2,2]{3,2,1,0:T(2,128)} fusion(f32[5,80,2,2]{3,2,1,0:T(2,128)} %collective-permute-done.5, f32[80,2,2]{2,1,0:T(2,128)S(1)} %get-tuple-element.37), kind=kLoop, calls=%fused_computation.105 | loop fusion | flops 1280 | bytes 11520 | tf_op jit(solution)/shard_map/mul | solution.py:165
  47.7 1.9 %collective-permute-start = (f32[5,80,2,2]{3,2,1,0:T(2,128)S(1)}, f32[5,80,2,2]{3,2,1,0:T(2,128)S(1)}, u32[]{:S(2)}, u32[]{:S(2)}) collective-permute-start(f32[5,80,2,2]{3,2,1,0:T(2,128)S(1)} %copy-done.25), channel_id=1, source_target_pairs={{0,9},{1,10},{2,11},{3,12},{4,13},{5,14},{6,15},{8,17},{9,18},{10,... | collective-permute-start | bytes 19208 | tf_op jit(solution)/shard_map/ppermute | solution.py:161
  49.7 0.9 slice_multiply_fusion.13
  50.5 11.0 %collective-permute-done = f32[5,80,2,2]{3,2,1,0:T(2,128)S(1)} collective-permute-done((f32[5,80,2,2]{3,2,1,0:T(2,128)S(1)}, f32[5,80,2,2]{3,2,1,0:T(2,128)S(1)}, u32[]{:S(2)}, u32[]{:S(2)}) %collective-permute-start) | collective-permute-done | bytes 6432 | tf_op jit(solution)/shard_map/ppermute | solution.py:161
  61.6 0.7 slice_bitcast_fusion.15
  62.2 0.9 slice_multiply_fusion.15
  63.2 0.6 copy.36
  63.8 0.6 pad_maximum_fusion.2
  64.4 1.4 copy.35
  65.8 1.1 slice_bitcast_fusion.11
  66.9 1.1 slice_multiply_fusion.11
  68.0 0.9 slice_bitcast_fusion.14
  69.0 1.1 slice_multiply_fusion.14
  70.1 11.7 %maximum_maximum_fusion.pad_ref = f32[5,80,12,132]{3,2,1,0:T(8,128)S(1)} fusion(f32[1,80,2,2]{3,2,1,0:T(2,128)S(1)} %get-tuple-element.42, f32[4,80,2,2]{3,2,1,0:T(2,128)S(1)} %copy-done.23, f32[1,80,2,128]{3,2,1,0:T(2,128)S(1)} %get-tuple-element.40, f32[4,80,2,128]{3,2,1,0:T(2,128)S(1)} %slice_multiply_fusion.11, f32[1,80,2,2]{3,2,1,0:T(2,128)S(1)} %get-tuple-element.38, ...), kind=kLoop, calls=%fused_computation | loop fusion | flops 10137600 | bytes 5068800 | tf_op jit(solution)/shard_map/concatenate | solution.py:184
  81.8 4.3 %fusion.62 = (f32[80,12,132]{2,1,0:T(8,128)}, f32[80,12,132]{2,1,0:T(8,128)}, f32[80,12,132]{2,1,0:T(8,128)}, f32[80,12,132]{2,1,0:T(8,128)}, f32[80,12,132]{2,1...) fusion(f32[5,80,12,132]{3,2,1,0:T(8,128)S(1)} %maximum_maximum_fusion.pad_ref), kind=kLoop, calls=%fused_computation.162 | loop fusion | flops 887040 | bytes 5575680 | tf_op jit(solution)/shard_map/mul | solution.py:49
  86.0 1.2 copy-done
  87.2 2.4 %slice_bitcast_fusion.3 = (f32[80,12,132]{2,1,0:T(8,128)S(1)}, f32[80,12,132]{2,1,0:T(8,128)}, f32[80,12,132]{2,1,0:T(8,128)}, f32[80,12,132]{2,1,0:T(8,128)}, f32[80,12,132]{2,1,0:T(8,128)S(1)}) fusion(f32[5,80,12,132]{3,2,1,0:T(8,128)S(1)} %maximum_maximum_fusion.pad_ref), kind=kLoop, calls=%fused_computation.29 | loop fusion | bytes 5068800 | tf_op jit(solution)/shard_map/squeeze | solution.py:48
  89.6 4.9 %shard_map.120 = f32[80,12,132]{2,1,0:T(8,128)} custom-call(f32[80]{0:T(128)} %th_ref.3, f32[5,80,12,132]{3,2,1,0:T(8,128)} %copy-done), custom_call_target="tpu_custom_call" | custom-call | tf_op jit(solution)/shard_map/pallas_call | solution.py:315
  94.5 6.1 %fusion.1 = f32[80,10,130]{2,1,0:T(8,128)S(1)} fusion(f32[80,12,132]{2,1,0:T(8,128)} %get-tuple-element.14, f32[80,12,132]{2,1,0:T(8,128)} %get-tuple-element.16), kind=kLoop, calls=%fused_computation.4 | loop fusion | flops 624000 | bytes 2912000 | tf_op jit(solution)/shard_map/mul | solution.py:29
  100.6 4.6 %fusion.7 = (f32[80,10,130]{2,1,0:T(8,128)S(1)}, f32[80,10,130]{2,1,0:T(8,128)S(1)}, f32[80,10,130]{2,1,0:T(8,128)S(1)}) fusion(f32[80,12,132]{2,1,0:T(8,128)S(1)} %get-tuple-element.13, f32[80,12,132]{2,1,0:T(8,128)S(1)} %copy-done.2, f32[80,12,132]{2,1,0:T(8,128)S(1)} %get-tuple-element.17, f32[80,12,132]{2,1,0:T(8,128)S(1)} %copy-done.1), kind=kLoop, calls=%fused_computation.25 | loop fusion | flops 1872000 | bytes 7904000 | tf_op jit(solution)/shard_map/mul | solution.py:29
  105.3 1.1 fusion.40
  106.7 1.1 fusion.29
  108.1 1.9 %collective-permute-start.9 = (f32[8,8,64]{2,1,0:T(8,128)S(1)}, f32[8,8,64]{2,1,0:T(8,128)S(1)}, u32[]{:S(2)}, u32[]{:S(2)}) collective-permute-start(f32[8,8,64]{2,1,0:T(8,128)S(1)} %get-tuple-element.50), channel_id=1, source_target_pairs={{8,0},{16,8},{24,16},{32,24},{40,32},{48,40},{56,48},{64,56},{72,6... | collective-permute-start | bytes 49160 | tf_op jit(solution)/shard_map/ppermute | solution.py:230
  110.0 1.2 collective-permute-start.8
  111.2 0.8 fusion.13
  112.9 0.8 fusion.21
  114.2 1.2 maximum_add_fusion.prov_ref
  115.5 5.1 %shard_map.121 = f32[4,80,8,128]{3,2,1,0:T(8,128)} custom-call(f32[80]{0:T(128)} %th_ref.3, f32[4,80,8,128]{3,2,1,0:T(8,128)} %maximum_add_fusion.prov_ref, f32[80,8,128]{2,1,0:T(8,128)} %mix_ref.1, f32[80,8,128]{2,1,0:T(8,128)} %copy-done.10), custom_call_target="tpu_custom_call" | custom-call | tf_op jit(solution)/shard_map/pallas_call | solution.py:366
  120.7 17.4 %collective-permute-start.10 = (f32[8,8,256]{2,1,0:T(8,128)S(1)}, f32[8,8,256]{2,1,0:T(8,128)S(1)}, u32[]{:S(2)}, u32[]{:S(2)}) collective-permute-start(f32[8,8,256]{2,1,0:T(8,128)S(1)} %get-tuple-element.5), channel_id=1, source_target_pairs={{0,7},{1,0},{2,1},{3,2},{4,3},{5,4},{6,5},{7,6},{8,15},{9,8},{10,9... | collective-permute-start | bytes 196616 | tf_op jit(solution)/shard_map/ppermute | solution.py:237
  138.1 1.2 multiply_reduce_fusion
  139.3 3.7 %collective-permute-start.11 = (f32[8,8,256]{2,1,0:T(8,128)S(1)}, f32[8,8,256]{2,1,0:T(8,128)S(1)}, u32[]{:S(2)}, u32[]{:S(2)}) collective-permute-start(f32[8,8,256]{2,1,0:T(8,128)S(1)} %get-tuple-element.5), channel_id=1, source_target_pairs={{0,6},{1,7},{2,0},{3,1},{4,2},{5,3},{6,4},{7,5},{8,14},{9,15},{10,... | collective-permute-start | bytes 196616 | tf_op jit(solution)/shard_map/ppermute | solution.py:237
  143.0 1.3 collective-permute-start.12
  144.4 0.7 collective-permute-start.13
  145.1 1.2 collective-permute-start.14
  146.3 2.8 %collective-permute-start.15 = (f32[8,8,256]{2,1,0:T(8,128)S(1)}, f32[8,8,256]{2,1,0:T(8,128)S(1)}, u32[]{:S(2)}, u32[]{:S(2)}) collective-permute-start(f32[8,8,256]{2,1,0:T(8,128)S(1)} %get-tuple-element.5), channel_id=1, source_target_pairs={{0,2},{1,3},{2,4},{3,5},{4,6},{5,7},{6,0},{7,1},{8,10},{9,11},{10,... | collective-permute-start | bytes 196616 | tf_op jit(solution)/shard_map/ppermute | solution.py:237
  149.1 1.1 collective-permute-start.16
  150.4 4.0 %collective-permute-done.16 = f32[8,8,256]{2,1,0:T(8,128)S(1)} collective-permute-done((f32[8,8,256]{2,1,0:T(8,128)S(1)}, f32[8,8,256]{2,1,0:T(8,128)S(1)}, u32[]{:S(2)}, u32[]{:S(2)}) %collective-permute-start.16) | collective-permute-done | bytes 65568 | tf_op jit(solution)/shard_map/ppermute | solution.py:237
  154.4 0.8 copy-done.24
  155.2 8.9 %shard_map.122 = f32[5,8,128]{2,1,0:T(8,128)} custom-call(s32[1]{0:T(128)} %bitcast.17.off_ref, f32[8,8,8,256]{3,2,1,0:T(8,128)} %copy-done.24), custom_call_target="tpu_custom_call" | custom-call | tf_op jit(solution)/shard_map/pallas_call | solution.py:295
  164.1 1.3 slice_bitcast_fusion.5
  165.4 1.3 fusion.68
  166.7 1.2 fusion.66
  (117 shorter events, 4.1 us)
Async XLA Ops:
  2.0 0.7 copy-start.18
  6.3 25.5 %collective-permute-start.7 = (f32[5,80,2,2]{3,2,1,0:T(2,128)}, f32[5,80,2,2]{3,2,1,0:T(2,128)}, u32[]{:S(2)}, u32[]{:S(2)}) collective-permute-start(f32[5,80,2,2]{3,2,1,0:T(2,128)} %get-tuple-element.19), channel_id=1, source_target_pairs={{1,248},{2,249},{3,250},{4,251},{5,252},{6,253},{7,254},{9,0},{10,... | collective-permute-start | bytes 19208 | tf_op jit(solution)/shard_map/ppermute | solution.py:161
  14.7 51.1 %collective-permute-start.6 = (f32[5,80,2,128]{3,2,1,0:T(2,128)}, f32[5,80,2,128]{3,2,1,0:T(2,128)}, u32[]{:S(2)}, u32[]{:S(2)}) collective-permute-start(f32[5,80,2,128]{3,2,1,0:T(2,128)} %get-tuple-element.23), channel_id=1, source_target_pairs={{1,0},{2,1},{3,2},{4,3},{5,4},{6,5},{7,6},{9,8},{10,9},{11,10},{12... | collective-permute-start | bytes 1228808 | tf_op jit(solution)/shard_map/ppermute | solution.py:160
  18.0 24.6 %collective-permute-start.5 = (f32[5,80,2,2]{3,2,1,0:T(2,128)}, f32[5,80,2,2]{3,2,1,0:T(2,128)}, u32[]{:S(2)}, u32[]{:S(2)}) collective-permute-start(f32[5,80,2,2]{3,2,1,0:T(2,128)} %get-tuple-element.20), channel_id=1, source_target_pairs={{1,8},{2,9},{3,10},{4,11},{5,12},{6,13},{7,14},{9,16},{10,17},{11,... | collective-permute-start | bytes 19208 | tf_op jit(solution)/shard_map/ppermute | solution.py:161
  20.5 6.0 %copy-start.31 = (s32[8,128]{1,0:T(8,128)S(1)}, s32[8,128]{1,0:T(8,128)}, u32[]{:S(2)}) copy-start(s32[8,128]{1,0:T(8,128)} %param.15) | copy-start | bytes 12292
  20.5 6.0 %copy-start.34 = (f32[80]{0:T(128)S(1)}, f32[80]{0:T(128)}, u32[]{:S(2)}) copy-start(f32[80]{0:T(128)} %th_ref.3) | copy-start | bytes 964
  21.7 6.4 %copy-start.20 = (f32[2,80,8,128]{3,2,1,0:T(8,128)S(1)}, f32[2,80,8,128]{3,2,1,0:T(8,128)}, u32[]{:S(2)}) copy-start(f32[2,80,8,128]{3,2,1,0:T(8,128)} %param.9) | copy-start | bytes 1966084
  21.7 6.4 %copy-start.21 = (f32[2,80,8,128]{3,2,1,0:T(8,128)S(1)}, f32[2,80,8,128]{3,2,1,0:T(8,128)}, u32[]{:S(2)}) copy-start(f32[2,80,8,128]{3,2,1,0:T(8,128)} %param.10) | copy-start | bytes 1966084
  21.7 41.4 %collective-permute-start.4 = (f32[5,80,8,2]{1,2,3,0:T(8,128)}, f32[5,80,8,2]{1,2,3,0:T(8,128)S(1)}, u32[]{:S(2)}, u32[]{:S(2)}) collective-permute-start(f32[5,80,8,2]{1,2,3,0:T(8,128)} %copy.34), channel_id=1, source_target_pairs={{0,248},{8,0},{16,8},{24,16},{32,24},{40,32},{48,40},{56,48},{64,5... | collective-permute-start | bytes 76808 | tf_op jit(solution)/shard_map/ppermute | solution.py:152
  26.4 36.7 %collective-permute-start.3 = (f32[5,80,8,2]{1,2,3,0:T(8,128)S(1)}, f32[5,80,8,2]{1,2,3,0:T(8,128)S(1)}, u32[]{:S(2)}, u32[]{:S(2)}) collective-permute-start(f32[5,80,8,2]{1,2,3,0:T(8,128)S(1)} %copy.33), channel_id=1, source_target_pairs={{0,8},{8,16},{16,24},{24,32},{32,40},{40,48},{48,56},{56,64},{64,7... | collective-permute-start | bytes 76808 | tf_op jit(solution)/shard_map/ppermute | solution.py:152
  27.4 0.7 copy-start.10
  27.4 3.1 %copy-start.27 = (f32[8,128]{1,0:T(8,128)}, f32[8,128]{1,0:T(8,128)S(1)}, u32[]{:S(2)}) copy-start(f32[8,128]{1,0:T(8,128)S(1)} %get-tuple-element.54) | copy-start | bytes 12292
  28.1 3.1 %copy-start.29 = (s32[8,128]{1,0:T(8,128)S(1)}, s32[8,128]{1,0:T(8,128)}, u32[]{:S(2)}) copy-start(s32[8,128]{1,0:T(8,128)} %param.14) | copy-start | bytes 12292
  28.1 3.1 %copy-start.37 = (f32[8]{0:T(128)S(1)}, f32[8]{0:T(128)}, u32[]{:S(2)}) copy-start(f32[8]{0:T(128)} %param.13) | copy-start | bytes 100
  28.1 3.7 %copy-start.26 = (f32[5,80,2,2]{3,2,1,0:T(2,128)S(1)}, f32[5,80,2,2]{3,2,1,0:T(2,128)}, u32[]{:S(2)}) copy-start(f32[5,80,2,2]{3,2,1,0:T(2,128)} %get-tuple-element.21) | copy-start | bytes 19204
  29.3 18.4 %copy-start.25 = (f32[5,80,2,2]{3,2,1,0:T(2,128)S(1)}, f32[5,80,2,2]{3,2,1,0:T(2,128)}, u32[]{:S(2)}) copy-start(f32[5,80,2,2]{3,2,1,0:T(2,128)} %get-tuple-element.18) | copy-start | bytes 19204
  31.8 15.8 %collective-permute-start.2 = (f32[5,80,2,2]{3,2,1,0:T(2,128)S(1)}, f32[5,80,2,2]{3,2,1,0:T(2,128)S(1)}, u32[]{:S(2)}, u32[]{:S(2)}) collective-permute-start(f32[5,80,2,2]{3,2,1,0:T(2,128)S(1)} %copy-done.26), channel_id=1, source_target_pairs={{0,249},{1,250},{2,251},{3,252},{4,253},{5,254},{6,255},{8,1},{9,2... | collective-permute-start | bytes 19208 | tf_op jit(solution)/shard_map/ppermute | solution.py:161
  42.6 25.4 %collective-permute-start.1 = (f32[5,80,2,128]{3,2,1,0:T(2,128)}, f32[5,80,2,128]{3,2,1,0:T(2,128)}, u32[]{:S(2)}, u32[]{:S(2)}) collective-permute-start(f32[5,80,2,128]{3,2,1,0:T(2,128)} %get-tuple-element.22), channel_id=1, source_target_pairs={{0,1},{1,2},{2,3},{3,4},{4,5},{5,6},{6,7},{8,9},{9,10},{10,11},{11... | collective-permute-start | bytes 1228808 | tf_op jit(solution)/shard_map/ppermute | solution.py:160
  47.7 13.9 %collective-permute-start = (f32[5,80,2,2]{3,2,1,0:T(2,128)S(1)}, f32[5,80,2,2]{3,2,1,0:T(2,128)S(1)}, u32[]{:S(2)}, u32[]{:S(2)}) collective-permute-start(f32[5,80,2,2]{3,2,1,0:T(2,128)S(1)} %copy-done.25), channel_id=1, source_target_pairs={{0,9},{1,10},{2,11},{3,12},{4,13},{5,14},{6,15},{8,17},{9,18},{10,... | collective-permute-start | bytes 19208 | tf_op jit(solution)/shard_map/ppermute | solution.py:161
  65.8 4.3 %copy-start.4 = (f32[2,80,8,128]{3,2,1,0:T(8,128)S(1)}, f32[2,80,8,128]{3,2,1,0:T(8,128)}, u32[]{:S(2)}) copy-start(f32[2,80,8,128]{3,2,1,0:T(8,128)} %get-tuple-element.43) | copy-start | bytes 1966084
  65.8 4.3 %copy-start.6 = (f32[2,80,8,128]{3,2,1,0:T(8,128)S(1)}, f32[2,80,8,128]{3,2,1,0:T(8,128)}, u32[]{:S(2)}) copy-start(f32[2,80,8,128]{3,2,1,0:T(8,128)} %get-tuple-element.44) | copy-start | bytes 1966084
  65.8 4.3 %copy-start.19 = (f32[1,80,8,128]{3,2,1,0:T(8,128)S(1)}, f32[1,80,8,128]{3,2,1,0:T(8,128)}, u32[]{:S(2)}) copy-start(f32[1,80,8,128]{3,2,1,0:T(8,128)} %copy-done.18) | copy-start | bytes 983044
  65.8 4.3 %copy-start.23 = (f32[4,80,2,2]{3,2,1,0:T(2,128)S(1)}, f32[4,80,2,2]{3,2,1,0:T(2,128)}, u32[]{:S(2)}) copy-start(f32[4,80,2,2]{3,2,1,0:T(2,128)} %slice_multiply_fusion.10) | copy-start | bytes 15364
  81.8 5.5 %copy-start = (f32[5,80,12,132]{3,2,1,0:T(8,128)}, f32[5,80,12,132]{3,2,1,0:T(8,128)S(1)}, u32[]{:S(2)}) copy-start(f32[5,80,12,132]{3,2,1,0:T(8,128)S(1)} %maximum_maximum_fusion.pad_ref) | copy-start | bytes 7603204
  94.5 6.1 %copy-start.1 = (f32[80,12,132]{2,1,0:T(8,128)S(1)}, f32[80,12,132]{2,1,0:T(8,128)}, u32[]{:S(2)}) copy-start(f32[80,12,132]{2,1,0:T(8,128)} %get-tuple-element.15) | copy-start | bytes 1520644
  94.5 6.1 %copy-start.2 = (f32[80,12,132]{2,1,0:T(8,128)S(1)}, f32[80,12,132]{2,1,0:T(8,128)}, u32[]{:S(2)}) copy-start(f32[80,12,132]{2,1,0:T(8,128)} %get-tuple-element.16) | copy-start | bytes 1520644
  100.6 4.7 %copy-start.8 = (f32[80,12,132]{2,1,0:T(8,128)S(1)}, f32[80,12,132]{2,1,0:T(8,128)}, u32[]{:S(2)}) copy-start(f32[80,12,132]{2,1,0:T(8,128)} %get-tuple-element.7) | copy-start | bytes 1520644
  100.6 4.7 %copy-start.9 = (f32[80,12,132]{2,1,0:T(8,128)S(1)}, f32[80,12,132]{2,1,0:T(8,128)}, u32[]{:S(2)}) copy-start(f32[80,12,132]{2,1,0:T(8,128)} %shard_map.120) | copy-start | bytes 1520644
  100.6 4.7 %copy-start.17 = (f32[80,12,132]{2,1,0:T(8,128)S(1)}, f32[80,12,132]{2,1,0:T(8,128)}, u32[]{:S(2)}) copy-start(f32[80,12,132]{2,1,0:T(8,128)} %get-tuple-element.6) | copy-start | bytes 1520644
  100.6 4.7 %copy-start.38 = (f32[8]{0:T(128)S(1)}, f32[8]{0:T(128)}, u32[]{:S(2)}) copy-start(f32[8]{0:T(128)} %param.13) | copy-start | bytes 100
  105.3 1.3 copy-start.16
  105.3 1.3 copy-start.39
  106.6 1.2 copy-start.35
  106.6 1.3 copy-start.28
  106.6 1.3 copy-start.30
  106.7 1.4 copy-start.36
  106.7 1.4 copy-start.33
  106.7 4.5 %copy-start.14 = (f32[80,12,132]{2,1,0:T(8,128)S(1)}, f32[80,12,132]{2,1,0:T(8,128)}, u32[]{:S(2)}) copy-start(f32[80,12,132]{2,1,0:T(8,128)} %get-tuple-element.9) | copy-start | bytes 1520644
  106.7 4.5 %copy-start.15 = (f32[80,12,132]{2,1,0:T(8,128)S(1)}, f32[80,12,132]{2,1,0:T(8,128)}, u32[]{:S(2)}) copy-start(f32[80,12,132]{2,1,0:T(8,128)} %get-tuple-element.10) | copy-start | bytes 1520644
  108.1 12.5 %collective-permute-start.9 = (f32[8,8,64]{2,1,0:T(8,128)S(1)}, f32[8,8,64]{2,1,0:T(8,128)S(1)}, u32[]{:S(2)}, u32[]{:S(2)}) collective-permute-start(f32[8,8,64]{2,1,0:T(8,128)S(1)} %get-tuple-element.50), channel_id=1, source_target_pairs={{8,0},{16,8},{24,16},{32,24},{40,32},{48,40},{56,48},{64,56},{72,6... | collective-permute-start | bytes 49160 | tf_op jit(solution)/shard_map/ppermute | solution.py:230
  110.0 10.6 %collective-permute-start.8 = (f32[8,8,64]{2,1,0:T(8,128)S(1)}, f32[8,8,64]{2,1,0:T(8,128)S(1)}, u32[]{:S(2)}, u32[]{:S(2)}) collective-permute-start(f32[8,8,64]{2,1,0:T(8,128)S(1)} %get-tuple-element.49), channel_id=1, source_target_pairs={{0,8},{8,16},{16,24},{24,32},{32,40},{40,48},{48,56},{56,64},{64,7... | collective-permute-start | bytes 49160 | tf_op jit(solution)/shard_map/ppermute | solution.py:229
  111.2 1.3 copy-start.12
  111.2 1.7 %copy-start.13 = (f32[80,12,132]{2,1,0:T(8,128)S(1)}, f32[80,12,132]{2,1,0:T(8,128)}, u32[]{:S(2)}) copy-start(f32[80,12,132]{2,1,0:T(8,128)} %get-tuple-element.12) | copy-start | bytes 1520644
  112.9 1.1 copy-start.5
  112.9 1.3 copy-start.7
  115.5 22.7 %copy-start.22 = (f32[80,8,128]{2,1,0:T(8,128)S(1)}, f32[80,8,128]{2,1,0:T(8,128)}, u32[]{:S(2)}) copy-start(f32[80,8,128]{2,1,0:T(8,128)} %get-tuple-element.53) | copy-start | bytes 983044
  120.6 44.7 %copy-start.32 = (f32[8,128]{1,0:T(8,128)S(1)}, f32[8,128]{1,0:T(8,128)}, u32[]{:S(2)}) copy-start(f32[8,128]{1,0:T(8,128)} %broadcast_maximum_fusion) | copy-start | bytes 12292
  120.7 46.0 %copy-start.3 = (f32[4,80,8,128]{3,2,1,0:T(8,128)S(1)}, f32[4,80,8,128]{3,2,1,0:T(8,128)}, u32[]{:S(2)}) copy-start(f32[4,80,8,128]{3,2,1,0:T(8,128)} %shard_map.121) | copy-start | bytes 3932164
  120.7 45.9 %copy-start.11 = (f32[80,8,128]{2,1,0:T(8,128)S(1)}, f32[80,8,128]{2,1,0:T(8,128)}, u32[]{:S(2)}) copy-start(f32[80,8,128]{2,1,0:T(8,128)} %copy-done.10) | copy-start | bytes 983044
  120.7 25.6 %collective-permute-start.10 = (f32[8,8,256]{2,1,0:T(8,128)S(1)}, f32[8,8,256]{2,1,0:T(8,128)S(1)}, u32[]{:S(2)}, u32[]{:S(2)}) collective-permute-start(f32[8,8,256]{2,1,0:T(8,128)S(1)} %get-tuple-element.5), channel_id=1, source_target_pairs={{0,7},{1,0},{2,1},{3,2},{4,3},{5,4},{6,5},{7,6},{8,15},{9,8},{10,9... | collective-permute-start | bytes 196616 | tf_op jit(solution)/shard_map/ppermute | solution.py:237
  139.3 9.8 %collective-permute-start.11 = (f32[8,8,256]{2,1,0:T(8,128)S(1)}, f32[8,8,256]{2,1,0:T(8,128)S(1)}, u32[]{:S(2)}, u32[]{:S(2)}) collective-permute-start(f32[8,8,256]{2,1,0:T(8,128)S(1)} %get-tuple-element.5), channel_id=1, source_target_pairs={{0,6},{1,7},{2,0},{3,1},{4,2},{5,3},{6,4},{7,5},{8,14},{9,15},{10,... | collective-permute-start | bytes 196616 | tf_op jit(solution)/shard_map/ppermute | solution.py:237
  143.0 7.2 %collective-permute-start.12 = (f32[8,8,256]{2,1,0:T(8,128)S(1)}, f32[8,8,256]{2,1,0:T(8,128)S(1)}, u32[]{:S(2)}, u32[]{:S(2)}) collective-permute-start(f32[8,8,256]{2,1,0:T(8,128)S(1)} %get-tuple-element.5), channel_id=1, source_target_pairs={{0,5},{1,6},{2,7},{3,0},{4,1},{5,2},{6,3},{7,4},{8,13},{9,14},{10,... | collective-permute-start | bytes 196616 | tf_op jit(solution)/shard_map/ppermute | solution.py:237
  144.4 5.9 %collective-permute-start.13 = (f32[8,8,256]{2,1,0:T(8,128)S(1)}, f32[8,8,256]{2,1,0:T(8,128)S(1)}, u32[]{:S(2)}, u32[]{:S(2)}) collective-permute-start(f32[8,8,256]{2,1,0:T(8,128)S(1)} %get-tuple-element.5), channel_id=1, source_target_pairs={{0,4},{1,5},{2,6},{3,7},{4,0},{5,1},{6,2},{7,3},{8,12},{9,13},{10,... | collective-permute-start | bytes 196616 | tf_op jit(solution)/shard_map/ppermute | solution.py:237
  145.1 5.2 %collective-permute-start.14 = (f32[8,8,256]{2,1,0:T(8,128)S(1)}, f32[8,8,256]{2,1,0:T(8,128)S(1)}, u32[]{:S(2)}, u32[]{:S(2)}) collective-permute-start(f32[8,8,256]{2,1,0:T(8,128)S(1)} %get-tuple-element.5), channel_id=1, source_target_pairs={{0,3},{1,4},{2,5},{3,6},{4,7},{5,0},{6,1},{7,2},{8,11},{9,12},{10,... | collective-permute-start | bytes 196616 | tf_op jit(solution)/shard_map/ppermute | solution.py:237
  146.3 4.1 %collective-permute-start.15 = (f32[8,8,256]{2,1,0:T(8,128)S(1)}, f32[8,8,256]{2,1,0:T(8,128)S(1)}, u32[]{:S(2)}, u32[]{:S(2)}) collective-permute-start(f32[8,8,256]{2,1,0:T(8,128)S(1)} %get-tuple-element.5), channel_id=1, source_target_pairs={{0,2},{1,3},{2,4},{3,5},{4,6},{5,7},{6,0},{7,1},{8,10},{9,11},{10,... | collective-permute-start | bytes 196616 | tf_op jit(solution)/shard_map/ppermute | solution.py:237
  149.1 5.3 %collective-permute-start.16 = (f32[8,8,256]{2,1,0:T(8,128)S(1)}, f32[8,8,256]{2,1,0:T(8,128)S(1)}, u32[]{:S(2)}, u32[]{:S(2)}) collective-permute-start(f32[8,8,256]{2,1,0:T(8,128)S(1)} %get-tuple-element.5), channel_id=1, source_target_pairs={{0,1},{1,2},{2,3},{3,4},{4,5},{5,6},{6,7},{7,0},{8,9},{9,10},{10,1... | collective-permute-start | bytes 196616 | tf_op jit(solution)/shard_map/ppermute | solution.py:237
  154.4 0.8 copy-start.24

commit v7 on v5

--- a/solution.py
+++ b/solution.py
@@ -300,7 +300,7 @@
         o_ref[k] = press_scale * (overlying + 0.5 * weight)
         return overlying + weight
 
-    lax.fori_loop(0, levels, body, jnp.zeros(pad_ref.shape[2:], jnp.float32))
+    lax.fori_loop(0, levels, body, jnp.zeros(pad_ref.shape[2:], jnp.float32), unroll=8)
 
 
 def pressure_run(thickness, padded):
@@ -329,17 +329,18 @@
         depth = th_ref[k]
         diagonal = depth + upper + below
         divisor = diagonal - upper * ratio_prev
-        ratio = below / divisor
+        inverse = 1.0 / divisor
+        ratio = below * inverse
         ratio_ref[k] = ratio
         values = []
         for c in range(comps):
-            value = (depth * prov_ref[c, k] + upper * value_prev[c]) / divisor
+            value = (depth * prov_ref[c, k] + upper * value_prev[c]) * inverse
             o_ref[c, k] = value
             values.append(value)
         return (below, ratio, tuple(values))
 
     zeros = jnp.zeros(shape, jnp.float32)
-    lax.fori_loop(0, levels, forward, (zeros, zeros, (zeros,) * comps))
+    lax.fori_loop(0, levels, forward, (zeros, zeros, (zeros,) * comps), unroll=4)
 
     def backward(step, following):
         k = levels - 1 - step
@@ -351,7 +352,7 @@
             results.append(result)
         return tuple(results)
 
-    lax.fori_loop(0, levels, backward, (zeros,) * comps)
+    lax.fori_loop(0, levels, backward, (zeros,) * comps, unroll=4)
 
 
 def solve_columns(provisional, mixing, wet_mask, thickness):

time: 148 us -> 146 us (0.986)
  Pallas kernels: 18.9 us -> 17.3 us
  transfers between devices with their start and end apart: 17 -> 17, of which waited for: 3 -> 3; matrix products, arithmetic and copies ran while one was open for 9% -> 9% of each run, Pallas kernels for 4% -> 3%
where the time goes in v7:
time: 146 us; the launch traced here: 145 us
  starting transfers between devices  53.6 us (37%)
  other arithmetic  39 us (27%)
  Pallas kernels  17.3 us (12%)
  waiting for transfers between devices  17.2 us (12%)
  local copies, waits for them, and re-layouts  17.1 us (12%)
    ppermute x4, starting transfers between devices, send(): return lax.ppermute(piece, both, pairs)  26.9 us
    ppermute x4, waiting for transfers between devices, send(): return lax.ppermute(piece, both, pairs)  14.4 us
    ppermute x7, starting transfers between devices, gather_baro(): blocks.append(lax.ppermute(wide, merid, pairs))  11.1 us
    mul x2, other arithmetic, laplace(): return (beside_all - 4.0 * centre) * wet_mask[..., 1:-1, 1:-1]  10.4 us
    concatenate x1, other arithmetic, halo_3d(): return jnp.concatenate([low_band, middle, high_band], axis=-2)  9.53 us
    pallas_call x1, Pallas kernels, baro_run(): pl.pallas_call(baro_kernel, out_shape=jax.ShapeDtypeStruct((5, whole.shap...  8.88 us
    ppermute x1, starting transfers between devices, gather_baro(): high = lax.ppermute(fields[..., :BARO_HALO], 'gx', backward)  7.31 us
    ppermute x2, starting transfers between devices, send(): lax.ppermute(piece, merid, [(s % merid_n, t % merid_n) for s, t in pairs[...  6.76 us
  transfers between devices with their start and end apart: 17, of which 3 were waited for; matrix products, arithmetic and copies ran while one was open for 9% of the time, Pallas kernels for 3%

profile of v7, /device:TPU:1, one launch (start us, length us, event | category | flops | bytes accessed | tf_op | source)
XLA Modules:
  0.0 145.4 jit_solution(14054515931168891603)
XLA Ops:
  0.6 0.8 convert_element_type.4
  1.4 0.7 fusion.48
  2.1 1.6 %broadcast_multiply_fusion.2 = (f32[80,8,128]{2,1,0:T(8,128)}, f32[8,128]{1,0:T(8,128)S(1)}, f32[80,8,128]{2,1,0:T(8,128)S(1)}) fusion(f32[80]{0:T(128)} %th_ref.3, f32[8,128]{1,0:T(8,128)S(1)} %convert_element_type.4, s32[8,128]{1,0:T(8,128)} %param.15), kind=kLoop, calls=%fused_computation.109 | loop fusion | flops 326656 | bytes 667968 | tf_op jit(solution)/shard_map/mul | solution.py:208
  3.7 1.3 broadcast_multiply_fusion.1
  5.0 0.0 copy-start.3
  5.0 0.1 pad_maximum_fusion
  5.1 2.1 %fusion.63 = (f32[5,80,2,2]{3,2,1,0:T(2,128)}, f32[5,80,2,2]{3,2,1,0:T(2,128)}, f32[5,80,2,2]{3,2,1,0:T(2,128)}, f32[5,80,2,2]{3,2,1,0:T(2,128)}) fusion(f32[5,80,8,128]{3,2,1,0:T(8,128)S(1)} %pad_maximum_fusion), kind=kLoop, calls=%fused_computation.145 | loop fusion | bytes 51200 | tf_op jit(solution)/shard_map/slice | solution.py:170
  7.3 13.8 %collective-permute-start.7 = (f32[5,80,2,2]{3,2,1,0:T(2,128)}, f32[5,80,2,2]{3,2,1,0:T(2,128)}, u32[]{:S(2)}, u32[]{:S(2)}) collective-permute-start(f32[5,80,2,2]{3,2,1,0:T(2,128)} %get-tuple-element.20), channel_id=1, source_target_pairs={{1,248},{2,249},{3,250},{4,251},{5,252},{6,253},{7,254},{9,0},{10,... | collective-permute-start | bytes 19208 | tf_op jit(solution)/shard_map/ppermute | solution.py:161
  21.0 1.2 fusion.64
  22.2 2.4 %collective-permute-start.6 = (f32[5,80,2,128]{3,2,1,0:T(2,128)}, f32[5,80,2,128]{3,2,1,0:T(2,128)}, u32[]{:S(2)}, u32[]{:S(2)}) collective-permute-start(f32[5,80,2,128]{3,2,1,0:T(2,128)} %get-tuple-element.23), channel_id=1, source_target_pairs={{1,0},{2,1},{3,2},{4,3},{5,4},{6,5},{7,6},{9,8},{10,9},{11,10},{12... | collective-permute-start | bytes 1228808 | tf_op jit(solution)/shard_map/ppermute | solution.py:160
  24.6 1.7 %fusion.65 = (f32[5,80,8,2]{3,2,1,0:T(8,128)S(1)}, f32[5,80,8,2]{3,2,1,0:T(8,128)}) fusion(f32[5,80,8,128]{3,2,1,0:T(8,128)S(1)} %pad_maximum_fusion), kind=kLoop, calls=%fused_computation.147 | loop fusion | bytes 102400 | tf_op jit(solution)/shard_map/slice | solution.py:166
  26.3 2.0 %copy.14 = f32[5,80,8,2]{1,2,3,0:T(8,128)S(1)} copy(f32[5,80,8,2]{3,2,1,0:T(8,128)} %get-tuple-element.25) | data formatting | bytes 51200 | tf_op jit(solution)/shard_map/slice | solution.py:167
  28.3 0.5 collective-permute-start.4
  28.9 0.5 copy.13
  29.4 1.1 collective-permute-start.3
  30.5 4.4 %collective-permute-start.1 = (f32[5,80,2,128]{3,2,1,0:T(2,128)}, f32[5,80,2,128]{3,2,1,0:T(2,128)}, u32[]{:S(2)}, u32[]{:S(2)}) collective-permute-start(f32[5,80,2,128]{3,2,1,0:T(2,128)} %get-tuple-element.22), channel_id=1, source_target_pairs={{0,1},{1,2},{2,3},{3,4},{4,5},{5,6},{6,7},{8,9},{9,10},{10,11},{11... | collective-permute-start | bytes 1228808 | tf_op jit(solution)/shard_map/ppermute | solution.py:160
  34.8 0.6 reduce_sum.38
  35.4 0.6 constant_dynamic-update-slice_fusion.6
  36.1 0.0 collective-permute-done.7
  36.1 2.4 %collective-permute-start.5 = (f32[5,80,2,2]{3,2,1,0:T(2,128)}, f32[5,80,2,2]{3,2,1,0:T(2,128)}, u32[]{:S(2)}, u32[]{:S(2)}) collective-permute-start(f32[5,80,2,2]{3,2,1,0:T(2,128)} %get-tuple-element.19), channel_id=1, source_target_pairs={{1,8},{2,9},{3,10},{4,11},{5,12},{6,13},{7,14},{9,16},{10,17},{11,... | collective-permute-start | bytes 19208 | tf_op jit(solution)/shard_map/ppermute | solution.py:161
  38.6 0.0 collective-permute-done.4
  38.6 8.6 %collective-permute-start.2 = (f32[5,80,2,2]{3,2,1,0:T(2,128)}, f32[5,80,2,2]{3,2,1,0:T(2,128)}, u32[]{:S(2)}, u32[]{:S(2)}) collective-permute-start(f32[5,80,2,2]{3,2,1,0:T(2,128)} %get-tuple-element.21), channel_id=1, source_target_pairs={{0,249},{1,250},{2,251},{3,252},{4,253},{5,254},{6,255},{8,1},{9,2... | collective-permute-start | bytes 19208 | tf_op jit(solution)/shard_map/ppermute | solution.py:161
  47.2 0.0 collective-permute-done.3
  47.2 2.1 %collective-permute-start = (f32[5,80,2,2]{3,2,1,0:T(2,128)}, f32[5,80,2,2]{3,2,1,0:T(2,128)}, u32[]{:S(2)}, u32[]{:S(2)}) collective-permute-start(f32[5,80,2,2]{3,2,1,0:T(2,128)} %get-tuple-element.18), channel_id=1, source_target_pairs={{0,9},{1,10},{2,11},{3,12},{4,13},{5,14},{6,15},{8,17},{9,18},{10,... | collective-permute-start | bytes 19208 | tf_op jit(solution)/shard_map/ppermute | solution.py:161
  49.3 0.1 constant_dynamic-update-slice_fusion.4
  49.4 0.6 copy.16
  50.0 1.8 %copy.15 = f32[5,80,8,2]{3,2,1,0:T(8,128)} copy(f32[5,80,8,2]{1,2,3,0:T(8,128)S(1)} %collective-permute-done.3) | data formatting | bytes 51200 | tf_op jit(solution)/shard_map/ppermute | solution.py:152
  51.7 8.9 %collective-permute-done.5 = f32[5,80,2,2]{3,2,1,0:T(2,128)} collective-permute-done((f32[5,80,2,2]{3,2,1,0:T(2,128)}, f32[5,80,2,2]{3,2,1,0:T(2,128)}, u32[]{:S(2)}, u32[]{:S(2)}) %collective-permute-start.5) | collective-permute-done | bytes 6432 | tf_op jit(solution)/shard_map/ppermute | solution.py:161
  60.7 5.5 %collective-permute-done = f32[5,80,2,2]{3,2,1,0:T(2,128)} collective-permute-done((f32[5,80,2,2]{3,2,1,0:T(2,128)}, f32[5,80,2,2]{3,2,1,0:T(2,128)}, u32[]{:S(2)}, u32[]{:S(2)}) %collective-permute-start) | collective-permute-done | bytes 6432 | tf_op jit(solution)/shard_map/ppermute | solution.py:161
  66.2 0.0 collective-permute-done.1
  66.2 9.5 %maximum_maximum_fusion.pad_ref = f32[5,80,12,132]{3,2,1,0:T(8,128)S(1)} fusion(f32[5,80,2,2]{3,2,1,0:T(2,128)} %collective-permute-done.7, f32[5,80,2,128]{3,2,1,0:T(2,128)} %collective-permute-done.6, f32[5,80,2,2]{3,2,1,0:T(2,128)} %collective-permute-done.5, f32[5,80,8,2]{3,2,1,0:T(8,128)S(1)} %copy.16, f32[1,80,8,128]{3,2,1,0:T(8,128)S(1)} %fusion.48, ...), kind=kLoop, calls=%fused_computation | loop fusion | flops 6336000 | bytes 5068800 | tf_op jit(solution)/shard_map/concatenate | solution.py:177
  75.7 4.2 %fusion.62 = (f32[80,12,132]{2,1,0:T(8,128)}, f32[80,12,132]{2,1,0:T(8,128)}, f32[80,12,132]{2,1,0:T(8,128)}, f32[80,12,132]{2,1,0:T(8,128)}, f32[80,12,132]{2,1...) fusion(f32[5,80,12,132]{3,2,1,0:T(8,128)S(1)} %maximum_maximum_fusion.pad_ref), kind=kLoop, calls=%fused_computation.144 | loop fusion | flops 887040 | bytes 5575680 | tf_op jit(solution)/shard_map/mul | solution.py:49
  80.0 1.2 copy-done
  81.2 2.3 %slice_bitcast_fusion.3 = (f32[80,12,132]{2,1,0:T(8,128)S(1)}, f32[80,12,132]{2,1,0:T(8,128)}, f32[80,12,132]{2,1,0:T(8,128)}, f32[80,12,132]{2,1,0:T(8,128)}, f32[80,12,132]{2,1,0:T(8,128)S(1)}) fusion(f32[5,80,12,132]{3,2,1,0:T(8,128)S(1)} %maximum_maximum_fusion.pad_ref), kind=kLoop, calls=%fused_computation.29 | loop fusion | bytes 5068800 | tf_op jit(solution)/shard_map/squeeze | solution.py:48
  83.5 4.4 %shard_map.120 = f32[80,12,132]{2,1,0:T(8,128)} custom-call(f32[80]{0:T(128)} %th_ref.3, f32[5,80,12,132]{3,2,1,0:T(8,128)} %copy-done), custom_call_target="tpu_custom_call" | custom-call | tf_op jit(solution)/shard_map/pallas_call | solution.py:307
  87.9 5.8 %fusion.1 = f32[80,10,130]{2,1,0:T(8,128)S(1)} fusion(f32[80,12,132]{2,1,0:T(8,128)} %get-tuple-element.14, f32[80,12,132]{2,1,0:T(8,128)} %get-tuple-element.16), kind=kLoop, calls=%fused_computation.4 | loop fusion | flops 624000 | bytes 2912000 | tf_op jit(solution)/shard_map/mul | solution.py:29
  93.8 4.6 %fusion.7 = (f32[80,10,130]{2,1,0:T(8,128)S(1)}, f32[80,10,130]{2,1,0:T(8,128)S(1)}, f32[80,10,130]{2,1,0:T(8,128)S(1)}) fusion(f32[80,12,132]{2,1,0:T(8,128)S(1)} %get-tuple-element.13, f32[80,12,132]{2,1,0:T(8,128)S(1)} %copy-done.2, f32[80,12,132]{2,1,0:T(8,128)S(1)} %get-tuple-element.17, f32[80,12,132]{2,1,0:T(8,128)S(1)} %copy-done.1), kind=kLoop, calls=%fused_computation.25 | loop fusion | flops 1872000 | bytes 7904000 | tf_op jit(solution)/shard_map/mul | solution.py:29
  98.4 1.1 fusion.40
  99.5 0.2 copy-done.14
  99.8 1.1 fusion.29
  100.9 0.2 fusion.8
  101.1 0.1 fusion.67
  101.2 7.3 %collective-permute-start.9 = (f32[8,8,64]{2,1,0:T(8,128)S(1)}, f32[8,8,64]{2,1,0:T(8,128)S(1)}, u32[]{:S(2)}, u32[]{:S(2)}) collective-permute-start(f32[8,8,64]{2,1,0:T(8,128)S(1)} %get-tuple-element.34), channel_id=1, source_target_pairs={{8,0},{16,8},{24,16},{32,24},{40,32},{48,40},{56,48},{64,56},{72,6... | collective-permute-start | bytes 49160 | tf_op jit(solution)/shard_map/ppermute | solution.py:222
  108.5 0.8 fusion.13
  109.4 0.5 copy-done.10
  109.8 0.4 copy-done.11
  110.2 0.8 fusion.21
  111.1 0.2 copy-done.4
  111.3 1.3 maximum_add_fusion.prov_ref
  112.6 4.0 %shard_map.121 = f32[4,80,8,128]{3,2,1,0:T(8,128)} custom-call(f32[80]{0:T(128)} %th_ref.3, f32[4,80,8,128]{3,2,1,0:T(8,128)} %maximum_add_fusion.prov_ref, f32[80,8,128]{2,1,0:T(8,128)} %mix_ref.1, f32[80,8,128]{2,1,0:T(8,128)} %copy-done.8), custom_call_target="tpu_custom_call" | custom-call | tf_op jit(solution)/shard_map/pallas_call | solution.py:359
  116.6 0.1 bitcast_dynamic-update-slice_fusion.7
  116.7 0.1 collective-permute-start.10
  116.8 1.3 multiply_reduce_fusion
  118.1 0.1 collective-permute-start.11
  118.2 6.4 %collective-permute-start.12 = (f32[8,8,256]{2,1,0:T(8,128)S(1)}, f32[8,8,256]{2,1,0:T(8,128)S(1)}, u32[]{:S(2)}, u32[]{:S(2)}) collective-permute-start(f32[8,8,256]{2,1,0:T(8,128)S(1)} %get-tuple-element.5), channel_id=1, source_target_pairs={{0,5},{1,6},{2,7},{3,0},{4,1},{5,2},{6,3},{7,4},{8,13},{9,14},{10,... | collective-permute-start | bytes 196616 | tf_op jit(solution)/shard_map/ppermute | solution.py:229
  124.6 0.2 collective-permute-start.14
  124.8 1.8 %collective-permute-start.15 = (f32[8,8,256]{2,1,0:T(8,128)S(1)}, f32[8,8,256]{2,1,0:T(8,128)S(1)}, u32[]{:S(2)}, u32[]{:S(2)}) collective-permute-start(f32[8,8,256]{2,1,0:T(8,128)S(1)} %get-tuple-element.5), channel_id=1, source_target_pairs={{0,2},{1,3},{2,4},{3,5},{4,6},{5,7},{6,0},{7,1},{8,10},{9,11},{10,... | collective-permute-start | bytes 196616 | tf_op jit(solution)/shard_map/ppermute | solution.py:229
  126.6 2.5 %collective-permute-start.16 = (f32[8,8,256]{2,1,0:T(8,128)S(1)}, f32[8,8,256]{2,1,0:T(8,128)S(1)}, u32[]{:S(2)}, u32[]{:S(2)}) collective-permute-start(f32[8,8,256]{2,1,0:T(8,128)S(1)} %get-tuple-element.5), channel_id=1, source_target_pairs={{0,1},{1,2},{2,3},{3,4},{4,5},{5,6},{6,7},{7,0},{8,9},{9,10},{10,1... | collective-permute-start | bytes 196616 | tf_op jit(solution)/shard_map/ppermute | solution.py:229
  129.2 2.7 %collective-permute-done.16 = f32[8,8,256]{2,1,0:T(8,128)S(1)} collective-permute-done((f32[8,8,256]{2,1,0:T(8,128)S(1)}, f32[8,8,256]{2,1,0:T(8,128)S(1)}, u32[]{:S(2)}, u32[]{:S(2)}) %collective-permute-start.16) | collective-permute-done | bytes 65568 | tf_op jit(solution)/shard_map/ppermute | solution.py:229
  131.9 0.8 copy-done.17
  132.7 8.9 %shard_map.122 = f32[5,8,128]{2,1,0:T(8,128)} custom-call(s32[1]{0:T(128)} %bitcast.9.off_ref, f32[8,8,8,256]{3,2,1,0:T(8,128)} %copy-done.17), custom_call_target="tpu_custom_call" | custom-call | tf_op jit(solution)/shard_map/pallas_call | solution.py:287
  141.6 1.3 slice_bitcast_fusion.5
  142.9 1.3 fusion.68
  144.2 1.2 fusion.66
  (69 shorter events, 0.2 us)
Async XLA Ops:
  0.6 3.1 %copy-start.18 = (f32[2,80,8,128]{3,2,1,0:T(8,128)S(1)}, f32[2,80,8,128]{3,2,1,0:T(8,128)}, u32[]{:S(2)}) copy-start(f32[2,80,8,128]{3,2,1,0:T(8,128)} %param.9) | copy-start | bytes 1966084
  3.7 1.3 copy-start.8
  5.0 61.2 %copy-start.3 = (f32[2,80,8,128]{3,2,1,0:T(8,128)}, f32[2,80,8,128]{3,2,1,0:T(8,128)S(1)}, u32[]{:S(2)}) copy-start(f32[2,80,8,128]{3,2,1,0:T(8,128)S(1)} %get-tuple-element.32) | copy-start | bytes 1966084
  7.3 28.8 %collective-permute-start.7 = (f32[5,80,2,2]{3,2,1,0:T(2,128)}, f32[5,80,2,2]{3,2,1,0:T(2,128)}, u32[]{:S(2)}, u32[]{:S(2)}) collective-permute-start(f32[5,80,2,2]{3,2,1,0:T(2,128)} %get-tuple-element.20), channel_id=1, source_target_pairs={{1,248},{2,249},{3,250},{4,251},{5,252},{6,253},{7,254},{9,0},{10,... | collective-permute-start | bytes 19208 | tf_op jit(solution)/shard_map/ppermute | solution.py:161
  22.2 44.0 %collective-permute-start.6 = (f32[5,80,2,128]{3,2,1,0:T(2,128)}, f32[5,80,2,128]{3,2,1,0:T(2,128)}, u32[]{:S(2)}, u32[]{:S(2)}) collective-permute-start(f32[5,80,2,128]{3,2,1,0:T(2,128)} %get-tuple-element.23), channel_id=1, source_target_pairs={{1,0},{2,1},{3,2},{4,3},{5,4},{6,5},{7,6},{9,8},{10,9},{11,10},{12... | collective-permute-start | bytes 1228808 | tf_op jit(solution)/shard_map/ppermute | solution.py:160
  26.3 8.5 %copy-start.21 = (f32[80]{0:T(128)S(1)}, f32[80]{0:T(128)}, u32[]{:S(2)}) copy-start(f32[80]{0:T(128)} %th_ref.3) | copy-start | bytes 964
  26.3 9.8 %copy-start.19 = (s32[8,128]{1,0:T(8,128)S(1)}, s32[8,128]{1,0:T(8,128)}, u32[]{:S(2)}) copy-start(s32[8,128]{1,0:T(8,128)} %param.14) | copy-start | bytes 12292
  26.3 22.9 %copy-start.24 = (f32[8]{0:T(128)S(1)}, f32[8]{0:T(128)}, u32[]{:S(2)}) copy-start(f32[8]{0:T(128)} %param.13) | copy-start | bytes 100
  28.3 10.2 %collective-permute-start.4 = (f32[5,80,8,2]{1,2,3,0:T(8,128)S(1)}, f32[5,80,8,2]{1,2,3,0:T(8,128)S(1)}, u32[]{:S(2)}, u32[]{:S(2)}) collective-permute-start(f32[5,80,8,2]{1,2,3,0:T(8,128)S(1)} %copy.14), channel_id=1, source_target_pairs={{0,248},{8,0},{16,8},{24,16},{32,24},{40,32},{48,40},{56,48},{64,5... | collective-permute-start | bytes 76808 | tf_op jit(solution)/shard_map/ppermute | solution.py:152
  29.4 17.8 %collective-permute-start.3 = (f32[5,80,8,2]{1,2,3,0:T(8,128)S(1)}, f32[5,80,8,2]{1,2,3,0:T(8,128)S(1)}, u32[]{:S(2)}, u32[]{:S(2)}) collective-permute-start(f32[5,80,8,2]{1,2,3,0:T(8,128)S(1)} %copy.13), channel_id=1, source_target_pairs={{0,8},{8,16},{16,24},{24,32},{32,40},{40,48},{48,56},{56,64},{64,7... | collective-permute-start | bytes 76808 | tf_op jit(solution)/shard_map/ppermute | solution.py:152
  30.5 35.7 %collective-permute-start.1 = (f32[5,80,2,128]{3,2,1,0:T(2,128)}, f32[5,80,2,128]{3,2,1,0:T(2,128)}, u32[]{:S(2)}, u32[]{:S(2)}) collective-permute-start(f32[5,80,2,128]{3,2,1,0:T(2,128)} %get-tuple-element.22), channel_id=1, source_target_pairs={{0,1},{1,2},{2,3},{3,4},{4,5},{5,6},{6,7},{8,9},{9,10},{10,11},{11... | collective-permute-start | bytes 1228808 | tf_op jit(solution)/shard_map/ppermute | solution.py:160
  36.1 24.6 %collective-permute-start.5 = (f32[5,80,2,2]{3,2,1,0:T(2,128)}, f32[5,80,2,2]{3,2,1,0:T(2,128)}, u32[]{:S(2)}, u32[]{:S(2)}) collective-permute-start(f32[5,80,2,2]{3,2,1,0:T(2,128)} %get-tuple-element.19), channel_id=1, source_target_pairs={{1,8},{2,9},{3,10},{4,11},{5,12},{6,13},{7,14},{9,16},{10,17},{11,... | collective-permute-start | bytes 19208 | tf_op jit(solution)/shard_map/ppermute | solution.py:161
  38.6 22.1 %collective-permute-start.2 = (f32[5,80,2,2]{3,2,1,0:T(2,128)}, f32[5,80,2,2]{3,2,1,0:T(2,128)}, u32[]{:S(2)}, u32[]{:S(2)}) collective-permute-start(f32[5,80,2,2]{3,2,1,0:T(2,128)} %get-tuple-element.21), channel_id=1, source_target_pairs={{0,249},{1,250},{2,251},{3,252},{4,253},{5,254},{6,255},{8,1},{9,2... | collective-permute-start | bytes 19208 | tf_op jit(solution)/shard_map/ppermute | solution.py:161
  47.2 19.0 %collective-permute-start = (f32[5,80,2,2]{3,2,1,0:T(2,128)}, f32[5,80,2,2]{3,2,1,0:T(2,128)}, u32[]{:S(2)}, u32[]{:S(2)}) collective-permute-start(f32[5,80,2,2]{3,2,1,0:T(2,128)} %get-tuple-element.18), channel_id=1, source_target_pairs={{0,9},{1,10},{2,11},{3,12},{4,13},{5,14},{6,15},{8,17},{9,18},{10,... | collective-permute-start | bytes 19208 | tf_op jit(solution)/shard_map/ppermute | solution.py:161
  75.7 5.5 %copy-start = (f32[5,80,12,132]{3,2,1,0:T(8,128)}, f32[5,80,12,132]{3,2,1,0:T(8,128)S(1)}, u32[]{:S(2)}) copy-start(f32[5,80,12,132]{3,2,1,0:T(8,128)S(1)} %maximum_maximum_fusion.pad_ref) | copy-start | bytes 7603204
  87.9 5.8 %copy-start.1 = (f32[80,12,132]{2,1,0:T(8,128)S(1)}, f32[80,12,132]{2,1,0:T(8,128)}, u32[]{:S(2)}) copy-start(f32[80,12,132]{2,1,0:T(8,128)} %get-tuple-element.15) | copy-start | bytes 1520644
  87.9 5.8 %copy-start.2 = (f32[80,12,132]{2,1,0:T(8,128)S(1)}, f32[80,12,132]{2,1,0:T(8,128)}, u32[]{:S(2)}) copy-start(f32[80,12,132]{2,1,0:T(8,128)} %get-tuple-element.16) | copy-start | bytes 1520644
  93.7 4.7 %copy-start.6 = (f32[80,12,132]{2,1,0:T(8,128)S(1)}, f32[80,12,132]{2,1,0:T(8,128)}, u32[]{:S(2)}) copy-start(f32[80,12,132]{2,1,0:T(8,128)} %get-tuple-element.7) | copy-start | bytes 1520644
  93.7 4.7 %copy-start.7 = (f32[80,12,132]{2,1,0:T(8,128)S(1)}, f32[80,12,132]{2,1,0:T(8,128)}, u32[]{:S(2)}) copy-start(f32[80,12,132]{2,1,0:T(8,128)} %shard_map.120) | copy-start | bytes 1520644
  93.8 4.7 %copy-start.15 = (f32[80,12,132]{2,1,0:T(8,128)S(1)}, f32[80,12,132]{2,1,0:T(8,128)}, u32[]{:S(2)}) copy-start(f32[80,12,132]{2,1,0:T(8,128)} %get-tuple-element.6) | copy-start | bytes 1520644
  98.4 1.3 copy-start.14
  99.8 1.1 copy-start.22
  99.8 1.3 copy-start.23
  99.8 1.3 copy-start.20
  99.8 8.7 %copy-start.12 = (f32[80,12,132]{2,1,0:T(8,128)S(1)}, f32[80,12,132]{2,1,0:T(8,128)}, u32[]{:S(2)}) copy-start(f32[80,12,132]{2,1,0:T(8,128)} %get-tuple-element.9) | copy-start | bytes 1520644
  99.8 8.7 %copy-start.13 = (f32[80,12,132]{2,1,0:T(8,128)S(1)}, f32[80,12,132]{2,1,0:T(8,128)}, u32[]{:S(2)}) copy-start(f32[80,12,132]{2,1,0:T(8,128)} %get-tuple-element.10) | copy-start | bytes 1520644
  101.2 15.4 %collective-permute-start.9 = (f32[8,8,64]{2,1,0:T(8,128)S(1)}, f32[8,8,64]{2,1,0:T(8,128)S(1)}, u32[]{:S(2)}, u32[]{:S(2)}) collective-permute-start(f32[8,8,64]{2,1,0:T(8,128)S(1)} %get-tuple-element.34), channel_id=1, source_target_pairs={{8,0},{16,8},{24,16},{32,24},{40,32},{48,40},{56,48},{64,56},{72,6... | collective-permute-start | bytes 49160 | tf_op jit(solution)/shard_map/ppermute | solution.py:222
  108.5 8.1 %collective-permute-start.8 = (f32[8,8,64]{2,1,0:T(8,128)S(1)}, f32[8,8,64]{2,1,0:T(8,128)S(1)}, u32[]{:S(2)}, u32[]{:S(2)}) collective-permute-start(f32[8,8,64]{2,1,0:T(8,128)S(1)} %get-tuple-element.33), channel_id=1, source_target_pairs={{0,8},{8,16},{16,24},{24,32},{32,40},{40,48},{48,56},{56,64},{64,7... | collective-permute-start | bytes 49160 | tf_op jit(solution)/shard_map/ppermute | solution.py:221
  108.5 1.3 copy-start.10
  108.5 1.7 %copy-start.11 = (f32[80,12,132]{2,1,0:T(8,128)S(1)}, f32[80,12,132]{2,1,0:T(8,128)}, u32[]{:S(2)}) copy-start(f32[80,12,132]{2,1,0:T(8,128)} %get-tuple-element.12) | copy-start | bytes 1520644
  110.2 1.1 copy-start.4
  112.6 4.2 %copy-start.16 = (f32[80,8,128]{2,1,0:T(8,128)S(1)}, f32[80,8,128]{2,1,0:T(8,128)}, u32[]{:S(2)}) copy-start(f32[80,8,128]{2,1,0:T(8,128)} %get-tuple-element.37) | copy-start | bytes 983044
  116.7 27.5 %copy-start.5 = (f32[4,80,8,128]{3,2,1,0:T(8,128)S(1)}, f32[4,80,8,128]{3,2,1,0:T(8,128)}, u32[]{:S(2)}) copy-start(f32[4,80,8,128]{3,2,1,0:T(8,128)} %shard_map.121) | copy-start | bytes 3932164
  116.7 27.5 %copy-start.9 = (f32[80,8,128]{2,1,0:T(8,128)S(1)}, f32[80,8,128]{2,1,0:T(8,128)}, u32[]{:S(2)}) copy-start(f32[80,8,128]{2,1,0:T(8,128)} %copy-done.8) | copy-start | bytes 983044
  116.7 8.1 %collective-permute-start.10 = (f32[8,8,256]{2,1,0:T(8,128)S(1)}, f32[8,8,256]{2,1,0:T(8,128)S(1)}, u32[]{:S(2)}, u32[]{:S(2)}) collective-permute-start(f32[8,8,256]{2,1,0:T(8,128)S(1)} %get-tuple-element.5), channel_id=1, source_target_pairs={{0,7},{1,0},{2,1},{3,2},{4,3},{5,4},{6,5},{7,6},{8,15},{9,8},{10,9... | collective-permute-start | bytes 196616 | tf_op jit(solution)/shard_map/ppermute | solution.py:229
  118.1 8.5 %collective-permute-start.11 = (f32[8,8,256]{2,1,0:T(8,128)S(1)}, f32[8,8,256]{2,1,0:T(8,128)S(1)}, u32[]{:S(2)}, u32[]{:S(2)}) collective-permute-start(f32[8,8,256]{2,1,0:T(8,128)S(1)} %get-tuple-element.5), channel_id=1, source_target_pairs={{0,6},{1,7},{2,0},{3,1},{4,2},{5,3},{6,4},{7,5},{8,14},{9,15},{10,... | collective-permute-start | bytes 196616 | tf_op jit(solution)/shard_map/ppermute | solution.py:229
  118.2 10.9 %collective-permute-start.12 = (f32[8,8,256]{2,1,0:T(8,128)S(1)}, f32[8,8,256]{2,1,0:T(8,128)S(1)}, u32[]{:S(2)}, u32[]{:S(2)}) collective-permute-start(f32[8,8,256]{2,1,0:T(8,128)S(1)} %get-tuple-element.5), channel_id=1, source_target_pairs={{0,5},{1,6},{2,7},{3,0},{4,1},{5,2},{6,3},{7,4},{8,13},{9,14},{10,... | collective-permute-start | bytes 196616 | tf_op jit(solution)/shard_map/ppermute | solution.py:229
  124.6 4.5 %collective-permute-start.13 = (f32[8,8,256]{2,1,0:T(8,128)S(1)}, f32[8,8,256]{2,1,0:T(8,128)S(1)}, u32[]{:S(2)}, u32[]{:S(2)}) collective-permute-start(f32[8,8,256]{2,1,0:T(8,128)S(1)} %get-tuple-element.5), channel_id=1, source_target_pairs={{0,4},{1,5},{2,6},{3,7},{4,0},{5,1},{6,2},{7,3},{8,12},{9,13},{10,... | collective-permute-start | bytes 196616 | tf_op jit(solution)/shard_map/ppermute | solution.py:229
  124.6 4.6 %collective-permute-start.14 = (f32[8,8,256]{2,1,0:T(8,128)S(1)}, f32[8,8,256]{2,1,0:T(8,128)S(1)}, u32[]{:S(2)}, u32[]{:S(2)}) collective-permute-start(f32[8,8,256]{2,1,0:T(8,128)S(1)} %get-tuple-element.5), channel_id=1, source_target_pairs={{0,3},{1,4},{2,5},{3,6},{4,7},{5,0},{6,1},{7,2},{8,11},{9,12},{10,... | collective-permute-start | bytes 196616 | tf_op jit(solution)/shard_map/ppermute | solution.py:229
  124.8 4.4 %collective-permute-start.15 = (f32[8,8,256]{2,1,0:T(8,128)S(1)}, f32[8,8,256]{2,1,0:T(8,128)S(1)}, u32[]{:S(2)}, u32[]{:S(2)}) collective-permute-start(f32[8,8,256]{2,1,0:T(8,128)S(1)} %get-tuple-element.5), channel_id=1, source_target_pairs={{0,2},{1,3},{2,4},{3,5},{4,6},{5,7},{6,0},{7,1},{8,10},{9,11},{10,... | collective-permute-start | bytes 196616 | tf_op jit(solution)/shard_map/ppermute | solution.py:229
  126.6 5.3 %collective-permute-start.16 = (f32[8,8,256]{2,1,0:T(8,128)S(1)}, f32[8,8,256]{2,1,0:T(8,128)S(1)}, u32[]{:S(2)}, u32[]{:S(2)}) collective-permute-start(f32[8,8,256]{2,1,0:T(8,128)S(1)} %get-tuple-element.5), channel_id=1, source_target_pairs={{0,1},{1,2},{2,3},{3,4},{4,5},{5,6},{6,7},{7,0},{8,9},{9,10},{10,1... | collective-permute-start | bytes 196616 | tf_op jit(solution)/shard_map/ppermute | solution.py:229
  131.9 0.8 copy-start.17

commit v8 on v7

--- a/solution.py
+++ b/solution.py
@@ -201,13 +201,10 @@
     whole = gather_baro(fields)
     rows = land.shape[0]
     row_offset = jnp.full((1,), lax.axis_index(("gy", "ga")) * rows, jnp.int32)
-    mine = baro_run(whole, row_offset, land.shape[1])
-    average = mine[3:]
-    solved = solve_columns(provisional, mixing, wet_mask, thickness)
+    solved_uv, new_tracers = solve_columns(provisional, mixing, wet_mask, thickness)
     thick_col = thickness.reshape((levels, 1, 1))
-    depth_mean = jnp.sum(thick_col[None] * wet_mask[None] * solved[:2], axis=1) / safe_depth
-    new_velocity = (solved[:2] - depth_mean[:, None] + average[:, None]) * wet_mask[None]
-    new_tracers = solved[2:]
+    depth_mean = jnp.sum(thick_col[None] * wet_mask[None] * solved_uv, axis=1) / safe_depth
+    new_velocity, mine = baro_run(whole, row_offset, solved_uv, depth_mean, wet_mask)
     return (new_velocity, new_tracers, mine[0], mine[1:3])
 
 
@@ -230,7 +227,7 @@
     return jnp.stack(blocks)
 
 
-def baro_kernel(off_ref, f_ref, o_ref):
+def baro_kernel(off_ref, f_ref, uv_ref, dm_ref, wet_ref, nv_ref, o_ref):
     parts = f_ref.shape[0]
     block_rows = f_ref.shape[2]
     rows = parts * block_rows
@@ -279,17 +276,34 @@
     height, east_vel, north_vel, sum_east, sum_north = lax.fori_loop(0, NSUB, body, carry)
     finals = (height, east_vel, north_vel, sum_east / NSUB, sum_north / NSUB)
     out_cols = o_ref.shape[2]
-    for index in range(5):
-        o_ref[index] = pltpu.roll(finals[index][:block_rows], cols - BARO_HALO, 1)[:, :out_cols]
-
-
-def baro_run(whole, row_offset, out_cols):
+    mine = [
+        pltpu.roll(finals[index][:block_rows], cols - BARO_HALO, 1)[:, :out_cols] for index in range(5)
+    ]
+    for index in range(3):
+        o_ref[index] = mine[index]
+    mean_east = dm_ref[0]
+    mean_north = dm_ref[1]
+
+    def level(k, carry):
+        wet = wet_ref[k]
+        nv_ref[0, k] = (uv_ref[0, k] - mean_east + mine[3]) * wet
+        nv_ref[1, k] = (uv_ref[1, k] - mean_north + mine[4]) * wet
+        return carry
+
+    lax.fori_loop(0, wet_ref.shape[0], level, 0, unroll=4)
+
+
+def baro_run(whole, row_offset, solved_uv, depth_mean, wet_mask):
+    vmem = pl.BlockSpec(memory_space=pltpu.VMEM)
     return pl.pallas_call(
         baro_kernel,
-        out_shape=jax.ShapeDtypeStruct((5, whole.shape[2], out_cols), jnp.float32),
-        in_specs=[pl.BlockSpec(memory_space=pltpu.SMEM), pl.BlockSpec(memory_space=pltpu.VMEM)],
-        out_specs=pl.BlockSpec(memory_space=pltpu.VMEM),
-    )(row_offset, whole)
+        out_shape=[
+            jax.ShapeDtypeStruct(solved_uv.shape, jnp.float32),
+            jax.ShapeDtypeStruct((3,) + wet_mask.shape[1:], jnp.float32),
+        ],
+        in_specs=[pl.BlockSpec(memory_space=pltpu.SMEM)] + [vmem] * 4,
+        out_specs=[vmem, vmem],
+    )(row_offset, whole, solved_uv, depth_mean, wet_mask)
 
 
 def pressure_kernel(th_ref, pad_ref, o_ref):
@@ -312,10 +326,11 @@
     )(thickness, padded)
 
 
-def solve_kernel(th_ref, prov_ref, mix_ref, wet_ref, o_ref, ratio_ref):
+def solve_kernel(th_ref, prov_ref, mix_ref, wet_ref, uv_ref, ts_ref, ratio_ref):
     levels = mix_ref.shape[0]
     shape = mix_ref.shape[1:]
     comps = prov_ref.shape[0]
+    outs = [uv_ref.at[0], uv_ref.at[1], ts_ref.at[0], ts_ref.at[1]]
 
     def below_of(k):
         nxt = jnp.minimum(k + 1, levels - 1)
@@ -335,7 +350,7 @@
         values = []
         for c in range(comps):
             value = (depth * prov_ref[c, k] + upper * value_prev[c]) * inverse
-            o_ref[c, k] = value
+            outs[c][k] = value
             values.append(value)
         return (below, ratio, tuple(values))
 
@@ -347,8 +362,8 @@
         ratio = ratio_ref[k]
         results = []
         for c in range(comps):
-            result = o_ref[c, k] + ratio * following[c]
-            o_ref[c, k] = result
+            result = outs[c][k] + ratio * following[c]
+            outs[c][k] = result
             results.append(result)
         return tuple(results)
 
@@ -358,10 +373,10 @@
 def solve_columns(provisional, mixing, wet_mask, thickness):
     return pl.pallas_call(
         solve_kernel,
-        out_shape=jax.ShapeDtypeStruct(provisional.shape, jnp.float32),
+        out_shape=[jax.ShapeDtypeStruct((2,) + provisional.shape[1:], jnp.float32)] * 2,
         in_specs=[pl.BlockSpec(memory_space=pltpu.SMEM)]
         + [pl.BlockSpec(memory_space=pltpu.VMEM)] * 3,
-        out_specs=pl.BlockSpec(memory_space=pltpu.VMEM),
+        out_specs=[pl.BlockSpec(memory_space=pltpu.VMEM)] * 2,
         scratch_shapes=[pltpu.VMEM(mixing.shape, jnp.float32)],
     )(thickness, provisional, mixing, wet_mask)
 

time: 146 us -> 149 us (1.021)
  starting transfers between devices: 53.6 us -> 61.7 us
  other arithmetic: 39 us -> 33.9 us
  waiting for transfers between devices: 17.2 us -> 12.7 us
  local copies, waits for them, and re-layouts: 17.1 us -> 20.6 us
    ppermute x7, starting transfers between devices: 11.1 us -> 18.5 us  [gather_baro(): blocks.append(lax.ppermute(wide, merid, pairs))]
    ppermute x4, waiting for transfers between devices: 14.4 us -> 9.28 us  [send(): return lax.ppermute(piece, both, pairs)]
    ppermute x1, starting transfers between devices: 7.31 us -> 3.29 us  [gather_baro(): high = lax.ppermute(fields[..., :BARO_HALO], 'gx', backward)]
    ppermute x2, starting transfers between devices: 1.56 us -> 4.89 us  [send(): return lax.ppermute(piece, zonal, pairs)]
    mul x2, other arithmetic: 10.4 us -> 7.84 us  [laplace(): return (beside_all - 4.0 * centre) * wet_mask[..., 1:-1, 1:-1]]
    slice x2 -> x0, other arithmetic: 2.47 us -> none  [the longest x1 1.31 us: shards(): return (new_velocity, new_tracers, mine[0], mine[1:3])]
    slice x2, local copies, waits for them, and re-layouts: 2.28 us -> 4.14 us  [halo_3d(): west = send(block[..., -w:], 1, 0)]
    ppermute x1, starting transfers between devices: 0.01 us -> 1.52 us  [gather_baro(): low = lax.ppermute(fields[..., -BARO_HALO:], 'gx', forward)]
  transfers between devices with their start and end apart: 17 -> 17, of which waited for: 3 -> 2; matrix products, arithmetic and copies ran while one was open for 9% -> 11% of each run, Pallas kernels for 3% -> 3%
where the time goes in v8:
time: 149 us; the launch traced here: 148 us
  starting transfers between devices  61.7 us (41%)
  other arithmetic  33.9 us (23%)
  local copies, waits for them, and re-layouts  20.6 us (14%)
  Pallas kernels  17.9 us (12%)
  waiting for transfers between devices  12.7 us (9%)
    ppermute x4, starting transfers between devices, send(): return lax.ppermute(piece, both, pairs)  26.4 us
    ppermute x7, starting transfers between devices, gather_baro(): blocks.append(lax.ppermute(wide, merid, pairs))  18.5 us
    pallas_call x1, Pallas kernels, baro_run(): pl.pallas_call(baro_kernel, out_shape=[jax.ShapeDtypeStruct(solved_uv.sha...  9.55 us
    concatenate x1, other arithmetic, halo_3d(): return jnp.concatenate([low_band, middle, high_band], axis=-2)  9.53 us
    ppermute x4, waiting for transfers between devices, send(): return lax.ppermute(piece, both, pairs)  9.28 us
    mul x2, other arithmetic, laplace(): return (beside_all - 4.0 * centre) * wet_mask[..., 1:-1, 1:-1]  7.84 us
    ppermute x2, starting transfers between devices, send(): lax.ppermute(piece, merid, [(s % merid_n, t % merid_n) for s, t in pairs[...  7.06 us
    ppermute x2, starting transfers between devices, send(): return lax.ppermute(piece, zonal, pairs)  4.89 us
  transfers between devices with their start and end apart: 17, of which 2 were waited for; matrix products, arithmetic and copies ran while one was open for 11% of the time, Pallas kernels for 3%

profile of v8, /device:TPU:1, one launch (start us, length us, event | category | flops | bytes accessed | tf_op | source)
XLA Modules:
  0.0 148.0 jit_solution(8236576303294555111)
XLA Ops:
  0.6 0.8 convert_element_type.4
  1.4 0.7 fusion.48
  2.1 1.6 %broadcast_multiply_fusion.2 = (f32[80,8,128]{2,1,0:T(8,128)}, f32[8,128]{1,0:T(8,128)S(1)}, f32[80,8,128]{2,1,0:T(8,128)S(1)}) fusion(f32[80]{0:T(128)} %th_ref.3, f32[8,128]{1,0:T(8,128)S(1)} %convert_element_type.4, s32[8,128]{1,0:T(8,128)} %param.15), kind=kLoop, calls=%fused_computation.108 | loop fusion | flops 326656 | bytes 667968 | tf_op jit(solution)/shard_map/mul | solution.py:194
  3.7 1.3 broadcast_multiply_fusion.1
  5.0 0.0 copy-start.4
  5.0 0.1 pad_maximum_fusion
  5.2 2.1 %fusion.63 = (f32[5,80,2,2]{3,2,1,0:T(2,128)}, f32[5,80,2,2]{3,2,1,0:T(2,128)}, f32[5,80,2,2]{3,2,1,0:T(2,128)}, f32[5,80,2,2]{3,2,1,0:T(2,128)}) fusion(f32[5,80,8,128]{3,2,1,0:T(8,128)S(1)} %pad_maximum_fusion), kind=kLoop, calls=%fused_computation.144 | loop fusion | bytes 51200 | tf_op jit(solution)/shard_map/slice | solution.py:170
  7.3 6.5 %collective-permute-start = (f32[5,80,2,2]{3,2,1,0:T(2,128)}, f32[5,80,2,2]{3,2,1,0:T(2,128)}, u32[]{:S(2)}, u32[]{:S(2)}) collective-permute-start(f32[5,80,2,2]{3,2,1,0:T(2,128)} %get-tuple-element.26), channel_id=1, source_target_pairs={{0,9},{1,10},{2,11},{3,12},{4,13},{5,14},{6,15},{8,17},{9,18},{10,... | collective-permute-start | bytes 19208 | tf_op jit(solution)/shard_map/ppermute | solution.py:161
  13.8 2.2 %fusion.65 = (f32[5,80,8,2]{3,2,1,0:T(8,128)}, f32[5,80,8,2]{3,2,1,0:T(8,128)}) fusion(f32[5,80,8,128]{3,2,1,0:T(8,128)S(1)} %pad_maximum_fusion), kind=kLoop, calls=%fused_computation.146 | loop fusion | bytes 102400 | tf_op jit(solution)/shard_map/slice | solution.py:166
  15.9 2.0 %copy.13 = f32[5,80,8,2]{1,2,3,0:T(8,128)S(1)} copy(f32[5,80,8,2]{3,2,1,0:T(8,128)} %get-tuple-element.32) | data formatting | bytes 51200 | tf_op jit(solution)/shard_map/slice | solution.py:166
  17.9 1.3 collective-permute-start.3
  19.3 2.0 %copy.14 = f32[5,80,8,2]{1,2,3,0:T(8,128)S(1)} copy(f32[5,80,8,2]{3,2,1,0:T(8,128)} %get-tuple-element.33) | data formatting | bytes 51200 | tf_op jit(solution)/shard_map/slice | solution.py:167
  21.2 3.5 %collective-permute-start.4 = (f32[5,80,8,2]{1,2,3,0:T(8,128)S(1)}, f32[5,80,8,2]{1,2,3,0:T(8,128)S(1)}, u32[]{:S(2)}, u32[]{:S(2)}) collective-permute-start(f32[5,80,8,2]{1,2,3,0:T(8,128)S(1)} %copy.14), channel_id=1, source_target_pairs={{0,248},{8,0},{16,8},{24,16},{32,24},{40,32},{48,40},{56,48},{64,5... | collective-permute-start | bytes 76808 | tf_op jit(solution)/shard_map/ppermute | solution.py:152
  24.8 1.2 fusion.64
  25.9 4.2 %collective-permute-start.1 = (f32[5,80,2,128]{3,2,1,0:T(2,128)}, f32[5,80,2,128]{3,2,1,0:T(2,128)}, u32[]{:S(2)}, u32[]{:S(2)}) collective-permute-start(f32[5,80,2,128]{3,2,1,0:T(2,128)} %get-tuple-element.30), channel_id=1, source_target_pairs={{0,1},{1,2},{2,3},{3,4},{4,5},{5,6},{6,7},{8,9},{9,10},{10,11},{11... | collective-permute-start | bytes 1228808 | tf_op jit(solution)/shard_map/ppermute | solution.py:160
  30.1 2.9 %collective-permute-start.6 = (f32[5,80,2,128]{3,2,1,0:T(2,128)}, f32[5,80,2,128]{3,2,1,0:T(2,128)}, u32[]{:S(2)}, u32[]{:S(2)}) collective-permute-start(f32[5,80,2,128]{3,2,1,0:T(2,128)} %get-tuple-element.31), channel_id=1, source_target_pairs={{1,0},{2,1},{3,2},{4,3},{5,4},{6,5},{7,6},{9,8},{10,9},{11,10},{12... | collective-permute-start | bytes 1228808 | tf_op jit(solution)/shard_map/ppermute | solution.py:160
  33.0 0.6 reduce_sum.37
  33.6 0.6 constant_dynamic-update-slice_fusion.6
  34.3 0.0 collective-permute-done
  34.3 5.6 %collective-permute-start.2 = (f32[5,80,2,2]{3,2,1,0:T(2,128)}, f32[5,80,2,2]{3,2,1,0:T(2,128)}, u32[]{:S(2)}, u32[]{:S(2)}) collective-permute-start(f32[5,80,2,2]{3,2,1,0:T(2,128)} %get-tuple-element.29), channel_id=1, source_target_pairs={{0,249},{1,250},{2,251},{3,252},{4,253},{5,254},{6,255},{8,1},{9,2... | collective-permute-start | bytes 19208 | tf_op jit(solution)/shard_map/ppermute | solution.py:161
  39.9 2.4 %collective-permute-start.5 = (f32[5,80,2,2]{3,2,1,0:T(2,128)}, f32[5,80,2,2]{3,2,1,0:T(2,128)}, u32[]{:S(2)}, u32[]{:S(2)}) collective-permute-start(f32[5,80,2,2]{3,2,1,0:T(2,128)} %get-tuple-element.27), channel_id=1, source_target_pairs={{1,8},{2,9},{3,10},{4,11},{5,12},{6,13},{7,14},{9,16},{10,17},{11,... | collective-permute-start | bytes 19208 | tf_op jit(solution)/shard_map/ppermute | solution.py:161
  42.3 0.0 collective-permute-done.4
  42.3 12.0 %collective-permute-start.7 = (f32[5,80,2,2]{3,2,1,0:T(2,128)}, f32[5,80,2,2]{3,2,1,0:T(2,128)}, u32[]{:S(2)}, u32[]{:S(2)}) collective-permute-start(f32[5,80,2,2]{3,2,1,0:T(2,128)} %get-tuple-element.28), channel_id=1, source_target_pairs={{1,248},{2,249},{3,250},{4,251},{5,252},{6,253},{7,254},{9,0},{10,... | collective-permute-start | bytes 19208 | tf_op jit(solution)/shard_map/ppermute | solution.py:161
  54.3 0.1 constant_dynamic-update-slice_fusion.4
  54.4 0.6 copy.15
  55.0 1.7 %copy.16 = f32[5,80,8,2]{3,2,1,0:T(8,128)} copy(f32[5,80,8,2]{1,2,3,0:T(8,128)S(1)} %collective-permute-done.4) | data formatting | bytes 51200 | tf_op jit(solution)/shard_map/ppermute | solution.py:152
  56.8 9.3 %collective-permute-done.5 = f32[5,80,2,2]{3,2,1,0:T(2,128)} collective-permute-done((f32[5,80,2,2]{3,2,1,0:T(2,128)}, f32[5,80,2,2]{3,2,1,0:T(2,128)}, u32[]{:S(2)}, u32[]{:S(2)}) %collective-permute-start.5) | collective-permute-done | bytes 6432 | tf_op jit(solution)/shard_map/ppermute | solution.py:161
  66.1 0.0 collective-permute-done.1
  66.1 0.0 collective-permute-done.6
  66.1 9.5 %maximum_maximum_fusion.pad_ref = f32[5,80,12,132]{3,2,1,0:T(8,128)S(1)} fusion(f32[5,80,2,2]{3,2,1,0:T(2,128)} %collective-permute-done.7, f32[5,80,2,128]{3,2,1,0:T(2,128)} %collective-permute-done.6, f32[5,80,2,2]{3,2,1,0:T(2,128)} %collective-permute-done.5, f32[5,80,8,2]{3,2,1,0:T(8,128)} %copy.16, f32[1,80,8,128]{3,2,1,0:T(8,128)S(1)} %fusion.48, ...), kind=kLoop, calls=%fused_computation | loop fusion | flops 6336000 | bytes 5068800 | tf_op jit(solution)/shard_map/concatenate | solution.py:177
  75.6 2.9 %slice_bitcast_fusion.1 = (f32[80,12,132]{2,1,0:T(8,128)}, f32[80,12,132]{2,1,0:T(8,128)}, f32[80,12,132]{2,1,0:T(8,128)}, f32[80,12,132]{2,1,0:T(8,128)S(1)}, f32[80,12,132]{2,1,0:T(8,128)S(1)}) fusion(f32[5,80,12,132]{3,2,1,0:T(8,128)S(1)} %maximum_maximum_fusion.pad_ref), kind=kLoop, calls=%fused_computation.15 | loop fusion | bytes 5068800 | tf_op jit(solution)/shard_map/squeeze | solution.py:48
  78.5 1.0 copy-done
  79.5 3.6 %fusion.56 = (f32[80,12,132]{2,1,0:T(8,128)}, f32[80,12,132]{2,1,0:T(8,128)}, f32[80,12,132]{2,1,0:T(8,128)}, f32[80,12,132]{2,1,0:T(8,128)}, f32[80,12,132]{2,1...) fusion(f32[5,80,12,132]{3,2,1,0:T(8,128)S(1)} %maximum_maximum_fusion.pad_ref), kind=kLoop, calls=%fused_computation.137 | loop fusion | flops 887040 | bytes 5575680 | tf_op jit(solution)/shard_map/mul | solution.py:49
  83.2 4.4 %shard_map.120 = f32[80,12,132]{2,1,0:T(8,128)} custom-call(f32[80]{0:T(128)} %th_ref.3, f32[5,80,12,132]{3,2,1,0:T(8,128)} %copy-done), custom_call_target="tpu_custom_call" | custom-call | tf_op jit(solution)/shard_map/pallas_call | solution.py:321
  87.6 3.2 %fusion.7 = f32[80,10,130]{2,1,0:T(8,128)S(1)} fusion(f32[80,12,132]{2,1,0:T(8,128)S(1)} %get-tuple-element.17, f32[80,12,132]{2,1,0:T(8,128)} %get-tuple-element.16), kind=kLoop, calls=%fused_computation.25 | loop fusion | flops 624000 | bytes 2912000 | tf_op jit(solution)/shard_map/mul | solution.py:29
  90.9 4.6 %fusion.3 = (f32[80,10,130]{2,1,0:T(8,128)S(1)}, f32[80,10,130]{2,1,0:T(8,128)S(1)}, f32[80,10,130]{2,1,0:T(8,128)S(1)}) fusion(f32[80,12,132]{2,1,0:T(8,128)S(1)} %copy-done.1, f32[80,12,132]{2,1,0:T(8,128)S(1)} %copy-done.3, f32[80,12,132]{2,1,0:T(8,128)S(1)} %get-tuple-element.18, f32[80,12,132]{2,1,0:T(8,128)S(1)} %copy-done.2), kind=kLoop, calls=%fused_computation.11 | loop fusion | flops 1872000 | bytes 7904000 | tf_op jit(solution)/shard_map/mul | solution.py:29
  95.5 1.1 fusion.40
  96.6 0.2 copy-done.13
  96.9 1.1 fusion.29
  98.0 0.2 fusion.8
  98.2 0.1 fusion.66
  98.3 1.5 %collective-permute-start.8 = (f32[8,8,64]{2,1,0:T(8,128)S(1)}, f32[8,8,64]{2,1,0:T(8,128)S(1)}, u32[]{:S(2)}, u32[]{:S(2)}) collective-permute-start(f32[8,8,64]{2,1,0:T(8,128)S(1)} %get-tuple-element.39), channel_id=1, source_target_pairs={{0,8},{8,16},{16,24},{24,32},{32,40},{40,48},{48,56},{56,64},{64,7... | collective-permute-start | bytes 49160 | tf_op jit(solution)/shard_map/ppermute | solution.py:218
  99.8 3.3 %collective-permute-start.9 = (f32[8,8,64]{2,1,0:T(8,128)S(1)}, f32[8,8,64]{2,1,0:T(8,128)S(1)}, u32[]{:S(2)}, u32[]{:S(2)}) collective-permute-start(f32[8,8,64]{2,1,0:T(8,128)S(1)} %get-tuple-element.40), channel_id=1, source_target_pairs={{8,0},{16,8},{24,16},{32,24},{40,32},{48,40},{56,48},{64,56},{72,6... | collective-permute-start | bytes 49160 | tf_op jit(solution)/shard_map/ppermute | solution.py:219
  103.1 0.8 fusion.21
  103.9 0.5 copy-done.9
  104.4 0.4 copy-done.10
  104.8 0.8 fusion.13
  105.7 0.2 copy-done.5
  105.9 1.3 maximum_add_fusion.prov_ref
  107.2 4.0 %shard_map.121 = (f32[2,80,8,128]{3,2,1,0:T(8,128)}, f32[2,80,8,128]{3,2,1,0:T(8,128)}) custom-call(f32[80]{0:T(128)} %th_ref.3, f32[4,80,8,128]{3,2,1,0:T(8,128)} %maximum_add_fusion.prov_ref, f32[80,8,128]{2,1,0:T(8,128)} %mix_ref.1, f32[80,8,128]{2,1,0:T(8,128)} %copy-done.8), custom_call_target="tpu_custom_call" | custom-call | tf_op jit(solution)/shard_map/pallas_call | solution.py:374
  111.1 1.2 multiply_reduce_fusion
  112.3 0.0 collective-permute-done.8
  112.3 0.1 bitcast_dynamic-update-slice_fusion.7
  112.4 2.2 %collective-permute-start.10 = (f32[8,8,256]{2,1,0:T(8,128)S(1)}, f32[8,8,256]{2,1,0:T(8,128)S(1)}, u32[]{:S(2)}, u32[]{:S(2)}) collective-permute-start(f32[8,8,256]{2,1,0:T(8,128)S(1)} %get-tuple-element.13), channel_id=1, source_target_pairs={{0,7},{1,0},{2,1},{3,2},{4,3},{5,4},{6,5},{7,6},{8,15},{9,8},{10,9... | collective-permute-start | bytes 196616 | tf_op jit(solution)/shard_map/ppermute | solution.py:226
  114.6 0.6 broadcast_divide_fusion.dm_ref
  115.2 2.3 %collective-permute-start.11 = (f32[8,8,256]{2,1,0:T(8,128)S(1)}, f32[8,8,256]{2,1,0:T(8,128)S(1)}, u32[]{:S(2)}, u32[]{:S(2)}) collective-permute-start(f32[8,8,256]{2,1,0:T(8,128)S(1)} %get-tuple-element.13), channel_id=1, source_target_pairs={{0,6},{1,7},{2,0},{3,1},{4,2},{5,3},{6,4},{7,5},{8,14},{9,15},{10,... | collective-permute-start | bytes 196616 | tf_op jit(solution)/shard_map/ppermute | solution.py:226
  117.5 9.7 %collective-permute-start.12 = (f32[8,8,256]{2,1,0:T(8,128)S(1)}, f32[8,8,256]{2,1,0:T(8,128)S(1)}, u32[]{:S(2)}, u32[]{:S(2)}) collective-permute-start(f32[8,8,256]{2,1,0:T(8,128)S(1)} %get-tuple-element.13), channel_id=1, source_target_pairs={{0,5},{1,6},{2,7},{3,0},{4,1},{5,2},{6,3},{7,4},{8,13},{9,14},{10,... | collective-permute-start | bytes 196616 | tf_op jit(solution)/shard_map/ppermute | solution.py:226
  127.1 2.6 %collective-permute-start.15 = (f32[8,8,256]{2,1,0:T(8,128)S(1)}, f32[8,8,256]{2,1,0:T(8,128)S(1)}, u32[]{:S(2)}, u32[]{:S(2)}) collective-permute-start(f32[8,8,256]{2,1,0:T(8,128)S(1)} %get-tuple-element.13), channel_id=1, source_target_pairs={{0,2},{1,3},{2,4},{3,5},{4,6},{5,7},{6,0},{7,1},{8,10},{9,11},{10,... | collective-permute-start | bytes 196616 | tf_op jit(solution)/shard_map/ppermute | solution.py:226
  129.8 1.8 %collective-permute-start.16 = (f32[8,8,256]{2,1,0:T(8,128)S(1)}, f32[8,8,256]{2,1,0:T(8,128)S(1)}, u32[]{:S(2)}, u32[]{:S(2)}) collective-permute-start(f32[8,8,256]{2,1,0:T(8,128)S(1)} %get-tuple-element.13), channel_id=1, source_target_pairs={{0,1},{1,2},{2,3},{3,4},{4,5},{5,6},{6,7},{7,0},{8,9},{9,10},{10,1... | collective-permute-start | bytes 196616 | tf_op jit(solution)/shard_map/ppermute | solution.py:226
  131.6 3.4 %collective-permute-done.16 = f32[8,8,256]{2,1,0:T(8,128)S(1)} collective-permute-done((f32[8,8,256]{2,1,0:T(8,128)S(1)}, f32[8,8,256]{2,1,0:T(8,128)S(1)}, u32[]{:S(2)}, u32[]{:S(2)}) %collective-permute-start.16) | collective-permute-done | bytes 65568 | tf_op jit(solution)/shard_map/ppermute | solution.py:226
  135.1 0.8 copy-done.16
  135.9 9.6 %shard_map.122 = (f32[2,80,8,128]{3,2,1,0:T(8,128)}, f32[3,8,128]{2,1,0:T(8,128)}) custom-call(s32[1]{0:T(128)} %bitcast.off_ref, f32[8,8,8,256]{3,2,1,0:T(8,128)} %copy-done.16, f32[2,80,8,128]{3,2,1,0:T(8,128)} %get-tuple-element.8.uv_ref, f32[2,8,128]{2,1,0:T(8,128)} %broadcast_divide_fusion.dm_ref, f32[80,8,128]{2,1,0:T(8,128)} %copy-done.8), custom_call_target="tpu_custom_call" | custom-call | tf_op jit(solution)/shard_map/pallas_call | solution.py:298
  145.4 1.3 slice.356
  146.7 1.3 slice_bitcast_fusion.7
  (67 shorter events, 0.2 us)
Async XLA Ops:
  0.6 3.1 %copy-start.17 = (f32[2,80,8,128]{3,2,1,0:T(8,128)S(1)}, f32[2,80,8,128]{3,2,1,0:T(8,128)}, u32[]{:S(2)}) copy-start(f32[2,80,8,128]{3,2,1,0:T(8,128)} %param.9) | copy-start | bytes 1966084
  3.7 1.3 copy-start.8
  5.0 61.1 %copy-start.4 = (f32[2,80,8,128]{3,2,1,0:T(8,128)}, f32[2,80,8,128]{3,2,1,0:T(8,128)S(1)}, u32[]{:S(2)}) copy-start(f32[2,80,8,128]{3,2,1,0:T(8,128)S(1)} %get-tuple-element.38) | copy-start | bytes 1966084
  7.3 27.1 %collective-permute-start = (f32[5,80,2,2]{3,2,1,0:T(2,128)}, f32[5,80,2,2]{3,2,1,0:T(2,128)}, u32[]{:S(2)}, u32[]{:S(2)}) collective-permute-start(f32[5,80,2,2]{3,2,1,0:T(2,128)} %get-tuple-element.26), channel_id=1, source_target_pairs={{0,9},{1,10},{2,11},{3,12},{4,13},{5,14},{6,15},{8,17},{9,18},{10,... | collective-permute-start | bytes 19208 | tf_op jit(solution)/shard_map/ppermute | solution.py:161
  17.9 22.0 %collective-permute-start.3 = (f32[5,80,8,2]{1,2,3,0:T(8,128)S(1)}, f32[5,80,8,2]{1,2,3,0:T(8,128)S(1)}, u32[]{:S(2)}, u32[]{:S(2)}) collective-permute-start(f32[5,80,8,2]{1,2,3,0:T(8,128)S(1)} %copy.13), channel_id=1, source_target_pairs={{0,8},{8,16},{16,24},{24,32},{32,40},{40,48},{48,56},{56,64},{64,7... | collective-permute-start | bytes 76808 | tf_op jit(solution)/shard_map/ppermute | solution.py:152
  19.2 13.8 %copy-start.19 = (f32[80]{0:T(128)S(1)}, f32[80]{0:T(128)}, u32[]{:S(2)}) copy-start(f32[80]{0:T(128)} %th_ref.3) | copy-start | bytes 964
  19.2 15.1 %copy-start.18 = (s32[8,128]{1,0:T(8,128)S(1)}, s32[8,128]{1,0:T(8,128)}, u32[]{:S(2)}) copy-start(s32[8,128]{1,0:T(8,128)} %param.14) | copy-start | bytes 12292
  19.2 35.1 %copy-start.23 = (f32[8]{0:T(128)S(1)}, f32[8]{0:T(128)}, u32[]{:S(2)}) copy-start(f32[8]{0:T(128)} %param.13) | copy-start | bytes 100
  21.2 21.1 %collective-permute-start.4 = (f32[5,80,8,2]{1,2,3,0:T(8,128)S(1)}, f32[5,80,8,2]{1,2,3,0:T(8,128)S(1)}, u32[]{:S(2)}, u32[]{:S(2)}) collective-permute-start(f32[5,80,8,2]{1,2,3,0:T(8,128)S(1)} %copy.14), channel_id=1, source_target_pairs={{0,248},{8,0},{16,8},{24,16},{32,24},{40,32},{48,40},{56,48},{64,5... | collective-permute-start | bytes 76808 | tf_op jit(solution)/shard_map/ppermute | solution.py:152
  25.9 40.1 %collective-permute-start.1 = (f32[5,80,2,128]{3,2,1,0:T(2,128)}, f32[5,80,2,128]{3,2,1,0:T(2,128)}, u32[]{:S(2)}, u32[]{:S(2)}) collective-permute-start(f32[5,80,2,128]{3,2,1,0:T(2,128)} %get-tuple-element.30), channel_id=1, source_target_pairs={{0,1},{1,2},{2,3},{3,4},{4,5},{5,6},{6,7},{8,9},{9,10},{10,11},{11... | collective-permute-start | bytes 1228808 | tf_op jit(solution)/shard_map/ppermute | solution.py:160
  30.1 36.0 %collective-permute-start.6 = (f32[5,80,2,128]{3,2,1,0:T(2,128)}, f32[5,80,2,128]{3,2,1,0:T(2,128)}, u32[]{:S(2)}, u32[]{:S(2)}) collective-permute-start(f32[5,80,2,128]{3,2,1,0:T(2,128)} %get-tuple-element.31), channel_id=1, source_target_pairs={{1,0},{2,1},{3,2},{4,3},{5,4},{6,5},{7,6},{9,8},{10,9},{11,10},{12... | collective-permute-start | bytes 1228808 | tf_op jit(solution)/shard_map/ppermute | solution.py:160
  34.3 22.5 %collective-permute-start.2 = (f32[5,80,2,2]{3,2,1,0:T(2,128)}, f32[5,80,2,2]{3,2,1,0:T(2,128)}, u32[]{:S(2)}, u32[]{:S(2)}) collective-permute-start(f32[5,80,2,2]{3,2,1,0:T(2,128)} %get-tuple-element.29), channel_id=1, source_target_pairs={{0,249},{1,250},{2,251},{3,252},{4,253},{5,254},{6,255},{8,1},{9,2... | collective-permute-start | bytes 19208 | tf_op jit(solution)/shard_map/ppermute | solution.py:161
  39.9 26.1 %collective-permute-start.5 = (f32[5,80,2,2]{3,2,1,0:T(2,128)}, f32[5,80,2,2]{3,2,1,0:T(2,128)}, u32[]{:S(2)}, u32[]{:S(2)}) collective-permute-start(f32[5,80,2,2]{3,2,1,0:T(2,128)} %get-tuple-element.27), channel_id=1, source_target_pairs={{1,8},{2,9},{3,10},{4,11},{5,12},{6,13},{7,14},{9,16},{10,17},{11,... | collective-permute-start | bytes 19208 | tf_op jit(solution)/shard_map/ppermute | solution.py:161
  42.3 23.7 %collective-permute-start.7 = (f32[5,80,2,2]{3,2,1,0:T(2,128)}, f32[5,80,2,2]{3,2,1,0:T(2,128)}, u32[]{:S(2)}, u32[]{:S(2)}) collective-permute-start(f32[5,80,2,2]{3,2,1,0:T(2,128)} %get-tuple-element.28), channel_id=1, source_target_pairs={{1,248},{2,249},{3,250},{4,251},{5,252},{6,253},{7,254},{9,0},{10,... | collective-permute-start | bytes 19208 | tf_op jit(solution)/shard_map/ppermute | solution.py:161
  75.6 3.9 %copy-start = (f32[5,80,12,132]{3,2,1,0:T(8,128)}, f32[5,80,12,132]{3,2,1,0:T(8,128)S(1)}, u32[]{:S(2)}) copy-start(f32[5,80,12,132]{3,2,1,0:T(8,128)S(1)} %maximum_maximum_fusion.pad_ref) | copy-start | bytes 7603204
  87.6 3.2 %copy-start.1 = (f32[80,12,132]{2,1,0:T(8,128)S(1)}, f32[80,12,132]{2,1,0:T(8,128)}, u32[]{:S(2)}) copy-start(f32[80,12,132]{2,1,0:T(8,128)} %get-tuple-element.14) | copy-start | bytes 1520644
  87.6 3.2 %copy-start.2 = (f32[80,12,132]{2,1,0:T(8,128)S(1)}, f32[80,12,132]{2,1,0:T(8,128)}, u32[]{:S(2)}) copy-start(f32[80,12,132]{2,1,0:T(8,128)} %get-tuple-element.15) | copy-start | bytes 1520644
  87.6 3.2 %copy-start.3 = (f32[80,12,132]{2,1,0:T(8,128)S(1)}, f32[80,12,132]{2,1,0:T(8,128)}, u32[]{:S(2)}) copy-start(f32[80,12,132]{2,1,0:T(8,128)} %get-tuple-element.16) | copy-start | bytes 1520644
  90.8 4.7 %copy-start.6 = (f32[80,12,132]{2,1,0:T(8,128)S(1)}, f32[80,12,132]{2,1,0:T(8,128)}, u32[]{:S(2)}) copy-start(f32[80,12,132]{2,1,0:T(8,128)} %get-tuple-element.21) | copy-start | bytes 1520644
  90.9 4.7 %copy-start.7 = (f32[80,12,132]{2,1,0:T(8,128)S(1)}, f32[80,12,132]{2,1,0:T(8,128)}, u32[]{:S(2)}) copy-start(f32[80,12,132]{2,1,0:T(8,128)} %shard_map.120) | copy-start | bytes 1520644
  90.9 4.7 %copy-start.14 = (f32[80,12,132]{2,1,0:T(8,128)S(1)}, f32[80,12,132]{2,1,0:T(8,128)}, u32[]{:S(2)}) copy-start(f32[80,12,132]{2,1,0:T(8,128)} %get-tuple-element.20) | copy-start | bytes 1520644
  95.5 1.3 copy-start.13
  96.8 1.1 copy-start.20
  96.8 1.3 copy-start.22
  96.9 1.3 copy-start.21
  96.9 6.2 %copy-start.11 = (f32[80,12,132]{2,1,0:T(8,128)S(1)}, f32[80,12,132]{2,1,0:T(8,128)}, u32[]{:S(2)}) copy-start(f32[80,12,132]{2,1,0:T(8,128)} %get-tuple-element.19) | copy-start | bytes 1520644
  96.9 6.2 %copy-start.12 = (f32[80,12,132]{2,1,0:T(8,128)S(1)}, f32[80,12,132]{2,1,0:T(8,128)}, u32[]{:S(2)}) copy-start(f32[80,12,132]{2,1,0:T(8,128)} %get-tuple-element.25) | copy-start | bytes 1520644
  98.3 14.1 %collective-permute-start.8 = (f32[8,8,64]{2,1,0:T(8,128)S(1)}, f32[8,8,64]{2,1,0:T(8,128)S(1)}, u32[]{:S(2)}, u32[]{:S(2)}) collective-permute-start(f32[8,8,64]{2,1,0:T(8,128)S(1)} %get-tuple-element.39), channel_id=1, source_target_pairs={{0,8},{8,16},{16,24},{24,32},{32,40},{40,48},{48,56},{56,64},{64,7... | collective-permute-start | bytes 49160 | tf_op jit(solution)/shard_map/ppermute | solution.py:218
  99.8 12.5 %collective-permute-start.9 = (f32[8,8,64]{2,1,0:T(8,128)S(1)}, f32[8,8,64]{2,1,0:T(8,128)S(1)}, u32[]{:S(2)}, u32[]{:S(2)}) collective-permute-start(f32[8,8,64]{2,1,0:T(8,128)S(1)} %get-tuple-element.40), channel_id=1, source_target_pairs={{8,0},{16,8},{24,16},{32,24},{40,32},{48,40},{56,48},{64,56},{72,6... | collective-permute-start | bytes 49160 | tf_op jit(solution)/shard_map/ppermute | solution.py:219
  103.1 1.3 copy-start.9
  103.1 1.7 %copy-start.10 = (f32[80,12,132]{2,1,0:T(8,128)S(1)}, f32[80,12,132]{2,1,0:T(8,128)}, u32[]{:S(2)}) copy-start(f32[80,12,132]{2,1,0:T(8,128)} %get-tuple-element.24) | copy-start | bytes 1520644
  104.8 1.1 copy-start.5
  107.2 4.0 %copy-start.15 = (f32[80,8,128]{2,1,0:T(8,128)S(1)}, f32[80,8,128]{2,1,0:T(8,128)}, u32[]{:S(2)}) copy-start(f32[80,8,128]{2,1,0:T(8,128)} %get-tuple-element.41) | copy-start | bytes 983044
  112.4 14.7 %collective-permute-start.10 = (f32[8,8,256]{2,1,0:T(8,128)S(1)}, f32[8,8,256]{2,1,0:T(8,128)S(1)}, u32[]{:S(2)}, u32[]{:S(2)}) collective-permute-start(f32[8,8,256]{2,1,0:T(8,128)S(1)} %get-tuple-element.13), channel_id=1, source_target_pairs={{0,7},{1,0},{2,1},{3,2},{4,3},{5,4},{6,5},{7,6},{8,15},{9,8},{10,9... | collective-permute-start | bytes 196616 | tf_op jit(solution)/shard_map/ppermute | solution.py:226
  115.2 14.6 %collective-permute-start.11 = (f32[8,8,256]{2,1,0:T(8,128)S(1)}, f32[8,8,256]{2,1,0:T(8,128)S(1)}, u32[]{:S(2)}, u32[]{:S(2)}) collective-permute-start(f32[8,8,256]{2,1,0:T(8,128)S(1)} %get-tuple-element.13), channel_id=1, source_target_pairs={{0,6},{1,7},{2,0},{3,1},{4,2},{5,3},{6,4},{7,5},{8,14},{9,15},{10,... | collective-permute-start | bytes 196616 | tf_op jit(solution)/shard_map/ppermute | solution.py:226
  117.5 14.1 %collective-permute-start.12 = (f32[8,8,256]{2,1,0:T(8,128)S(1)}, f32[8,8,256]{2,1,0:T(8,128)S(1)}, u32[]{:S(2)}, u32[]{:S(2)}) collective-permute-start(f32[8,8,256]{2,1,0:T(8,128)S(1)} %get-tuple-element.13), channel_id=1, source_target_pairs={{0,5},{1,6},{2,7},{3,0},{4,1},{5,2},{6,3},{7,4},{8,13},{9,14},{10,... | collective-permute-start | bytes 196616 | tf_op jit(solution)/shard_map/ppermute | solution.py:226
  127.1 4.4 %collective-permute-start.13 = (f32[8,8,256]{2,1,0:T(8,128)S(1)}, f32[8,8,256]{2,1,0:T(8,128)S(1)}, u32[]{:S(2)}, u32[]{:S(2)}) collective-permute-start(f32[8,8,256]{2,1,0:T(8,128)S(1)} %get-tuple-element.13), channel_id=1, source_target_pairs={{0,4},{1,5},{2,6},{3,7},{4,0},{5,1},{6,2},{7,3},{8,12},{9,13},{10,... | collective-permute-start | bytes 196616 | tf_op jit(solution)/shard_map/ppermute | solution.py:226
  127.1 4.5 %collective-permute-start.14 = (f32[8,8,256]{2,1,0:T(8,128)S(1)}, f32[8,8,256]{2,1,0:T(8,128)S(1)}, u32[]{:S(2)}, u32[]{:S(2)}) collective-permute-start(f32[8,8,256]{2,1,0:T(8,128)S(1)} %get-tuple-element.13), channel_id=1, source_target_pairs={{0,3},{1,4},{2,5},{3,6},{4,7},{5,0},{6,1},{7,2},{8,11},{9,12},{10,... | collective-permute-start | bytes 196616 | tf_op jit(solution)/shard_map/ppermute | solution.py:226
  127.1 4.5 %collective-permute-start.15 = (f32[8,8,256]{2,1,0:T(8,128)S(1)}, f32[8,8,256]{2,1,0:T(8,128)S(1)}, u32[]{:S(2)}, u32[]{:S(2)}) collective-permute-start(f32[8,8,256]{2,1,0:T(8,128)S(1)} %get-tuple-element.13), channel_id=1, source_target_pairs={{0,2},{1,3},{2,4},{3,5},{4,6},{5,7},{6,0},{7,1},{8,10},{9,11},{10,... | collective-permute-start | bytes 196616 | tf_op jit(solution)/shard_map/ppermute | solution.py:226
  129.8 5.3 %collective-permute-start.16 = (f32[8,8,256]{2,1,0:T(8,128)S(1)}, f32[8,8,256]{2,1,0:T(8,128)S(1)}, u32[]{:S(2)}, u32[]{:S(2)}) collective-permute-start(f32[8,8,256]{2,1,0:T(8,128)S(1)} %get-tuple-element.13), channel_id=1, source_target_pairs={{0,1},{1,2},{2,3},{3,4},{4,5},{5,6},{6,7},{7,0},{8,9},{9,10},{10,1... | collective-permute-start | bytes 196616 | tf_op jit(solution)/shard_map/ppermute | solution.py:226
  135.1 0.8 copy-start.16

commit v9 on v7

--- a/solution.py
+++ b/solution.py
@@ -201,14 +201,13 @@
     whole = gather_baro(fields)
     rows = land.shape[0]
     row_offset = jnp.full((1,), lax.axis_index(("gy", "ga")) * rows, jnp.int32)
-    mine = baro_run(whole, row_offset, land.shape[1])
-    average = mine[3:]
+    new_surface, new_barotropic, average = baro_run(whole, row_offset, land.shape[1])
     solved = solve_columns(provisional, mixing, wet_mask, thickness)
     thick_col = thickness.reshape((levels, 1, 1))
     depth_mean = jnp.sum(thick_col[None] * wet_mask[None] * solved[:2], axis=1) / safe_depth
     new_velocity = (solved[:2] - depth_mean[:, None] + average[:, None]) * wet_mask[None]
     new_tracers = solved[2:]
-    return (new_velocity, new_tracers, mine[0], mine[1:3])
+    return (new_velocity, new_tracers, new_surface, new_barotropic)
 
 
 BARO_HALO = 64
@@ -230,7 +229,7 @@
     return jnp.stack(blocks)
 
 
-def baro_kernel(off_ref, f_ref, o_ref):
+def baro_kernel(off_ref, f_ref, eta_ref, vel_ref, avg_ref):
     parts = f_ref.shape[0]
     block_rows = f_ref.shape[2]
     rows = parts * block_rows
@@ -278,17 +277,22 @@
     carry = (field(5), field(6), field(7), zeros, zeros)
     height, east_vel, north_vel, sum_east, sum_north = lax.fori_loop(0, NSUB, body, carry)
     finals = (height, east_vel, north_vel, sum_east / NSUB, sum_north / NSUB)
-    out_cols = o_ref.shape[2]
+    out_cols = eta_ref.shape[1]
+    targets = [eta_ref, vel_ref.at[0], vel_ref.at[1], avg_ref.at[0], avg_ref.at[1]]
     for index in range(5):
-        o_ref[index] = pltpu.roll(finals[index][:block_rows], cols - BARO_HALO, 1)[:, :out_cols]
+        targets[index][...] = pltpu.roll(finals[index][:block_rows], cols - BARO_HALO, 1)[:, :out_cols]
 
 
 def baro_run(whole, row_offset, out_cols):
     return pl.pallas_call(
         baro_kernel,
-        out_shape=jax.ShapeDtypeStruct((5, whole.shape[2], out_cols), jnp.float32),
+        out_shape=[
+            jax.ShapeDtypeStruct((whole.shape[2], out_cols), jnp.float32),
+            jax.ShapeDtypeStruct((2, whole.shape[2], out_cols), jnp.float32),
+            jax.ShapeDtypeStruct((2, whole.shape[2], out_cols), jnp.float32),
+        ],
         in_specs=[pl.BlockSpec(memory_space=pltpu.SMEM), pl.BlockSpec(memory_space=pltpu.VMEM)],
-        out_specs=pl.BlockSpec(memory_space=pltpu.VMEM),
+        out_specs=[pl.BlockSpec(memory_space=pltpu.VMEM)] * 3,
     )(row_offset, whole)
 
 

time: 146 us -> 146 us (level)
  no operation moved by 1% of the time
where the time goes in v9:
time: 146 us; the launch traced here: 145 us
  starting transfers between devices  54.3 us (37%)
  other arithmetic  38.4 us (26%)
  waiting for transfers between devices  18.1 us (12%)
  Pallas kernels  17.3 us (12%)
  local copies, waits for them, and re-layouts  15.9 us (11%)
    ppermute x4, starting transfers between devices, send(): return lax.ppermute(piece, both, pairs)  26.9 us
    ppermute x4, waiting for transfers between devices, send(): return lax.ppermute(piece, both, pairs)  14.4 us
    ppermute x7, starting transfers between devices, gather_baro(): blocks.append(lax.ppermute(wide, merid, pairs))  11.8 us
    mul x2, other arithmetic, laplace(): return (beside_all - 4.0 * centre) * wet_mask[..., 1:-1, 1:-1]  10.4 us
    concatenate x1, other arithmetic, halo_3d(): return jnp.concatenate([low_band, middle, high_band], axis=-2)  9.53 us
    pallas_call x1, Pallas kernels, baro_run(): pl.pallas_call(baro_kernel, out_shape=[jax.ShapeDtypeStruct((whole.shape[...  8.87 us
    ppermute x1, starting transfers between devices, gather_baro(): high = lax.ppermute(fields[..., :BARO_HALO], 'gx', backward)  7.31 us
    ppermute x2, starting transfers between devices, send(): lax.ppermute(piece, merid, [(s % merid_n, t % merid_n) for s, t in pairs[...  6.76 us
  transfers between devices with their start and end apart: 17, of which 3 were waited for; matrix products, arithmetic and copies ran while one was open for 9% of the time, Pallas kernels for 3%

profile of v9, /device:TPU:1, one launch (start us, length us, event | category | flops | bytes accessed | tf_op | source)
XLA Modules:
  0.0 145.2 jit_solution(9638535855454256617)
XLA Ops:
  0.6 0.8 convert_element_type.4
  1.4 0.7 fusion.48
  2.1 1.6 %broadcast_multiply_fusion.2 = (f32[80,8,128]{2,1,0:T(8,128)}, f32[8,128]{1,0:T(8,128)S(1)}, f32[80,8,128]{2,1,0:T(8,128)S(1)}) fusion(f32[80]{0:T(128)} %th_ref.3, f32[8,128]{1,0:T(8,128)S(1)} %convert_element_type.4, s32[8,128]{1,0:T(8,128)} %param.15), kind=kLoop, calls=%fused_computation.109 | loop fusion | flops 326656 | bytes 667968 | tf_op jit(solution)/shard_map/mul | solution.py:207
  3.7 1.3 broadcast_multiply_fusion.1
  5.0 0.0 copy-start.3
  5.0 0.1 pad_maximum_fusion
  5.1 2.1 %fusion.63 = (f32[5,80,2,2]{3,2,1,0:T(2,128)}, f32[5,80,2,2]{3,2,1,0:T(2,128)}, f32[5,80,2,2]{3,2,1,0:T(2,128)}, f32[5,80,2,2]{3,2,1,0:T(2,128)}) fusion(f32[5,80,8,128]{3,2,1,0:T(8,128)S(1)} %pad_maximum_fusion), kind=kLoop, calls=%fused_computation.144 | loop fusion | bytes 51200 | tf_op jit(solution)/shard_map/slice | solution.py:170
  7.3 13.8 %collective-permute-start.7 = (f32[5,80,2,2]{3,2,1,0:T(2,128)}, f32[5,80,2,2]{3,2,1,0:T(2,128)}, u32[]{:S(2)}, u32[]{:S(2)}) collective-permute-start(f32[5,80,2,2]{3,2,1,0:T(2,128)} %get-tuple-element.26), channel_id=1, source_target_pairs={{1,248},{2,249},{3,250},{4,251},{5,252},{6,253},{7,254},{9,0},{10,... | collective-permute-start | bytes 19208 | tf_op jit(solution)/shard_map/ppermute | solution.py:161
  21.0 1.2 fusion.64
  22.2 2.4 %collective-permute-start.6 = (f32[5,80,2,128]{3,2,1,0:T(2,128)}, f32[5,80,2,128]{3,2,1,0:T(2,128)}, u32[]{:S(2)}, u32[]{:S(2)}) collective-permute-start(f32[5,80,2,128]{3,2,1,0:T(2,128)} %get-tuple-element.29), channel_id=1, source_target_pairs={{1,0},{2,1},{3,2},{4,3},{5,4},{6,5},{7,6},{9,8},{10,9},{11,10},{12... | collective-permute-start | bytes 1228808 | tf_op jit(solution)/shard_map/ppermute | solution.py:160
  24.6 1.7 %fusion.65 = (f32[5,80,8,2]{3,2,1,0:T(8,128)S(1)}, f32[5,80,8,2]{3,2,1,0:T(8,128)}) fusion(f32[5,80,8,128]{3,2,1,0:T(8,128)S(1)} %pad_maximum_fusion), kind=kLoop, calls=%fused_computation.146 | loop fusion | bytes 102400 | tf_op jit(solution)/shard_map/slice | solution.py:166
  26.3 2.0 %copy.14 = f32[5,80,8,2]{1,2,3,0:T(8,128)S(1)} copy(f32[5,80,8,2]{3,2,1,0:T(8,128)} %get-tuple-element.31) | data formatting | bytes 51200 | tf_op jit(solution)/shard_map/slice | solution.py:167
  28.3 0.5 collective-permute-start.4
  28.9 0.5 copy.13
  29.4 1.1 collective-permute-start.3
  30.5 4.4 %collective-permute-start.1 = (f32[5,80,2,128]{3,2,1,0:T(2,128)}, f32[5,80,2,128]{3,2,1,0:T(2,128)}, u32[]{:S(2)}, u32[]{:S(2)}) collective-permute-start(f32[5,80,2,128]{3,2,1,0:T(2,128)} %get-tuple-element.28), channel_id=1, source_target_pairs={{0,1},{1,2},{2,3},{3,4},{4,5},{5,6},{6,7},{8,9},{9,10},{10,11},{11... | collective-permute-start | bytes 1228808 | tf_op jit(solution)/shard_map/ppermute | solution.py:160
  34.8 0.6 reduce_sum.38
  35.4 0.6 constant_dynamic-update-slice_fusion.6
  36.1 0.0 collective-permute-done.7
  36.1 2.4 %collective-permute-start.5 = (f32[5,80,2,2]{3,2,1,0:T(2,128)}, f32[5,80,2,2]{3,2,1,0:T(2,128)}, u32[]{:S(2)}, u32[]{:S(2)}) collective-permute-start(f32[5,80,2,2]{3,2,1,0:T(2,128)} %get-tuple-element.25), channel_id=1, source_target_pairs={{1,8},{2,9},{3,10},{4,11},{5,12},{6,13},{7,14},{9,16},{10,17},{11,... | collective-permute-start | bytes 19208 | tf_op jit(solution)/shard_map/ppermute | solution.py:161
  38.6 0.0 collective-permute-done.4
  38.6 8.6 %collective-permute-start.2 = (f32[5,80,2,2]{3,2,1,0:T(2,128)}, f32[5,80,2,2]{3,2,1,0:T(2,128)}, u32[]{:S(2)}, u32[]{:S(2)}) collective-permute-start(f32[5,80,2,2]{3,2,1,0:T(2,128)} %get-tuple-element.27), channel_id=1, source_target_pairs={{0,249},{1,250},{2,251},{3,252},{4,253},{5,254},{6,255},{8,1},{9,2... | collective-permute-start | bytes 19208 | tf_op jit(solution)/shard_map/ppermute | solution.py:161
  47.2 0.0 collective-permute-done.3
  47.2 2.1 %collective-permute-start = (f32[5,80,2,2]{3,2,1,0:T(2,128)}, f32[5,80,2,2]{3,2,1,0:T(2,128)}, u32[]{:S(2)}, u32[]{:S(2)}) collective-permute-start(f32[5,80,2,2]{3,2,1,0:T(2,128)} %get-tuple-element.24), channel_id=1, source_target_pairs={{0,9},{1,10},{2,11},{3,12},{4,13},{5,14},{6,15},{8,17},{9,18},{10,... | collective-permute-start | bytes 19208 | tf_op jit(solution)/shard_map/ppermute | solution.py:161
  49.3 0.1 constant_dynamic-update-slice_fusion.4
  49.4 0.6 copy.16
  50.0 1.8 %copy.15 = f32[5,80,8,2]{3,2,1,0:T(8,128)} copy(f32[5,80,8,2]{1,2,3,0:T(8,128)S(1)} %collective-permute-done.3) | data formatting | bytes 51200 | tf_op jit(solution)/shard_map/ppermute | solution.py:152
  51.7 8.9 %collective-permute-done.5 = f32[5,80,2,2]{3,2,1,0:T(2,128)} collective-permute-done((f32[5,80,2,2]{3,2,1,0:T(2,128)}, f32[5,80,2,2]{3,2,1,0:T(2,128)}, u32[]{:S(2)}, u32[]{:S(2)}) %collective-permute-start.5) | collective-permute-done | bytes 6432 | tf_op jit(solution)/shard_map/ppermute | solution.py:161
  60.7 5.5 %collective-permute-done = f32[5,80,2,2]{3,2,1,0:T(2,128)} collective-permute-done((f32[5,80,2,2]{3,2,1,0:T(2,128)}, f32[5,80,2,2]{3,2,1,0:T(2,128)}, u32[]{:S(2)}, u32[]{:S(2)}) %collective-permute-start) | collective-permute-done | bytes 6432 | tf_op jit(solution)/shard_map/ppermute | solution.py:161
  66.2 0.0 collective-permute-done.1
  66.2 9.5 %maximum_maximum_fusion.pad_ref = f32[5,80,12,132]{3,2,1,0:T(8,128)S(1)} fusion(f32[5,80,2,2]{3,2,1,0:T(2,128)} %collective-permute-done.7, f32[5,80,2,128]{3,2,1,0:T(2,128)} %collective-permute-done.6, f32[5,80,2,2]{3,2,1,0:T(2,128)} %collective-permute-done.5, f32[5,80,8,2]{3,2,1,0:T(8,128)S(1)} %copy.16, f32[1,80,8,128]{3,2,1,0:T(8,128)S(1)} %fusion.48, ...), kind=kLoop, calls=%fused_computation | loop fusion | flops 6336000 | bytes 5068800 | tf_op jit(solution)/shard_map/concatenate | solution.py:177
  75.7 4.2 %fusion.62 = (f32[80,12,132]{2,1,0:T(8,128)}, f32[80,12,132]{2,1,0:T(8,128)}, f32[80,12,132]{2,1,0:T(8,128)}, f32[80,12,132]{2,1,0:T(8,128)}, f32[80,12,132]{2,1...) fusion(f32[5,80,12,132]{3,2,1,0:T(8,128)S(1)} %maximum_maximum_fusion.pad_ref), kind=kLoop, calls=%fused_computation.143 | loop fusion | flops 887040 | bytes 5575680 | tf_op jit(solution)/shard_map/mul | solution.py:49
  80.0 1.2 copy-done
  81.2 2.3 %slice_bitcast_fusion.3 = (f32[80,12,132]{2,1,0:T(8,128)S(1)}, f32[80,12,132]{2,1,0:T(8,128)}, f32[80,12,132]{2,1,0:T(8,128)}, f32[80,12,132]{2,1,0:T(8,128)}, f32[80,12,132]{2,1,0:T(8,128)S(1)}) fusion(f32[5,80,12,132]{3,2,1,0:T(8,128)S(1)} %maximum_maximum_fusion.pad_ref), kind=kLoop, calls=%fused_computation.29 | loop fusion | bytes 5068800 | tf_op jit(solution)/shard_map/squeeze | solution.py:48
  83.5 4.4 %shard_map.120 = f32[80,12,132]{2,1,0:T(8,128)} custom-call(f32[80]{0:T(128)} %th_ref.3, f32[5,80,12,132]{3,2,1,0:T(8,128)} %copy-done), custom_call_target="tpu_custom_call" | custom-call | tf_op jit(solution)/shard_map/pallas_call | solution.py:311
  87.9 5.8 %fusion.1 = f32[80,10,130]{2,1,0:T(8,128)S(1)} fusion(f32[80,12,132]{2,1,0:T(8,128)} %get-tuple-element.20, f32[80,12,132]{2,1,0:T(8,128)} %get-tuple-element.22), kind=kLoop, calls=%fused_computation.4 | loop fusion | flops 624000 | bytes 2912000 | tf_op jit(solution)/shard_map/mul | solution.py:29
  93.8 4.6 %fusion.7 = (f32[80,10,130]{2,1,0:T(8,128)S(1)}, f32[80,10,130]{2,1,0:T(8,128)S(1)}, f32[80,10,130]{2,1,0:T(8,128)S(1)}) fusion(f32[80,12,132]{2,1,0:T(8,128)S(1)} %get-tuple-element.19, f32[80,12,132]{2,1,0:T(8,128)S(1)} %copy-done.2, f32[80,12,132]{2,1,0:T(8,128)S(1)} %get-tuple-element.23, f32[80,12,132]{2,1,0:T(8,128)S(1)} %copy-done.1), kind=kLoop, calls=%fused_computation.25 | loop fusion | flops 1872000 | bytes 7904000 | tf_op jit(solution)/shard_map/mul | solution.py:29
  98.4 1.1 fusion.40
  99.5 0.2 copy-done.14
  99.8 1.1 fusion.29
  100.9 0.2 fusion.8
  101.1 0.1 fusion.67
  101.2 7.3 %collective-permute-start.9 = (f32[8,8,64]{2,1,0:T(8,128)S(1)}, f32[8,8,64]{2,1,0:T(8,128)S(1)}, u32[]{:S(2)}, u32[]{:S(2)}) collective-permute-start(f32[8,8,64]{2,1,0:T(8,128)S(1)} %get-tuple-element.40), channel_id=1, source_target_pairs={{8,0},{16,8},{24,16},{32,24},{40,32},{48,40},{56,48},{64,56},{72,6... | collective-permute-start | bytes 49160 | tf_op jit(solution)/shard_map/ppermute | solution.py:221
  108.5 0.0 collective-permute-start.8
  108.5 0.8 fusion.13
  109.4 0.5 copy-done.10
  109.8 0.4 copy-done.11
  110.2 0.8 fusion.21
  111.1 0.2 copy-done.4
  111.3 1.3 maximum_add_fusion.prov_ref
  112.6 4.0 %shard_map.121 = f32[4,80,8,128]{3,2,1,0:T(8,128)} custom-call(f32[80]{0:T(128)} %th_ref.3, f32[4,80,8,128]{3,2,1,0:T(8,128)} %maximum_add_fusion.prov_ref, f32[80,8,128]{2,1,0:T(8,128)} %mix_ref.1, f32[80,8,128]{2,1,0:T(8,128)} %copy-done.8), custom_call_target="tpu_custom_call" | custom-call | tf_op jit(solution)/shard_map/pallas_call | solution.py:363
  116.6 1.3 multiply_reduce_fusion
  117.9 0.0 collective-permute-done.9
  117.9 0.1 bitcast_dynamic-update-slice_fusion.7
  118.0 0.1 collective-permute-start.10
  118.1 0.1 collective-permute-start.11
  118.2 6.5 %collective-permute-start.12 = (f32[8,8,256]{2,1,0:T(8,128)S(1)}, f32[8,8,256]{2,1,0:T(8,128)S(1)}, u32[]{:S(2)}, u32[]{:S(2)}) collective-permute-start(f32[8,8,256]{2,1,0:T(8,128)S(1)} %get-tuple-element.11), channel_id=1, source_target_pairs={{0,5},{1,6},{2,7},{3,0},{4,1},{5,2},{6,3},{7,4},{8,13},{9,14},{10,... | collective-permute-start | bytes 196616 | tf_op jit(solution)/shard_map/ppermute | solution.py:228
  124.7 0.1 collective-permute-start.14
  124.8 3.6 %collective-permute-start.15 = (f32[8,8,256]{2,1,0:T(8,128)S(1)}, f32[8,8,256]{2,1,0:T(8,128)S(1)}, u32[]{:S(2)}, u32[]{:S(2)}) collective-permute-start(f32[8,8,256]{2,1,0:T(8,128)S(1)} %get-tuple-element.11), channel_id=1, source_target_pairs={{0,2},{1,3},{2,4},{3,5},{4,6},{5,7},{6,0},{7,1},{8,10},{9,11},{10,... | collective-permute-start | bytes 196616 | tf_op jit(solution)/shard_map/ppermute | solution.py:228
  128.4 1.5 %collective-permute-start.16 = (f32[8,8,256]{2,1,0:T(8,128)S(1)}, f32[8,8,256]{2,1,0:T(8,128)S(1)}, u32[]{:S(2)}, u32[]{:S(2)}) collective-permute-start(f32[8,8,256]{2,1,0:T(8,128)S(1)} %get-tuple-element.11), channel_id=1, source_target_pairs={{0,1},{1,2},{2,3},{3,4},{4,5},{5,6},{6,7},{7,0},{8,9},{9,10},{10,1... | collective-permute-start | bytes 196616 | tf_op jit(solution)/shard_map/ppermute | solution.py:228
  130.0 3.7 %collective-permute-done.16 = f32[8,8,256]{2,1,0:T(8,128)S(1)} collective-permute-done((f32[8,8,256]{2,1,0:T(8,128)S(1)}, f32[8,8,256]{2,1,0:T(8,128)S(1)}, u32[]{:S(2)}, u32[]{:S(2)}) %collective-permute-start.16) | collective-permute-done | bytes 65568 | tf_op jit(solution)/shard_map/ppermute | solution.py:228
  133.7 0.8 copy-done.17
  134.4 8.9 %shard_map.122 = (f32[8,128]{1,0:T(8,128)}, f32[2,8,128]{2,1,0:T(8,128)}, f32[2,8,128]{2,1,0:T(8,128)}) custom-call(s32[1]{0:T(128)} %bitcast.9.off_ref, f32[8,8,8,256]{3,2,1,0:T(8,128)} %copy-done.17), custom_call_target="tpu_custom_call" | custom-call | tf_op jit(solution)/shard_map/pallas_call | solution.py:287
  143.3 1.8 %fusion.66 = (f32[2,80,8,128]{3,2,1,0:T(8,128)}, f32[2,80,8,128]{3,2,1,0:T(8,128)}) fusion(f32[4,80,8,128]{3,2,1,0:T(8,128)S(1)} %copy-done.5, f32[80,8,128]{2,1,0:T(8,128)S(1)} %copy-done.9, f32[2,8,128]{2,1,0:T(8,128)} %get-tuple-element.7, f32[2,8,128]{2,1,0:T(8,128)S(1)} %broadcast_divide_fusion), kind=kLoop, calls=%fused_computation.147 | loop fusion | flops 491520 | bytes 2965504 | tf_op jit(solution)/shard_map/slice | solution.py:209
  (68 shorter events, 0.2 us)
Async XLA Ops:
  0.6 3.1 %copy-start.18 = (f32[2,80,8,128]{3,2,1,0:T(8,128)S(1)}, f32[2,80,8,128]{3,2,1,0:T(8,128)}, u32[]{:S(2)}) copy-start(f32[2,80,8,128]{3,2,1,0:T(8,128)} %param.9) | copy-start | bytes 1966084
  3.7 1.3 copy-start.8
  5.0 61.2 %copy-start.3 = (f32[2,80,8,128]{3,2,1,0:T(8,128)}, f32[2,80,8,128]{3,2,1,0:T(8,128)S(1)}, u32[]{:S(2)}) copy-start(f32[2,80,8,128]{3,2,1,0:T(8,128)S(1)} %get-tuple-element.38) | copy-start | bytes 1966084
  7.3 28.8 %collective-permute-start.7 = (f32[5,80,2,2]{3,2,1,0:T(2,128)}, f32[5,80,2,2]{3,2,1,0:T(2,128)}, u32[]{:S(2)}, u32[]{:S(2)}) collective-permute-start(f32[5,80,2,2]{3,2,1,0:T(2,128)} %get-tuple-element.26), channel_id=1, source_target_pairs={{1,248},{2,249},{3,250},{4,251},{5,252},{6,253},{7,254},{9,0},{10,... | collective-permute-start | bytes 19208 | tf_op jit(solution)/shard_map/ppermute | solution.py:161
  22.2 44.0 %collective-permute-start.6 = (f32[5,80,2,128]{3,2,1,0:T(2,128)}, f32[5,80,2,128]{3,2,1,0:T(2,128)}, u32[]{:S(2)}, u32[]{:S(2)}) collective-permute-start(f32[5,80,2,128]{3,2,1,0:T(2,128)} %get-tuple-element.29), channel_id=1, source_target_pairs={{1,0},{2,1},{3,2},{4,3},{5,4},{6,5},{7,6},{9,8},{10,9},{11,10},{12... | collective-permute-start | bytes 1228808 | tf_op jit(solution)/shard_map/ppermute | solution.py:160
  26.3 8.5 %copy-start.21 = (f32[80]{0:T(128)S(1)}, f32[80]{0:T(128)}, u32[]{:S(2)}) copy-start(f32[80]{0:T(128)} %th_ref.3) | copy-start | bytes 964
  26.3 9.8 %copy-start.19 = (s32[8,128]{1,0:T(8,128)S(1)}, s32[8,128]{1,0:T(8,128)}, u32[]{:S(2)}) copy-start(s32[8,128]{1,0:T(8,128)} %param.14) | copy-start | bytes 12292
  26.3 22.9 %copy-start.24 = (f32[8]{0:T(128)S(1)}, f32[8]{0:T(128)}, u32[]{:S(2)}) copy-start(f32[8]{0:T(128)} %param.13) | copy-start | bytes 100
  28.3 10.2 %collective-permute-start.4 = (f32[5,80,8,2]{1,2,3,0:T(8,128)S(1)}, f32[5,80,8,2]{1,2,3,0:T(8,128)S(1)}, u32[]{:S(2)}, u32[]{:S(2)}) collective-permute-start(f32[5,80,8,2]{1,2,3,0:T(8,128)S(1)} %copy.14), channel_id=1, source_target_pairs={{0,248},{8,0},{16,8},{24,16},{32,24},{40,32},{48,40},{56,48},{64,5... | collective-permute-start | bytes 76808 | tf_op jit(solution)/shard_map/ppermute | solution.py:152
  29.4 17.8 %collective-permute-start.3 = (f32[5,80,8,2]{1,2,3,0:T(8,128)S(1)}, f32[5,80,8,2]{1,2,3,0:T(8,128)S(1)}, u32[]{:S(2)}, u32[]{:S(2)}) collective-permute-start(f32[5,80,8,2]{1,2,3,0:T(8,128)S(1)} %copy.13), channel_id=1, source_target_pairs={{0,8},{8,16},{16,24},{24,32},{32,40},{40,48},{48,56},{56,64},{64,7... | collective-permute-start | bytes 76808 | tf_op jit(solution)/shard_map/ppermute | solution.py:152
  30.5 35.7 %collective-permute-start.1 = (f32[5,80,2,128]{3,2,1,0:T(2,128)}, f32[5,80,2,128]{3,2,1,0:T(2,128)}, u32[]{:S(2)}, u32[]{:S(2)}) collective-permute-start(f32[5,80,2,128]{3,2,1,0:T(2,128)} %get-tuple-element.28), channel_id=1, source_target_pairs={{0,1},{1,2},{2,3},{3,4},{4,5},{5,6},{6,7},{8,9},{9,10},{10,11},{11... | collective-permute-start | bytes 1228808 | tf_op jit(solution)/shard_map/ppermute | solution.py:160
  36.1 24.6 %collective-permute-start.5 = (f32[5,80,2,2]{3,2,1,0:T(2,128)}, f32[5,80,2,2]{3,2,1,0:T(2,128)}, u32[]{:S(2)}, u32[]{:S(2)}) collective-permute-start(f32[5,80,2,2]{3,2,1,0:T(2,128)} %get-tuple-element.25), channel_id=1, source_target_pairs={{1,8},{2,9},{3,10},{4,11},{5,12},{6,13},{7,14},{9,16},{10,17},{11,... | collective-permute-start | bytes 19208 | tf_op jit(solution)/shard_map/ppermute | solution.py:161
  38.6 22.1 %collective-permute-start.2 = (f32[5,80,2,2]{3,2,1,0:T(2,128)}, f32[5,80,2,2]{3,2,1,0:T(2,128)}, u32[]{:S(2)}, u32[]{:S(2)}) collective-permute-start(f32[5,80,2,2]{3,2,1,0:T(2,128)} %get-tuple-element.27), channel_id=1, source_target_pairs={{0,249},{1,250},{2,251},{3,252},{4,253},{5,254},{6,255},{8,1},{9,2... | collective-permute-start | bytes 19208 | tf_op jit(solution)/shard_map/ppermute | solution.py:161
  47.2 19.0 %collective-permute-start = (f32[5,80,2,2]{3,2,1,0:T(2,128)}, f32[5,80,2,2]{3,2,1,0:T(2,128)}, u32[]{:S(2)}, u32[]{:S(2)}) collective-permute-start(f32[5,80,2,2]{3,2,1,0:T(2,128)} %get-tuple-element.24), channel_id=1, source_target_pairs={{0,9},{1,10},{2,11},{3,12},{4,13},{5,14},{6,15},{8,17},{9,18},{10,... | collective-permute-start | bytes 19208 | tf_op jit(solution)/shard_map/ppermute | solution.py:161
  75.7 5.5 %copy-start = (f32[5,80,12,132]{3,2,1,0:T(8,128)}, f32[5,80,12,132]{3,2,1,0:T(8,128)S(1)}, u32[]{:S(2)}) copy-start(f32[5,80,12,132]{3,2,1,0:T(8,128)S(1)} %maximum_maximum_fusion.pad_ref) | copy-start | bytes 7603204
  87.9 5.8 %copy-start.1 = (f32[80,12,132]{2,1,0:T(8,128)S(1)}, f32[80,12,132]{2,1,0:T(8,128)}, u32[]{:S(2)}) copy-start(f32[80,12,132]{2,1,0:T(8,128)} %get-tuple-element.21) | copy-start | bytes 1520644
  87.9 5.8 %copy-start.2 = (f32[80,12,132]{2,1,0:T(8,128)S(1)}, f32[80,12,132]{2,1,0:T(8,128)}, u32[]{:S(2)}) copy-start(f32[80,12,132]{2,1,0:T(8,128)} %get-tuple-element.22) | copy-start | bytes 1520644
  93.7 4.7 %copy-start.6 = (f32[80,12,132]{2,1,0:T(8,128)S(1)}, f32[80,12,132]{2,1,0:T(8,128)}, u32[]{:S(2)}) copy-start(f32[80,12,132]{2,1,0:T(8,128)} %get-tuple-element.13) | copy-start | bytes 1520644
  93.7 4.7 %copy-start.7 = (f32[80,12,132]{2,1,0:T(8,128)S(1)}, f32[80,12,132]{2,1,0:T(8,128)}, u32[]{:S(2)}) copy-start(f32[80,12,132]{2,1,0:T(8,128)} %shard_map.120) | copy-start | bytes 1520644
  93.8 4.7 %copy-start.15 = (f32[80,12,132]{2,1,0:T(8,128)S(1)}, f32[80,12,132]{2,1,0:T(8,128)}, u32[]{:S(2)}) copy-start(f32[80,12,132]{2,1,0:T(8,128)} %get-tuple-element.12) | copy-start | bytes 1520644
  98.4 1.3 copy-start.14
  99.8 1.1 copy-start.22
  99.8 1.3 copy-start.23
  99.8 1.3 copy-start.20
  99.8 8.7 %copy-start.12 = (f32[80,12,132]{2,1,0:T(8,128)S(1)}, f32[80,12,132]{2,1,0:T(8,128)}, u32[]{:S(2)}) copy-start(f32[80,12,132]{2,1,0:T(8,128)} %get-tuple-element.15) | copy-start | bytes 1520644
  99.8 8.7 %copy-start.13 = (f32[80,12,132]{2,1,0:T(8,128)S(1)}, f32[80,12,132]{2,1,0:T(8,128)}, u32[]{:S(2)}) copy-start(f32[80,12,132]{2,1,0:T(8,128)} %get-tuple-element.16) | copy-start | bytes 1520644
  101.2 16.7 %collective-permute-start.9 = (f32[8,8,64]{2,1,0:T(8,128)S(1)}, f32[8,8,64]{2,1,0:T(8,128)S(1)}, u32[]{:S(2)}, u32[]{:S(2)}) collective-permute-start(f32[8,8,64]{2,1,0:T(8,128)S(1)} %get-tuple-element.40), channel_id=1, source_target_pairs={{8,0},{16,8},{24,16},{32,24},{40,32},{48,40},{56,48},{64,56},{72,6... | collective-permute-start | bytes 49160 | tf_op jit(solution)/shard_map/ppermute | solution.py:221
  108.5 9.4 %collective-permute-start.8 = (f32[8,8,64]{2,1,0:T(8,128)S(1)}, f32[8,8,64]{2,1,0:T(8,128)S(1)}, u32[]{:S(2)}, u32[]{:S(2)}) collective-permute-start(f32[8,8,64]{2,1,0:T(8,128)S(1)} %get-tuple-element.39), channel_id=1, source_target_pairs={{0,8},{8,16},{16,24},{24,32},{32,40},{40,48},{48,56},{56,64},{64,7... | collective-permute-start | bytes 49160 | tf_op jit(solution)/shard_map/ppermute | solution.py:220
  108.5 1.3 copy-start.10
  108.5 1.7 %copy-start.11 = (f32[80,12,132]{2,1,0:T(8,128)S(1)}, f32[80,12,132]{2,1,0:T(8,128)}, u32[]{:S(2)}) copy-start(f32[80,12,132]{2,1,0:T(8,128)} %get-tuple-element.18) | copy-start | bytes 1520644
  110.2 1.1 copy-start.4
  112.6 4.0 %copy-start.16 = (f32[80,8,128]{2,1,0:T(8,128)S(1)}, f32[80,8,128]{2,1,0:T(8,128)}, u32[]{:S(2)}) copy-start(f32[80,8,128]{2,1,0:T(8,128)} %get-tuple-element.41) | copy-start | bytes 983044
  116.6 26.7 %copy-start.5 = (f32[4,80,8,128]{3,2,1,0:T(8,128)S(1)}, f32[4,80,8,128]{3,2,1,0:T(8,128)}, u32[]{:S(2)}) copy-start(f32[4,80,8,128]{3,2,1,0:T(8,128)} %shard_map.121) | copy-start | bytes 3932164
  116.6 26.7 %copy-start.9 = (f32[80,8,128]{2,1,0:T(8,128)S(1)}, f32[80,8,128]{2,1,0:T(8,128)}, u32[]{:S(2)}) copy-start(f32[80,8,128]{2,1,0:T(8,128)} %copy-done.8) | copy-start | bytes 983044
  118.0 6.7 %collective-permute-start.10 = (f32[8,8,256]{2,1,0:T(8,128)S(1)}, f32[8,8,256]{2,1,0:T(8,128)S(1)}, u32[]{:S(2)}, u32[]{:S(2)}) collective-permute-start(f32[8,8,256]{2,1,0:T(8,128)S(1)} %get-tuple-element.11), channel_id=1, source_target_pairs={{0,7},{1,0},{2,1},{3,2},{4,3},{5,4},{6,5},{7,6},{8,15},{9,8},{10,9... | collective-permute-start | bytes 196616 | tf_op jit(solution)/shard_map/ppermute | solution.py:228
  118.1 10.2 %collective-permute-start.11 = (f32[8,8,256]{2,1,0:T(8,128)S(1)}, f32[8,8,256]{2,1,0:T(8,128)S(1)}, u32[]{:S(2)}, u32[]{:S(2)}) collective-permute-start(f32[8,8,256]{2,1,0:T(8,128)S(1)} %get-tuple-element.11), channel_id=1, source_target_pairs={{0,6},{1,7},{2,0},{3,1},{4,2},{5,3},{6,4},{7,5},{8,14},{9,15},{10,... | collective-permute-start | bytes 196616 | tf_op jit(solution)/shard_map/ppermute | solution.py:228
  118.2 11.7 %collective-permute-start.12 = (f32[8,8,256]{2,1,0:T(8,128)S(1)}, f32[8,8,256]{2,1,0:T(8,128)S(1)}, u32[]{:S(2)}, u32[]{:S(2)}) collective-permute-start(f32[8,8,256]{2,1,0:T(8,128)S(1)} %get-tuple-element.11), channel_id=1, source_target_pairs={{0,5},{1,6},{2,7},{3,0},{4,1},{5,2},{6,3},{7,4},{8,13},{9,14},{10,... | collective-permute-start | bytes 196616 | tf_op jit(solution)/shard_map/ppermute | solution.py:228
  124.7 5.2 %collective-permute-start.13 = (f32[8,8,256]{2,1,0:T(8,128)S(1)}, f32[8,8,256]{2,1,0:T(8,128)S(1)}, u32[]{:S(2)}, u32[]{:S(2)}) collective-permute-start(f32[8,8,256]{2,1,0:T(8,128)S(1)} %get-tuple-element.11), channel_id=1, source_target_pairs={{0,4},{1,5},{2,6},{3,7},{4,0},{5,1},{6,2},{7,3},{8,12},{9,13},{10,... | collective-permute-start | bytes 196616 | tf_op jit(solution)/shard_map/ppermute | solution.py:228
  124.7 5.3 %collective-permute-start.14 = (f32[8,8,256]{2,1,0:T(8,128)S(1)}, f32[8,8,256]{2,1,0:T(8,128)S(1)}, u32[]{:S(2)}, u32[]{:S(2)}) collective-permute-start(f32[8,8,256]{2,1,0:T(8,128)S(1)} %get-tuple-element.11), channel_id=1, source_target_pairs={{0,3},{1,4},{2,5},{3,6},{4,7},{5,0},{6,1},{7,2},{8,11},{9,12},{10,... | collective-permute-start | bytes 196616 | tf_op jit(solution)/shard_map/ppermute | solution.py:228
  124.8 5.2 %collective-permute-start.15 = (f32[8,8,256]{2,1,0:T(8,128)S(1)}, f32[8,8,256]{2,1,0:T(8,128)S(1)}, u32[]{:S(2)}, u32[]{:S(2)}) collective-permute-start(f32[8,8,256]{2,1,0:T(8,128)S(1)} %get-tuple-element.11), channel_id=1, source_target_pairs={{0,2},{1,3},{2,4},{3,5},{4,6},{5,7},{6,0},{7,1},{8,10},{9,11},{10,... | collective-permute-start | bytes 196616 | tf_op jit(solution)/shard_map/ppermute | solution.py:228
  128.4 5.3 %collective-permute-start.16 = (f32[8,8,256]{2,1,0:T(8,128)S(1)}, f32[8,8,256]{2,1,0:T(8,128)S(1)}, u32[]{:S(2)}, u32[]{:S(2)}) collective-permute-start(f32[8,8,256]{2,1,0:T(8,128)S(1)} %get-tuple-element.11), channel_id=1, source_target_pairs={{0,1},{1,2},{2,3},{3,4},{4,5},{5,6},{6,7},{7,0},{8,9},{9,10},{10,1... | collective-permute-start | bytes 196616 | tf_op jit(solution)/shard_map/ppermute | solution.py:228
  133.6 0.8 copy-start.17

commit v10 on v9

--- a/solution.py
+++ b/solution.py
@@ -275,7 +275,7 @@
 
     zeros = jnp.zeros((rows, cols), jnp.float32)
     carry = (field(5), field(6), field(7), zeros, zeros)
-    height, east_vel, north_vel, sum_east, sum_north = lax.fori_loop(0, NSUB, body, carry)
+    height, east_vel, north_vel, sum_east, sum_north = lax.fori_loop(0, NSUB, body, carry, unroll=2)
     finals = (height, east_vel, north_vel, sum_east / NSUB, sum_north / NSUB)
     out_cols = eta_ref.shape[1]
     targets = [eta_ref, vel_ref.at[0], vel_ref.at[1], avg_ref.at[0], avg_ref.at[1]]

time: 146 us -> 145 us (level)
  no operation moved by 1% of the time
where the time goes in v10:
time: 145 us
  starting transfers between devices  54.3 us (37%)
  other arithmetic  38.4 us (26%)
  waiting for transfers between devices  18.1 us (12%)
  Pallas kernels  16.9 us (12%)
  local copies, waits for them, and re-layouts  15.9 us (11%)
    ppermute x4, starting transfers between devices, send(): return lax.ppermute(piece, both, pairs)  26.9 us
    ppermute x4, waiting for transfers between devices, send(): return lax.ppermute(piece, both, pairs)  14.4 us
    ppermute x7, starting transfers between devices, gather_baro(): blocks.append(lax.ppermute(wide, merid, pairs))  11.8 us
    mul x2, other arithmetic, laplace(): return (beside_all - 4.0 * centre) * wet_mask[..., 1:-1, 1:-1]  10.4 us
    concatenate x1, other arithmetic, halo_3d(): return jnp.concatenate([low_band, middle, high_band], axis=-2)  9.53 us
    pallas_call x1, Pallas kernels, baro_run(): pl.pallas_call(baro_kernel, out_shape=[jax.ShapeDtypeStruct((whole.shape[...  8.51 us
    ppermute x1, starting transfers between devices, gather_baro(): high = lax.ppermute(fields[..., :BARO_HALO], 'gx', backward)  7.31 us
    ppermute x2, starting transfers between devices, send(): lax.ppermute(piece, merid, [(s % merid_n, t % merid_n) for s, t in pairs[...  6.76 us
  transfers between devices with their start and end apart: 17, of which 3 were waited for; matrix products, arithmetic and copies ran while one was open for 9% of the time, Pallas kernels for 3%

profile of v10, /device:TPU:1, one launch (start us, length us, event | category | flops | bytes accessed | tf_op | source)
XLA Modules:
  0.0 144.8 jit_solution(13056811697773929950)
XLA Ops:
  0.6 0.8 convert_element_type.4
  1.4 0.7 fusion.48
  2.1 1.6 %broadcast_multiply_fusion.2 = (f32[80,8,128]{2,1,0:T(8,128)}, f32[8,128]{1,0:T(8,128)S(1)}, f32[80,8,128]{2,1,0:T(8,128)S(1)}) fusion(f32[80]{0:T(128)} %th_ref.3, f32[8,128]{1,0:T(8,128)S(1)} %convert_element_type.4, s32[8,128]{1,0:T(8,128)} %param.15), kind=kLoop, calls=%fused_computation.109 | loop fusion | flops 326656 | bytes 667968 | tf_op jit(solution)/shard_map/mul | solution.py:207
  3.7 1.3 broadcast_multiply_fusion.1
  5.0 0.0 copy-start.3
  5.0 0.1 pad_maximum_fusion
  5.1 2.1 %fusion.63 = (f32[5,80,2,2]{3,2,1,0:T(2,128)}, f32[5,80,2,2]{3,2,1,0:T(2,128)}, f32[5,80,2,2]{3,2,1,0:T(2,128)}, f32[5,80,2,2]{3,2,1,0:T(2,128)}) fusion(f32[5,80,8,128]{3,2,1,0:T(8,128)S(1)} %pad_maximum_fusion), kind=kLoop, calls=%fused_computation.144 | loop fusion | bytes 51200 | tf_op jit(solution)/shard_map/slice | solution.py:170
  7.3 13.8 %collective-permute-start.7 = (f32[5,80,2,2]{3,2,1,0:T(2,128)}, f32[5,80,2,2]{3,2,1,0:T(2,128)}, u32[]{:S(2)}, u32[]{:S(2)}) collective-permute-start(f32[5,80,2,2]{3,2,1,0:T(2,128)} %get-tuple-element.26), channel_id=1, source_target_pairs={{1,248},{2,249},{3,250},{4,251},{5,252},{6,253},{7,254},{9,0},{10,... | collective-permute-start | bytes 19208 | tf_op jit(solution)/shard_map/ppermute | solution.py:161
  21.0 1.2 fusion.64
  22.2 2.4 %collective-permute-start.6 = (f32[5,80,2,128]{3,2,1,0:T(2,128)}, f32[5,80,2,128]{3,2,1,0:T(2,128)}, u32[]{:S(2)}, u32[]{:S(2)}) collective-permute-start(f32[5,80,2,128]{3,2,1,0:T(2,128)} %get-tuple-element.29), channel_id=1, source_target_pairs={{1,0},{2,1},{3,2},{4,3},{5,4},{6,5},{7,6},{9,8},{10,9},{11,10},{12... | collective-permute-start | bytes 1228808 | tf_op jit(solution)/shard_map/ppermute | solution.py:160
  24.6 1.7 %fusion.65 = (f32[5,80,8,2]{3,2,1,0:T(8,128)S(1)}, f32[5,80,8,2]{3,2,1,0:T(8,128)}) fusion(f32[5,80,8,128]{3,2,1,0:T(8,128)S(1)} %pad_maximum_fusion), kind=kLoop, calls=%fused_computation.146 | loop fusion | bytes 102400 | tf_op jit(solution)/shard_map/slice | solution.py:166
  26.3 2.0 %copy.14 = f32[5,80,8,2]{1,2,3,0:T(8,128)S(1)} copy(f32[5,80,8,2]{3,2,1,0:T(8,128)} %get-tuple-element.31) | data formatting | bytes 51200 | tf_op jit(solution)/shard_map/slice | solution.py:167
  28.3 0.5 collective-permute-start.4
  28.9 0.5 copy.13
  29.4 1.1 collective-permute-start.3
  30.5 4.4 %collective-permute-start.1 = (f32[5,80,2,128]{3,2,1,0:T(2,128)}, f32[5,80,2,128]{3,2,1,0:T(2,128)}, u32[]{:S(2)}, u32[]{:S(2)}) collective-permute-start(f32[5,80,2,128]{3,2,1,0:T(2,128)} %get-tuple-element.28), channel_id=1, source_target_pairs={{0,1},{1,2},{2,3},{3,4},{4,5},{5,6},{6,7},{8,9},{9,10},{10,11},{11... | collective-permute-start | bytes 1228808 | tf_op jit(solution)/shard_map/ppermute | solution.py:160
  34.8 0.6 reduce_sum.38
  35.4 0.6 constant_dynamic-update-slice_fusion.6
  36.1 0.0 collective-permute-done.7
  36.1 2.4 %collective-permute-start.5 = (f32[5,80,2,2]{3,2,1,0:T(2,128)}, f32[5,80,2,2]{3,2,1,0:T(2,128)}, u32[]{:S(2)}, u32[]{:S(2)}) collective-permute-start(f32[5,80,2,2]{3,2,1,0:T(2,128)} %get-tuple-element.25), channel_id=1, source_target_pairs={{1,8},{2,9},{3,10},{4,11},{5,12},{6,13},{7,14},{9,16},{10,17},{11,... | collective-permute-start | bytes 19208 | tf_op jit(solution)/shard_map/ppermute | solution.py:161
  38.6 0.0 collective-permute-done.4
  38.6 8.6 %collective-permute-start.2 = (f32[5,80,2,2]{3,2,1,0:T(2,128)}, f32[5,80,2,2]{3,2,1,0:T(2,128)}, u32[]{:S(2)}, u32[]{:S(2)}) collective-permute-start(f32[5,80,2,2]{3,2,1,0:T(2,128)} %get-tuple-element.27), channel_id=1, source_target_pairs={{0,249},{1,250},{2,251},{3,252},{4,253},{5,254},{6,255},{8,1},{9,2... | collective-permute-start | bytes 19208 | tf_op jit(solution)/shard_map/ppermute | solution.py:161
  47.2 0.0 collective-permute-done.3
  47.2 2.1 %collective-permute-start = (f32[5,80,2,2]{3,2,1,0:T(2,128)}, f32[5,80,2,2]{3,2,1,0:T(2,128)}, u32[]{:S(2)}, u32[]{:S(2)}) collective-permute-start(f32[5,80,2,2]{3,2,1,0:T(2,128)} %get-tuple-element.24), channel_id=1, source_target_pairs={{0,9},{1,10},{2,11},{3,12},{4,13},{5,14},{6,15},{8,17},{9,18},{10,... | collective-permute-start | bytes 19208 | tf_op jit(solution)/shard_map/ppermute | solution.py:161
  49.3 0.1 constant_dynamic-update-slice_fusion.4
  49.4 0.6 copy.16
  50.0 1.8 %copy.15 = f32[5,80,8,2]{3,2,1,0:T(8,128)} copy(f32[5,80,8,2]{1,2,3,0:T(8,128)S(1)} %collective-permute-done.3) | data formatting | bytes 51200 | tf_op jit(solution)/shard_map/ppermute | solution.py:152
  51.7 8.9 %collective-permute-done.5 = f32[5,80,2,2]{3,2,1,0:T(2,128)} collective-permute-done((f32[5,80,2,2]{3,2,1,0:T(2,128)}, f32[5,80,2,2]{3,2,1,0:T(2,128)}, u32[]{:S(2)}, u32[]{:S(2)}) %collective-permute-start.5) | collective-permute-done | bytes 6432 | tf_op jit(solution)/shard_map/ppermute | solution.py:161
  60.7 5.5 %collective-permute-done = f32[5,80,2,2]{3,2,1,0:T(2,128)} collective-permute-done((f32[5,80,2,2]{3,2,1,0:T(2,128)}, f32[5,80,2,2]{3,2,1,0:T(2,128)}, u32[]{:S(2)}, u32[]{:S(2)}) %collective-permute-start) | collective-permute-done | bytes 6432 | tf_op jit(solution)/shard_map/ppermute | solution.py:161
  66.2 0.0 collective-permute-done.1
  66.2 9.5 %maximum_maximum_fusion.pad_ref = f32[5,80,12,132]{3,2,1,0:T(8,128)S(1)} fusion(f32[5,80,2,2]{3,2,1,0:T(2,128)} %collective-permute-done.7, f32[5,80,2,128]{3,2,1,0:T(2,128)} %collective-permute-done.6, f32[5,80,2,2]{3,2,1,0:T(2,128)} %collective-permute-done.5, f32[5,80,8,2]{3,2,1,0:T(8,128)S(1)} %copy.16, f32[1,80,8,128]{3,2,1,0:T(8,128)S(1)} %fusion.48, ...), kind=kLoop, calls=%fused_computation | loop fusion | flops 6336000 | bytes 5068800 | tf_op jit(solution)/shard_map/concatenate | solution.py:177
  75.7 4.2 %fusion.62 = (f32[80,12,132]{2,1,0:T(8,128)}, f32[80,12,132]{2,1,0:T(8,128)}, f32[80,12,132]{2,1,0:T(8,128)}, f32[80,12,132]{2,1,0:T(8,128)}, f32[80,12,132]{2,1...) fusion(f32[5,80,12,132]{3,2,1,0:T(8,128)S(1)} %maximum_maximum_fusion.pad_ref), kind=kLoop, calls=%fused_computation.143 | loop fusion | flops 887040 | bytes 5575680 | tf_op jit(solution)/shard_map/mul | solution.py:49
  80.0 1.2 copy-done
  81.2 2.3 %slice_bitcast_fusion.3 = (f32[80,12,132]{2,1,0:T(8,128)S(1)}, f32[80,12,132]{2,1,0:T(8,128)}, f32[80,12,132]{2,1,0:T(8,128)}, f32[80,12,132]{2,1,0:T(8,128)}, f32[80,12,132]{2,1,0:T(8,128)S(1)}) fusion(f32[5,80,12,132]{3,2,1,0:T(8,128)S(1)} %maximum_maximum_fusion.pad_ref), kind=kLoop, calls=%fused_computation.29 | loop fusion | bytes 5068800 | tf_op jit(solution)/shard_map/squeeze | solution.py:48
  83.5 4.4 %shard_map.120 = f32[80,12,132]{2,1,0:T(8,128)} custom-call(f32[80]{0:T(128)} %th_ref.3, f32[5,80,12,132]{3,2,1,0:T(8,128)} %copy-done), custom_call_target="tpu_custom_call" | custom-call | tf_op jit(solution)/shard_map/pallas_call | solution.py:311
  87.9 5.8 %fusion.1 = f32[80,10,130]{2,1,0:T(8,128)S(1)} fusion(f32[80,12,132]{2,1,0:T(8,128)} %get-tuple-element.20, f32[80,12,132]{2,1,0:T(8,128)} %get-tuple-element.22), kind=kLoop, calls=%fused_computation.4 | loop fusion | flops 624000 | bytes 2912000 | tf_op jit(solution)/shard_map/mul | solution.py:29
  93.8 4.6 %fusion.7 = (f32[80,10,130]{2,1,0:T(8,128)S(1)}, f32[80,10,130]{2,1,0:T(8,128)S(1)}, f32[80,10,130]{2,1,0:T(8,128)S(1)}) fusion(f32[80,12,132]{2,1,0:T(8,128)S(1)} %get-tuple-element.19, f32[80,12,132]{2,1,0:T(8,128)S(1)} %copy-done.2, f32[80,12,132]{2,1,0:T(8,128)S(1)} %get-tuple-element.23, f32[80,12,132]{2,1,0:T(8,128)S(1)} %copy-done.1), kind=kLoop, calls=%fused_computation.25 | loop fusion | flops 1872000 | bytes 7904000 | tf_op jit(solution)/shard_map/mul | solution.py:29
  98.4 1.1 fusion.40
  99.5 0.2 copy-done.14
  99.8 1.1 fusion.29
  100.9 0.2 fusion.8
  101.1 0.1 fusion.67
  101.2 7.3 %collective-permute-start.9 = (f32[8,8,64]{2,1,0:T(8,128)S(1)}, f32[8,8,64]{2,1,0:T(8,128)S(1)}, u32[]{:S(2)}, u32[]{:S(2)}) collective-permute-start(f32[8,8,64]{2,1,0:T(8,128)S(1)} %get-tuple-element.40), channel_id=1, source_target_pairs={{8,0},{16,8},{24,16},{32,24},{40,32},{48,40},{56,48},{64,56},{72,6... | collective-permute-start | bytes 49160 | tf_op jit(solution)/shard_map/ppermute | solution.py:221
  108.5 0.0 collective-permute-start.8
  108.5 0.8 fusion.13
  109.4 0.5 copy-done.10
  109.8 0.4 copy-done.11
  110.2 0.8 fusion.21
  111.1 0.2 copy-done.4
  111.3 1.3 maximum_add_fusion.prov_ref
  112.6 4.0 %shard_map.121 = f32[4,80,8,128]{3,2,1,0:T(8,128)} custom-call(f32[80]{0:T(128)} %th_ref.3, f32[4,80,8,128]{3,2,1,0:T(8,128)} %maximum_add_fusion.prov_ref, f32[80,8,128]{2,1,0:T(8,128)} %mix_ref.1, f32[80,8,128]{2,1,0:T(8,128)} %copy-done.8), custom_call_target="tpu_custom_call" | custom-call | tf_op jit(solution)/shard_map/pallas_call | solution.py:363
  116.6 1.3 multiply_reduce_fusion
  117.9 0.0 collective-permute-done.9
  117.9 0.1 bitcast_dynamic-update-slice_fusion.7
  118.0 0.1 collective-permute-start.10
  118.1 0.1 collective-permute-start.11
  118.2 6.5 %collective-permute-start.12 = (f32[8,8,256]{2,1,0:T(8,128)S(1)}, f32[8,8,256]{2,1,0:T(8,128)S(1)}, u32[]{:S(2)}, u32[]{:S(2)}) collective-permute-start(f32[8,8,256]{2,1,0:T(8,128)S(1)} %get-tuple-element.11), channel_id=1, source_target_pairs={{0,5},{1,6},{2,7},{3,0},{4,1},{5,2},{6,3},{7,4},{8,13},{9,14},{10,... | collective-permute-start | bytes 196616 | tf_op jit(solution)/shard_map/ppermute | solution.py:228
  124.7 0.1 collective-permute-start.14
  124.8 3.6 %collective-permute-start.15 = (f32[8,8,256]{2,1,0:T(8,128)S(1)}, f32[8,8,256]{2,1,0:T(8,128)S(1)}, u32[]{:S(2)}, u32[]{:S(2)}) collective-permute-start(f32[8,8,256]{2,1,0:T(8,128)S(1)} %get-tuple-element.11), channel_id=1, source_target_pairs={{0,2},{1,3},{2,4},{3,5},{4,6},{5,7},{6,0},{7,1},{8,10},{9,11},{10,... | collective-permute-start | bytes 196616 | tf_op jit(solution)/shard_map/ppermute | solution.py:228
  128.4 1.5 %collective-permute-start.16 = (f32[8,8,256]{2,1,0:T(8,128)S(1)}, f32[8,8,256]{2,1,0:T(8,128)S(1)}, u32[]{:S(2)}, u32[]{:S(2)}) collective-permute-start(f32[8,8,256]{2,1,0:T(8,128)S(1)} %get-tuple-element.11), channel_id=1, source_target_pairs={{0,1},{1,2},{2,3},{3,4},{4,5},{5,6},{6,7},{7,0},{8,9},{9,10},{10,1... | collective-permute-start | bytes 196616 | tf_op jit(solution)/shard_map/ppermute | solution.py:228
  130.0 3.7 %collective-permute-done.16 = f32[8,8,256]{2,1,0:T(8,128)S(1)} collective-permute-done((f32[8,8,256]{2,1,0:T(8,128)S(1)}, f32[8,8,256]{2,1,0:T(8,128)S(1)}, u32[]{:S(2)}, u32[]{:S(2)}) %collective-permute-start.16) | collective-permute-done | bytes 65568 | tf_op jit(solution)/shard_map/ppermute | solution.py:228
  133.7 0.8 copy-done.17
  134.4 8.5 %shard_map.122 = (f32[8,128]{1,0:T(8,128)}, f32[2,8,128]{2,1,0:T(8,128)}, f32[2,8,128]{2,1,0:T(8,128)}) custom-call(s32[1]{0:T(128)} %bitcast.9.off_ref, f32[8,8,8,256]{3,2,1,0:T(8,128)} %copy-done.17), custom_call_target="tpu_custom_call" | custom-call | tf_op jit(solution)/shard_map/pallas_call | solution.py:287
  143.0 1.8 %fusion.66 = (f32[2,80,8,128]{3,2,1,0:T(8,128)}, f32[2,80,8,128]{3,2,1,0:T(8,128)}) fusion(f32[4,80,8,128]{3,2,1,0:T(8,128)S(1)} %copy-done.5, f32[80,8,128]{2,1,0:T(8,128)S(1)} %copy-done.9, f32[2,8,128]{2,1,0:T(8,128)} %get-tuple-element.7, f32[2,8,128]{2,1,0:T(8,128)S(1)} %broadcast_divide_fusion), kind=kLoop, calls=%fused_computation.147 | loop fusion | flops 491520 | bytes 2965504 | tf_op jit(solution)/shard_map/slice | solution.py:209
  (68 shorter events, 0.2 us)
Async XLA Ops:
  0.6 3.1 %copy-start.18 = (f32[2,80,8,128]{3,2,1,0:T(8,128)S(1)}, f32[2,80,8,128]{3,2,1,0:T(8,128)}, u32[]{:S(2)}) copy-start(f32[2,80,8,128]{3,2,1,0:T(8,128)} %param.9) | copy-start | bytes 1966084
  3.7 1.3 copy-start.8
  5.0 61.2 %copy-start.3 = (f32[2,80,8,128]{3,2,1,0:T(8,128)}, f32[2,80,8,128]{3,2,1,0:T(8,128)S(1)}, u32[]{:S(2)}) copy-start(f32[2,80,8,128]{3,2,1,0:T(8,128)S(1)} %get-tuple-element.38) | copy-start | bytes 1966084
  7.3 28.8 %collective-permute-start.7 = (f32[5,80,2,2]{3,2,1,0:T(2,128)}, f32[5,80,2,2]{3,2,1,0:T(2,128)}, u32[]{:S(2)}, u32[]{:S(2)}) collective-permute-start(f32[5,80,2,2]{3,2,1,0:T(2,128)} %get-tuple-element.26), channel_id=1, source_target_pairs={{1,248},{2,249},{3,250},{4,251},{5,252},{6,253},{7,254},{9,0},{10,... | collective-permute-start | bytes 19208 | tf_op jit(solution)/shard_map/ppermute | solution.py:161
  22.2 44.0 %collective-permute-start.6 = (f32[5,80,2,128]{3,2,1,0:T(2,128)}, f32[5,80,2,128]{3,2,1,0:T(2,128)}, u32[]{:S(2)}, u32[]{:S(2)}) collective-permute-start(f32[5,80,2,128]{3,2,1,0:T(2,128)} %get-tuple-element.29), channel_id=1, source_target_pairs={{1,0},{2,1},{3,2},{4,3},{5,4},{6,5},{7,6},{9,8},{10,9},{11,10},{12... | collective-permute-start | bytes 1228808 | tf_op jit(solution)/shard_map/ppermute | solution.py:160
  26.3 8.5 %copy-start.21 = (f32[80]{0:T(128)S(1)}, f32[80]{0:T(128)}, u32[]{:S(2)}) copy-start(f32[80]{0:T(128)} %th_ref.3) | copy-start | bytes 964
  26.3 9.8 %copy-start.19 = (s32[8,128]{1,0:T(8,128)S(1)}, s32[8,128]{1,0:T(8,128)}, u32[]{:S(2)}) copy-start(s32[8,128]{1,0:T(8,128)} %param.14) | copy-start | bytes 12292
  26.3 22.9 %copy-start.24 = (f32[8]{0:T(128)S(1)}, f32[8]{0:T(128)}, u32[]{:S(2)}) copy-start(f32[8]{0:T(128)} %param.13) | copy-start | bytes 100
  28.3 10.2 %collective-permute-start.4 = (f32[5,80,8,2]{1,2,3,0:T(8,128)S(1)}, f32[5,80,8,2]{1,2,3,0:T(8,128)S(1)}, u32[]{:S(2)}, u32[]{:S(2)}) collective-permute-start(f32[5,80,8,2]{1,2,3,0:T(8,128)S(1)} %copy.14), channel_id=1, source_target_pairs={{0,248},{8,0},{16,8},{24,16},{32,24},{40,32},{48,40},{56,48},{64,5... | collective-permute-start | bytes 76808 | tf_op jit(solution)/shard_map/ppermute | solution.py:152
  29.4 17.8 %collective-permute-start.3 = (f32[5,80,8,2]{1,2,3,0:T(8,128)S(1)}, f32[5,80,8,2]{1,2,3,0:T(8,128)S(1)}, u32[]{:S(2)}, u32[]{:S(2)}) collective-permute-start(f32[5,80,8,2]{1,2,3,0:T(8,128)S(1)} %copy.13), channel_id=1, source_target_pairs={{0,8},{8,16},{16,24},{24,32},{32,40},{40,48},{48,56},{56,64},{64,7... | collective-permute-start | bytes 76808 | tf_op jit(solution)/shard_map/ppermute | solution.py:152
  30.5 35.7 %collective-permute-start.1 = (f32[5,80,2,128]{3,2,1,0:T(2,128)}, f32[5,80,2,128]{3,2,1,0:T(2,128)}, u32[]{:S(2)}, u32[]{:S(2)}) collective-permute-start(f32[5,80,2,128]{3,2,1,0:T(2,128)} %get-tuple-element.28), channel_id=1, source_target_pairs={{0,1},{1,2},{2,3},{3,4},{4,5},{5,6},{6,7},{8,9},{9,10},{10,11},{11... | collective-permute-start | bytes 1228808 | tf_op jit(solution)/shard_map/ppermute | solution.py:160
  36.1 24.6 %collective-permute-start.5 = (f32[5,80,2,2]{3,2,1,0:T(2,128)}, f32[5,80,2,2]{3,2,1,0:T(2,128)}, u32[]{:S(2)}, u32[]{:S(2)}) collective-permute-start(f32[5,80,2,2]{3,2,1,0:T(2,128)} %get-tuple-element.25), channel_id=1, source_target_pairs={{1,8},{2,9},{3,10},{4,11},{5,12},{6,13},{7,14},{9,16},{10,17},{11,... | collective-permute-start | bytes 19208 | tf_op jit(solution)/shard_map/ppermute | solution.py:161
  38.6 22.1 %collective-permute-start.2 = (f32[5,80,2,2]{3,2,1,0:T(2,128)}, f32[5,80,2,2]{3,2,1,0:T(2,128)}, u32[]{:S(2)}, u32[]{:S(2)}) collective-permute-start(f32[5,80,2,2]{3,2,1,0:T(2,128)} %get-tuple-element.27), channel_id=1, source_target_pairs={{0,249},{1,250},{2,251},{3,252},{4,253},{5,254},{6,255},{8,1},{9,2... | collective-permute-start | bytes 19208 | tf_op jit(solution)/shard_map/ppermute | solution.py:161
  47.2 19.0 %collective-permute-start = (f32[5,80,2,2]{3,2,1,0:T(2,128)}, f32[5,80,2,2]{3,2,1,0:T(2,128)}, u32[]{:S(2)}, u32[]{:S(2)}) collective-permute-start(f32[5,80,2,2]{3,2,1,0:T(2,128)} %get-tuple-element.24), channel_id=1, source_target_pairs={{0,9},{1,10},{2,11},{3,12},{4,13},{5,14},{6,15},{8,17},{9,18},{10,... | collective-permute-start | bytes 19208 | tf_op jit(solution)/shard_map/ppermute | solution.py:161
  75.7 5.5 %copy-start = (f32[5,80,12,132]{3,2,1,0:T(8,128)}, f32[5,80,12,132]{3,2,1,0:T(8,128)S(1)}, u32[]{:S(2)}) copy-start(f32[5,80,12,132]{3,2,1,0:T(8,128)S(1)} %maximum_maximum_fusion.pad_ref) | copy-start | bytes 7603204
  87.9 5.8 %copy-start.1 = (f32[80,12,132]{2,1,0:T(8,128)S(1)}, f32[80,12,132]{2,1,0:T(8,128)}, u32[]{:S(2)}) copy-start(f32[80,12,132]{2,1,0:T(8,128)} %get-tuple-element.21) | copy-start | bytes 1520644
  87.9 5.8 %copy-start.2 = (f32[80,12,132]{2,1,0:T(8,128)S(1)}, f32[80,12,132]{2,1,0:T(8,128)}, u32[]{:S(2)}) copy-start(f32[80,12,132]{2,1,0:T(8,128)} %get-tuple-element.22) | copy-start | bytes 1520644
  93.7 4.7 %copy-start.6 = (f32[80,12,132]{2,1,0:T(8,128)S(1)}, f32[80,12,132]{2,1,0:T(8,128)}, u32[]{:S(2)}) copy-start(f32[80,12,132]{2,1,0:T(8,128)} %get-tuple-element.13) | copy-start | bytes 1520644
  93.7 4.7 %copy-start.7 = (f32[80,12,132]{2,1,0:T(8,128)S(1)}, f32[80,12,132]{2,1,0:T(8,128)}, u32[]{:S(2)}) copy-start(f32[80,12,132]{2,1,0:T(8,128)} %shard_map.120) | copy-start | bytes 1520644
  93.8 4.7 %copy-start.15 = (f32[80,12,132]{2,1,0:T(8,128)S(1)}, f32[80,12,132]{2,1,0:T(8,128)}, u32[]{:S(2)}) copy-start(f32[80,12,132]{2,1,0:T(8,128)} %get-tuple-element.12) | copy-start | bytes 1520644
  98.4 1.3 copy-start.14
  99.8 1.1 copy-start.22
  99.8 1.3 copy-start.23
  99.8 1.3 copy-start.20
  99.8 8.7 %copy-start.12 = (f32[80,12,132]{2,1,0:T(8,128)S(1)}, f32[80,12,132]{2,1,0:T(8,128)}, u32[]{:S(2)}) copy-start(f32[80,12,132]{2,1,0:T(8,128)} %get-tuple-element.15) | copy-start | bytes 1520644
  99.8 8.7 %copy-start.13 = (f32[80,12,132]{2,1,0:T(8,128)S(1)}, f32[80,12,132]{2,1,0:T(8,128)}, u32[]{:S(2)}) copy-start(f32[80,12,132]{2,1,0:T(8,128)} %get-tuple-element.16) | copy-start | bytes 1520644
  101.2 16.7 %collective-permute-start.9 = (f32[8,8,64]{2,1,0:T(8,128)S(1)}, f32[8,8,64]{2,1,0:T(8,128)S(1)}, u32[]{:S(2)}, u32[]{:S(2)}) collective-permute-start(f32[8,8,64]{2,1,0:T(8,128)S(1)} %get-tuple-element.40), channel_id=1, source_target_pairs={{8,0},{16,8},{24,16},{32,24},{40,32},{48,40},{56,48},{64,56},{72,6... | collective-permute-start | bytes 49160 | tf_op jit(solution)/shard_map/ppermute | solution.py:221
  108.5 9.4 %collective-permute-start.8 = (f32[8,8,64]{2,1,0:T(8,128)S(1)}, f32[8,8,64]{2,1,0:T(8,128)S(1)}, u32[]{:S(2)}, u32[]{:S(2)}) collective-permute-start(f32[8,8,64]{2,1,0:T(8,128)S(1)} %get-tuple-element.39), channel_id=1, source_target_pairs={{0,8},{8,16},{16,24},{24,32},{32,40},{40,48},{48,56},{56,64},{64,7... | collective-permute-start | bytes 49160 | tf_op jit(solution)/shard_map/ppermute | solution.py:220
  108.5 1.3 copy-start.10
  108.5 1.7 %copy-start.11 = (f32[80,12,132]{2,1,0:T(8,128)S(1)}, f32[80,12,132]{2,1,0:T(8,128)}, u32[]{:S(2)}) copy-start(f32[80,12,132]{2,1,0:T(8,128)} %get-tuple-element.18) | copy-start | bytes 1520644
  110.2 1.1 copy-start.4
  112.6 4.0 %copy-start.16 = (f32[80,8,128]{2,1,0:T(8,128)S(1)}, f32[80,8,128]{2,1,0:T(8,128)}, u32[]{:S(2)}) copy-start(f32[80,8,128]{2,1,0:T(8,128)} %get-tuple-element.41) | copy-start | bytes 983044
  116.6 26.4 %copy-start.5 = (f32[4,80,8,128]{3,2,1,0:T(8,128)S(1)}, f32[4,80,8,128]{3,2,1,0:T(8,128)}, u32[]{:S(2)}) copy-start(f32[4,80,8,128]{3,2,1,0:T(8,128)} %shard_map.121) | copy-start | bytes 3932164
  116.6 26.4 %copy-start.9 = (f32[80,8,128]{2,1,0:T(8,128)S(1)}, f32[80,8,128]{2,1,0:T(8,128)}, u32[]{:S(2)}) copy-start(f32[80,8,128]{2,1,0:T(8,128)} %copy-done.8) | copy-start | bytes 983044
  118.0 6.7 %collective-permute-start.10 = (f32[8,8,256]{2,1,0:T(8,128)S(1)}, f32[8,8,256]{2,1,0:T(8,128)S(1)}, u32[]{:S(2)}, u32[]{:S(2)}) collective-permute-start(f32[8,8,256]{2,1,0:T(8,128)S(1)} %get-tuple-element.11), channel_id=1, source_target_pairs={{0,7},{1,0},{2,1},{3,2},{4,3},{5,4},{6,5},{7,6},{8,15},{9,8},{10,9... | collective-permute-start | bytes 196616 | tf_op jit(solution)/shard_map/ppermute | solution.py:228
  118.1 10.2 %collective-permute-start.11 = (f32[8,8,256]{2,1,0:T(8,128)S(1)}, f32[8,8,256]{2,1,0:T(8,128)S(1)}, u32[]{:S(2)}, u32[]{:S(2)}) collective-permute-start(f32[8,8,256]{2,1,0:T(8,128)S(1)} %get-tuple-element.11), channel_id=1, source_target_pairs={{0,6},{1,7},{2,0},{3,1},{4,2},{5,3},{6,4},{7,5},{8,14},{9,15},{10,... | collective-permute-start | bytes 196616 | tf_op jit(solution)/shard_map/ppermute | solution.py:228
  118.2 11.7 %collective-permute-start.12 = (f32[8,8,256]{2,1,0:T(8,128)S(1)}, f32[8,8,256]{2,1,0:T(8,128)S(1)}, u32[]{:S(2)}, u32[]{:S(2)}) collective-permute-start(f32[8,8,256]{2,1,0:T(8,128)S(1)} %get-tuple-element.11), channel_id=1, source_target_pairs={{0,5},{1,6},{2,7},{3,0},{4,1},{5,2},{6,3},{7,4},{8,13},{9,14},{10,... | collective-permute-start | bytes 196616 | tf_op jit(solution)/shard_map/ppermute | solution.py:228
  124.7 5.2 %collective-permute-start.13 = (f32[8,8,256]{2,1,0:T(8,128)S(1)}, f32[8,8,256]{2,1,0:T(8,128)S(1)}, u32[]{:S(2)}, u32[]{:S(2)}) collective-permute-start(f32[8,8,256]{2,1,0:T(8,128)S(1)} %get-tuple-element.11), channel_id=1, source_target_pairs={{0,4},{1,5},{2,6},{3,7},{4,0},{5,1},{6,2},{7,3},{8,12},{9,13},{10,... | collective-permute-start | bytes 196616 | tf_op jit(solution)/shard_map/ppermute | solution.py:228
  124.7 5.3 %collective-permute-start.14 = (f32[8,8,256]{2,1,0:T(8,128)S(1)}, f32[8,8,256]{2,1,0:T(8,128)S(1)}, u32[]{:S(2)}, u32[]{:S(2)}) collective-permute-start(f32[8,8,256]{2,1,0:T(8,128)S(1)} %get-tuple-element.11), channel_id=1, source_target_pairs={{0,3},{1,4},{2,5},{3,6},{4,7},{5,0},{6,1},{7,2},{8,11},{9,12},{10,... | collective-permute-start | bytes 196616 | tf_op jit(solution)/shard_map/ppermute | solution.py:228
  124.8 5.2 %collective-permute-start.15 = (f32[8,8,256]{2,1,0:T(8,128)S(1)}, f32[8,8,256]{2,1,0:T(8,128)S(1)}, u32[]{:S(2)}, u32[]{:S(2)}) collective-permute-start(f32[8,8,256]{2,1,0:T(8,128)S(1)} %get-tuple-element.11), channel_id=1, source_target_pairs={{0,2},{1,3},{2,4},{3,5},{4,6},{5,7},{6,0},{7,1},{8,10},{9,11},{10,... | collective-permute-start | bytes 196616 | tf_op jit(solution)/shard_map/ppermute | solution.py:228
  128.4 5.3 %collective-permute-start.16 = (f32[8,8,256]{2,1,0:T(8,128)S(1)}, f32[8,8,256]{2,1,0:T(8,128)S(1)}, u32[]{:S(2)}, u32[]{:S(2)}) collective-permute-start(f32[8,8,256]{2,1,0:T(8,128)S(1)} %get-tuple-element.11), channel_id=1, source_target_pairs={{0,1},{1,2},{2,3},{3,4},{4,5},{5,6},{6,7},{7,0},{8,9},{9,10},{10,1... | collective-permute-start | bytes 196616 | tf_op jit(solution)/shard_map/ppermute | solution.py:228
  133.6 0.8 copy-start.17

commit v11 on v10

--- a/solution.py
+++ b/solution.py
@@ -55,7 +55,7 @@
         else:
             change = -diff_four * smooth
         changes.append((change - advect) * inner_wet)
-    return jnp.stack(changes)
+    return changes
 
 
 def vertical_solve(provisional, mixing, wet_mask, thickness):
@@ -189,8 +189,7 @@
     depth_col = thickness.reshape((levels, 1, 1))
     pressure = pressure_run(thickness, padded)
     growth = tendency(padded, pressure, coriolis)
-    provisional = stacked[:4] + step_main * growth
-    forcing = jnp.sum(depth_col * growth[:2], axis=1)
+    forcing = jnp.sum(depth_col * jnp.stack(growth[:2]), axis=1)
     depth_sum = jnp.sum(depth_col * wet_mask, axis=0)
     safe_depth = jnp.maximum(depth_sum, 1.0)
     dr = depth_sum / jnp.sum(thickness)
@@ -202,7 +201,7 @@
     rows = land.shape[0]
     row_offset = jnp.full((1,), lax.axis_index(("gy", "ga")) * rows, jnp.int32)
     new_surface, new_barotropic, average = baro_run(whole, row_offset, land.shape[1])
-    solved = solve_columns(provisional, mixing, wet_mask, thickness)
+    solved = solve_columns(velocity, tracers, growth, mixing, wet_mask, thickness)
     thick_col = thickness.reshape((levels, 1, 1))
     depth_mean = jnp.sum(thick_col[None] * wet_mask[None] * solved[:2], axis=1) / safe_depth
     new_velocity = (solved[:2] - depth_mean[:, None] + average[:, None]) * wet_mask[None]
@@ -316,10 +315,12 @@
     )(thickness, padded)
 
 
-def solve_kernel(th_ref, prov_ref, mix_ref, wet_ref, o_ref, ratio_ref):
+def solve_kernel(th_ref, vel_ref, tra_ref, g0_ref, g1_ref, g2_ref, g3_ref, mix_ref, wet_ref, o_ref, ratio_ref):
     levels = mix_ref.shape[0]
     shape = mix_ref.shape[1:]
-    comps = prov_ref.shape[0]
+    comps = o_ref.shape[0]
+    fields = [vel_ref.at[0], vel_ref.at[1], tra_ref.at[0], tra_ref.at[1]]
+    grows = [g0_ref, g1_ref, g2_ref, g3_ref]
 
     def below_of(k):
         nxt = jnp.minimum(k + 1, levels - 1)
@@ -338,7 +339,8 @@
         ratio_ref[k] = ratio
         values = []
         for c in range(comps):
-            value = (depth * prov_ref[c, k] + upper * value_prev[c]) * inverse
+            provisional = fields[c][k] * wet_ref[k] + step_main * grows[c][k]
+            value = (depth * provisional + upper * value_prev[c]) * inverse
             o_ref[c, k] = value
             values.append(value)
         return (below, ratio, tuple(values))
@@ -359,15 +361,15 @@
     lax.fori_loop(0, levels, backward, (zeros,) * comps, unroll=4)
 
 
-def solve_columns(provisional, mixing, wet_mask, thickness):
+def solve_columns(velocity, tracers, growth, mixing, wet_mask, thickness):
     return pl.pallas_call(
         solve_kernel,
-        out_shape=jax.ShapeDtypeStruct(provisional.shape, jnp.float32),
+        out_shape=jax.ShapeDtypeStruct((4,) + mixing.shape, jnp.float32),
         in_specs=[pl.BlockSpec(memory_space=pltpu.SMEM)]
-        + [pl.BlockSpec(memory_space=pltpu.VMEM)] * 3,
+        + [pl.BlockSpec(memory_space=pltpu.VMEM)] * 8,
         out_specs=pl.BlockSpec(memory_space=pltpu.VMEM),
         scratch_shapes=[pltpu.VMEM(mixing.shape, jnp.float32)],
-    )(thickness, provisional, mixing, wet_mask)
+    )(thickness, velocity, tracers, growth[0], growth[1], growth[2], growth[3], mixing, wet_mask)
 
 
 def solution(mesh):

time: 145 us -> 146 us (level)
  starting transfers between devices: 54.3 us -> 62.4 us
  waiting for transfers between devices: 18.1 us -> 14.1 us
  other arithmetic: 38.4 us -> 35.7 us
    ppermute x7, starting transfers between devices: 11.8 us -> 19.3 us  [gather_baro(): blocks.append(lax.ppermute(wide, merid, pairs))]
    mul x0 -> x4, other arithmetic: none -> 5.38 us  [tendency(): changes.append((change - advect) * inner_wet)]
    ppermute x4, waiting for transfers between devices: 14.4 us -> 10.4 us  [send(): return lax.ppermute(piece, both, pairs)]
    ppermute x1, starting transfers between devices: 7.31 us -> 3.35 us  [gather_baro(): high = lax.ppermute(fields[..., :BARO_HALO], 'gx', backward)]
    another operation x4 -> x0, other arithmetic: 3.85 us -> none  [tendency(): return jnp.stack(changes)]
    ppermute x2, starting transfers between devices: 1.56 us -> 4.88 us  [send(): return lax.ppermute(piece, zonal, pairs)]
    mul x2, other arithmetic: 10.4 us -> 7.84 us  [laplace(): return (beside_all - 4.0 * centre) * wet_mask[..., 1:-1, 1:-1]]
    unnamed x58 -> x66, local copies, waits for them, and re-layouts: 3.51 us -> 3.33 us
  transfers between devices with their start and end apart: 17 -> 17, of which waited for: 3 -> 2; matrix products, arithmetic and copies ran while one was open for 9% -> 9% of each run, Pallas kernels for 3% -> 3%
where the time goes in v11:
time: 146 us
  starting transfers between devices  62.4 us (43%)
  other arithmetic  35.7 us (24%)
  Pallas kernels  17.3 us (12%)
  local copies, waits for them, and re-layouts  15.1 us (10%)
  waiting for transfers between devices  14.1 us (10%)
    ppermute x4, starting transfers between devices, send(): return lax.ppermute(piece, both, pairs)  26.4 us
    ppermute x7, starting transfers between devices, gather_baro(): blocks.append(lax.ppermute(wide, merid, pairs))  19.3 us
    ppermute x4, waiting for transfers between devices, send(): return lax.ppermute(piece, both, pairs)  10.4 us
    concatenate x1, other arithmetic, halo_3d(): return jnp.concatenate([low_band, middle, high_band], axis=-2)  9.57 us
    pallas_call x1, Pallas kernels, baro_run(): pl.pallas_call(baro_kernel, out_shape=[jax.ShapeDtypeStruct((whole.shape[...  8.5 us
    mul x2, other arithmetic, laplace(): return (beside_all - 4.0 * centre) * wet_mask[..., 1:-1, 1:-1]  7.84 us
    ppermute x2, starting transfers between devices, send(): lax.ppermute(piece, merid, [(s % merid_n, t % merid_n) for s, t in pairs[...  7.06 us
    mul x4, other arithmetic, tendency(): changes.append((change - advect) * inner_wet)  5.38 us
  transfers between devices with their start and end apart: 17, of which 2 were waited for; matrix products, arithmetic and copies ran while one was open for 9% of the time, Pallas kernels for 3%

profile of v11, /device:TPU:1, one launch (start us, length us, event | category | flops | bytes accessed | tf_op | source)
XLA Modules:
  0.0 145.8 jit_solution(13197382815912343607)
XLA Ops:
  0.6 0.0 copy-start.20
  0.6 0.8 convert_element_type.4
  1.4 0.7 fusion.44
  2.1 1.7 %broadcast_multiply_fusion.2 = (f32[80,8,128]{2,1,0:T(8,128)}, f32[8,128]{1,0:T(8,128)S(1)}, f32[80,8,128]{2,1,0:T(8,128)S(1)}) fusion(f32[80]{0:T(128)} %th_ref.3, f32[8,128]{1,0:T(8,128)S(1)} %convert_element_type.4, s32[8,128]{1,0:T(8,128)} %param.15), kind=kLoop, calls=%fused_computation.103 | loop fusion | flops 326656 | bytes 667968 | tf_op jit(solution)/shard_map/mul | solution.py:206
  3.8 1.3 broadcast_multiply_fusion.1
  5.1 0.0 copy-start.5
  5.1 0.0 copy-start.6
  5.1 0.8 copy-done.5
  5.9 0.2 copy-done.6
  6.2 0.1 pad_maximum_fusion
  6.3 2.1 %fusion.59 = (f32[5,80,2,2]{3,2,1,0:T(2,128)}, f32[5,80,2,2]{3,2,1,0:T(2,128)}, f32[5,80,2,2]{3,2,1,0:T(2,128)}, f32[5,80,2,2]{3,2,1,0:T(2,128)}) fusion(f32[5,80,8,128]{3,2,1,0:T(8,128)S(1)} %pad_maximum_fusion), kind=kLoop, calls=%fused_computation.138 | loop fusion | bytes 51200 | tf_op jit(solution)/shard_map/slice | solution.py:170
  8.4 6.5 %collective-permute-start = (f32[5,80,2,2]{3,2,1,0:T(2,128)}, f32[5,80,2,2]{3,2,1,0:T(2,128)}, u32[]{:S(2)}, u32[]{:S(2)}) collective-permute-start(f32[5,80,2,2]{3,2,1,0:T(2,128)} %get-tuple-element.24), channel_id=1, source_target_pairs={{0,9},{1,10},{2,11},{3,12},{4,13},{5,14},{6,15},{8,17},{9,18},{10,... | collective-permute-start | bytes 19208 | tf_op jit(solution)/shard_map/ppermute | solution.py:161
  14.9 1.7 %fusion.61 = (f32[5,80,8,2]{3,2,1,0:T(8,128)}, f32[5,80,8,2]{3,2,1,0:T(8,128)S(1)}) fusion(f32[5,80,8,128]{3,2,1,0:T(8,128)S(1)} %pad_maximum_fusion), kind=kLoop, calls=%fused_computation.140 | loop fusion | bytes 102400 | tf_op jit(solution)/shard_map/slice | solution.py:166
  16.6 2.0 %copy.13 = f32[5,80,8,2]{1,2,3,0:T(8,128)S(1)} copy(f32[5,80,8,2]{3,2,1,0:T(8,128)} %get-tuple-element.30) | data formatting | bytes 51200 | tf_op jit(solution)/shard_map/slice | solution.py:166
  18.6 1.3 collective-permute-start.3
  19.9 0.5 copy.14
  20.5 3.5 %collective-permute-start.4 = (f32[5,80,8,2]{1,2,3,0:T(8,128)S(1)}, f32[5,80,8,2]{1,2,3,0:T(8,128)S(1)}, u32[]{:S(2)}, u32[]{:S(2)}) collective-permute-start(f32[5,80,8,2]{1,2,3,0:T(8,128)S(1)} %copy.14), channel_id=1, source_target_pairs={{0,248},{8,0},{16,8},{24,16},{32,24},{40,32},{48,40},{56,48},{64,5... | collective-permute-start | bytes 76808 | tf_op jit(solution)/shard_map/ppermute | solution.py:152
  24.0 1.1 fusion.60
  25.1 4.2 %collective-permute-start.1 = (f32[5,80,2,128]{3,2,1,0:T(2,128)}, f32[5,80,2,128]{3,2,1,0:T(2,128)}, u32[]{:S(2)}, u32[]{:S(2)}) collective-permute-start(f32[5,80,2,128]{3,2,1,0:T(2,128)} %get-tuple-element.28), channel_id=1, source_target_pairs={{0,1},{1,2},{2,3},{3,4},{4,5},{5,6},{6,7},{8,9},{9,10},{10,11},{11... | collective-permute-start | bytes 1228808 | tf_op jit(solution)/shard_map/ppermute | solution.py:160
  29.3 2.9 %collective-permute-start.6 = (f32[5,80,2,128]{3,2,1,0:T(2,128)}, f32[5,80,2,128]{3,2,1,0:T(2,128)}, u32[]{:S(2)}, u32[]{:S(2)}) collective-permute-start(f32[5,80,2,128]{3,2,1,0:T(2,128)} %get-tuple-element.29), channel_id=1, source_target_pairs={{1,0},{2,1},{3,2},{4,3},{5,4},{6,5},{7,6},{9,8},{10,9},{11,10},{12... | collective-permute-start | bytes 1228808 | tf_op jit(solution)/shard_map/ppermute | solution.py:160
  32.2 0.6 reduce_sum.38
  32.8 0.6 constant_dynamic-update-slice_fusion.6
  33.5 5.6 %collective-permute-start.2 = (f32[5,80,2,2]{3,2,1,0:T(2,128)}, f32[5,80,2,2]{3,2,1,0:T(2,128)}, u32[]{:S(2)}, u32[]{:S(2)}) collective-permute-start(f32[5,80,2,2]{3,2,1,0:T(2,128)} %get-tuple-element.27), channel_id=1, source_target_pairs={{0,249},{1,250},{2,251},{3,252},{4,253},{5,254},{6,255},{8,1},{9,2... | collective-permute-start | bytes 19208 | tf_op jit(solution)/shard_map/ppermute | solution.py:161
  39.2 2.4 %collective-permute-start.5 = (f32[5,80,2,2]{3,2,1,0:T(2,128)}, f32[5,80,2,2]{3,2,1,0:T(2,128)}, u32[]{:S(2)}, u32[]{:S(2)}) collective-permute-start(f32[5,80,2,2]{3,2,1,0:T(2,128)} %get-tuple-element.25), channel_id=1, source_target_pairs={{1,8},{2,9},{3,10},{4,11},{5,12},{6,13},{7,14},{9,16},{10,17},{11,... | collective-permute-start | bytes 19208 | tf_op jit(solution)/shard_map/ppermute | solution.py:161
  41.5 0.0 collective-permute-done.4
  41.5 12.0 %collective-permute-start.7 = (f32[5,80,2,2]{3,2,1,0:T(2,128)}, f32[5,80,2,2]{3,2,1,0:T(2,128)}, u32[]{:S(2)}, u32[]{:S(2)}) collective-permute-start(f32[5,80,2,2]{3,2,1,0:T(2,128)} %get-tuple-element.26), channel_id=1, source_target_pairs={{1,248},{2,249},{3,250},{4,251},{5,252},{6,253},{7,254},{9,0},{10,... | collective-permute-start | bytes 19208 | tf_op jit(solution)/shard_map/ppermute | solution.py:161
  53.5 0.1 constant_dynamic-update-slice_fusion.4
  53.6 0.6 copy.15
  54.2 0.6 copy.16
  54.9 0.0 collective-permute-done.2
  54.9 10.4 %collective-permute-done.5 = f32[5,80,2,2]{3,2,1,0:T(2,128)} collective-permute-done((f32[5,80,2,2]{3,2,1,0:T(2,128)}, f32[5,80,2,2]{3,2,1,0:T(2,128)}, u32[]{:S(2)}, u32[]{:S(2)}) %collective-permute-start.5) | collective-permute-done | bytes 6432 | tf_op jit(solution)/shard_map/ppermute | solution.py:161
  65.3 0.0 collective-permute-done.7
  65.3 9.6 %maximum_maximum_fusion.pad_ref = f32[5,80,12,132]{3,2,1,0:T(8,128)S(1)} fusion(f32[5,80,2,2]{3,2,1,0:T(2,128)} %collective-permute-done.7, f32[5,80,2,128]{3,2,1,0:T(2,128)} %collective-permute-done.6, f32[5,80,2,2]{3,2,1,0:T(2,128)} %collective-permute-done.5, f32[5,80,8,2]{3,2,1,0:T(8,128)S(1)} %copy.16, f32[1,80,8,128]{3,2,1,0:T(8,128)} %copy-done.19, ...), kind=kLoop, calls=%fused_computation | loop fusion | flops 6336000 | bytes 5068800 | tf_op jit(solution)/shard_map/concatenate | solution.py:177
  74.9 2.9 %slice_bitcast_fusion = (f32[80,12,132]{2,1,0:T(8,128)}, f32[80,12,132]{2,1,0:T(8,128)}, f32[80,12,132]{2,1,0:T(8,128)}, f32[80,12,132]{2,1,0:T(8,128)S(1)}, f32[80,12,132]{2,1,0:T(8,128)S(1)}) fusion(f32[5,80,12,132]{3,2,1,0:T(8,128)S(1)} %maximum_maximum_fusion.pad_ref), kind=kLoop, calls=%fused_computation.8 | loop fusion | bytes 5068800 | tf_op jit(solution)/shard_map/squeeze | solution.py:48
  77.8 1.0 copy-done
  78.8 3.7 %fusion.54 = (f32[80,12,132]{2,1,0:T(8,128)}, f32[80,12,132]{2,1,0:T(8,128)}, f32[80,12,132]{2,1,0:T(8,128)}, f32[80,12,132]{2,1,0:T(8,128)}, f32[80,12,132]{2,1...) fusion(f32[5,80,12,132]{3,2,1,0:T(8,128)S(1)} %maximum_maximum_fusion.pad_ref), kind=kLoop, calls=%fused_computation.133 | loop fusion | flops 887040 | bytes 5575680 | tf_op jit(solution)/shard_map/mul | solution.py:49
  82.5 4.4 %shard_map.120 = f32[80,12,132]{2,1,0:T(8,128)} custom-call(f32[80]{0:T(128)} %th_ref.3, f32[5,80,12,132]{3,2,1,0:T(8,128)} %copy-done), custom_call_target="tpu_custom_call" | custom-call | tf_op jit(solution)/shard_map/pallas_call | solution.py:310
  86.9 3.2 %fusion.7 = f32[80,10,130]{2,1,0:T(8,128)S(1)} fusion(f32[80,12,132]{2,1,0:T(8,128)S(1)} %get-tuple-element.15, f32[80,12,132]{2,1,0:T(8,128)} %get-tuple-element.14), kind=kLoop, calls=%fused_computation.25 | loop fusion | flops 624000 | bytes 2912000 | tf_op jit(solution)/shard_map/mul | solution.py:29
  90.2 4.6 %fusion.1 = (f32[80,10,130]{2,1,0:T(8,128)S(1)}, f32[80,10,130]{2,1,0:T(8,128)S(1)}, f32[80,10,130]{2,1,0:T(8,128)S(1)}) fusion(f32[80,12,132]{2,1,0:T(8,128)S(1)} %copy-done.1, f32[80,12,132]{2,1,0:T(8,128)S(1)} %copy-done.3, f32[80,12,132]{2,1,0:T(8,128)S(1)} %get-tuple-element.16, f32[80,12,132]{2,1,0:T(8,128)S(1)} %copy-done.2), kind=kLoop, calls=%fused_computation.4 | loop fusion | flops 1872000 | bytes 7904000 | tf_op jit(solution)/shard_map/mul | solution.py:29
  94.9 1.1 fusion.36.g0_ref
  96.0 0.0 copy-start.11
  96.0 0.2 copy-done.17
  96.2 1.1 fusion.26.g1_ref
  97.3 0.0 copy-start.12
  97.3 0.2 fusion.8
  97.6 0.1 fusion.63
  97.7 1.5 %collective-permute-start.8 = (f32[8,8,64]{2,1,0:T(8,128)S(1)}, f32[8,8,64]{2,1,0:T(8,128)S(1)}, u32[]{:S(2)}, u32[]{:S(2)}) collective-permute-start(f32[8,8,64]{2,1,0:T(8,128)S(1)} %get-tuple-element.39), channel_id=1, source_target_pairs={{0,8},{8,16},{16,24},{24,32},{32,40},{40,48},{48,56},{56,64},{64,7... | collective-permute-start | bytes 49160 | tf_op jit(solution)/shard_map/ppermute | solution.py:219
  99.1 3.3 %collective-permute-start.9 = (f32[8,8,64]{2,1,0:T(8,128)S(1)}, f32[8,8,64]{2,1,0:T(8,128)S(1)}, u32[]{:S(2)}, u32[]{:S(2)}) collective-permute-start(f32[8,8,64]{2,1,0:T(8,128)S(1)} %get-tuple-element.40), channel_id=1, source_target_pairs={{8,0},{16,8},{24,16},{32,24},{40,32},{48,40},{56,48},{64,56},{72,6... | collective-permute-start | bytes 49160 | tf_op jit(solution)/shard_map/ppermute | solution.py:220
  102.5 1.6 %fusion.12.g3_ref = f32[80,8,128]{2,1,0:T(8,128)} fusion(f32[80,12,132]{2,1,0:T(8,128)S(1)} %copy-done.16, f32[80,12,132]{2,1,0:T(8,128)S(1)} %copy-done.15, f32[80,10,130]{2,1,0:T(8,128)S(1)} %get-tuple-element.34, f32[80,12,132]{2,1,0:T(8,128)S(1)} %copy-done.3), kind=kLoop, calls=%fused_computation.39 | loop fusion | flops 1064960 | bytes 3604480 | tf_op jit(solution)/shard_map/mul | solution.py:57
  104.1 0.1 copy-done.14
  104.2 1.6 %fusion.19.g2_ref = f32[80,8,128]{2,1,0:T(8,128)} fusion(f32[80,12,132]{2,1,0:T(8,128)S(1)} %copy-done.13, f32[80,12,132]{2,1,0:T(8,128)S(1)} %copy-done.14, f32[80,10,130]{2,1,0:T(8,128)S(1)} %get-tuple-element.36, f32[80,12,132]{2,1,0:T(8,128)S(1)} %copy-done.3), kind=kLoop, calls=%fused_computation.52 | loop fusion | flops 1064960 | bytes 3604480 | tf_op jit(solution)/shard_map/mul | solution.py:57
  105.8 4.4 %shard_map.121 = f32[4,80,8,128]{3,2,1,0:T(8,128)} custom-call(f32[80]{0:T(128)} %th_ref.3, f32[2,80,8,128]{3,2,1,0:T(8,128)} %vel_ref.1, f32[2,80,8,128]{3,2,1,0:T(8,128)} %tra_ref.1, f32[80,8,128]{2,1,0:T(8,128)} %copy-done.11, f32[80,8,128]{2,1,0:T(8,128)} %copy-done.12, f32[80,8,128]{2,1,0:T(8,128)} %fusion.19.g2_ref, f32[80,8,128]{2,1,0:T(8,128)} %fusion.12.g3_ref, ...), custom_call_target="tpu_custom_call" | custom-call | tf_op jit(solution)/shard_map/pallas_call | solution.py:365
  110.2 1.3 multiply_reduce_fusion
  111.5 0.1 bitcast_dynamic-update-slice_fusion.7
  111.6 2.1 %collective-permute-start.10 = (f32[8,8,256]{2,1,0:T(8,128)S(1)}, f32[8,8,256]{2,1,0:T(8,128)S(1)}, u32[]{:S(2)}, u32[]{:S(2)}) collective-permute-start(f32[8,8,256]{2,1,0:T(8,128)S(1)} %get-tuple-element.11), channel_id=1, source_target_pairs={{0,7},{1,0},{2,1},{3,2},{4,3},{5,4},{6,5},{7,6},{8,15},{9,8},{10,9... | collective-permute-start | bytes 196616 | tf_op jit(solution)/shard_map/ppermute | solution.py:227
  113.8 2.3 %collective-permute-start.11 = (f32[8,8,256]{2,1,0:T(8,128)S(1)}, f32[8,8,256]{2,1,0:T(8,128)S(1)}, u32[]{:S(2)}, u32[]{:S(2)}) collective-permute-start(f32[8,8,256]{2,1,0:T(8,128)S(1)} %get-tuple-element.11), channel_id=1, source_target_pairs={{0,6},{1,7},{2,0},{3,1},{4,2},{5,3},{6,4},{7,5},{8,14},{9,15},{10,... | collective-permute-start | bytes 196616 | tf_op jit(solution)/shard_map/ppermute | solution.py:227
  116.1 9.6 %collective-permute-start.12 = (f32[8,8,256]{2,1,0:T(8,128)S(1)}, f32[8,8,256]{2,1,0:T(8,128)S(1)}, u32[]{:S(2)}, u32[]{:S(2)}) collective-permute-start(f32[8,8,256]{2,1,0:T(8,128)S(1)} %get-tuple-element.11), channel_id=1, source_target_pairs={{0,5},{1,6},{2,7},{3,0},{4,1},{5,2},{6,3},{7,4},{8,13},{9,14},{10,... | collective-permute-start | bytes 196616 | tf_op jit(solution)/shard_map/ppermute | solution.py:227
  125.7 0.1 collective-permute-start.14
  125.8 3.6 %collective-permute-start.15 = (f32[8,8,256]{2,1,0:T(8,128)S(1)}, f32[8,8,256]{2,1,0:T(8,128)S(1)}, u32[]{:S(2)}, u32[]{:S(2)}) collective-permute-start(f32[8,8,256]{2,1,0:T(8,128)S(1)} %get-tuple-element.11), channel_id=1, source_target_pairs={{0,2},{1,3},{2,4},{3,5},{4,6},{5,7},{6,0},{7,1},{8,10},{9,11},{10,... | collective-permute-start | bytes 196616 | tf_op jit(solution)/shard_map/ppermute | solution.py:227
  129.4 1.5 %collective-permute-start.16 = (f32[8,8,256]{2,1,0:T(8,128)S(1)}, f32[8,8,256]{2,1,0:T(8,128)S(1)}, u32[]{:S(2)}, u32[]{:S(2)}) collective-permute-start(f32[8,8,256]{2,1,0:T(8,128)S(1)} %get-tuple-element.11), channel_id=1, source_target_pairs={{0,1},{1,2},{2,3},{3,4},{4,5},{5,6},{6,7},{7,0},{8,9},{9,10},{10,1... | collective-permute-start | bytes 196616 | tf_op jit(solution)/shard_map/ppermute | solution.py:227
  131.0 3.7 %collective-permute-done.16 = f32[8,8,256]{2,1,0:T(8,128)S(1)} collective-permute-done((f32[8,8,256]{2,1,0:T(8,128)S(1)}, f32[8,8,256]{2,1,0:T(8,128)S(1)}, u32[]{:S(2)}, u32[]{:S(2)}) %collective-permute-start.16) | collective-permute-done | bytes 65568 | tf_op jit(solution)/shard_map/ppermute | solution.py:227
  134.7 0.8 copy-done.22
  135.5 8.5 %shard_map.122 = (f32[8,128]{1,0:T(8,128)}, f32[2,8,128]{2,1,0:T(8,128)}, f32[2,8,128]{2,1,0:T(8,128)}) custom-call(s32[1]{0:T(128)} %bitcast.5.off_ref, f32[8,8,8,256]{3,2,1,0:T(8,128)} %copy-done.22), custom_call_target="tpu_custom_call" | custom-call | tf_op jit(solution)/shard_map/pallas_call | solution.py:286
  144.0 1.8 %fusion.62 = (f32[2,80,8,128]{3,2,1,0:T(8,128)}, f32[2,80,8,128]{3,2,1,0:T(8,128)}) fusion(f32[4,80,8,128]{3,2,1,0:T(8,128)S(1)} %copy-done.4, f32[80,8,128]{2,1,0:T(8,128)S(1)} %copy-done.10, f32[2,8,128]{2,1,0:T(8,128)} %get-tuple-element.7, f32[2,8,128]{2,1,0:T(8,128)S(1)} %broadcast_divide_fusion), kind=kLoop, calls=%fused_computation.141 | loop fusion | flops 491520 | bytes 2965504 | tf_op jit(solution)/shard_map/slice | solution.py:208
  (75 shorter events, 0.2 us)
Async XLA Ops:
  0.6 3.1 %copy-start.20 = (f32[2,80,8,128]{3,2,1,0:T(8,128)S(1)}, f32[2,80,8,128]{3,2,1,0:T(8,128)}, u32[]{:S(2)}) copy-start(f32[2,80,8,128]{3,2,1,0:T(8,128)} %vel_ref.1) | copy-start | bytes 1966084
  2.1 3.0 %copy-start.19 = (f32[1,80,8,128]{3,2,1,0:T(8,128)}, f32[1,80,8,128]{3,2,1,0:T(8,128)S(1)}, u32[]{:S(2)}) copy-start(f32[1,80,8,128]{3,2,1,0:T(8,128)S(1)} %fusion.44) | copy-start | bytes 983044
  3.8 1.3 copy-start.9
  5.1 0.8 copy-start.5
  5.1 1.0 copy-start.6
  8.4 25.1 %collective-permute-start = (f32[5,80,2,2]{3,2,1,0:T(2,128)}, f32[5,80,2,2]{3,2,1,0:T(2,128)}, u32[]{:S(2)}, u32[]{:S(2)}) collective-permute-start(f32[5,80,2,2]{3,2,1,0:T(2,128)} %get-tuple-element.24), channel_id=1, source_target_pairs={{0,9},{1,10},{2,11},{3,12},{4,13},{5,14},{6,15},{8,17},{9,18},{10,... | collective-permute-start | bytes 19208 | tf_op jit(solution)/shard_map/ppermute | solution.py:161
  18.6 20.6 %collective-permute-start.3 = (f32[5,80,8,2]{1,2,3,0:T(8,128)S(1)}, f32[5,80,8,2]{1,2,3,0:T(8,128)S(1)}, u32[]{:S(2)}, u32[]{:S(2)}) collective-permute-start(f32[5,80,8,2]{1,2,3,0:T(8,128)S(1)} %copy.13), channel_id=1, source_target_pairs={{0,8},{8,16},{16,24},{24,32},{32,40},{40,48},{48,56},{56,64},{64,7... | collective-permute-start | bytes 76808 | tf_op jit(solution)/shard_map/ppermute | solution.py:152
  19.9 12.3 %copy-start.24 = (f32[80]{0:T(128)S(1)}, f32[80]{0:T(128)}, u32[]{:S(2)}) copy-start(f32[80]{0:T(128)} %th_ref.3) | copy-start | bytes 964
  19.9 13.6 %copy-start.23 = (s32[8,128]{1,0:T(8,128)S(1)}, s32[8,128]{1,0:T(8,128)}, u32[]{:S(2)}) copy-start(s32[8,128]{1,0:T(8,128)} %param.14) | copy-start | bytes 12292
  19.9 33.6 %copy-start.28 = (f32[8]{0:T(128)S(1)}, f32[8]{0:T(128)}, u32[]{:S(2)}) copy-start(f32[8]{0:T(128)} %param.13) | copy-start | bytes 100
  20.5 21.1 %collective-permute-start.4 = (f32[5,80,8,2]{1,2,3,0:T(8,128)S(1)}, f32[5,80,8,2]{1,2,3,0:T(8,128)S(1)}, u32[]{:S(2)}, u32[]{:S(2)}) collective-permute-start(f32[5,80,8,2]{1,2,3,0:T(8,128)S(1)} %copy.14), channel_id=1, source_target_pairs={{0,248},{8,0},{16,8},{24,16},{32,24},{40,32},{48,40},{56,48},{64,5... | collective-permute-start | bytes 76808 | tf_op jit(solution)/shard_map/ppermute | solution.py:152
  25.1 40.2 %collective-permute-start.1 = (f32[5,80,2,128]{3,2,1,0:T(2,128)}, f32[5,80,2,128]{3,2,1,0:T(2,128)}, u32[]{:S(2)}, u32[]{:S(2)}) collective-permute-start(f32[5,80,2,128]{3,2,1,0:T(2,128)} %get-tuple-element.28), channel_id=1, source_target_pairs={{0,1},{1,2},{2,3},{3,4},{4,5},{5,6},{6,7},{8,9},{9,10},{10,11},{11... | collective-permute-start | bytes 1228808 | tf_op jit(solution)/shard_map/ppermute | solution.py:160
  29.3 36.0 %collective-permute-start.6 = (f32[5,80,2,128]{3,2,1,0:T(2,128)}, f32[5,80,2,128]{3,2,1,0:T(2,128)}, u32[]{:S(2)}, u32[]{:S(2)}) collective-permute-start(f32[5,80,2,128]{3,2,1,0:T(2,128)} %get-tuple-element.29), channel_id=1, source_target_pairs={{1,0},{2,1},{3,2},{4,3},{5,4},{6,5},{7,6},{9,8},{10,9},{11,10},{12... | collective-permute-start | bytes 1228808 | tf_op jit(solution)/shard_map/ppermute | solution.py:160
  33.5 21.3 %collective-permute-start.2 = (f32[5,80,2,2]{3,2,1,0:T(2,128)}, f32[5,80,2,2]{3,2,1,0:T(2,128)}, u32[]{:S(2)}, u32[]{:S(2)}) collective-permute-start(f32[5,80,2,2]{3,2,1,0:T(2,128)} %get-tuple-element.27), channel_id=1, source_target_pairs={{0,249},{1,250},{2,251},{3,252},{4,253},{5,254},{6,255},{8,1},{9,2... | collective-permute-start | bytes 19208 | tf_op jit(solution)/shard_map/ppermute | solution.py:161
  39.2 26.1 %collective-permute-start.5 = (f32[5,80,2,2]{3,2,1,0:T(2,128)}, f32[5,80,2,2]{3,2,1,0:T(2,128)}, u32[]{:S(2)}, u32[]{:S(2)}) collective-permute-start(f32[5,80,2,2]{3,2,1,0:T(2,128)} %get-tuple-element.25), channel_id=1, source_target_pairs={{1,8},{2,9},{3,10},{4,11},{5,12},{6,13},{7,14},{9,16},{10,17},{11,... | collective-permute-start | bytes 19208 | tf_op jit(solution)/shard_map/ppermute | solution.py:161
  41.5 23.8 %collective-permute-start.7 = (f32[5,80,2,2]{3,2,1,0:T(2,128)}, f32[5,80,2,2]{3,2,1,0:T(2,128)}, u32[]{:S(2)}, u32[]{:S(2)}) collective-permute-start(f32[5,80,2,2]{3,2,1,0:T(2,128)} %get-tuple-element.26), channel_id=1, source_target_pairs={{1,248},{2,249},{3,250},{4,251},{5,252},{6,253},{7,254},{9,0},{10,... | collective-permute-start | bytes 19208 | tf_op jit(solution)/shard_map/ppermute | solution.py:161
  74.9 3.9 %copy-start = (f32[5,80,12,132]{3,2,1,0:T(8,128)}, f32[5,80,12,132]{3,2,1,0:T(8,128)S(1)}, u32[]{:S(2)}) copy-start(f32[5,80,12,132]{3,2,1,0:T(8,128)S(1)} %maximum_maximum_fusion.pad_ref) | copy-start | bytes 7603204
  86.9 3.2 %copy-start.1 = (f32[80,12,132]{2,1,0:T(8,128)S(1)}, f32[80,12,132]{2,1,0:T(8,128)}, u32[]{:S(2)}) copy-start(f32[80,12,132]{2,1,0:T(8,128)} %get-tuple-element.12) | copy-start | bytes 1520644
  86.9 3.2 %copy-start.2 = (f32[80,12,132]{2,1,0:T(8,128)S(1)}, f32[80,12,132]{2,1,0:T(8,128)}, u32[]{:S(2)}) copy-start(f32[80,12,132]{2,1,0:T(8,128)} %get-tuple-element.13) | copy-start | bytes 1520644
  86.9 3.2 %copy-start.3 = (f32[80,12,132]{2,1,0:T(8,128)S(1)}, f32[80,12,132]{2,1,0:T(8,128)}, u32[]{:S(2)}) copy-start(f32[80,12,132]{2,1,0:T(8,128)} %get-tuple-element.14) | copy-start | bytes 1520644
  90.2 4.7 %copy-start.7 = (f32[80,12,132]{2,1,0:T(8,128)S(1)}, f32[80,12,132]{2,1,0:T(8,128)}, u32[]{:S(2)}) copy-start(f32[80,12,132]{2,1,0:T(8,128)} %get-tuple-element.19) | copy-start | bytes 1520644
  90.2 4.7 %copy-start.8 = (f32[80,12,132]{2,1,0:T(8,128)S(1)}, f32[80,12,132]{2,1,0:T(8,128)}, u32[]{:S(2)}) copy-start(f32[80,12,132]{2,1,0:T(8,128)} %shard_map.120) | copy-start | bytes 1520644
  90.2 4.7 %copy-start.18 = (f32[80,12,132]{2,1,0:T(8,128)S(1)}, f32[80,12,132]{2,1,0:T(8,128)}, u32[]{:S(2)}) copy-start(f32[80,12,132]{2,1,0:T(8,128)} %get-tuple-element.18) | copy-start | bytes 1520644
  94.9 1.3 copy-start.17
  96.0 1.3 copy-start.11
  96.2 1.1 copy-start.25
  96.2 1.3 copy-start.27
  96.2 1.4 copy-start.26
  96.2 6.3 %copy-start.15 = (f32[80,12,132]{2,1,0:T(8,128)S(1)}, f32[80,12,132]{2,1,0:T(8,128)}, u32[]{:S(2)}) copy-start(f32[80,12,132]{2,1,0:T(8,128)} %get-tuple-element.17) | copy-start | bytes 1520644
  96.2 6.3 %copy-start.16 = (f32[80,12,132]{2,1,0:T(8,128)S(1)}, f32[80,12,132]{2,1,0:T(8,128)}, u32[]{:S(2)}) copy-start(f32[80,12,132]{2,1,0:T(8,128)} %get-tuple-element.21) | copy-start | bytes 1520644
  97.3 6.8 %copy-start.12 = (f32[80,8,128]{2,1,0:T(8,128)}, f32[80,8,128]{2,1,0:T(8,128)S(1)}, u32[]{:S(2)}) copy-start(f32[80,8,128]{2,1,0:T(8,128)S(1)} %fusion.26.g1_ref) | copy-start | bytes 983044
  97.7 13.9 %collective-permute-start.8 = (f32[8,8,64]{2,1,0:T(8,128)S(1)}, f32[8,8,64]{2,1,0:T(8,128)S(1)}, u32[]{:S(2)}, u32[]{:S(2)}) collective-permute-start(f32[8,8,64]{2,1,0:T(8,128)S(1)} %get-tuple-element.39), channel_id=1, source_target_pairs={{0,8},{8,16},{16,24},{24,32},{32,40},{40,48},{48,56},{56,64},{64,7... | collective-permute-start | bytes 49160 | tf_op jit(solution)/shard_map/ppermute | solution.py:219
  99.1 12.4 %collective-permute-start.9 = (f32[8,8,64]{2,1,0:T(8,128)S(1)}, f32[8,8,64]{2,1,0:T(8,128)S(1)}, u32[]{:S(2)}, u32[]{:S(2)}) collective-permute-start(f32[8,8,64]{2,1,0:T(8,128)S(1)} %get-tuple-element.40), channel_id=1, source_target_pairs={{8,0},{16,8},{24,16},{32,24},{40,32},{48,40},{56,48},{64,56},{72,6... | collective-permute-start | bytes 49160 | tf_op jit(solution)/shard_map/ppermute | solution.py:220
  102.5 1.6 %copy-start.13 = (f32[80,12,132]{2,1,0:T(8,128)S(1)}, f32[80,12,132]{2,1,0:T(8,128)}, u32[]{:S(2)}) copy-start(f32[80,12,132]{2,1,0:T(8,128)} %get-tuple-element.22) | copy-start | bytes 1520644
  102.5 1.7 %copy-start.14 = (f32[80,12,132]{2,1,0:T(8,128)S(1)}, f32[80,12,132]{2,1,0:T(8,128)}, u32[]{:S(2)}) copy-start(f32[80,12,132]{2,1,0:T(8,128)} %get-tuple-element.23) | copy-start | bytes 1520644
  105.8 4.4 %copy-start.21 = (f32[80,8,128]{2,1,0:T(8,128)S(1)}, f32[80,8,128]{2,1,0:T(8,128)}, u32[]{:S(2)}) copy-start(f32[80,8,128]{2,1,0:T(8,128)} %get-tuple-element.41) | copy-start | bytes 983044
  110.2 33.8 %copy-start.4 = (f32[4,80,8,128]{3,2,1,0:T(8,128)S(1)}, f32[4,80,8,128]{3,2,1,0:T(8,128)}, u32[]{:S(2)}) copy-start(f32[4,80,8,128]{3,2,1,0:T(8,128)} %shard_map.121) | copy-start | bytes 3932164
  110.2 33.8 %copy-start.10 = (f32[80,8,128]{2,1,0:T(8,128)S(1)}, f32[80,8,128]{2,1,0:T(8,128)}, u32[]{:S(2)}) copy-start(f32[80,8,128]{2,1,0:T(8,128)} %copy-done.9) | copy-start | bytes 983044
  111.6 14.2 %collective-permute-start.10 = (f32[8,8,256]{2,1,0:T(8,128)S(1)}, f32[8,8,256]{2,1,0:T(8,128)S(1)}, u32[]{:S(2)}, u32[]{:S(2)}) collective-permute-start(f32[8,8,256]{2,1,0:T(8,128)S(1)} %get-tuple-element.11), channel_id=1, source_target_pairs={{0,7},{1,0},{2,1},{3,2},{4,3},{5,4},{6,5},{7,6},{8,15},{9,8},{10,9... | collective-permute-start | bytes 196616 | tf_op jit(solution)/shard_map/ppermute | solution.py:227
  113.8 15.6 %collective-permute-start.11 = (f32[8,8,256]{2,1,0:T(8,128)S(1)}, f32[8,8,256]{2,1,0:T(8,128)S(1)}, u32[]{:S(2)}, u32[]{:S(2)}) collective-permute-start(f32[8,8,256]{2,1,0:T(8,128)S(1)} %get-tuple-element.11), channel_id=1, source_target_pairs={{0,6},{1,7},{2,0},{3,1},{4,2},{5,3},{6,4},{7,5},{8,14},{9,15},{10,... | collective-permute-start | bytes 196616 | tf_op jit(solution)/shard_map/ppermute | solution.py:227
  116.1 14.8 %collective-permute-start.12 = (f32[8,8,256]{2,1,0:T(8,128)S(1)}, f32[8,8,256]{2,1,0:T(8,128)S(1)}, u32[]{:S(2)}, u32[]{:S(2)}) collective-permute-start(f32[8,8,256]{2,1,0:T(8,128)S(1)} %get-tuple-element.11), channel_id=1, source_target_pairs={{0,5},{1,6},{2,7},{3,0},{4,1},{5,2},{6,3},{7,4},{8,13},{9,14},{10,... | collective-permute-start | bytes 196616 | tf_op jit(solution)/shard_map/ppermute | solution.py:227
  125.7 5.2 %collective-permute-start.13 = (f32[8,8,256]{2,1,0:T(8,128)S(1)}, f32[8,8,256]{2,1,0:T(8,128)S(1)}, u32[]{:S(2)}, u32[]{:S(2)}) collective-permute-start(f32[8,8,256]{2,1,0:T(8,128)S(1)} %get-tuple-element.11), channel_id=1, source_target_pairs={{0,4},{1,5},{2,6},{3,7},{4,0},{5,1},{6,2},{7,3},{8,12},{9,13},{10,... | collective-permute-start | bytes 196616 | tf_op jit(solution)/shard_map/ppermute | solution.py:227
  125.7 5.3 %collective-permute-start.14 = (f32[8,8,256]{2,1,0:T(8,128)S(1)}, f32[8,8,256]{2,1,0:T(8,128)S(1)}, u32[]{:S(2)}, u32[]{:S(2)}) collective-permute-start(f32[8,8,256]{2,1,0:T(8,128)S(1)} %get-tuple-element.11), channel_id=1, source_target_pairs={{0,3},{1,4},{2,5},{3,6},{4,7},{5,0},{6,1},{7,2},{8,11},{9,12},{10,... | collective-permute-start | bytes 196616 | tf_op jit(solution)/shard_map/ppermute | solution.py:227
  125.8 5.2 %collective-permute-start.15 = (f32[8,8,256]{2,1,0:T(8,128)S(1)}, f32[8,8,256]{2,1,0:T(8,128)S(1)}, u32[]{:S(2)}, u32[]{:S(2)}) collective-permute-start(f32[8,8,256]{2,1,0:T(8,128)S(1)} %get-tuple-element.11), channel_id=1, source_target_pairs={{0,2},{1,3},{2,4},{3,5},{4,6},{5,7},{6,0},{7,1},{8,10},{9,11},{10,... | collective-permute-start | bytes 196616 | tf_op jit(solution)/shard_map/ppermute | solution.py:227
  129.4 5.3 %collective-permute-start.16 = (f32[8,8,256]{2,1,0:T(8,128)S(1)}, f32[8,8,256]{2,1,0:T(8,128)S(1)}, u32[]{:S(2)}, u32[]{:S(2)}) collective-permute-start(f32[8,8,256]{2,1,0:T(8,128)S(1)} %get-tuple-element.11), channel_id=1, source_target_pairs={{0,1},{1,2},{2,3},{3,4},{4,5},{5,6},{6,7},{7,0},{8,9},{9,10},{10,1... | collective-permute-start | bytes 196616 | tf_op jit(solution)/shard_map/ppermute | solution.py:227
  134.7 0.8 copy-start.22
